TPU v7x, 128 devices: a whole 4x4x4 slice. The times are simulated.
128 devices in a mesh: gx: 8 (over z, core), gy: 16 (over y, x).
Axes of the slice: x: 4, y: 4, z: 4, core: 2. Of those that a mesh axis runs over, the one named last changes fastest.
Arguments:
- atm_state: float32 [128, 512, 4096], P(None, 'gy', 'gx'), may hold values from -6 to 6
- atm_kappa: float32 [128], replicated, may hold values from 0.05 to 0.24
- vert_weight: float32 [4, 128], replicated, may hold values from -0.5 to 0.5
- remap_src: int32 [4096, 4], replicated, may hold values from 0 to 16383, as said below
- remap_count: int32 [4096], replicated, may hold values from 2 to 4, as said below
- remap_weight: bfloat16 [4096, 4, 128, 128], P(('gx', 'gy')), may hold values from -1 to 1
- land_mask: int32 [256, 2048], P('gy', 'gx'), may hold values from 0 to 1
- ocean_term: float32 [256, 2048], P('gy', 'gx'), may hold values from 0.5 to 8
Outputs:
- atm_out: float32 [128, 512, 4096], P(None, 'gy', 'gx')
- ocean_flux: float32 [4, 256, 2048], P(None, 'gy', 'gx')
- surface_height: float32 [256, 2048], P('gy', 'gx')
- residual: float32 [256, 2048], P('gy', 'gx')
Inputs may be any that keep to these rules, and one draw needn't show every extreme that they name: `remap_src`: entries are global atmosphere block numbers covering the ocean block's area: each names a block of the atmosphere device with the same tile indices or of the next device along gx (gx index plus one, the last wrapping to 0, same gy index). Among the live entries of the 32 ocean blocks of one device, exactly 32 name blocks of the next device. `remap_count`: the first ocean block of every device has all 4 entries live.
All inputs are finite; a program needn't handle non-finite values.
Results may differ from a plain program's by a relative error of at most 0.003.
Values may be sent and summed in bfloat16 or wider, within the bound.
No kernel may reach another device: no remote copies, remote signals or barrier semaphores. Data moves between devices by JAX's collectives and lax.ppermute only.
A program may use at most 128 MiB of HBM per device.

v0:
```python
import jax
import jax.numpy as jnp
from jax import lax
from jax.sharding import PartitionSpec as P

STEPS = 4
ITERS = 3


def with_halo(x, sides, width):
    for axis, dim in sides:
        size, length = (lax.axis_size(axis), x.shape[dim])
        up = [(i, (i + 1) % size) for i in range(size - 1)]
        down = [(j, i) for i, j in up]
        last = lax.slice_in_dim(x, length - width, length, axis=dim)
        first = lax.slice_in_dim(x, 0, width, axis=dim)
        before = lax.ppermute(last, axis, up)
        after = lax.ppermute(first, axis, down)
        x = jnp.concatenate([before, x, after], axis=dim)
    return x


def shifted(x, axis, by):
    size = lax.axis_size(axis)
    return lax.ppermute(x, axis, [(i, (i + by) % size) for i in range(size)])


def ocean_operator(vector, maskf, ocean_term):
    padded = with_halo(maskf * vector, (("gx", 1), ("gy", 0)), 1)
    beside = padded[2:, 1:-1] + padded[:-2, 1:-1] + padded[1:-1, 2:] + padded[1:-1, :-2]
    return maskf * ((4.0 + ocean_term) * vector - beside) + (1.0 - maskf) * vector


def square_total(residual):
    return lax.psum(jnp.sum(residual * residual), ("gx", "gy"))


def doubling_gather(x, axis, dim):
    size = lax.axis_size(axis)
    index = lax.axis_index(axis)
    distance = 1
    while distance < size:
        other = lax.ppermute(x, axis, [(j, j ^ distance) for j in range(size)])
        low = jnp.concatenate([x, other], axis=dim)
        high = jnp.concatenate([other, x], axis=dim)
        x = jnp.where((index & distance) == 0, low, high)
        distance *= 2
    return x


def whole_grid(tile):
    return doubling_gather(doubling_gather(tile, "gx", 1), "gy", 0)


def grid_operator(vector, maskf, ocean_term):
    padded = jnp.pad(maskf * vector, 1)
    beside = padded[2:, 1:-1] + padded[:-2, 1:-1] + padded[1:-1, 2:] + padded[1:-1, :-2]
    return maskf * ((4.0 + ocean_term) * vector - beside) + (1.0 - maskf) * vector


def body(
    atm_state, atm_kappa, vert_weight, remap_src, remap_count, remap_weight, land_mask, ocean_term
):
    levels, tile_lat, tile_lon = atm_state.shape
    kappa = atm_kappa[:, None, None]
    count_gx = lax.axis_size("gx")
    count_gy = lax.axis_size("gy")
    coded_all = whole_grid(jnp.where(land_mask != 0, ocean_term, -1.0))
    maskf = (coded_all >= 0.0).astype(jnp.float32)
    field = atm_state
    for step in range(STEPS):
        padded = with_halo(field, (("gx", 2), ("gy", 1)), 1)
        lap = (
            padded[:, 2:, 1:-1]
            + padded[:, :-2, 1:-1]
            + padded[:, 1:-1, 2:]
            + padded[:, 1:-1, :-2]
            - 4.0 * field
        )
        field = field + kappa * lap
    flux = jnp.dot(
        vert_weight,
        field.reshape(levels, tile_lat * tile_lon),
        precision=lax.Precision.HIGHEST,
        preferred_element_type=jnp.float32,
    )
    ocean_blocks, lists, width, _ = remap_weight.shape
    comps = vert_weight.shape[0]
    own_blocks = tile_lat * tile_lon // width
    blocks = flux.astype(jnp.bfloat16).reshape(comps, own_blocks, width).transpose(1, 0, 2)
    devices = count_gx * count_gy
    gx_index = lax.axis_index("gx")
    gy_index = lax.axis_index("gy")
    me_index = gx_index * count_gy + gy_index
    east_index = (gx_index + 1) % count_gx * count_gy + gy_index
    west_index = (gx_index + count_gx - 1) % count_gx * count_gy + gy_index
    entries = ocean_blocks * lists
    slots = 2 * land_mask.shape[0]
    src_all = remap_src.reshape(devices, entries)
    live_all = (
        jnp.arange(lists, dtype=jnp.int32)[None, None, :]
        < remap_count.reshape(devices, ocean_blocks)[:, :, None]
    ).reshape(devices, entries)
    owner_all = src_all // own_blocks
    inside_all = src_all % own_blocks
    mine_owner = lax.dynamic_slice_in_dim(owner_all, me_index, 1, 0)[0]
    mine_inside = lax.dynamic_slice_in_dim(inside_all, me_index, 1, 0)[0]
    mine_live = lax.dynamic_slice_in_dim(live_all, me_index, 1, 0)[0]
    from_east = mine_live & (mine_owner == east_index)
    from_self = mine_live & (mine_owner == me_index)
    local_part = blocks[jnp.where(from_self, mine_inside, 0)]
    west_owner = lax.dynamic_slice_in_dim(owner_all, west_index, 1, 0)[0]
    west_inside = lax.dynamic_slice_in_dim(inside_all, west_index, 1, 0)[0]
    west_live = lax.dynamic_slice_in_dim(live_all, west_index, 1, 0)[0]
    wanted = (west_live & (west_owner == me_index)).astype(jnp.int32)
    wanted_rank = jnp.cumsum(wanted) - 1
    slot_ids = jnp.arange(slots, dtype=jnp.int32)
    picker = wanted[None, :] * (wanted_rank[None, :] == slot_ids[:, None]).astype(jnp.int32)
    send_index = jnp.sum(picker * west_inside[None, :], axis=1)
    send_valid = jnp.sum(picker, axis=1).astype(jnp.bfloat16)
    outgoing = blocks[send_index] * send_valid[:, None, None]
    incoming = shifted(outgoing, "gx", -1)
    east_int = from_east.astype(jnp.int32)
    east_rank = jnp.cumsum(east_int) - 1
    remote_part = incoming[jnp.where(from_east, east_rank, 0)]
    gathered = jnp.where(
        from_self[:, None, None],
        local_part,
        jnp.where(from_east[:, None, None], remote_part, jnp.zeros_like(local_part)),
    )
    gathered = gathered.reshape(ocean_blocks, lists, comps, width)
    ocean_rows, ocean_cols = land_mask.shape
    remapped = jnp.einsum(
        "bkij,bkcj->cbi", remap_weight, gathered, preferred_element_type=jnp.float32
    )
    ocean_flux = remapped.reshape(comps, ocean_rows, ocean_cols)
    rhs_tile = land_mask.astype(jnp.float32) * (ocean_flux[0] + ocean_flux[1])
    rhs = whole_grid(rhs_tile)
    height = jnp.zeros_like(rhs)
    residual = rhs
    direction = rhs
    norm_now = jnp.sum(residual * residual)
    for step in range(ITERS):
        image = grid_operator(direction, maskf, coded_all)
        alpha = norm_now / jnp.sum(direction * image)
        height = height + alpha * direction
        residual = residual - alpha * image
        norm_next = jnp.sum(residual * residual)
        direction = residual + norm_next / norm_now * direction
        norm_now = norm_next
    height = lax.dynamic_slice(height, (gy_index * ocean_rows, gx_index * ocean_cols), (ocean_rows, ocean_cols))
    residual = lax.dynamic_slice(residual, (gy_index * ocean_rows, gx_index * ocean_cols), (ocean_rows, ocean_cols))
    return (field, ocean_flux, height, residual)


def solution(mesh):
    return jax.shard_map(
        body,
        mesh=mesh,
        in_specs=(
            P(None, "gy", "gx"),
            P(),
            P(),
            P(),
            P(),
            P(("gx", "gy"), None, None, None),
            P("gy", "gx"),
            P("gy", "gx"),
        ),
        out_specs=(P(None, "gy", "gx"), P(None, "gy", "gx"), P("gy", "gx"), P("gy", "gx")),
        check_vma=False,
    )
```

profile of v0, /device:TPU:6, one launch (start us, length us, event | category | flops | bytes accessed | tf_op | source)
XLA Modules:
  0.0 324.9 jit_solution(92662217561911953)
XLA Ops:
  0.6 4.3 %fusion.68 = (f32[128,32,1]{2,1,0:T(8,128)S(1)}, f32[128,32,1]{2,1,0:T(8,128)}) fusion(f32[128,32,512]{2,1,0:T(8,128)} %param.8), kind=kLoop, calls=%fused_computation.187 | loop fusion | bytes 65536 | tf_op jit(solution)/shard_map/slice | solution.py:16
  4.9 2.7 copy.137
  7.6 1.7 collective-permute-start
  9.3 1.4 copy.138
  10.7 1.4 collective-permute-start.1
  12.1 10.0 %copy.102 = f32[128,32,512]{0,2,1:T(8,128)} copy(f32[128,32,512]{2,1,0:T(8,128)} %param.8) | data formatting | bytes 16777216 | tf_op args[0]
  23.5 2.7 collective-permute-start.2
  26.3 5.2 %collective-permute-start.3 = (f32[128,1,514]{0,2,1:T(8,128)S(1)}, f32[128,1,514]{0,2,1:T(8,128)S(1)}, u32[]{:S(2)}, u32[]{:S(2)}) collective-permute-start(f32[128,1,514]{0,2,1:T(8,128)S(1)} %get-tuple-element.43), channel_id=1, source_target_pairs={{0,1},{1,2},{2,3},{3,4},{4,5},{5,6},{6,7},{7,8},{8,9},{9,10},{10,1... | collective-permute-start | bytes 789512 | tf_op jit(solution)/shard_map/ppermute | solution.py:17
  32.3 1.7 reshape.211
  34.9 1.7 collective-permute-done.3
  36.6 19.9 %fusion.21 = f32[128,32,512]{0,2,1:T(8,128)S(1)} fusion(f32[128,32,512]{0,2,1:T(8,128)} %copy.102, f32[128,32,1]{0,2,1:T(1,128)S(1)} %bitcast.59, f32[128,32,1]{0,2,1:T(1,128)S(1)} %bitcast.61, f32[128,1,514]{0,2,1:T(8,128)S(1)} %collective-permute-done.3, f32[128,1,514]{0,2,1:T(8,128)S(1)} %collective-permute-done.2, f32[128]{0:T(128)S(1)} %copy-done.21), kind=kLoop, calls=%fused_computation.50 | loop fusion | flops 31457280 | bytes 17336832 | tf_op jit(solution)/shard_map/add | solution.py:80
  56.5 3.4 %copy-done.3 = f32[128,32,512]{0,2,1:T(8,128)} copy-done((f32[128,32,512]{0,2,1:T(8,128)}, f32[128,32,512]{0,2,1:T(8,128)S(1)}, u32[]{:S(2)}) %copy-start.3) | copy-done | bytes 8388632
  59.9 3.7 %collective-permute-start.4 = (f32[128,32,1]{0,1,2:T(8,128)S(1)}, f32[128,32,1]{0,1,2:T(8,128)S(1)}, u32[]{:S(2)}, u32[]{:S(2)}) collective-permute-start(f32[128,32,1]{0,1,2:T(8,128)S(1)} %bitcast.75), channel_id=1, source_target_pairs={{0,16},{16,32},{32,48},{48,64},{64,80},{80,96},{96,112},{1,17},{17... | collective-permute-start | bytes 49160 | tf_op jit(solution)/shard_map/ppermute | solution.py:17
  65.3 4.4 %collective-permute-done.5 = f32[128,32,1]{0,1,2:T(8,128)S(1)} collective-permute-done((f32[128,32,1]{0,1,2:T(8,128)S(1)}, f32[128,32,1]{0,1,2:T(8,128)S(1)}, u32[]{:S(2)}, u32[]{:S(2)}) %collective-permute-start.5) | collective-permute-done | bytes 16416 | tf_op jit(solution)/shard_map/ppermute | solution.py:18
  70.9 2.2 collective-permute-start.6
  73.1 6.5 %collective-permute-start.7 = (f32[128,1,514]{0,2,1:T(8,128)S(1)}, f32[128,1,514]{0,2,1:T(8,128)S(1)}, u32[]{:S(2)}, u32[]{:S(2)}) collective-permute-start(f32[128,1,514]{0,2,1:T(8,128)S(1)} %get-tuple-element.41), channel_id=1, source_target_pairs={{0,1},{1,2},{2,3},{3,4},{4,5},{5,6},{6,7},{7,8},{8,9},{9,10},{10,1... | collective-permute-start | bytes 789512 | tf_op jit(solution)/shard_map/ppermute | solution.py:17
  79.7 3.3 %collective-permute-done.6 = f32[128,1,514]{0,2,1:T(8,128)S(1)} collective-permute-done((f32[128,1,514]{0,2,1:T(8,128)S(1)}, f32[128,1,514]{0,2,1:T(8,128)S(1)}, u32[]{:S(2)}, u32[]{:S(2)}) %collective-permute-start.6) | collective-permute-done | bytes 263200 | tf_op jit(solution)/shard_map/ppermute | solution.py:18
  83.0 1.7 collective-permute-done.7
  84.8 11.1 %fusion.15 = f32[128,32,512]{0,2,1:T(8,128)S(1)} fusion(f32[128,32,512]{0,2,1:T(8,128)S(1)} %copy-done.4, f32[128,32,1]{0,2,1:T(1,128)S(1)} %bitcast.65, f32[128,32,1]{0,2,1:T(1,128)S(1)} %bitcast.71, f32[128,1,514]{0,2,1:T(8,128)S(1)} %collective-permute-done.7, f32[128,1,514]{0,2,1:T(8,128)S(1)} %collective-permute-done.6, f32[128]{0:T(128)S(1)} %copy-done.21), kind=kLoop, calls=%fused_computation.36 | loop fusion | flops 31457280 | bytes 17336832 | tf_op jit(solution)/shard_map/add | solution.py:80
  95.9 3.6 %collective-permute-start.8 = (f32[128,32,1]{0,1,2:T(8,128)S(1)}, f32[128,32,1]{0,1,2:T(8,128)S(1)}, u32[]{:S(2)}, u32[]{:S(2)}) collective-permute-start(f32[128,32,1]{0,1,2:T(8,128)S(1)} %bitcast.78), channel_id=1, source_target_pairs={{0,16},{16,32},{32,48},{48,64},{64,80},{80,96},{96,112},{1,17},{17... | collective-permute-start | bytes 49160 | tf_op jit(solution)/shard_map/ppermute | solution.py:17
  101.0 2.8 collective-permute-done.9
  103.8 1.9 collective-permute-start.10
  105.8 6.7 %collective-permute-start.11 = (f32[128,1,514]{0,2,1:T(8,128)S(1)}, f32[128,1,514]{0,2,1:T(8,128)S(1)}, u32[]{:S(2)}, u32[]{:S(2)}) collective-permute-start(f32[128,1,514]{0,2,1:T(8,128)S(1)} %get-tuple-element.39), channel_id=1, source_target_pairs={{0,1},{1,2},{2,3},{3,4},{4,5},{5,6},{6,7},{7,8},{8,9},{9,10},{10,1... | collective-permute-start | bytes 789512 | tf_op jit(solution)/shard_map/ppermute | solution.py:17
  112.6 3.1 collective-permute-done.10
  115.7 1.7 collective-permute-done.11
  117.5 11.1 %fusion.9 = f32[128,32,512]{0,2,1:T(8,128)S(1)} fusion(f32[128,32,512]{0,2,1:T(8,128)S(1)} %fusion.15, f32[128,32,1]{0,2,1:T(1,128)S(1)} %bitcast.67, f32[128,32,1]{0,2,1:T(1,128)S(1)} %bitcast.73, f32[128,1,514]{0,2,1:T(8,128)S(1)} %collective-permute-done.11, f32[128,1,514]{0,2,1:T(8,128)S(1)} %collective-permute-done.10, f32[128]{0:T(128)S(1)} %copy-done.21), kind=kLoop, calls=%fused_computation.22 | loop fusion | flops 31457280 | bytes 17336832 | tf_op jit(solution)/shard_map/add | solution.py:80
  128.6 3.6 %collective-permute-start.12 = (f32[128,32,1]{0,1,2:T(8,128)S(1)}, f32[128,32,1]{0,1,2:T(8,128)S(1)}, u32[]{:S(2)}, u32[]{:S(2)}) collective-permute-start(f32[128,32,1]{0,1,2:T(8,128)S(1)} %bitcast.79), channel_id=1, source_target_pairs={{0,16},{16,32},{32,48},{48,64},{64,80},{80,96},{96,112},{1,17},{17... | collective-permute-start | bytes 49160 | tf_op jit(solution)/shard_map/ppermute | solution.py:17
  133.7 2.5 collective-permute-done.13
  136.3 1.9 collective-permute-start.14
  138.2 6.5 %collective-permute-start.15 = (f32[128,1,514]{0,2,1:T(8,128)S(1)}, f32[128,1,514]{0,2,1:T(8,128)S(1)}, u32[]{:S(2)}, u32[]{:S(2)}) collective-permute-start(f32[128,1,514]{0,2,1:T(8,128)S(1)} %get-tuple-element.37), channel_id=1, source_target_pairs={{0,1},{1,2},{2,3},{3,4},{4,5},{5,6},{6,7},{7,8},{8,9},{9,10},{10,1... | collective-permute-start | bytes 789512 | tf_op jit(solution)/shard_map/ppermute | solution.py:17
  145.1 3.0 collective-permute-done.14
  148.1 1.7 collective-permute-done.15
  149.9 19.9 %fusion.3 = f32[128,32,512]{0,2,1:T(8,128)S(1)} fusion(f32[128,32,512]{0,2,1:T(8,128)} %copy-done.2, f32[128,32,1]{0,2,1:T(1,128)S(1)} %bitcast.63, f32[128,32,1]{0,2,1:T(1,128)S(1)} %bitcast.69, f32[128,1,514]{0,2,1:T(8,128)S(1)} %collective-permute-done.15, f32[128,1,514]{0,2,1:T(8,128)S(1)} %collective-permute-done.14, f32[128]{0:T(128)S(1)} %copy-done.21), kind=kLoop, calls=%fused_computation.8 | loop fusion | flops 31457280 | bytes 17336832 | tf_op jit(solution)/shard_map/add | solution.py:80
  169.8 3.2 copy-done.5
  173.0 7.2 %fusion.42 = bf16[128,4,128]{2,1,0:T(4,128)(2,1)S(1)} fusion(f32[128,16384]{0,1:T(8,128)S(1)} %bitcast.54, f32[4,128]{1,0:T(4,128)S(1)} %copy-done), kind=kOutput, calls=%fused_computation.103 | convolution fusion | flops 100728832 | bytes 8521728 | tf_op jit(solution)/shard_map/dot_general | solution.py:81
  181.9 1.4 collective-permute-done.16
  184.1 3.0 convolution_bitcast_fusion
  187.2 2.8 collective-permute-start.24
  190.9 2.3 collective-permute-start.25
  193.5 1.6 collective-permute-done.25
  195.1 2.4 collective-permute-start.26
  198.8 2.7 collective-permute-done.26
  201.6 1.7 collective-permute-done.19
  203.7 4.2 %collective-permute-done.27 = f32[16,2048]{1,0:T(8,128)S(1)} collective-permute-done((f32[16,2048]{1,0:T(8,128)S(1)}, f32[16,2048]{1,0:T(8,128)S(1)}, u32[]{:S(2)}, u32[]{:S(2)}) %collective-permute-start.27) | collective-permute-done | bytes 131104 | tf_op jit(solution)/shard_map/ppermute | solution.py:43
  208.1 2.7 collective-permute-done.20
  211.7 4.5 %collective-permute-done.28 = f32[32,2048]{1,0:T(8,128)S(1)} collective-permute-done((f32[32,2048]{1,0:T(8,128)S(1)}, f32[32,2048]{1,0:T(8,128)S(1)}, u32[]{:S(2)}, u32[]{:S(2)}) %collective-permute-start.28) | collective-permute-done | bytes 262176 | tf_op jit(solution)/shard_map/ppermute | solution.py:43
  216.3 4.5 %collective-permute-start.29 = (f32[64,2048]{1,0:T(8,128)S(1)}, f32[64,2048]{1,0:T(8,128)S(1)}, u32[]{:S(2)}, u32[]{:S(2)}) collective-permute-start(f32[64,2048]{1,0:T(8,128)S(1)} %maximum_select_fusion.5), channel_id=1, source_target_pairs={{0,4},{1,5},{2,6},{3,7},{4,0},{5,1},{6,2},{7,3},{8,12},{9,13},{10,... | collective-permute-start | bytes 1572872 | tf_op jit(solution)/shard_map/ppermute | solution.py:43
  220.8 3.3 %collective-permute-start.22 = (f32[64,2048]{1,0:T(8,128)S(1)}, f32[64,2048]{1,0:T(8,128)}, u32[]{:S(2)}, u32[]{:S(2)}) collective-permute-start(f32[64,2048]{1,0:T(8,128)S(1)} %maximum_select_fusion.4), channel_id=1, source_target_pairs={{0,4},{1,5},{2,6},{3,7},{4,0},{5,1},{6,2},{7,3},{8,12},{9,13},{10,... | collective-permute-start | bytes 1572872 | tf_op jit(solution)/shard_map/ppermute | solution.py:43
  224.2 9.4 %collective-permute-done.29 = f32[64,2048]{1,0:T(8,128)S(1)} collective-permute-done((f32[64,2048]{1,0:T(8,128)S(1)}, f32[64,2048]{1,0:T(8,128)S(1)}, u32[]{:S(2)}, u32[]{:S(2)}) %collective-permute-start.29) | collective-permute-done | bytes 524320 | tf_op jit(solution)/shard_map/ppermute | solution.py:43
  233.7 3.7 %collective-permute-start.30 = (f32[128,2048]{1,0:T(8,128)S(1)}, f32[128,2048]{1,0:T(8,128)S(1)}, u32[]{:S(2)}, u32[]{:S(2)}) collective-permute-start(f32[128,2048]{1,0:T(8,128)S(1)} %maximum_select_fusion.3), channel_id=1, source_target_pairs={{0,8},{1,9},{2,10},{3,11},{4,12},{5,13},{6,14},{7,15},{8,0},{9,1},... | collective-permute-start | bytes 3145736 | tf_op jit(solution)/shard_map/ppermute | solution.py:43
  237.4 7.5 %collective-permute-done.22 = f32[64,2048]{1,0:T(8,128)} collective-permute-done((f32[64,2048]{1,0:T(8,128)S(1)}, f32[64,2048]{1,0:T(8,128)}, u32[]{:S(2)}, u32[]{:S(2)}) %collective-permute-start.22) | collective-permute-done | bytes 524320 | tf_op jit(solution)/shard_map/ppermute | solution.py:43
  245.0 1.7 maximum_select_fusion.2
  246.7 3.7 %collective-permute-start.23 = (f32[128,2048]{1,0:T(8,128)S(1)}, f32[128,2048]{1,0:T(8,128)}, u32[]{:S(2)}, u32[]{:S(2)}) collective-permute-start(f32[128,2048]{1,0:T(8,128)S(1)} %maximum_select_fusion.2), channel_id=1, source_target_pairs={{0,8},{1,9},{2,10},{3,11},{4,12},{5,13},{6,14},{7,15},{8,0},{9,1},... | collective-permute-start | bytes 3145736 | tf_op jit(solution)/shard_map/ppermute | solution.py:43
  250.4 10.3 %copy.135 = f32[128,32,512]{2,1,0:T(8,128)} copy(f32[128,32,512]{0,2,1:T(8,128)} %copy-done.5) | data formatting | bytes 16777216
  261.3 9.2 %collective-permute-done.30 = f32[128,2048]{1,0:T(8,128)S(1)} collective-permute-done((f32[128,2048]{1,0:T(8,128)S(1)}, f32[128,2048]{1,0:T(8,128)S(1)}, u32[]{:S(2)}, u32[]{:S(2)}) %collective-permute-start.30) | collective-permute-done | bytes 1048608 | tf_op jit(solution)/shard_map/ppermute | solution.py:43
  271.5 16.2 %collective-permute-done.23 = f32[128,2048]{1,0:T(8,128)} collective-permute-done((f32[128,2048]{1,0:T(8,128)S(1)}, f32[128,2048]{1,0:T(8,128)}, u32[]{:S(2)}, u32[]{:S(2)}) %collective-permute-start.23) | collective-permute-done | bytes 1048608 | tf_op jit(solution)/shard_map/ppermute | solution.py:43
  287.7 3.4 %broadcast_select_fusion.2 = (f32[256,2048]{1,0:T(8,128)S(1)}, f32[256,2048]{1,0:T(8,128)S(1)}, pred[256,2048]{1,0:T(8,128)(4,1)S(1)}) fusion(f32[128,2048]{1,0:T(8,128)} %copy-done.15, f32[128,2048]{1,0:T(8,128)} %collective-permute-done.23, pred[]{:T(512)S(6)} %eq.105, f32[128,2048]{1,0:T(8,128)S(1)} %maximum_select_fusion.3, f32[128,2048]{1,0:T(8,128)} %copy-done.10), kind=kLoop, calls=%fused_computation.109 | loop fusion | flops 4194304 | bytes 8912897 | tf_op jit(solution)/shard_map/mul | solution.py:56
  291.1 3.9 %multiply_reduce_fusion.4 = (f32[]{:T(128)}, f32[]{:T(128)}, f32[256,2048]{1,0:T(8,128)}) fusion(f32[256,2048]{1,0:T(8,128)S(1)} %get-tuple-element.28, pred[256,2048]{1,0:T(8,128)(4,1)S(1)} %get-tuple-element.29, f32[256,2048]{1,0:T(8,128)S(1)} %get-tuple-element.27, f32[128,2048]{1,0:T(8,128)S(1)} %maximum_select_fusion.3, f32[128,2048]{1,0:T(8,128)S(1)} %copy-done.11, ...), kind=kLoop, calls=%fused_computation.100 | loop fusion | flops 9437182 | bytes 8912905 | tf_op jit(solution)/shard_map/reduce_sum | solution.py:145
  296.3 2.7 multiply_reduce_fusion.3
  300.4 2.5 broadcast_select_fusion.1
  303.0 3.6 %multiply_reduce_fusion.2 = (f32[]{:T(128)}, f32[256,2048]{1,0:T(8,128)}) fusion(f32[256,2048]{1,0:T(8,128)S(1)} %get-tuple-element.25, pred[256,2048]{1,0:T(8,128)(4,1)S(1)} %copy-done.8, f32[256,2048]{1,0:T(8,128)S(1)} %get-tuple-element.24, f32[128,2048]{1,0:T(8,128)S(1)} %maximum_select_fusion.3, f32[128,2048]{1,0:T(8,128)S(1)} %copy-done.12, pred[]{:T(512)S(6)} %eq.105), kind=kLoop, calls=%fused_computation.96 | loop fusion | flops 8388607 | bytes 8912901 | tf_op jit(solution)/shard_map/reduce_sum | solution.py:145
  307.9 4.8 %multiply_reduce_fusion.1 = (f32[]{:T(128)}, f32[256,2048]{1,0:T(8,128)}) fusion(f32[256,2048]{1,0:T(8,128)} %get-tuple-element.23, f32[]{:T(128)S(6)} %div.33, f32[256,2048]{1,0:T(8,128)S(1)} %get-tuple-element.28, f32[256,2048]{1,0:T(8,128)} %get-tuple-element.26, f32[]{:T(128)S(6)} %div.31), kind=kLoop, calls=%fused_computation.94 | loop fusion | flops 3145727 | bytes 8388620 | tf_op jit(solution)/shard_map/reduce_sum | solution.py:148
  314.1 3.1 broadcast_select_fusion
  317.2 3.6 %multiply_reduce_fusion = (f32[]{:T(128)}, f32[256,2048]{1,0:T(8,128)}) fusion(f32[256,2048]{1,0:T(8,128)S(1)} %get-tuple-element.19, pred[256,2048]{1,0:T(8,128)(4,1)S(1)} %copy-done.9, f32[256,2048]{1,0:T(8,128)S(1)} %get-tuple-element.18, f32[128,2048]{1,0:T(8,128)S(1)} %maximum_select_fusion.3, f32[128,2048]{1,0:T(8,128)S(1)} %copy-done.13, pred[]{:T(512)S(6)} %eq.105), kind=kLoop, calls=%fused_computation.92 | loop fusion | flops 8388607 | bytes 8912901 | tf_op jit(solution)/shard_map/reduce_sum | solution.py:145
  (118 shorter events, 20.8 us)
Async XLA Ops:
  0.6 172.4 %copy-start = (f32[4,128]{1,0:T(4,128)S(1)}, f32[4,128]{1,0:T(4,128)}, u32[]{:S(2)}) copy-start(f32[4,128]{1,0:T(4,128)} %param.10) | copy-start | bytes 6148
  7.6 14.8 %collective-permute-start = (f32[128,32,1]{0,1,2:T(8,128)S(1)}, f32[128,32,1]{0,1,2:T(8,128)S(1)}, u32[]{:S(2)}, u32[]{:S(2)}) collective-permute-start(f32[128,32,1]{0,1,2:T(8,128)S(1)} %copy.137), channel_id=1, source_target_pairs={{0,16},{16,32},{32,48},{48,64},{64,80},{80,96},{96,112},{1,17},{17... | collective-permute-start | bytes 49160 | tf_op jit(solution)/shard_map/ppermute | solution.py:17
  10.7 11.5 %copy-start.18 = (s32[4096]{0:T(1024)S(1)}, s32[4096]{0:T(1024)}, u32[]{:S(2)}) copy-start(s32[4096]{0:T(1024)} %param.12) | copy-start | bytes 49156
  10.7 11.7 %collective-permute-start.1 = (f32[128,32,1]{0,1,2:T(8,128)S(1)}, f32[128,32,1]{0,1,2:T(8,128)S(1)}, u32[]{:S(2)}, u32[]{:S(2)}) collective-permute-start(f32[128,32,1]{0,1,2:T(8,128)S(1)} %copy.138), channel_id=1, source_target_pairs={{16,0},{32,16},{48,32},{64,48},{80,64},{96,80},{112,96},{17,1},{33... | collective-permute-start | bytes 49160 | tf_op jit(solution)/shard_map/ppermute | solution.py:18
  22.4 9.2 %copy-start.17 = (s32[4096,4]{0,1:T(4,128)S(1)}, s32[4096,4]{0,1:T(4,128)}, u32[]{:S(2)}) copy-start(s32[4096,4]{0,1:T(4,128)} %param.11) | copy-start | bytes 196612
  23.5 11.3 %collective-permute-start.2 = (f32[128,1,514]{0,2,1:T(8,128)S(1)}, f32[128,1,514]{0,2,1:T(8,128)S(1)}, u32[]{:S(2)}, u32[]{:S(2)}) collective-permute-start(f32[128,1,514]{0,2,1:T(8,128)S(1)} %get-tuple-element.42), channel_id=1, source_target_pairs={{1,0},{2,1},{3,2},{4,3},{5,4},{6,5},{7,6},{8,7},{9,8},{10,9},{11,1... | collective-permute-start | bytes 789512 | tf_op jit(solution)/shard_map/ppermute | solution.py:18
  26.3 10.3 %collective-permute-start.3 = (f32[128,1,514]{0,2,1:T(8,128)S(1)}, f32[128,1,514]{0,2,1:T(8,128)S(1)}, u32[]{:S(2)}, u32[]{:S(2)}) collective-permute-start(f32[128,1,514]{0,2,1:T(8,128)S(1)} %get-tuple-element.43), channel_id=1, source_target_pairs={{0,1},{1,2},{2,3},{3,4},{4,5},{5,6},{6,7},{7,8},{8,9},{9,10},{10,1... | collective-permute-start | bytes 789512 | tf_op jit(solution)/shard_map/ppermute | solution.py:17
  31.6 5.0 %copy-start.21 = (f32[128]{0:T(128)S(1)}, f32[128]{0:T(128)}, u32[]{:S(2)}) copy-start(f32[128]{0:T(128)} %param.9) | copy-start | bytes 1540
  56.5 3.4 %copy-start.3 = (f32[128,32,512]{0,2,1:T(8,128)}, f32[128,32,512]{0,2,1:T(8,128)S(1)}, u32[]{:S(2)}) copy-start(f32[128,32,512]{0,2,1:T(8,128)S(1)} %fusion.21) | copy-start | bytes 25165828
  59.9 5.4 %collective-permute-start.4 = (f32[128,32,1]{0,1,2:T(8,128)S(1)}, f32[128,32,1]{0,1,2:T(8,128)S(1)}, u32[]{:S(2)}, u32[]{:S(2)}) collective-permute-start(f32[128,32,1]{0,1,2:T(8,128)S(1)} %bitcast.75), channel_id=1, source_target_pairs={{0,16},{16,32},{32,48},{48,64},{64,80},{80,96},{96,112},{1,17},{17... | collective-permute-start | bytes 49160 | tf_op jit(solution)/shard_map/ppermute | solution.py:17
  63.6 6.1 %collective-permute-start.5 = (f32[128,32,1]{0,1,2:T(8,128)S(1)}, f32[128,32,1]{0,1,2:T(8,128)S(1)}, u32[]{:S(2)}, u32[]{:S(2)}) collective-permute-start(f32[128,32,1]{0,1,2:T(8,128)S(1)} %bitcast.74), channel_id=1, source_target_pairs={{16,0},{32,16},{48,32},{64,48},{80,64},{96,80},{112,96},{17,1},{33... | collective-permute-start | bytes 49160 | tf_op jit(solution)/shard_map/ppermute | solution.py:18
  69.7 15.1 %copy-start.4 = (f32[128,32,512]{0,2,1:T(8,128)S(1)}, f32[128,32,512]{0,2,1:T(8,128)}, u32[]{:S(2)}) copy-start(f32[128,32,512]{0,2,1:T(8,128)} %copy-done.3) | copy-start | bytes 25165828
  70.9 12.1 %collective-permute-start.6 = (f32[128,1,514]{0,2,1:T(8,128)S(1)}, f32[128,1,514]{0,2,1:T(8,128)S(1)}, u32[]{:S(2)}, u32[]{:S(2)}) collective-permute-start(f32[128,1,514]{0,2,1:T(8,128)S(1)} %get-tuple-element.40), channel_id=1, source_target_pairs={{1,0},{2,1},{3,2},{4,3},{5,4},{6,5},{7,6},{8,7},{9,8},{10,9},{11,1... | collective-permute-start | bytes 789512 | tf_op jit(solution)/shard_map/ppermute | solution.py:18
  73.1 11.7 %collective-permute-start.7 = (f32[128,1,514]{0,2,1:T(8,128)S(1)}, f32[128,1,514]{0,2,1:T(8,128)S(1)}, u32[]{:S(2)}, u32[]{:S(2)}) collective-permute-start(f32[128,1,514]{0,2,1:T(8,128)S(1)} %get-tuple-element.41), channel_id=1, source_target_pairs={{0,1},{1,2},{2,3},{3,4},{4,5},{5,6},{6,7},{7,8},{8,9},{9,10},{10,1... | collective-permute-start | bytes 789512 | tf_op jit(solution)/shard_map/ppermute | solution.py:17
  95.9 5.1 %collective-permute-start.8 = (f32[128,32,1]{0,1,2:T(8,128)S(1)}, f32[128,32,1]{0,1,2:T(8,128)S(1)}, u32[]{:S(2)}, u32[]{:S(2)}) collective-permute-start(f32[128,32,1]{0,1,2:T(8,128)S(1)} %bitcast.78), channel_id=1, source_target_pairs={{0,16},{16,32},{32,48},{48,64},{64,80},{80,96},{96,112},{1,17},{17... | collective-permute-start | bytes 49160 | tf_op jit(solution)/shard_map/ppermute | solution.py:17
  99.5 4.3 %collective-permute-start.9 = (f32[128,32,1]{0,1,2:T(8,128)S(1)}, f32[128,32,1]{0,1,2:T(8,128)S(1)}, u32[]{:S(2)}, u32[]{:S(2)}) collective-permute-start(f32[128,32,1]{0,1,2:T(8,128)S(1)} %bitcast.76), channel_id=1, source_target_pairs={{16,0},{32,16},{48,32},{64,48},{80,64},{96,80},{112,96},{17,1},{33... | collective-permute-start | bytes 49160 | tf_op jit(solution)/shard_map/ppermute | solution.py:18
  103.8 11.9 %collective-permute-start.10 = (f32[128,1,514]{0,2,1:T(8,128)S(1)}, f32[128,1,514]{0,2,1:T(8,128)S(1)}, u32[]{:S(2)}, u32[]{:S(2)}) collective-permute-start(f32[128,1,514]{0,2,1:T(8,128)S(1)} %get-tuple-element.38), channel_id=1, source_target_pairs={{1,0},{2,1},{3,2},{4,3},{5,4},{6,5},{7,6},{8,7},{9,8},{10,9},{11,1... | collective-permute-start | bytes 789512 | tf_op jit(solution)/shard_map/ppermute | solution.py:18
  105.8 11.7 %collective-permute-start.11 = (f32[128,1,514]{0,2,1:T(8,128)S(1)}, f32[128,1,514]{0,2,1:T(8,128)S(1)}, u32[]{:S(2)}, u32[]{:S(2)}) collective-permute-start(f32[128,1,514]{0,2,1:T(8,128)S(1)} %get-tuple-element.39), channel_id=1, source_target_pairs={{0,1},{1,2},{2,3},{3,4},{4,5},{5,6},{6,7},{7,8},{8,9},{9,10},{10,1... | collective-permute-start | bytes 789512 | tf_op jit(solution)/shard_map/ppermute | solution.py:17
  128.5 7.7 %copy-start.2 = (f32[128,32,512]{0,2,1:T(8,128)}, f32[128,32,512]{0,2,1:T(8,128)S(1)}, u32[]{:S(2)}) copy-start(f32[128,32,512]{0,2,1:T(8,128)S(1)} %fusion.9) | copy-start | bytes 25165828
  128.6 5.1 %collective-permute-start.12 = (f32[128,32,1]{0,1,2:T(8,128)S(1)}, f32[128,32,1]{0,1,2:T(8,128)S(1)}, u32[]{:S(2)}, u32[]{:S(2)}) collective-permute-start(f32[128,32,1]{0,1,2:T(8,128)S(1)} %bitcast.79), channel_id=1, source_target_pairs={{0,16},{16,32},{32,48},{48,64},{64,80},{80,96},{96,112},{1,17},{17... | collective-permute-start | bytes 49160 | tf_op jit(solution)/shard_map/ppermute | solution.py:17
  132.2 4.0 %collective-permute-start.13 = (f32[128,32,1]{0,1,2:T(8,128)S(1)}, f32[128,32,1]{0,1,2:T(8,128)S(1)}, u32[]{:S(2)}, u32[]{:S(2)}) collective-permute-start(f32[128,32,1]{0,1,2:T(8,128)S(1)} %bitcast.77), channel_id=1, source_target_pairs={{16,0},{32,16},{48,32},{64,48},{80,64},{96,80},{112,96},{17,1},{33... | collective-permute-start | bytes 49160 | tf_op jit(solution)/shard_map/ppermute | solution.py:18
  136.3 11.9 %collective-permute-start.14 = (f32[128,1,514]{0,2,1:T(8,128)S(1)}, f32[128,1,514]{0,2,1:T(8,128)S(1)}, u32[]{:S(2)}, u32[]{:S(2)}) collective-permute-start(f32[128,1,514]{0,2,1:T(8,128)S(1)} %get-tuple-element.36), channel_id=1, source_target_pairs={{1,0},{2,1},{3,2},{4,3},{5,4},{6,5},{7,6},{8,7},{9,8},{10,9},{11,1... | collective-permute-start | bytes 789512 | tf_op jit(solution)/shard_map/ppermute | solution.py:18
  138.2 11.7 %collective-permute-start.15 = (f32[128,1,514]{0,2,1:T(8,128)S(1)}, f32[128,1,514]{0,2,1:T(8,128)S(1)}, u32[]{:S(2)}, u32[]{:S(2)}) collective-permute-start(f32[128,1,514]{0,2,1:T(8,128)S(1)} %get-tuple-element.37), channel_id=1, source_target_pairs={{0,1},{1,2},{2,3},{3,4},{4,5},{5,6},{6,7},{7,8},{8,9},{9,10},{10,1... | collective-permute-start | bytes 789512 | tf_op jit(solution)/shard_map/ppermute | solution.py:17
  169.8 3.2 copy-start.5
  180.9 2.4 collective-permute-start.16
  184.1 3.2 copy-start.19
  184.1 3.2 copy-start.20
  187.2 3.6 %collective-permute-start.24 = (f32[16,256]{1,0:T(8,128)S(1)}, f32[16,256]{1,0:T(8,128)S(1)}, u32[]{:S(2)}, u32[]{:S(2)}) collective-permute-start(f32[16,256]{1,0:T(8,128)S(1)} %get-tuple-element.58), channel_id=1, source_target_pairs={{0,16},{16,0},{32,48},{48,32},{64,80},{80,64},{96,112},{112,96},{1... | collective-permute-start | bytes 49160 | tf_op jit(solution)/shard_map/ppermute | solution.py:43
  190.0 3.2 collective-permute-start.17
  190.9 4.2 %collective-permute-start.25 = (f32[16,512]{1,0:T(8,128)S(1)}, f32[16,512]{1,0:T(8,128)S(1)}, u32[]{:S(2)}, u32[]{:S(2)}) collective-permute-start(f32[16,512]{1,0:T(8,128)S(1)} %maximum_select_fusion.13), channel_id=1, source_target_pairs={{0,32},{16,48},{32,0},{48,16},{64,96},{80,112},{96,64},{112,80},{1... | collective-permute-start | bytes 98312 | tf_op jit(solution)/shard_map/ppermute | solution.py:43
  193.2 4.3 %collective-permute-start.18 = (f32[16,512]{1,0:T(8,128)S(1)}, f32[16,512]{1,0:T(8,128)S(1)}, u32[]{:S(2)}, u32[]{:S(2)}) collective-permute-start(f32[16,512]{1,0:T(8,128)S(1)} %maximum_select_fusion.12), channel_id=1, source_target_pairs={{0,32},{16,48},{32,0},{48,16},{64,96},{80,112},{96,64},{112,80},{1... | collective-permute-start | bytes 98312 | tf_op jit(solution)/shard_map/ppermute | solution.py:43
  195.1 6.4 %collective-permute-start.26 = (f32[16,1024]{1,0:T(8,128)S(1)}, f32[16,1024]{1,0:T(8,128)S(1)}, u32[]{:S(2)}, u32[]{:S(2)}) collective-permute-start(f32[16,1024]{1,0:T(8,128)S(1)} %maximum_select_fusion.11), channel_id=1, source_target_pairs={{0,64},{16,80},{32,96},{48,112},{64,0},{80,16},{96,32},{112,48},{1... | collective-permute-start | bytes 196616 | tf_op jit(solution)/shard_map/ppermute | solution.py:43
  197.5 5.8 %collective-permute-start.19 = (f32[16,1024]{1,0:T(8,128)S(1)}, f32[16,1024]{1,0:T(8,128)S(1)}, u32[]{:S(2)}, u32[]{:S(2)}) collective-permute-start(f32[16,1024]{1,0:T(8,128)S(1)} %maximum_select_fusion.10), channel_id=1, source_target_pairs={{0,64},{16,80},{32,96},{48,112},{64,0},{80,16},{96,32},{112,48},{1... | collective-permute-start | bytes 196616 | tf_op jit(solution)/shard_map/ppermute | solution.py:43
  201.5 6.4 %collective-permute-start.27 = (f32[16,2048]{1,0:T(8,128)S(1)}, f32[16,2048]{1,0:T(8,128)S(1)}, u32[]{:S(2)}, u32[]{:S(2)}) collective-permute-start(f32[16,2048]{1,0:T(8,128)S(1)} %maximum_select_fusion.9), channel_id=1, source_target_pairs={{0,1},{1,0},{2,3},{3,2},{4,5},{5,4},{6,7},{7,6},{8,9},{9,8},{10,11... | collective-permute-start | bytes 393224 | tf_op jit(solution)/shard_map/ppermute | solution.py:43
  203.4 7.4 %collective-permute-start.20 = (f32[16,2048]{1,0:T(8,128)S(1)}, f32[16,2048]{1,0:T(8,128)S(1)}, u32[]{:S(2)}, u32[]{:S(2)}) collective-permute-start(f32[16,2048]{1,0:T(8,128)S(1)} %maximum_select_fusion.8), channel_id=1, source_target_pairs={{0,1},{1,0},{2,3},{3,2},{4,5},{5,4},{6,7},{7,6},{8,9},{9,8},{10,11... | collective-permute-start | bytes 393224 | tf_op jit(solution)/shard_map/ppermute | solution.py:43
  208.0 8.2 %collective-permute-start.28 = (f32[32,2048]{1,0:T(8,128)S(1)}, f32[32,2048]{1,0:T(8,128)S(1)}, u32[]{:S(2)}, u32[]{:S(2)}) collective-permute-start(f32[32,2048]{1,0:T(8,128)S(1)} %maximum_select_fusion.7), channel_id=1, source_target_pairs={{0,2},{1,3},{2,0},{3,1},{4,6},{5,7},{6,4},{7,5},{8,10},{9,11},{10,... | collective-permute-start | bytes 786440 | tf_op jit(solution)/shard_map/ppermute | solution.py:43
  210.8 10.0 %collective-permute-start.21 = (f32[32,2048]{1,0:T(8,128)S(1)}, f32[32,2048]{1,0:T(8,128)S(1)}, u32[]{:S(2)}, u32[]{:S(2)}) collective-permute-start(f32[32,2048]{1,0:T(8,128)S(1)} %maximum_select_fusion.6), channel_id=1, source_target_pairs={{0,2},{1,3},{2,0},{3,1},{4,6},{5,7},{6,4},{7,5},{8,10},{9,11},{10,... | collective-permute-start | bytes 786440 | tf_op jit(solution)/shard_map/ppermute | solution.py:43
  216.3 17.4 %collective-permute-start.29 = (f32[64,2048]{1,0:T(8,128)S(1)}, f32[64,2048]{1,0:T(8,128)S(1)}, u32[]{:S(2)}, u32[]{:S(2)}) collective-permute-start(f32[64,2048]{1,0:T(8,128)S(1)} %maximum_select_fusion.5), channel_id=1, source_target_pairs={{0,4},{1,5},{2,6},{3,7},{4,0},{5,1},{6,2},{7,3},{8,12},{9,13},{10,... | collective-permute-start | bytes 1572872 | tf_op jit(solution)/shard_map/ppermute | solution.py:43
  220.8 16.6 %copy-start.16 = (f32[64,2048]{1,0:T(8,128)}, f32[64,2048]{1,0:T(8,128)S(1)}, u32[]{:S(2)}) copy-start(f32[64,2048]{1,0:T(8,128)S(1)} %maximum_select_fusion.4) | copy-start | bytes 1572868
  220.8 24.1 %collective-permute-start.22 = (f32[64,2048]{1,0:T(8,128)S(1)}, f32[64,2048]{1,0:T(8,128)}, u32[]{:S(2)}, u32[]{:S(2)}) collective-permute-start(f32[64,2048]{1,0:T(8,128)S(1)} %maximum_select_fusion.4), channel_id=1, source_target_pairs={{0,4},{1,5},{2,6},{3,7},{4,0},{5,1},{6,2},{7,3},{8,12},{9,13},{10,... | collective-permute-start | bytes 1572872 | tf_op jit(solution)/shard_map/ppermute | solution.py:43
  233.7 36.8 %collective-permute-start.30 = (f32[128,2048]{1,0:T(8,128)S(1)}, f32[128,2048]{1,0:T(8,128)S(1)}, u32[]{:S(2)}, u32[]{:S(2)}) collective-permute-start(f32[128,2048]{1,0:T(8,128)S(1)} %maximum_select_fusion.3), channel_id=1, source_target_pairs={{0,8},{1,9},{2,10},{3,11},{4,12},{5,13},{6,14},{7,15},{8,0},{9,1},... | collective-permute-start | bytes 3145736 | tf_op jit(solution)/shard_map/ppermute | solution.py:43
  246.7 14.0 %copy-start.15 = (f32[128,2048]{1,0:T(8,128)}, f32[128,2048]{1,0:T(8,128)S(1)}, u32[]{:S(2)}) copy-start(f32[128,2048]{1,0:T(8,128)S(1)} %maximum_select_fusion.2) | copy-start | bytes 3145732
  246.7 41.0 %collective-permute-start.23 = (f32[128,2048]{1,0:T(8,128)S(1)}, f32[128,2048]{1,0:T(8,128)}, u32[]{:S(2)}, u32[]{:S(2)}) collective-permute-start(f32[128,2048]{1,0:T(8,128)S(1)} %maximum_select_fusion.2), channel_id=1, source_target_pairs={{0,8},{1,9},{2,10},{3,11},{4,12},{5,13},{6,14},{7,15},{8,0},{9,1},... | collective-permute-start | bytes 3145736 | tf_op jit(solution)/shard_map/ppermute | solution.py:43
  270.5 1.0 copy-start.10
  287.7 3.4 %copy-start.11 = (f32[128,2048]{1,0:T(8,128)S(1)}, f32[128,2048]{1,0:T(8,128)}, u32[]{:S(2)}) copy-start(f32[128,2048]{1,0:T(8,128)} %copy-done.10) | copy-start | bytes 3145732
  291.1 3.9 %copy-start.7 = (pred[256,2048]{1,0:T(8,128)(4,1)}, pred[256,2048]{1,0:T(8,128)(4,1)S(1)}, u32[]{:S(2)}) copy-start(pred[256,2048]{1,0:T(8,128)(4,1)S(1)} %get-tuple-element.29) | copy-start | bytes 1572868
  300.4 2.6 copy-start.8
  300.4 2.6 copy-start.12
  302.9 3.7 %copy-start.6 = (f32[256,2048]{1,0:T(8,128)}, f32[256,2048]{1,0:T(8,128)S(1)}, u32[]{:S(2)}) copy-start(f32[256,2048]{1,0:T(8,128)S(1)} %get-tuple-element.25) | copy-start | bytes 6291460
  314.1 3.1 copy-start.9
  314.1 3.1 copy-start.13
  317.1 3.7 %copy-start.14 = (f32[256,2048]{1,0:T(8,128)}, f32[256,2048]{1,0:T(8,128)S(1)}, u32[]{:S(2)}) copy-start(f32[256,2048]{1,0:T(8,128)S(1)} %get-tuple-element.19) | copy-start | bytes 6291460
  317.2 7.7 %copy-start.1 = (f32[4,128]{1,0:T(4,128)S(1)}, f32[4,128]{1,0:T(4,128)}, u32[]{:S(2)}) copy-start(f32[4,128]{1,0:T(4,128)} %param.10) | copy-start | bytes 6148
where the time goes:
time: 326 us; the launch traced here: 325 us
  other arithmetic  98.2 us (30%)
  waiting for transfers between devices  88.8 us (27%)
  starting transfers between devices  77.5 us (24%)
  local copies, waits for them, and re-layouts  42.1 us (13%)
  matrix products  10.2 us (3%)
  between operations  8.07 us (2%)
    add x4, other arithmetic, body(): field = field + kappa * lap  61.9 us
    ppermute x14, waiting for transfers between devices, doubling_gather(): other = lax.ppermute(x, axis, [(j, j ^ distance) for j in range(size)])  60.5 us
    ppermute x8, starting transfers between devices, with_halo(): before = lax.ppermute(last, axis, up)  37.5 us
    unnamed x49, local copies, waits for them, and re-layouts  32.6 us
    ppermute x14, starting transfers between devices, doubling_gather(): other = lax.ppermute(x, axis, [(j, j ^ distance) for j in range(size)])  26 us
    ppermute x8, waiting for transfers between devices, with_halo(): after = lax.ppermute(first, axis, down)  19.9 us
    ppermute x8, starting transfers between devices, with_halo(): after = lax.ppermute(first, axis, down)  14.1 us
    reduce_sum x3, other arithmetic, body(): alpha = norm_now / jnp.sum(direction * image)  11.1 us
  transfers between devices with their start and end apart: 31, of which 23 were waited for; matrix products, arithmetic and copies ran while one was open for 9% of the time, Pallas kernels for 0%

commit v1 on v0

--- a/solution.py
+++ b/solution.py
@@ -2,6 +2,8 @@
 import jax.numpy as jnp
 from jax import lax
 from jax.sharding import PartitionSpec as P
+from jax.experimental import pallas as pl
+from jax.experimental.pallas import tpu as pltpu
 
 STEPS = 4
 ITERS = 3
@@ -58,6 +60,98 @@
     return maskf * ((4.0 + ocean_term) * vector - beside) + (1.0 - maskf) * vector
 
 
+HALO = 4
+LEVEL_BLOCK = 8
+
+
+def diffusion_kernel(kappa_ref, weight_ref, core_ref, lanes_ref, rows_ref, mask_ref, out_ref, flux_ref):
+    block = pl.program_id(0)
+    levels, rows, cols = core_ref.shape
+
+    @pl.when(block == 0)
+    def _():
+        flux_ref[...] = jnp.zeros_like(flux_ref)
+
+    mask = mask_ref[...]
+
+    def level(l, carry):
+        lev = block * levels + l
+        kappa = kappa_ref[lev]
+        top = jnp.concatenate([core_ref[l], lanes_ref[l]], axis=1)
+        f = jnp.concatenate([top, rows_ref[l]], axis=0)
+        height, width = f.shape
+        for step in range(STEPS):
+            beside = (
+                pltpu.roll(f, height - 1, 0)
+                + pltpu.roll(f, 1, 0)
+                + pltpu.roll(f, width - 1, 1)
+                + pltpu.roll(f, 1, 1)
+            )
+            f = (f + kappa * (beside - 4.0 * f)) * mask
+        core = f[:rows, :cols]
+        out_ref[l] = core
+        for c in range(flux_ref.shape[0]):
+            flux_ref[c] += weight_ref[c, lev] * core
+        return carry
+
+    lax.fori_loop(0, levels, level, 0)
+
+
+def diffuse(field, atm_kappa, vert_weight):
+    levels, rows, cols = field.shape
+    comps = vert_weight.shape[0]
+    count_gx = lax.axis_size("gx")
+    count_gy = lax.axis_size("gy")
+    gx_index = lax.axis_index("gx")
+    gy_index = lax.axis_index("gy")
+    up_gx = [(i, i + 1) for i in range(count_gx - 1)]
+    down_gx = [(i + 1, i) for i in range(count_gx - 1)]
+    up_gy = [(i, i + 1) for i in range(count_gy - 1)]
+    down_gy = [(i + 1, i) for i in range(count_gy - 1)]
+    east = lax.ppermute(field[:, :, :HALO], "gx", down_gx)
+    west = lax.ppermute(field[:, :, cols - HALO :], "gx", up_gx)
+    gap = jnp.zeros((levels, rows, 128 - 2 * HALO), field.dtype)
+    lanes = jnp.concatenate([east, gap, west], axis=2)
+    first = jnp.concatenate([field[:, :HALO, :], lanes[:, :HALO, :]], axis=2)
+    last = jnp.concatenate([field[:, rows - HALO :, :], lanes[:, rows - HALO :, :]], axis=2)
+    south = lax.ppermute(first, "gy", down_gy)
+    north = lax.ppermute(last, "gy", up_gy)
+    halo_rows = jnp.concatenate([south, north], axis=1)
+    height = rows + 2 * HALO
+    width = cols + 128
+    r = jnp.arange(height, dtype=jnp.int32)
+    c = jnp.arange(width, dtype=jnp.int32)
+    global_r = gy_index * rows + jnp.where(r < rows + HALO, r, r - height)
+    global_c = gx_index * cols + jnp.where(c < cols + HALO, c, c - width)
+    inside_r = (global_r >= 0) & (global_r < count_gy * rows)
+    inside_c = (global_c >= 0) & (global_c < count_gx * cols) & ((c < cols + HALO) | (c >= width - HALO))
+    mask = (inside_r[:, None] & inside_c[None, :]).astype(jnp.float32)
+    blocks = levels // LEVEL_BLOCK
+    smem = pl.BlockSpec(memory_space=pltpu.SMEM)
+    out, flux = pl.pallas_call(
+        diffusion_kernel,
+        grid=(blocks,),
+        in_specs=[
+            smem,
+            smem,
+            pl.BlockSpec((LEVEL_BLOCK, rows, cols), lambda b: (b, 0, 0)),
+            pl.BlockSpec((LEVEL_BLOCK, rows, 128), lambda b: (b, 0, 0)),
+            pl.BlockSpec((LEVEL_BLOCK, 2 * HALO, width), lambda b: (b, 0, 0)),
+            pl.BlockSpec((height, width), lambda b: (0, 0)),
+        ],
+        out_specs=[
+            pl.BlockSpec((LEVEL_BLOCK, rows, cols), lambda b: (b, 0, 0)),
+            pl.BlockSpec((comps, rows, cols), lambda b: (0, 0, 0)),
+        ],
+        out_shape=[
+            jax.ShapeDtypeStruct(field.shape, field.dtype),
+            jax.ShapeDtypeStruct((comps, rows, cols), jnp.float32),
+        ],
+        compiler_params=pltpu.CompilerParams(dimension_semantics=("arbitrary",)),
+    )(atm_kappa, vert_weight, field, lanes, halo_rows, mask)
+    return out, flux
+
+
 def body(
     atm_state, atm_kappa, vert_weight, remap_src, remap_count, remap_weight, land_mask, ocean_term
 ):
@@ -67,23 +161,8 @@
     count_gy = lax.axis_size("gy")
     coded_all = whole_grid(jnp.where(land_mask != 0, ocean_term, -1.0))
     maskf = (coded_all >= 0.0).astype(jnp.float32)
-    field = atm_state
-    for step in range(STEPS):
-        padded = with_halo(field, (("gx", 2), ("gy", 1)), 1)
-        lap = (
-            padded[:, 2:, 1:-1]
-            + padded[:, :-2, 1:-1]
-            + padded[:, 1:-1, 2:]
-            + padded[:, 1:-1, :-2]
-            - 4.0 * field
-        )
-        field = field + kappa * lap
-    flux = jnp.dot(
-        vert_weight,
-        field.reshape(levels, tile_lat * tile_lon),
-        precision=lax.Precision.HIGHEST,
-        preferred_element_type=jnp.float32,
-    )
+    field, flux = diffuse(atm_state, atm_kappa, vert_weight)
+    flux = flux.reshape(flux.shape[0], tile_lat * tile_lon)
     ocean_blocks, lists, width, _ = remap_weight.shape
     comps = vert_weight.shape[0]
     own_blocks = tile_lat * tile_lon // width

time: 326 us -> 284 us (0.87); the launches traced: 325 us -> 279 us
  Pallas kernels: 0 us -> 66.6 us
  other arithmetic: 98.2 us -> 42.8 us
  starting transfers between devices: 77.5 us -> 31.3 us
  local copies, waits for them, and re-layouts: 42.1 us -> 26 us
  waiting for transfers between devices: 88.8 us -> 101 us
  matrix products: 10.2 us -> 3.03 us
    pallas_call x0 -> x1, Pallas kernels: none -> 66.6 us  [diffuse(): pl.pallas_call(diffusion_kernel, grid=(blocks,), in_specs=[smem, smem, pl...]
    add x4 -> x0, other arithmetic: 61.9 us -> none  [body(): field = field + kappa * lap]
    ppermute x16 -> x4, starting transfers between devices: 51.5 us -> 9.04 us  [the longest x1 3.4 us: diffuse(): north = lax.ppermute(last, 'gy', up_gy)]
    unnamed x49 -> x51, local copies, waits for them, and re-layouts: 32.6 us -> 6.27 us
    ppermute x14, waiting for transfers between devices: 60.5 us -> 70.9 us  [doubling_gather(): other = lax.ppermute(x, axis, [(j, j ^ distance) for j in range(size)])]
    dot_general x1 -> x0, matrix products: 7.15 us -> none  [body(): jnp.dot(vert_weight, field.reshape(levels, tile_lat * tile_lon), precisio...]
    ppermute x14, starting transfers between devices: 26 us -> 19.3 us  [doubling_gather(): other = lax.ppermute(x, axis, [(j, j ^ distance) for j in range(size)])]
    ppermute x0 -> x2, local copies, waits for them, and re-layouts: none -> 5.75 us  [the longest x1 2.89 us: diffuse(): east = lax.ppermute(field[:, :, :HALO], 'gx', down_gx)]
  transfers between devices with their start and end apart: 31 -> 19, of which waited for: 23 -> 15; matrix products, arithmetic and copies ran while one was open for 9% -> 7% of each run, Pallas kernels for 0% -> 0%
where the time goes in v1:
time: 284 us; the launch traced here: 279 us
  waiting for transfers between devices  101 us (36%)
  Pallas kernels  66.6 us (23%)
  other arithmetic  42.8 us (15%)
  starting transfers between devices  31.3 us (11%)
  local copies, waits for them, and re-layouts  26 us (9%)
  between operations  7.95 us (3%)
  matrix products  3.03 us (1%)
    ppermute x14, waiting for transfers between devices, doubling_gather(): other = lax.ppermute(x, axis, [(j, j ^ distance) for j in range(size)])  70.9 us
    pallas_call x1, Pallas kernels, diffuse(): pl.pallas_call(diffusion_kernel, grid=(blocks,), in_specs=[smem, smem, pl...  66.6 us
    ppermute x1, waiting for transfers between devices, diffuse(): north = lax.ppermute(last, 'gy', up_gy)  23.9 us
    ppermute x14, starting transfers between devices, doubling_gather(): other = lax.ppermute(x, axis, [(j, j ^ distance) for j in range(size)])  19.3 us
    reduce_sum x3, other arithmetic, body(): alpha = norm_now / jnp.sum(direction * image)  11.2 us
    mul x3, other arithmetic, grid_operator(): padded = jnp.pad(maskf * vector, 1)  8.85 us
    reduce_sum x2, other arithmetic, body(): norm_next = jnp.sum(residual * residual)  7.54 us
    unnamed x51, local copies, waits for them, and re-layouts  6.27 us
  transfers between devices with their start and end apart: 19, of which 15 were waited for; matrix products, arithmetic and copies ran while one was open for 7% of the time, Pallas kernels for 0%

profile of v1, /device:TPU:6, one launch (start us, length us, event | category | flops | bytes accessed | tf_op | source)
XLA Modules:
  0.0 279.1 jit_solution(8519675719690092627)
XLA Ops:
  0.6 4.3 %fusion.48 = (f32[128,32,4]{2,1,0:T(8,128)S(1)}, f32[128,32,4]{2,1,0:T(8,128)}) fusion(f32[128,32,512]{2,1,0:T(8,128)} %core_ref.1), kind=kLoop, calls=%fused_computation.134 | loop fusion | bytes 262144 | tf_op jit(solution)/shard_map/slice | solution.py:111
  4.9 2.7 copy.86
  7.5 1.7 collective-permute-start.1
  9.3 1.3 copy.85
  10.6 1.3 collective-permute-start
  11.9 3.8 %fusion.47 = (f32[128,4,512]{2,1,0:T(4,128)S(1)}, f32[128,4,512]{2,1,0:T(4,128)}) fusion(f32[128,32,512]{2,1,0:T(8,128)} %core_ref.1), kind=kLoop, calls=%fused_computation.133 | loop fusion | bytes 4194304 | tf_op jit(solution)/shard_map/slice | solution.py:115
  16.0 0.7 copy.71
  16.7 1.6 reshape.236
  18.6 1.4 fusion.45
  20.0 0.5 copy-done.20
  21.0 0.6 pad.76.clone
  21.6 0.6 add_reduce_fusion
  22.2 2.9 %copy.68 = f32[128,32,4]{2,1,0:T(8,128)} copy(f32[128,32,4]{0,1,2:T(8,128)S(1)} %collective-permute-done) | data formatting | bytes 131072 | tf_op jit(solution)/shard_map/ppermute | solution.py:111
  25.1 2.9 %copy.69 = f32[128,32,4]{2,1,0:T(8,128)} copy(f32[128,32,4]{0,1,2:T(8,128)S(1)} %collective-permute-done.1) | data formatting | bytes 131072 | tf_op jit(solution)/shard_map/ppermute | solution.py:112
  28.0 2.9 %pad_maximum_fusion.1.lanes_ref = f32[128,32,128]{2,1,0:T(8,128)S(1)} fusion(f32[128,32,4]{2,1,0:T(8,128)} %copy.69, f32[128,32,4]{2,1,0:T(8,128)} %copy.68, f32[128]{0:T(128)S(1)} %copy-done.23), kind=kLoop, calls=%fused_computation.34 | loop fusion | flops 1048576 | bytes 2228736 | tf_op jit(solution)/shard_map/concatenate | solution.py:114
  31.3 3.4 %collective-permute-start.3 = (f32[128,4,640]{2,1,0:T(4,128)S(1)}, f32[128,4,640]{2,1,0:T(4,128)S(1)}, u32[]{:S(2)}, u32[]{:S(2)}) collective-permute-start(f32[128,4,640]{2,1,0:T(4,128)S(1)} %pad_maximum_fusion.3), channel_id=1, source_target_pairs={{0,1},{1,2},{2,3},{3,4},{4,5},{5,6},{6,7},{7,8},{8,9},{9,10},{10,1... | collective-permute-start | bytes 3932168 | tf_op jit(solution)/shard_map/ppermute | solution.py:118
  35.0 2.6 collective-permute-start.2
  38.4 0.7 and_convert_fusion.mask_ref
  39.1 23.9 %collective-permute-done.3 = f32[128,4,640]{2,1,0:T(4,128)S(1)} collective-permute-done((f32[128,4,640]{2,1,0:T(4,128)S(1)}, f32[128,4,640]{2,1,0:T(4,128)S(1)}, u32[]{:S(2)}, u32[]{:S(2)}) %collective-permute-start.3) | collective-permute-done | bytes 1310752 | tf_op jit(solution)/shard_map/ppermute | solution.py:118
  63.0 6.1 %collective-permute-done.2 = f32[128,4,640]{2,1,0:T(4,128)S(1)} collective-permute-done((f32[128,4,640]{2,1,0:T(4,128)S(1)}, f32[128,4,640]{2,1,0:T(4,128)S(1)}, u32[]{:S(2)}, u32[]{:S(2)}) %collective-permute-start.2) | collective-permute-done | bytes 1310752 | tf_op jit(solution)/shard_map/ppermute | solution.py:117
  69.1 2.0 pad_maximum_fusion.rows_ref
  71.1 66.6 %shard_map.111 = (f32[128,32,512]{2,1,0:T(8,128)}, f32[4,32,512]{2,1,0:T(8,128)}) custom-call(f32[128]{0:T(128)} %kappa_ref.1, f32[4,128]{1,0:T(4,128)} %weight_ref.1, f32[128,32,512]{2,1,0:T(8,128)} %core_ref.1, f32[128,32,128]{2,1,0:T(8,128)} %copy-done.8, f32[128,8,640]{2,1,0:T(8,128)} %pad_maximum_fusion.rows_ref, f32[40,640]{1,0:T(8,128)} %and_convert_fusion.mask_ref), custom_call_target="tpu_custom_call" | custom-call | tf_op jit(solution)/shard_map/pallas_call | solution.py:131
  137.7 1.0 convert_element_type.47
  138.8 0.6 gather_fusion.1
  139.6 2.9 %collective-permute-start.4 = (bf16[32,4,128]{2,1,0:T(4,128)(2,1)S(1)}, bf16[32,4,128]{2,1,0:T(4,128)(2,1)S(1)}, u32[]{:S(2)}, u32[]{:S(2)}) collective-permute-start(bf16[32,4,128]{2,1,0:T(4,128)(2,1)S(1)} %broadcast_multiply_fusion), channel_id=1, source_target_pairs={{0,112},{16,0},{32,16},{48,32},{64,48},{80,64},{96,80},{112,96},{1... | collective-permute-start | bytes 98312 | tf_op jit(solution)/shard_map/ppermute | solution.py:27
  142.7 0.7 gather_fusion
  143.5 0.6 collective-permute-done.4
  144.1 0.7 gather_fusion.2
  144.8 3.0 %convolution_bitcast_fusion = f32[4,32,128]{2,0,1:T(4,128)S(1)} fusion(bf16[32,4,128,128]{3,2,1,0:T(8,128)(2,1)} %param.13, bf16[32,4,4,128]{3,2,1,0:T(4,128)(2,1)S(1)} %bitcast.29, bf16[32,4,4,128]{3,2,1,0:T(4,128)(2,1)S(1)} %bitcast.30, pred[32,4]{1,0:T(8,128)(4,1)S(1)} %and.145, pred[32,4]{1,0:T(8,128)(4,1)S(1)} %and.141), kind=kOutput, calls=%fused_computation.50 | convolution fusion | flops 16908288 | bytes 4522240 | tf_op jit(solution)/shard_map/bkij,bkcj->cbi/dot_general | solution.py:212
  148.0 2.4 collective-permute-start.12
  150.5 0.7 collective-permute-done.12
  151.3 1.6 collective-permute-start.13
  152.9 0.5 collective-permute-start.6
  153.4 1.8 collective-permute-done.13
  155.2 2.3 collective-permute-start.14
  157.5 1.4 collective-permute-start.7
  158.9 2.7 collective-permute-done.14
  161.7 1.7 collective-permute-done.7
  163.8 4.2 %collective-permute-done.15 = f32[16,2048]{1,0:T(8,128)S(1)} collective-permute-done((f32[16,2048]{1,0:T(8,128)S(1)}, f32[16,2048]{1,0:T(8,128)S(1)}, u32[]{:S(2)}, u32[]{:S(2)}) %collective-permute-start.15) | collective-permute-done | bytes 131104 | tf_op jit(solution)/shard_map/ppermute | solution.py:45
  168.1 2.7 collective-permute-done.8
  170.9 0.9 collective-permute-start.9
  171.8 4.5 %collective-permute-done.16 = f32[32,2048]{1,0:T(8,128)S(1)} collective-permute-done((f32[32,2048]{1,0:T(8,128)S(1)}, f32[32,2048]{1,0:T(8,128)S(1)}, u32[]{:S(2)}, u32[]{:S(2)}) %collective-permute-start.16) | collective-permute-done | bytes 262176 | tf_op jit(solution)/shard_map/ppermute | solution.py:45
  176.3 1.7 collective-permute-start.17
  178.0 1.1 collective-permute-done.9
  179.1 1.7 collective-permute-start.10
  180.8 10.5 %collective-permute-done.17 = f32[64,2048]{1,0:T(8,128)S(1)} collective-permute-done((f32[64,2048]{1,0:T(8,128)S(1)}, f32[64,2048]{1,0:T(8,128)S(1)}, u32[]{:S(2)}, u32[]{:S(2)}) %collective-permute-start.17) | collective-permute-done | bytes 524320 | tf_op jit(solution)/shard_map/ppermute | solution.py:45
  191.4 3.0 %collective-permute-start.18 = (f32[128,2048]{1,0:T(8,128)S(1)}, f32[128,2048]{1,0:T(8,128)S(1)}, u32[]{:S(2)}, u32[]{:S(2)}) collective-permute-start(f32[128,2048]{1,0:T(8,128)S(1)} %maximum_select_fusion.3), channel_id=1, source_target_pairs={{0,8},{1,9},{2,10},{3,11},{4,12},{5,13},{6,14},{7,15},{8,0},{9,1},... | collective-permute-start | bytes 3145736 | tf_op jit(solution)/shard_map/ppermute | solution.py:45
  194.4 8.3 %collective-permute-done.10 = f32[64,2048]{1,0:T(8,128)} collective-permute-done((f32[64,2048]{1,0:T(8,128)S(1)}, f32[64,2048]{1,0:T(8,128)}, u32[]{:S(2)}, u32[]{:S(2)}) %collective-permute-start.10) | collective-permute-done | bytes 524320 | tf_op jit(solution)/shard_map/ppermute | solution.py:45
  202.6 1.7 maximum_select_fusion.2
  204.3 3.2 %collective-permute-start.11 = (f32[128,2048]{1,0:T(8,128)S(1)}, f32[128,2048]{1,0:T(8,128)}, u32[]{:S(2)}, u32[]{:S(2)}) collective-permute-start(f32[128,2048]{1,0:T(8,128)S(1)} %maximum_select_fusion.2), channel_id=1, source_target_pairs={{0,8},{1,9},{2,10},{3,11},{4,12},{5,13},{6,14},{7,15},{8,0},{9,1},... | collective-permute-start | bytes 3145736 | tf_op jit(solution)/shard_map/ppermute | solution.py:45
  207.5 0.6 reshape.238
  208.1 17.9 %collective-permute-done.18 = f32[128,2048]{1,0:T(8,128)S(1)} collective-permute-done((f32[128,2048]{1,0:T(8,128)S(1)}, f32[128,2048]{1,0:T(8,128)S(1)}, u32[]{:S(2)}, u32[]{:S(2)}) %collective-permute-start.18) | collective-permute-done | bytes 1048608 | tf_op jit(solution)/shard_map/ppermute | solution.py:45
  226.1 1.0 copy-done.4
  227.1 14.9 %collective-permute-done.11 = f32[128,2048]{1,0:T(8,128)} collective-permute-done((f32[128,2048]{1,0:T(8,128)S(1)}, f32[128,2048]{1,0:T(8,128)}, u32[]{:S(2)}, u32[]{:S(2)}) %collective-permute-start.11) | collective-permute-done | bytes 1048608 | tf_op jit(solution)/shard_map/ppermute | solution.py:45
  242.0 3.3 %broadcast_select_fusion.2 = (f32[256,2048]{1,0:T(8,128)S(1)}, f32[256,2048]{1,0:T(8,128)S(1)}, pred[256,2048]{1,0:T(8,128)(4,1)S(1)}) fusion(f32[128,2048]{1,0:T(8,128)} %copy-done.10, f32[128,2048]{1,0:T(8,128)} %collective-permute-done.11, pred[]{:T(512)S(6)} %eq.105, f32[128,2048]{1,0:T(8,128)S(1)} %maximum_select_fusion.3, f32[128,2048]{1,0:T(8,128)} %copy-done.4), kind=kLoop, calls=%fused_computation.55 | loop fusion | flops 4194304 | bytes 8912897 | tf_op jit(solution)/shard_map/mul | solution.py:58
  245.3 3.8 %multiply_reduce_fusion.4 = (f32[]{:T(128)}, f32[]{:T(128)}, f32[256,2048]{1,0:T(8,128)}) fusion(f32[256,2048]{1,0:T(8,128)S(1)} %get-tuple-element.24, pred[256,2048]{1,0:T(8,128)(4,1)S(1)} %get-tuple-element.25, f32[256,2048]{1,0:T(8,128)S(1)} %get-tuple-element.23, f32[128,2048]{1,0:T(8,128)S(1)} %maximum_select_fusion.3, f32[128,2048]{1,0:T(8,128)S(1)} %copy-done.5, ...), kind=kLoop, calls=%fused_computation.45 | loop fusion | flops 9437182 | bytes 8912905 | tf_op jit(solution)/shard_map/reduce_sum | solution.py:224
  250.5 2.7 multiply_reduce_fusion.3
  254.6 2.5 broadcast_select_fusion.1
  257.1 3.7 %multiply_reduce_fusion.2 = (f32[]{:T(128)}, f32[256,2048]{1,0:T(8,128)}) fusion(f32[256,2048]{1,0:T(8,128)S(1)} %get-tuple-element.21, pred[256,2048]{1,0:T(8,128)(4,1)S(1)} %copy-done.2, f32[256,2048]{1,0:T(8,128)S(1)} %get-tuple-element.20, f32[128,2048]{1,0:T(8,128)S(1)} %maximum_select_fusion.3, f32[128,2048]{1,0:T(8,128)S(1)} %copy-done.6, pred[]{:T(512)S(6)} %eq.105), kind=kLoop, calls=%fused_computation.41 | loop fusion | flops 8388607 | bytes 8912901 | tf_op jit(solution)/shard_map/reduce_sum | solution.py:224
  262.2 4.8 %multiply_reduce_fusion.1 = (f32[]{:T(128)}, f32[256,2048]{1,0:T(8,128)}) fusion(f32[256,2048]{1,0:T(8,128)} %get-tuple-element.19, f32[]{:T(128)S(6)} %div.33, f32[256,2048]{1,0:T(8,128)S(1)} %get-tuple-element.24, f32[256,2048]{1,0:T(8,128)} %get-tuple-element.22, f32[]{:T(128)S(6)} %div.31), kind=kLoop, calls=%fused_computation.39 | loop fusion | flops 3145727 | bytes 8388620 | tf_op jit(solution)/shard_map/reduce_sum | solution.py:227
  268.3 3.1 %broadcast_select_fusion = (f32[256,2048]{1,0:T(8,128)S(1)}, f32[256,2048]{1,0:T(8,128)S(1)}) fusion(pred[256,2048]{1,0:T(8,128)(4,1)} %copy-done.1, f32[256,2048]{1,0:T(8,128)} %get-tuple-element.17, f32[256,2048]{1,0:T(8,128)} %copy-done, f32[]{:T(128)S(6)} %div.34), kind=kLoop, calls=%fused_computation.53 | loop fusion | flops 1572864 | bytes 8912900 | tf_op jit(solution)/shard_map/mul | solution.py:58
  271.4 3.7 %multiply_reduce_fusion = (f32[]{:T(128)}, f32[256,2048]{1,0:T(8,128)}) fusion(f32[256,2048]{1,0:T(8,128)S(1)} %get-tuple-element.15, pred[256,2048]{1,0:T(8,128)(4,1)S(1)} %copy-done.3, f32[256,2048]{1,0:T(8,128)S(1)} %get-tuple-element.14, f32[128,2048]{1,0:T(8,128)S(1)} %maximum_select_fusion.3, f32[128,2048]{1,0:T(8,128)S(1)} %copy-done.7, pred[]{:T(512)S(6)} %eq.105), kind=kLoop, calls=%fused_computation.37 | loop fusion | flops 8388607 | bytes 8912901 | tf_op jit(solution)/shard_map/reduce_sum | solution.py:224
  276.4 1.4 fusion.29
  277.8 1.3 dynamic-slice_subtract_fusion
  (101 shorter events, 3.9 us)
Async XLA Ops:
  7.5 17.5 %collective-permute-start.1 = (f32[128,32,4]{0,1,2:T(8,128)S(1)}, f32[128,32,4]{0,1,2:T(8,128)S(1)}, u32[]{:S(2)}, u32[]{:S(2)}) collective-permute-start(f32[128,32,4]{0,1,2:T(8,128)S(1)} %copy.86), channel_id=1, source_target_pairs={{0,16},{16,32},{32,48},{48,64},{64,80},{80,96},{96,112},{1,17},{17... | collective-permute-start | bytes 196616 | tf_op jit(solution)/shard_map/ppermute | solution.py:112
  10.6 11.6 %collective-permute-start = (f32[128,32,4]{0,1,2:T(8,128)S(1)}, f32[128,32,4]{0,1,2:T(8,128)S(1)}, u32[]{:S(2)}, u32[]{:S(2)}) collective-permute-start(f32[128,32,4]{0,1,2:T(8,128)S(1)} %copy.85), channel_id=1, source_target_pairs={{16,0},{32,16},{48,32},{64,48},{80,64},{96,80},{112,96},{17,1},{33... | collective-permute-start | bytes 196616 | tf_op jit(solution)/shard_map/ppermute | solution.py:111
  11.9 3.9 %copy-start.16 = (s32[4096]{0:T(1024)S(1)}, s32[4096]{0:T(1024)}, u32[]{:S(2)}) copy-start(s32[4096]{0:T(1024)} %param.12) | copy-start | bytes 49156
  11.9 4.1 %copy-start.13 = (s32[4096,4]{0,1:T(4,128)S(1)}, s32[4096,4]{0,1:T(4,128)}, u32[]{:S(2)}) copy-start(s32[4096,4]{0,1:T(4,128)} %param.11) | copy-start | bytes 196612
  20.0 0.5 copy-start.20
  22.2 5.8 %copy-start.23 = (f32[128]{0:T(128)S(1)}, f32[128]{0:T(128)}, u32[]{:S(2)}) copy-start(f32[128]{0:T(128)} %pad.76.clone) | copy-start | bytes 1540
  28.0 3.0 %copy-start.11 = (f32[128,4,512]{2,1,0:T(4,128)S(1)}, f32[128,4,512]{2,1,0:T(4,128)}, u32[]{:S(2)}) copy-start(f32[128,4,512]{2,1,0:T(4,128)} %get-tuple-element.33) | copy-start | bytes 3145732
  30.9 4.2 %copy-start.8 = (f32[128,32,128]{2,1,0:T(8,128)}, f32[128,32,128]{2,1,0:T(8,128)S(1)}, u32[]{:S(2)}) copy-start(f32[128,32,128]{2,1,0:T(8,128)S(1)} %pad_maximum_fusion.1.lanes_ref) | copy-start | bytes 6291460
  31.0 6.7 %copy-start.15 = (pred[1,128]{0,1:T(8,128)(4,1)S(1)}, pred[1,128]{0,1:T(8,128)(4,1)}, u32[]{:S(2)}) copy-start(pred[1,128]{0,1:T(8,128)(4,1)} %get-tuple-element.39) | copy-start | bytes 388
  31.0 6.9 %copy-start.22 = (s32[128]{0:T(128)S(1)}, s32[128]{0:T(128)}, u32[]{:S(2)}) copy-start(s32[128]{0:T(128)} %add_reduce_fusion) | copy-start | bytes 1540
  31.0 7.0 %copy-start.14 = (pred[1,128]{0,1:T(8,128)(4,1)S(1)}, pred[1,128]{0,1:T(8,128)(4,1)}, u32[]{:S(2)}) copy-start(pred[1,128]{0,1:T(8,128)(4,1)} %get-tuple-element.41) | copy-start | bytes 388
  31.3 31.6 %collective-permute-start.3 = (f32[128,4,640]{2,1,0:T(4,128)S(1)}, f32[128,4,640]{2,1,0:T(4,128)S(1)}, u32[]{:S(2)}, u32[]{:S(2)}) collective-permute-start(f32[128,4,640]{2,1,0:T(4,128)S(1)} %pad_maximum_fusion.3), channel_id=1, source_target_pairs={{0,1},{1,2},{2,3},{3,4},{4,5},{5,6},{6,7},{7,8},{8,9},{9,10},{10,1... | collective-permute-start | bytes 3932168 | tf_op jit(solution)/shard_map/ppermute | solution.py:118
  35.0 34.0 %collective-permute-start.2 = (f32[128,4,640]{2,1,0:T(4,128)S(1)}, f32[128,4,640]{2,1,0:T(4,128)S(1)}, u32[]{:S(2)}, u32[]{:S(2)}) collective-permute-start(f32[128,4,640]{2,1,0:T(4,128)S(1)} %pad_maximum_fusion.2), channel_id=1, source_target_pairs={{1,0},{2,1},{3,2},{4,3},{5,4},{6,5},{7,6},{8,7},{9,8},{10,9},{11,1... | collective-permute-start | bytes 3932168 | tf_op jit(solution)/shard_map/ppermute | solution.py:117
  71.1 71.4 %copy-start.21 = (pred[128]{0:T(512)(128)(4,1)S(1)}, pred[128]{0:T(512)(128)(4,1)}, u32[]{:S(2)}) copy-start(pred[128]{0:T(512)(128)(4,1)} %copy-done.20) | copy-start | bytes 388
  71.1 71.5 %copy-start.19 = (pred[128]{0:T(512)(128)(4,1)S(1)}, pred[128]{0:T(512)(128)(4,1)}, u32[]{:S(2)}) copy-start(pred[128]{0:T(512)(128)(4,1)} %get-tuple-element.40) | copy-start | bytes 388
  139.6 4.5 %collective-permute-start.4 = (bf16[32,4,128]{2,1,0:T(4,128)(2,1)S(1)}, bf16[32,4,128]{2,1,0:T(4,128)(2,1)S(1)}, u32[]{:S(2)}, u32[]{:S(2)}) collective-permute-start(bf16[32,4,128]{2,1,0:T(4,128)(2,1)S(1)} %broadcast_multiply_fusion), channel_id=1, source_target_pairs={{0,112},{16,0},{32,16},{48,32},{64,48},{80,64},{96,80},{112,96},{1... | collective-permute-start | bytes 98312 | tf_op jit(solution)/shard_map/ppermute | solution.py:27
  144.8 3.1 %copy-start.17 = (f32[16,256]{1,0:T(8,128)S(1)}, f32[16,256]{1,0:T(8,128)}, u32[]{:S(2)}) copy-start(f32[16,256]{1,0:T(8,128)} %param.15) | copy-start | bytes 49156
  144.8 3.1 %copy-start.18 = (s32[16,256]{1,0:T(8,128)S(1)}, s32[16,256]{1,0:T(8,128)}, u32[]{:S(2)}) copy-start(s32[16,256]{1,0:T(8,128)} %param.14) | copy-start | bytes 49156
  148.0 3.3 %collective-permute-start.12 = (f32[16,256]{1,0:T(8,128)S(1)}, f32[16,256]{1,0:T(8,128)S(1)}, u32[]{:S(2)}, u32[]{:S(2)}) collective-permute-start(f32[16,256]{1,0:T(8,128)S(1)} %get-tuple-element.44), channel_id=1, source_target_pairs={{0,16},{16,0},{32,48},{48,32},{64,80},{80,64},{96,112},{112,96},{1... | collective-permute-start | bytes 49160 | tf_op jit(solution)/shard_map/ppermute | solution.py:45
  150.4 2.5 collective-permute-start.5
  151.3 3.9 %collective-permute-start.13 = (f32[16,512]{1,0:T(8,128)S(1)}, f32[16,512]{1,0:T(8,128)S(1)}, u32[]{:S(2)}, u32[]{:S(2)}) collective-permute-start(f32[16,512]{1,0:T(8,128)S(1)} %maximum_select_fusion.13), channel_id=1, source_target_pairs={{0,32},{16,48},{32,0},{48,16},{64,96},{80,112},{96,64},{112,80},{1... | collective-permute-start | bytes 98312 | tf_op jit(solution)/shard_map/ppermute | solution.py:45
  152.9 4.6 %collective-permute-start.6 = (f32[16,512]{1,0:T(8,128)S(1)}, f32[16,512]{1,0:T(8,128)S(1)}, u32[]{:S(2)}, u32[]{:S(2)}) collective-permute-start(f32[16,512]{1,0:T(8,128)S(1)} %maximum_select_fusion.12), channel_id=1, source_target_pairs={{0,32},{16,48},{32,0},{48,16},{64,96},{80,112},{96,64},{112,80},{1... | collective-permute-start | bytes 98312 | tf_op jit(solution)/shard_map/ppermute | solution.py:45
  155.2 6.4 %collective-permute-start.14 = (f32[16,1024]{1,0:T(8,128)S(1)}, f32[16,1024]{1,0:T(8,128)S(1)}, u32[]{:S(2)}, u32[]{:S(2)}) collective-permute-start(f32[16,1024]{1,0:T(8,128)S(1)} %maximum_select_fusion.11), channel_id=1, source_target_pairs={{0,64},{16,80},{32,96},{48,112},{64,0},{80,16},{96,32},{112,48},{1... | collective-permute-start | bytes 196616 | tf_op jit(solution)/shard_map/ppermute | solution.py:45
  157.5 5.8 %collective-permute-start.7 = (f32[16,1024]{1,0:T(8,128)S(1)}, f32[16,1024]{1,0:T(8,128)S(1)}, u32[]{:S(2)}, u32[]{:S(2)}) collective-permute-start(f32[16,1024]{1,0:T(8,128)S(1)} %maximum_select_fusion.10), channel_id=1, source_target_pairs={{0,64},{16,80},{32,96},{48,112},{64,0},{80,16},{96,32},{112,48},{1... | collective-permute-start | bytes 196616 | tf_op jit(solution)/shard_map/ppermute | solution.py:45
  161.6 6.4 %collective-permute-start.15 = (f32[16,2048]{1,0:T(8,128)S(1)}, f32[16,2048]{1,0:T(8,128)S(1)}, u32[]{:S(2)}, u32[]{:S(2)}) collective-permute-start(f32[16,2048]{1,0:T(8,128)S(1)} %maximum_select_fusion.9), channel_id=1, source_target_pairs={{0,1},{1,0},{2,3},{3,2},{4,5},{5,4},{6,7},{7,6},{8,9},{9,8},{10,11... | collective-permute-start | bytes 393224 | tf_op jit(solution)/shard_map/ppermute | solution.py:45
  163.4 7.5 %collective-permute-start.8 = (f32[16,2048]{1,0:T(8,128)S(1)}, f32[16,2048]{1,0:T(8,128)S(1)}, u32[]{:S(2)}, u32[]{:S(2)}) collective-permute-start(f32[16,2048]{1,0:T(8,128)S(1)} %maximum_select_fusion.8), channel_id=1, source_target_pairs={{0,1},{1,0},{2,3},{3,2},{4,5},{5,4},{6,7},{7,6},{8,9},{9,8},{10,11... | collective-permute-start | bytes 393224 | tf_op jit(solution)/shard_map/ppermute | solution.py:45
  168.0 8.2 %collective-permute-start.16 = (f32[32,2048]{1,0:T(8,128)S(1)}, f32[32,2048]{1,0:T(8,128)S(1)}, u32[]{:S(2)}, u32[]{:S(2)}) collective-permute-start(f32[32,2048]{1,0:T(8,128)S(1)} %maximum_select_fusion.7), channel_id=1, source_target_pairs={{0,2},{1,3},{2,0},{3,1},{4,6},{5,7},{6,4},{7,5},{8,10},{9,11},{10,... | collective-permute-start | bytes 786440 | tf_op jit(solution)/shard_map/ppermute | solution.py:45
  170.9 8.2 %collective-permute-start.9 = (f32[32,2048]{1,0:T(8,128)S(1)}, f32[32,2048]{1,0:T(8,128)S(1)}, u32[]{:S(2)}, u32[]{:S(2)}) collective-permute-start(f32[32,2048]{1,0:T(8,128)S(1)} %maximum_select_fusion.6), channel_id=1, source_target_pairs={{0,2},{1,3},{2,0},{3,1},{4,6},{5,7},{6,4},{7,5},{8,10},{9,11},{10,... | collective-permute-start | bytes 786440 | tf_op jit(solution)/shard_map/ppermute | solution.py:45
  176.3 14.9 %collective-permute-start.17 = (f32[64,2048]{1,0:T(8,128)S(1)}, f32[64,2048]{1,0:T(8,128)S(1)}, u32[]{:S(2)}, u32[]{:S(2)}) collective-permute-start(f32[64,2048]{1,0:T(8,128)S(1)} %maximum_select_fusion.5), channel_id=1, source_target_pairs={{0,4},{1,5},{2,6},{3,7},{4,0},{5,1},{6,2},{7,3},{8,12},{9,13},{10,... | collective-permute-start | bytes 1572872 | tf_op jit(solution)/shard_map/ppermute | solution.py:45
  179.1 15.2 %copy-start.12 = (f32[64,2048]{1,0:T(8,128)}, f32[64,2048]{1,0:T(8,128)S(1)}, u32[]{:S(2)}) copy-start(f32[64,2048]{1,0:T(8,128)S(1)} %maximum_select_fusion.4) | copy-start | bytes 1572868
  179.1 23.5 %collective-permute-start.10 = (f32[64,2048]{1,0:T(8,128)S(1)}, f32[64,2048]{1,0:T(8,128)}, u32[]{:S(2)}, u32[]{:S(2)}) collective-permute-start(f32[64,2048]{1,0:T(8,128)S(1)} %maximum_select_fusion.4), channel_id=1, source_target_pairs={{0,4},{1,5},{2,6},{3,7},{4,0},{5,1},{6,2},{7,3},{8,12},{9,13},{10,... | collective-permute-start | bytes 1572872 | tf_op jit(solution)/shard_map/ppermute | solution.py:45
  191.4 34.7 %collective-permute-start.18 = (f32[128,2048]{1,0:T(8,128)S(1)}, f32[128,2048]{1,0:T(8,128)S(1)}, u32[]{:S(2)}, u32[]{:S(2)}) collective-permute-start(f32[128,2048]{1,0:T(8,128)S(1)} %maximum_select_fusion.3), channel_id=1, source_target_pairs={{0,8},{1,9},{2,10},{3,11},{4,12},{5,13},{6,14},{7,15},{8,0},{9,1},... | collective-permute-start | bytes 3145736 | tf_op jit(solution)/shard_map/ppermute | solution.py:45
  204.3 21.8 %copy-start.10 = (f32[128,2048]{1,0:T(8,128)}, f32[128,2048]{1,0:T(8,128)S(1)}, u32[]{:S(2)}) copy-start(f32[128,2048]{1,0:T(8,128)S(1)} %maximum_select_fusion.2) | copy-start | bytes 3145732
  204.3 37.7 %collective-permute-start.11 = (f32[128,2048]{1,0:T(8,128)S(1)}, f32[128,2048]{1,0:T(8,128)}, u32[]{:S(2)}, u32[]{:S(2)}) collective-permute-start(f32[128,2048]{1,0:T(8,128)S(1)} %maximum_select_fusion.2), channel_id=1, source_target_pairs={{0,8},{1,9},{2,10},{3,11},{4,12},{5,13},{6,14},{7,15},{8,0},{9,1},... | collective-permute-start | bytes 3145736 | tf_op jit(solution)/shard_map/ppermute | solution.py:45
  226.1 1.0 copy-start.4
  242.0 3.4 %copy-start.5 = (f32[128,2048]{1,0:T(8,128)S(1)}, f32[128,2048]{1,0:T(8,128)}, u32[]{:S(2)}) copy-start(f32[128,2048]{1,0:T(8,128)} %copy-done.4) | copy-start | bytes 3145732
  245.3 3.8 %copy-start.1 = (pred[256,2048]{1,0:T(8,128)(4,1)}, pred[256,2048]{1,0:T(8,128)(4,1)S(1)}, u32[]{:S(2)}) copy-start(pred[256,2048]{1,0:T(8,128)(4,1)S(1)} %get-tuple-element.25) | copy-start | bytes 1572868
  254.6 2.5 copy-start.2
  254.6 2.5 copy-start.6
  257.1 3.7 %copy-start = (f32[256,2048]{1,0:T(8,128)}, f32[256,2048]{1,0:T(8,128)S(1)}, u32[]{:S(2)}) copy-start(f32[256,2048]{1,0:T(8,128)S(1)} %get-tuple-element.21) | copy-start | bytes 6291460
  268.3 3.1 %copy-start.3 = (pred[256,2048]{1,0:T(8,128)(4,1)S(1)}, pred[256,2048]{1,0:T(8,128)(4,1)}, u32[]{:S(2)}) copy-start(pred[256,2048]{1,0:T(8,128)(4,1)} %copy-done.1) | copy-start | bytes 1572868
  268.3 3.1 %copy-start.7 = (f32[128,2048]{1,0:T(8,128)S(1)}, f32[128,2048]{1,0:T(8,128)}, u32[]{:S(2)}) copy-start(f32[128,2048]{1,0:T(8,128)} %copy-done.4) | copy-start | bytes 3145732
  271.4 3.7 %copy-start.9 = (f32[256,2048]{1,0:T(8,128)}, f32[256,2048]{1,0:T(8,128)S(1)}, u32[]{:S(2)}) copy-start(f32[256,2048]{1,0:T(8,128)S(1)} %get-tuple-element.15) | copy-start | bytes 6291460

commit v2 on v1

--- a/solution.py
+++ b/solution.py
@@ -37,21 +37,45 @@
     return lax.psum(jnp.sum(residual * residual), ("gx", "gy"))
 
 
-def doubling_gather(x, axis, dim):
-    size = lax.axis_size(axis)
-    index = lax.axis_index(axis)
-    distance = 1
-    while distance < size:
+def gather_rounds():
+    rounds = []
+    for axis, bits in (("gy", lax.axis_size("gy")), ("gx", lax.axis_size("gx"))):
+        distances = []
+        d = 1
+        while d < bits:
+            distances.append(d)
+            d *= 2
+        rounds.append([(axis, d) for d in distances])
+    gy_rounds, gx_rounds = rounds
+    far = gy_rounds[1::2] + gx_rounds[2:]
+    near = gy_rounds[0::2] + gx_rounds[1:2] + gx_rounds[:1]
+    return far + near
+
+
+def whole_grid(tile):
+    rows, cols = tile.shape
+    rounds = gather_rounds()
+    x = tile[None]
+    for axis, distance in rounds:
+        size = lax.axis_size(axis)
+        index = lax.axis_index(axis)
         other = lax.ppermute(x, axis, [(j, j ^ distance) for j in range(size)])
-        low = jnp.concatenate([x, other], axis=dim)
-        high = jnp.concatenate([other, x], axis=dim)
+        low = jnp.concatenate([x, other], axis=0)
+        high = jnp.concatenate([other, x], axis=0)
         x = jnp.where((index & distance) == 0, low, high)
-        distance *= 2
-    return x
-
-
-def whole_grid(tile):
-    return doubling_gather(doubling_gather(tile, "gx", 1), "gy", 0)
+    count = len(rounds)
+    x = x.reshape((2,) * count + (rows, cols))
+    order = []
+    for axis in ("gy", "gx"):
+        d = lax.axis_size(axis) // 2
+        while d >= 1:
+            order.append(count - 1 - rounds.index((axis, d)))
+            d //= 2
+    x = x.transpose(order + [count, count + 1])
+    count_gy = lax.axis_size("gy")
+    count_gx = lax.axis_size("gx")
+    x = x.reshape(count_gy, count_gx, rows, cols).transpose(0, 2, 1, 3)
+    return x.reshape(count_gy * rows, count_gx * cols)
 
 
 def grid_operator(vector, maskf, ocean_term):
@@ -148,6 +172,11 @@
             jax.ShapeDtypeStruct((comps, rows, cols), jnp.float32),
         ],
         compiler_params=pltpu.CompilerParams(dimension_semantics=("arbitrary",)),
+        cost_estimate=pl.CostEstimate(
+            flops=levels * height * width * STEPS * 10,
+            transcendentals=0,
+            bytes_accessed=2 * field.size * 4,
+        ),
     )(atm_kappa, vert_weight, field, lanes, halo_rows, mask)
     return out, flux
 

time: 284 us -> 250 us (0.88); the launches traced: 279 us -> 249 us
  waiting for transfers between devices: 101 us -> 66.6 us
  local copies, waits for them, and re-layouts: 26 us -> 30.2 us
  other arithmetic: 42.8 us -> 45.8 us
    ppermute x14, waiting for transfers between devices: 70.9 us -> 36.1 us  [whole_grid(): other = lax.ppermute(x, axis, [(j, j ^ distance) for j in range(size)])]
    mul x3, other arithmetic: 8.85 us -> 5.52 us  [grid_operator(): padded = jnp.pad(maskf * vector, 1)]
    unnamed x51 -> x42, local copies, waits for them, and re-layouts: 6.27 us -> 7.31 us
  transfers between devices with their start and end apart: 19 -> 19, of which waited for: 15 -> 11; matrix products, arithmetic and copies ran while one was open for 7% -> 9% of each run, Pallas kernels for 0% -> 0%
where the time goes in v2:
time: 250 us; the launch traced here: 249 us
  waiting for transfers between devices  66.6 us (27%)
  Pallas kernels  66.5 us (27%)
  other arithmetic  45.8 us (18%)
  local copies, waits for them, and re-layouts  30.2 us (12%)
  starting transfers between devices  28.5 us (11%)
  between operations  8.06 us (3%)
  matrix products  3.04 us (1%)
    pallas_call x1, Pallas kernels, diffuse(): pl.pallas_call(diffusion_kernel, grid=(blocks,), in_specs=[smem, smem, pl...  66.5 us
    ppermute x14, waiting for transfers between devices, whole_grid(): other = lax.ppermute(x, axis, [(j, j ^ distance) for j in range(size)])  36.1 us
    ppermute x1, waiting for transfers between devices, diffuse(): north = lax.ppermute(last, 'gy', up_gy)  23.8 us
    ppermute x14, starting transfers between devices, whole_grid(): other = lax.ppermute(x, axis, [(j, j ^ distance) for j in range(size)])  16.5 us
    reduce_sum x3, other arithmetic, body(): alpha = norm_now / jnp.sum(direction * image)  10.8 us
    reduce_sum x2, other arithmetic, body(): norm_next = jnp.sum(residual * residual)  7.5 us
    unnamed x42, local copies, waits for them, and re-layouts  7.31 us
    ppermute x1, waiting for transfers between devices, diffuse(): south = lax.ppermute(first, 'gy', down_gy)  6.1 us
  transfers between devices with their start and end apart: 19, of which 11 were waited for; matrix products, arithmetic and copies ran while one was open for 9% of the time, Pallas kernels for 0%

profile of v2, /device:TPU:6, one launch (start us, length us, event | category | flops | bytes accessed | tf_op | source)
XLA Modules:
  0.0 248.8 jit_solution(16134378823230032634)
XLA Ops:
  0.6 4.3 %fusion.50 = (f32[128,32,4]{2,1,0:T(8,128)S(1)}, f32[128,32,4]{2,1,0:T(8,128)}) fusion(f32[128,32,512]{2,1,0:T(8,128)} %core_ref.1), kind=kLoop, calls=%fused_computation.135 | loop fusion | bytes 262144 | tf_op jit(solution)/shard_map/slice | solution.py:135
  4.9 2.7 %copy.143 = f32[128,32,4]{0,1,2:T(8,128)S(1)} copy(f32[128,32,4]{2,1,0:T(8,128)} %get-tuple-element.31) | data formatting | bytes 131072
  7.5 1.7 collective-permute-start.1
  9.3 1.3 copy.142
  10.6 1.3 collective-permute-start
  11.9 3.8 %fusion.49 = (f32[128,4,512]{2,1,0:T(4,128)S(1)}, f32[128,4,512]{2,1,0:T(4,128)}) fusion(f32[128,32,512]{2,1,0:T(8,128)} %core_ref.1), kind=kLoop, calls=%fused_computation.134 | loop fusion | bytes 4194304 | tf_op jit(solution)/shard_map/slice | solution.py:139
  16.0 0.7 copy.122
  16.6 1.6 reshape.262
  18.6 1.4 fusion.47
  19.9 0.5 copy-done.14
  20.9 0.6 pad.76.clone
  21.5 0.6 add_reduce_fusion
  22.1 1.9 copy.119
  24.0 2.9 %copy.120 = f32[128,32,4]{2,1,0:T(8,128)} copy(f32[128,32,4]{0,1,2:T(8,128)S(1)} %collective-permute-done.1) | data formatting | bytes 131072 | tf_op jit(solution)/shard_map/ppermute | solution.py:136
  26.9 2.3 pad_maximum_fusion.1.lanes_ref
  29.6 3.4 %collective-permute-start.3 = (f32[128,4,640]{2,1,0:T(4,128)S(1)}, f32[128,4,640]{2,1,0:T(4,128)S(1)}, u32[]{:S(2)}, u32[]{:S(2)}) collective-permute-start(f32[128,4,640]{2,1,0:T(4,128)S(1)} %pad_maximum_fusion.3), channel_id=1, source_target_pairs={{0,1},{1,2},{2,3},{3,4},{4,5},{5,6},{6,7},{7,8},{8,9},{9,10},{10,1... | collective-permute-start | bytes 3932168 | tf_op jit(solution)/shard_map/ppermute | solution.py:142
  33.3 2.6 %collective-permute-start.2 = (f32[128,4,640]{2,1,0:T(4,128)S(1)}, f32[128,4,640]{2,1,0:T(4,128)S(1)}, u32[]{:S(2)}, u32[]{:S(2)}) collective-permute-start(f32[128,4,640]{2,1,0:T(4,128)S(1)} %pad_maximum_fusion.2), channel_id=1, source_target_pairs={{1,0},{2,1},{3,2},{4,3},{5,4},{6,5},{7,6},{8,7},{9,8},{10,9},{11,1... | collective-permute-start | bytes 3932168 | tf_op jit(solution)/shard_map/ppermute | solution.py:141
  36.7 0.7 and_convert_fusion.mask_ref
  37.4 23.8 %collective-permute-done.3 = f32[128,4,640]{2,1,0:T(4,128)S(1)} collective-permute-done((f32[128,4,640]{2,1,0:T(4,128)S(1)}, f32[128,4,640]{2,1,0:T(4,128)S(1)}, u32[]{:S(2)}, u32[]{:S(2)}) %collective-permute-start.3) | collective-permute-done | bytes 1310752 | tf_op jit(solution)/shard_map/ppermute | solution.py:142
  61.2 6.1 %collective-permute-done.2 = f32[128,4,640]{2,1,0:T(4,128)S(1)} collective-permute-done((f32[128,4,640]{2,1,0:T(4,128)S(1)}, f32[128,4,640]{2,1,0:T(4,128)S(1)}, u32[]{:S(2)}, u32[]{:S(2)}) %collective-permute-start.2) | collective-permute-done | bytes 1310752 | tf_op jit(solution)/shard_map/ppermute | solution.py:141
  67.3 2.0 pad_maximum_fusion.rows_ref
  69.4 66.5 %shard_map.111 = (f32[128,32,512]{2,1,0:T(8,128)}, f32[4,32,512]{2,1,0:T(8,128)}) custom-call(f32[128]{0:T(128)} %kappa_ref.1, f32[4,128]{1,0:T(4,128)} %weight_ref.1, f32[128,32,512]{2,1,0:T(8,128)} %core_ref.1, f32[128,32,128]{2,1,0:T(8,128)} %copy-done.4, f32[128,8,640]{2,1,0:T(8,128)} %pad_maximum_fusion.rows_ref, f32[40,640]{1,0:T(8,128)} %and_convert_fusion.mask_ref), custom_call_target="tpu_custom_call" | custom-call | flops 131072000 | bytes 16777216 | tf_op jit(solution)/shard_map/pallas_call | solution.py:155
  135.9 1.0 convert_element_type.47
  137.1 0.6 gather_fusion.1
  137.8 2.9 %collective-permute-start.4 = (bf16[32,4,128]{2,1,0:T(4,128)(2,1)S(1)}, bf16[32,4,128]{2,1,0:T(4,128)(2,1)S(1)}, u32[]{:S(2)}, u32[]{:S(2)}) collective-permute-start(bf16[32,4,128]{2,1,0:T(4,128)(2,1)S(1)} %broadcast_multiply_fusion), channel_id=1, source_target_pairs={{0,112},{16,0},{32,16},{48,32},{64,48},{80,64},{96,80},{112,96},{1... | collective-permute-start | bytes 98312 | tf_op jit(solution)/shard_map/ppermute | solution.py:27
  141.0 0.7 gather_fusion
  141.8 0.6 collective-permute-done.4
  142.3 0.7 gather_fusion.2
  143.1 3.0 %convolution_bitcast_fusion = f32[4,32,128]{2,0,1:T(4,128)S(1)} fusion(bf16[32,4,128,128]{3,2,1,0:T(8,128)(2,1)} %param.13, bf16[32,4,4,128]{3,2,1,0:T(4,128)(2,1)S(1)} %bitcast.85, bf16[32,4,4,128]{3,2,1,0:T(4,128)(2,1)S(1)} %bitcast.86, pred[32,4]{1,0:T(8,128)(4,1)S(1)} %and.145, pred[32,4]{1,0:T(8,128)(4,1)S(1)} %and.141), kind=kOutput, calls=%fused_computation.52 | convolution fusion | flops 16908288 | bytes 4522240 | tf_op jit(solution)/shard_map/bkij,bkcj->cbi/dot_general | solution.py:241
  146.4 5.2 %collective-permute-done.5 = f32[1,16,256]{2,1,0:T(8,128)S(1)} collective-permute-done((f32[1,16,256]{2,1,0:T(8,128)S(1)}, f32[1,16,256]{2,1,0:T(8,128)S(1)}, u32[]{:S(2)}, u32[]{:S(2)}) %collective-permute-start.5) | collective-permute-done | bytes 16416 | tf_op jit(solution)/shard_map/ppermute | solution.py:62
  151.6 2.9 %collective-permute-start.6 = (f32[2,16,256]{2,1,0:T(8,128)S(1)}, f32[2,16,256]{2,1,0:T(8,128)S(1)}, u32[]{:S(2)}, u32[]{:S(2)}) collective-permute-start(f32[2,16,256]{2,1,0:T(8,128)S(1)} %maximum_select_fusion.12), channel_id=1, source_target_pairs={{0,8},{1,9},{2,10},{3,11},{4,12},{5,13},{6,14},{7,15},{8,0},{9,1},... | collective-permute-start | bytes 98312 | tf_op jit(solution)/shard_map/ppermute | solution.py:62
  154.5 2.6 %collective-permute-done.6 = f32[2,16,256]{2,1,0:T(8,128)S(1)} collective-permute-done((f32[2,16,256]{2,1,0:T(8,128)S(1)}, f32[2,16,256]{2,1,0:T(8,128)S(1)}, u32[]{:S(2)}, u32[]{:S(2)}) %collective-permute-start.6) | collective-permute-done | bytes 32800 | tf_op jit(solution)/shard_map/ppermute | solution.py:62
  157.1 3.9 %collective-permute-start.7 = (f32[4,16,256]{2,1,0:T(8,128)S(1)}, f32[4,16,256]{2,1,0:T(8,128)S(1)}, u32[]{:S(2)}, u32[]{:S(2)}) collective-permute-start(f32[4,16,256]{2,1,0:T(8,128)S(1)} %maximum_select_fusion.10), channel_id=1, source_target_pairs={{0,64},{16,80},{32,96},{48,112},{64,0},{80,16},{96,32},{112,48},{1... | collective-permute-start | bytes 196616 | tf_op jit(solution)/shard_map/ppermute | solution.py:62
  161.0 3.0 %collective-permute-start.13 = (f32[2,16,256]{2,1,0:T(8,128)S(1)}, f32[2,16,256]{2,1,0:T(8,128)S(1)}, u32[]{:S(2)}, u32[]{:S(2)}) collective-permute-start(f32[2,16,256]{2,1,0:T(8,128)S(1)} %maximum_select_fusion.13), channel_id=1, source_target_pairs={{0,8},{1,9},{2,10},{3,11},{4,12},{5,13},{6,14},{7,15},{8,0},{9,1},... | collective-permute-start | bytes 98312 | tf_op jit(solution)/shard_map/ppermute | solution.py:62
  164.1 2.4 collective-permute-done.13
  166.5 2.6 %collective-permute-start.14 = (f32[4,16,256]{2,1,0:T(8,128)S(1)}, f32[4,16,256]{2,1,0:T(8,128)S(1)}, u32[]{:S(2)}, u32[]{:S(2)}) collective-permute-start(f32[4,16,256]{2,1,0:T(8,128)S(1)} %maximum_select_fusion.11), channel_id=1, source_target_pairs={{0,64},{16,80},{32,96},{48,112},{64,0},{80,16},{96,32},{112,48},{1... | collective-permute-start | bytes 196616 | tf_op jit(solution)/shard_map/ppermute | solution.py:62
  169.2 0.8 collective-permute-start.9
  170.0 2.4 collective-permute-done.14
  172.5 4.9 %collective-permute-done.15 = f32[8,16,256]{2,1,0:T(8,128)S(1)} collective-permute-done((f32[8,16,256]{2,1,0:T(8,128)S(1)}, f32[8,16,256]{2,1,0:T(8,128)S(1)}, u32[]{:S(2)}, u32[]{:S(2)}) %collective-permute-start.15) | collective-permute-done | bytes 131104 | tf_op jit(solution)/shard_map/ppermute | solution.py:62
  177.5 1.7 collective-permute-start.16
  179.3 4.6 %collective-permute-done.16 = f32[16,16,256]{2,1,0:T(8,128)S(1)} collective-permute-done((f32[16,16,256]{2,1,0:T(8,128)S(1)}, f32[16,16,256]{2,1,0:T(8,128)S(1)}, u32[]{:S(2)}, u32[]{:S(2)}) %collective-permute-start.16) | collective-permute-done | bytes 262176 | tf_op jit(solution)/shard_map/ppermute | solution.py:62
  184.0 1.0 collective-permute-start.17
  184.9 8.3 %collective-permute-done.10 = f32[32,16,256]{2,1,0:T(8,128)S(1)} collective-permute-done((f32[32,16,256]{2,1,0:T(8,128)S(1)}, f32[32,16,256]{2,1,0:T(8,128)S(1)}, u32[]{:S(2)}, u32[]{:S(2)}) %collective-permute-start.10) | collective-permute-done | bytes 524320 | tf_op jit(solution)/shard_map/ppermute | solution.py:62
  193.5 5.5 %collective-permute-done.17 = f32[32,16,256]{2,1,0:T(8,128)} collective-permute-done((f32[32,16,256]{2,1,0:T(8,128)S(1)}, f32[32,16,256]{2,1,0:T(8,128)}, u32[]{:S(2)}, u32[]{:S(2)}) %collective-permute-start.17) | collective-permute-done | bytes 524320 | tf_op jit(solution)/shard_map/ppermute | solution.py:62
  199.0 1.4 maximum_select_fusion.3
  200.7 0.6 reshape.264
  201.3 1.9 maximum_select_fusion
  203.4 1.6 copy.136
  205.1 0.9 copy.144
  206.0 1.1 multiply_reduce_fusion.5
  207.1 1.9 fusion.19
  209.2 1.6 copy.140
  210.9 0.9 copy.146
  211.8 2.8 %fusion.18 = pred[128,16,256]{2,1,0:T(8,128)(4,1)S(1)} fusion(f32[64,16,256]{2,1,0:T(8,128)S(1)} %maximum_select_fusion.3, f32[64,16,256]{2,1,0:T(8,128)} %collective-permute-done.18, pred[]{:T(512)S(6)} %eq.105), kind=kLoop, calls=%fused_computation.50 | loop fusion | flops 2097152 | bytes 2621441 | tf_op jit(solution)/shard_map/ge | solution.py:192
  215.1 0.3 copy.145
  215.7 3.5 %multiply_reduce_fusion.4 = (f32[]{:T(128)}, f32[256,2048]{1,0:T(8,128)}) fusion(f32[256,2048]{1,0:T(8,128)S(1)} %bitcast.58, pred[256,2048]{1,0:T(8,128)(4,1)S(1)} %bitcast.67, f32[256,2048]{1,0:T(8,128)S(1)} %broadcast_select_fusion.2, f32[256,2048]{1,0:T(8,128)S(1)} %bitcast.63), kind=kLoop, calls=%fused_computation.45 | loop fusion | flops 6291455 | bytes 8912900 | tf_op jit(solution)/shard_map/reduce_sum | solution.py:253
  220.6 2.7 %multiply_reduce_fusion.3 = f32[]{:T(128)} fusion(f32[256,2048]{1,0:T(8,128)S(1)} %bitcast.59, f32[256,2048]{1,0:T(8,128)} %get-tuple-element.21, f32[]{:T(128)S(6)} %div.31), kind=kLoop, calls=%fused_computation.43 | loop fusion | flops 2097151 | bytes 4194312 | tf_op jit(solution)/shard_map/reduce_sum | solution.py:256
  224.7 2.3 broadcast_select_fusion.1
  227.0 3.8 %multiply_reduce_fusion.2 = (f32[]{:T(128)}, f32[256,2048]{1,0:T(8,128)}) fusion(f32[256,2048]{1,0:T(8,128)S(1)} %get-tuple-element.19, pred[256,2048]{1,0:T(8,128)(4,1)S(1)} %bitcast.69, f32[256,2048]{1,0:T(8,128)S(1)} %get-tuple-element.18, f32[256,2048]{1,0:T(8,128)S(1)} %bitcast.64), kind=kLoop, calls=%fused_computation.41 | loop fusion | flops 6291455 | bytes 8912900 | tf_op jit(solution)/shard_map/reduce_sum | solution.py:253
  232.2 4.8 %multiply_reduce_fusion.1 = (f32[]{:T(128)}, f32[256,2048]{1,0:T(8,128)}) fusion(f32[256,2048]{1,0:T(8,128)} %get-tuple-element.17, f32[]{:T(128)S(6)} %div.33, f32[256,2048]{1,0:T(8,128)S(1)} %bitcast.61, f32[256,2048]{1,0:T(8,128)} %get-tuple-element.21, f32[]{:T(128)S(6)} %div.31), kind=kLoop, calls=%fused_computation.39 | loop fusion | flops 3145727 | bytes 8388620 | tf_op jit(solution)/shard_map/reduce_sum | solution.py:256
  238.3 2.9 %broadcast_select_fusion = (f32[256,2048]{1,0:T(8,128)S(1)}, f32[256,2048]{1,0:T(8,128)S(1)}) fusion(pred[256,2048]{1,0:T(8,128)(4,1)S(1)} %bitcast.70, f32[256,2048]{1,0:T(8,128)} %get-tuple-element.15, f32[256,2048]{1,0:T(8,128)} %copy-done.3, f32[]{:T(128)S(6)} %div.34), kind=kLoop, calls=%fused_computation.55 | loop fusion | flops 1572864 | bytes 8912900 | tf_op jit(solution)/shard_map/mul | solution.py:82
  241.2 3.5 %multiply_reduce_fusion = (f32[]{:T(128)}, f32[256,2048]{1,0:T(8,128)}) fusion(f32[256,2048]{1,0:T(8,128)S(1)} %get-tuple-element.13, pred[256,2048]{1,0:T(8,128)(4,1)S(1)} %bitcast.71, f32[256,2048]{1,0:T(8,128)S(1)} %get-tuple-element.12, f32[256,2048]{1,0:T(8,128)S(1)} %bitcast.65), kind=kLoop, calls=%fused_computation.37 | loop fusion | flops 6291455 | bytes 8912900 | tf_op jit(solution)/shard_map/reduce_sum | solution.py:253
  246.1 1.4 fusion.31
  247.4 1.3 dynamic-slice_subtract_fusion
  (102 shorter events, 5.1 us)
Async XLA Ops:
  7.5 16.5 %collective-permute-start.1 = (f32[128,32,4]{0,1,2:T(8,128)S(1)}, f32[128,32,4]{0,1,2:T(8,128)S(1)}, u32[]{:S(2)}, u32[]{:S(2)}) collective-permute-start(f32[128,32,4]{0,1,2:T(8,128)S(1)} %copy.143), channel_id=1, source_target_pairs={{0,16},{16,32},{32,48},{48,64},{64,80},{80,96},{96,112},{1,17},{17... | collective-permute-start | bytes 196616 | tf_op jit(solution)/shard_map/ppermute | solution.py:136
  10.6 11.5 %collective-permute-start = (f32[128,32,4]{0,1,2:T(8,128)S(1)}, f32[128,32,4]{0,1,2:T(8,128)S(1)}, u32[]{:S(2)}, u32[]{:S(2)}) collective-permute-start(f32[128,32,4]{0,1,2:T(8,128)S(1)} %copy.142), channel_id=1, source_target_pairs={{16,0},{32,16},{48,32},{64,48},{80,64},{96,80},{112,96},{17,1},{33... | collective-permute-start | bytes 196616 | tf_op jit(solution)/shard_map/ppermute | solution.py:135
  11.9 3.9 %copy-start.10 = (s32[4096]{0:T(1024)S(1)}, s32[4096]{0:T(1024)}, u32[]{:S(2)}) copy-start(s32[4096]{0:T(1024)} %param.12) | copy-start | bytes 49156
  11.9 4.0 %copy-start.7 = (s32[4096,4]{0,1:T(4,128)S(1)}, s32[4096,4]{0,1:T(4,128)}, u32[]{:S(2)}) copy-start(s32[4096,4]{0,1:T(4,128)} %param.11) | copy-start | bytes 196612
  19.9 0.5 copy-start.14
  22.1 4.8 %copy-start.17 = (f32[128]{0:T(128)S(1)}, f32[128]{0:T(128)}, u32[]{:S(2)}) copy-start(f32[128]{0:T(128)} %pad.76.clone) | copy-start | bytes 1540
  26.9 2.4 copy-start.6
  29.2 4.2 %copy-start.4 = (f32[128,32,128]{2,1,0:T(8,128)}, f32[128,32,128]{2,1,0:T(8,128)S(1)}, u32[]{:S(2)}) copy-start(f32[128,32,128]{2,1,0:T(8,128)S(1)} %pad_maximum_fusion.1.lanes_ref) | copy-start | bytes 6291460
  29.3 6.7 %copy-start.9 = (pred[1,128]{0,1:T(8,128)(4,1)S(1)}, pred[1,128]{0,1:T(8,128)(4,1)}, u32[]{:S(2)}) copy-start(pred[1,128]{0,1:T(8,128)(4,1)} %get-tuple-element.35) | copy-start | bytes 388
  29.3 6.9 %copy-start.16 = (s32[128]{0:T(128)S(1)}, s32[128]{0:T(128)}, u32[]{:S(2)}) copy-start(s32[128]{0:T(128)} %add_reduce_fusion) | copy-start | bytes 1540
  29.3 7.0 %copy-start.8 = (pred[1,128]{0,1:T(8,128)(4,1)S(1)}, pred[1,128]{0,1:T(8,128)(4,1)}, u32[]{:S(2)}) copy-start(pred[1,128]{0,1:T(8,128)(4,1)} %get-tuple-element.37) | copy-start | bytes 388
  29.6 31.6 %collective-permute-start.3 = (f32[128,4,640]{2,1,0:T(4,128)S(1)}, f32[128,4,640]{2,1,0:T(4,128)S(1)}, u32[]{:S(2)}, u32[]{:S(2)}) collective-permute-start(f32[128,4,640]{2,1,0:T(4,128)S(1)} %pad_maximum_fusion.3), channel_id=1, source_target_pairs={{0,1},{1,2},{2,3},{3,4},{4,5},{5,6},{6,7},{7,8},{8,9},{9,10},{10,1... | collective-permute-start | bytes 3932168 | tf_op jit(solution)/shard_map/ppermute | solution.py:142
  33.3 34.0 %collective-permute-start.2 = (f32[128,4,640]{2,1,0:T(4,128)S(1)}, f32[128,4,640]{2,1,0:T(4,128)S(1)}, u32[]{:S(2)}, u32[]{:S(2)}) collective-permute-start(f32[128,4,640]{2,1,0:T(4,128)S(1)} %pad_maximum_fusion.2), channel_id=1, source_target_pairs={{1,0},{2,1},{3,2},{4,3},{5,4},{6,5},{7,6},{8,7},{9,8},{10,9},{11,1... | collective-permute-start | bytes 3932168 | tf_op jit(solution)/shard_map/ppermute | solution.py:141
  69.4 71.4 %copy-start.15 = (pred[128]{0:T(512)(128)(4,1)S(1)}, pred[128]{0:T(512)(128)(4,1)}, u32[]{:S(2)}) copy-start(pred[128]{0:T(512)(128)(4,1)} %copy-done.14) | copy-start | bytes 388
  69.4 71.5 %copy-start.13 = (pred[128]{0:T(512)(128)(4,1)S(1)}, pred[128]{0:T(512)(128)(4,1)}, u32[]{:S(2)}) copy-start(pred[128]{0:T(512)(128)(4,1)} %get-tuple-element.36) | copy-start | bytes 388
  137.8 4.5 %collective-permute-start.4 = (bf16[32,4,128]{2,1,0:T(4,128)(2,1)S(1)}, bf16[32,4,128]{2,1,0:T(4,128)(2,1)S(1)}, u32[]{:S(2)}, u32[]{:S(2)}) collective-permute-start(bf16[32,4,128]{2,1,0:T(4,128)(2,1)S(1)} %broadcast_multiply_fusion), channel_id=1, source_target_pairs={{0,112},{16,0},{32,16},{48,32},{64,48},{80,64},{96,80},{112,96},{1... | collective-permute-start | bytes 98312 | tf_op jit(solution)/shard_map/ppermute | solution.py:27
  143.1 3.1 %copy-start.11 = (s32[16,256]{1,0:T(8,128)S(1)}, s32[16,256]{1,0:T(8,128)}, u32[]{:S(2)}) copy-start(s32[16,256]{1,0:T(8,128)} %param.14) | copy-start | bytes 49156
  143.1 3.1 %copy-start.12 = (f32[16,256]{1,0:T(8,128)S(1)}, f32[16,256]{1,0:T(8,128)}, u32[]{:S(2)}) copy-start(f32[16,256]{1,0:T(8,128)} %param.15) | copy-start | bytes 49156
  146.3 5.3 %collective-permute-start.5 = (f32[1,16,256]{2,1,0:T(8,128)S(1)}, f32[1,16,256]{2,1,0:T(8,128)S(1)}, u32[]{:S(2)}, u32[]{:S(2)}) collective-permute-start(f32[1,16,256]{2,1,0:T(8,128)S(1)} %get-tuple-element.40), channel_id=1, source_target_pairs={{0,2},{1,3},{2,0},{3,1},{4,6},{5,7},{6,4},{7,5},{8,10},{9,11},{10,... | collective-permute-start | bytes 49160 | tf_op jit(solution)/shard_map/ppermute | solution.py:62
  151.6 5.5 %collective-permute-start.6 = (f32[2,16,256]{2,1,0:T(8,128)S(1)}, f32[2,16,256]{2,1,0:T(8,128)S(1)}, u32[]{:S(2)}, u32[]{:S(2)}) collective-permute-start(f32[2,16,256]{2,1,0:T(8,128)S(1)} %maximum_select_fusion.12), channel_id=1, source_target_pairs={{0,8},{1,9},{2,10},{3,11},{4,12},{5,13},{6,14},{7,15},{8,0},{9,1},... | collective-permute-start | bytes 98312 | tf_op jit(solution)/shard_map/ppermute | solution.py:62
  154.5 6.5 %collective-permute-start.12 = (f32[1,16,256]{2,1,0:T(8,128)S(1)}, f32[1,16,256]{2,1,0:T(8,128)S(1)}, u32[]{:S(2)}, u32[]{:S(2)}) collective-permute-start(f32[1,16,256]{2,1,0:T(8,128)S(1)} %get-tuple-element.41), channel_id=1, source_target_pairs={{0,2},{1,3},{2,0},{3,1},{4,6},{5,7},{6,4},{7,5},{8,10},{9,11},{10,... | collective-permute-start | bytes 49160 | tf_op jit(solution)/shard_map/ppermute | solution.py:62
  157.1 6.9 %collective-permute-start.7 = (f32[4,16,256]{2,1,0:T(8,128)S(1)}, f32[4,16,256]{2,1,0:T(8,128)S(1)}, u32[]{:S(2)}, u32[]{:S(2)}) collective-permute-start(f32[4,16,256]{2,1,0:T(8,128)S(1)} %maximum_select_fusion.10), channel_id=1, source_target_pairs={{0,64},{16,80},{32,96},{48,112},{64,0},{80,16},{96,32},{112,48},{1... | collective-permute-start | bytes 196616 | tf_op jit(solution)/shard_map/ppermute | solution.py:62
  161.0 5.5 %collective-permute-start.13 = (f32[2,16,256]{2,1,0:T(8,128)S(1)}, f32[2,16,256]{2,1,0:T(8,128)S(1)}, u32[]{:S(2)}, u32[]{:S(2)}) collective-permute-start(f32[2,16,256]{2,1,0:T(8,128)S(1)} %maximum_select_fusion.13), channel_id=1, source_target_pairs={{0,8},{1,9},{2,10},{3,11},{4,12},{5,13},{6,14},{7,15},{8,0},{9,1},... | collective-permute-start | bytes 98312 | tf_op jit(solution)/shard_map/ppermute | solution.py:62
  164.0 5.1 %collective-permute-start.8 = (f32[8,16,256]{2,1,0:T(8,128)S(1)}, f32[8,16,256]{2,1,0:T(8,128)S(1)}, u32[]{:S(2)}, u32[]{:S(2)}) collective-permute-start(f32[8,16,256]{2,1,0:T(8,128)S(1)} %maximum_select_fusion.8), channel_id=1, source_target_pairs={{0,1},{1,0},{2,3},{3,2},{4,5},{5,4},{6,7},{7,6},{8,9},{9,8},{10,11... | collective-permute-start | bytes 393224 | tf_op jit(solution)/shard_map/ppermute | solution.py:62
  166.5 5.8 %collective-permute-start.14 = (f32[4,16,256]{2,1,0:T(8,128)S(1)}, f32[4,16,256]{2,1,0:T(8,128)S(1)}, u32[]{:S(2)}, u32[]{:S(2)}) collective-permute-start(f32[4,16,256]{2,1,0:T(8,128)S(1)} %maximum_select_fusion.11), channel_id=1, source_target_pairs={{0,64},{16,80},{32,96},{48,112},{64,0},{80,16},{96,32},{112,48},{1... | collective-permute-start | bytes 196616 | tf_op jit(solution)/shard_map/ppermute | solution.py:62
  169.2 9.9 %collective-permute-start.9 = (f32[16,16,256]{2,1,0:T(8,128)S(1)}, f32[16,16,256]{2,1,0:T(8,128)S(1)}, u32[]{:S(2)}, u32[]{:S(2)}) collective-permute-start(f32[16,16,256]{2,1,0:T(8,128)S(1)} %maximum_select_fusion.6), channel_id=1, source_target_pairs={{0,4},{1,5},{2,6},{3,7},{4,0},{5,1},{6,2},{7,3},{8,12},{9,13},{10,... | collective-permute-start | bytes 786440 | tf_op jit(solution)/shard_map/ppermute | solution.py:62
  172.4 5.0 %collective-permute-start.15 = (f32[8,16,256]{2,1,0:T(8,128)S(1)}, f32[8,16,256]{2,1,0:T(8,128)S(1)}, u32[]{:S(2)}, u32[]{:S(2)}) collective-permute-start(f32[8,16,256]{2,1,0:T(8,128)S(1)} %maximum_select_fusion.9), channel_id=1, source_target_pairs={{0,1},{1,0},{2,3},{3,2},{4,5},{5,4},{6,7},{7,6},{8,9},{9,8},{10,11... | collective-permute-start | bytes 393224 | tf_op jit(solution)/shard_map/ppermute | solution.py:62
  177.5 6.5 %collective-permute-start.16 = (f32[16,16,256]{2,1,0:T(8,128)S(1)}, f32[16,16,256]{2,1,0:T(8,128)S(1)}, u32[]{:S(2)}, u32[]{:S(2)}) collective-permute-start(f32[16,16,256]{2,1,0:T(8,128)S(1)} %maximum_select_fusion.7), channel_id=1, source_target_pairs={{0,4},{1,5},{2,6},{3,7},{4,0},{5,1},{6,2},{7,3},{8,12},{9,13},{10,... | collective-permute-start | bytes 786440 | tf_op jit(solution)/shard_map/ppermute | solution.py:62
  179.2 14.1 %collective-permute-start.10 = (f32[32,16,256]{2,1,0:T(8,128)S(1)}, f32[32,16,256]{2,1,0:T(8,128)S(1)}, u32[]{:S(2)}, u32[]{:S(2)}) collective-permute-start(f32[32,16,256]{2,1,0:T(8,128)S(1)} %maximum_select_fusion.4), channel_id=1, source_target_pairs={{0,32},{16,48},{32,0},{48,16},{64,96},{80,112},{96,64},{112,80},{1... | collective-permute-start | bytes 1572872 | tf_op jit(solution)/shard_map/ppermute | solution.py:62
  184.0 15.0 %collective-permute-start.17 = (f32[32,16,256]{2,1,0:T(8,128)S(1)}, f32[32,16,256]{2,1,0:T(8,128)}, u32[]{:S(2)}, u32[]{:S(2)}) collective-permute-start(f32[32,16,256]{2,1,0:T(8,128)S(1)} %maximum_select_fusion.5), channel_id=1, source_target_pairs={{0,32},{16,48},{32,0},{48,16},{64,96},{80,112},{96,64},{112,80},{1... | collective-permute-start | bytes 1572872 | tf_op jit(solution)/shard_map/ppermute | solution.py:62
  193.4 7.9 %collective-permute-start.11 = (f32[64,16,256]{2,1,0:T(8,128)S(1)}, f32[64,16,256]{2,1,0:T(8,128)}, u32[]{:S(2)}, u32[]{:S(2)}) collective-permute-start(f32[64,16,256]{2,1,0:T(8,128)S(1)} %maximum_select_fusion.2), channel_id=1, source_target_pairs={{0,16},{16,0},{32,48},{48,32},{64,80},{80,64},{96,112},{112,96},{1... | collective-permute-start | bytes 3145736 | tf_op jit(solution)/shard_map/ppermute | solution.py:62
  200.4 6.8 %collective-permute-start.18 = (f32[64,16,256]{2,1,0:T(8,128)S(1)}, f32[64,16,256]{2,1,0:T(8,128)}, u32[]{:S(2)}, u32[]{:S(2)}) collective-permute-start(f32[64,16,256]{2,1,0:T(8,128)S(1)} %maximum_select_fusion.3), channel_id=1, source_target_pairs={{0,16},{16,0},{32,48},{48,32},{64,80},{80,64},{96,112},{112,96},{1... | collective-permute-start | bytes 3145736 | tf_op jit(solution)/shard_map/ppermute | solution.py:62
  211.8 3.9 %copy-start = (f32[32,8,8,256]{3,1,2,0:T(8,128)}, f32[32,8,8,256]{3,1,2,0:T(8,128)S(1)}, u32[]{:S(2)}) copy-start(f32[32,8,8,256]{3,1,2,0:T(8,128)S(1)} %copy.146) | copy-start | bytes 6291460
  224.6 2.4 copy-start.1
  227.0 3.8 %copy-start.3 = (f32[256,2048]{1,0:T(8,128)}, f32[256,2048]{1,0:T(8,128)S(1)}, u32[]{:S(2)}) copy-start(f32[256,2048]{1,0:T(8,128)S(1)} %get-tuple-element.19) | copy-start | bytes 6291460
  238.3 3.0 %copy-start.2 = (f32[32,8,8,256]{3,1,2,0:T(8,128)S(1)}, f32[32,8,8,256]{3,1,2,0:T(8,128)}, u32[]{:S(2)}) copy-start(f32[32,8,8,256]{3,1,2,0:T(8,128)} %copy-done) | copy-start | bytes 6291460
  241.2 3.5 %copy-start.5 = (f32[256,2048]{1,0:T(8,128)}, f32[256,2048]{1,0:T(8,128)S(1)}, u32[]{:S(2)}) copy-start(f32[256,2048]{1,0:T(8,128)S(1)} %get-tuple-element.13) | copy-start | bytes 6291460

commit v3 on v2

--- a/solution.py
+++ b/solution.py
@@ -132,15 +132,31 @@
     down_gx = [(i + 1, i) for i in range(count_gx - 1)]
     up_gy = [(i, i + 1) for i in range(count_gy - 1)]
     down_gy = [(i + 1, i) for i in range(count_gy - 1)]
+    pairs = lambda di, dj: [
+        ((i + di) * count_gy + j + dj, i * count_gy + j)
+        for i in range(count_gx)
+        for j in range(count_gy)
+        if 0 <= i + di < count_gx and 0 <= j + dj < count_gy
+    ]
+    both = ("gx", "gy")
+    south = lax.ppermute(field[:, :HALO, :], "gy", down_gy)
+    north = lax.ppermute(field[:, rows - HALO :, :], "gy", up_gy)
     east = lax.ppermute(field[:, :, :HALO], "gx", down_gx)
     west = lax.ppermute(field[:, :, cols - HALO :], "gx", up_gx)
+    south_east = lax.ppermute(field[:, :HALO, :HALO], both, pairs(1, 1))
+    south_west = lax.ppermute(field[:, :HALO, cols - HALO :], both, pairs(-1, 1))
+    north_east = lax.ppermute(field[:, rows - HALO :, :HALO], both, pairs(1, -1))
+    north_west = lax.ppermute(field[:, rows - HALO :, cols - HALO :], both, pairs(-1, -1))
     gap = jnp.zeros((levels, rows, 128 - 2 * HALO), field.dtype)
     lanes = jnp.concatenate([east, gap, west], axis=2)
-    first = jnp.concatenate([field[:, :HALO, :], lanes[:, :HALO, :]], axis=2)
-    last = jnp.concatenate([field[:, rows - HALO :, :], lanes[:, rows - HALO :, :]], axis=2)
-    south = lax.ppermute(first, "gy", down_gy)
-    north = lax.ppermute(last, "gy", up_gy)
-    halo_rows = jnp.concatenate([south, north], axis=1)
+    corner_gap = jnp.zeros((levels, HALO, 128 - 2 * HALO), field.dtype)
+    halo_rows = jnp.concatenate(
+        [
+            jnp.concatenate([south, south_east, corner_gap, south_west], axis=2),
+            jnp.concatenate([north, north_east, corner_gap, north_west], axis=2),
+        ],
+        axis=1,
+    )
     height = rows + 2 * HALO
     width = cols + 128
     r = jnp.arange(height, dtype=jnp.int32)

time: 250 us -> 250 us (level); the launches traced: 249 us -> 246 us
  waiting for transfers between devices: 66.6 us -> 38.7 us
  starting transfers between devices: 28.5 us -> 46.5 us
  local copies, waits for them, and re-layouts: 30.2 us -> 35 us
  other arithmetic: 45.8 us -> 48.5 us
    ppermute x2 -> x6, waiting for transfers between devices: 29.9 us -> 2.9 us  [the longest x1 2.89 us: diffuse(): lax.ppermute(field[:, rows - HALO:, cols - HALO:], both, pairs(-1, -1))]
    ppermute x2 -> x6, starting transfers between devices: 6.02 us -> 22.3 us  [the longest x1 8.59 us: diffuse(): lax.ppermute(field[:, rows - HALO:, cols - HALO:], both, pairs(-1, -1))]
    slice x2, local copies, waits for them, and re-layouts: 3.86 us -> 7.02 us  [the longest x1 4.1 us: diffuse(): south = lax.ppermute(field[:, :HALO, :], 'gy', down_gy)]
    unnamed x42 -> x24, local copies, waits for them, and re-layouts: 7.31 us -> 8.03 us
  transfers between devices with their start and end apart: 19 -> 23, of which waited for: 11 -> 12; matrix products, arithmetic and copies ran while one was open for 9% -> 16% of each run, Pallas kernels for 0% -> 0%
where the time goes in v3:
time: 250 us; the launch traced here: 246 us
  Pallas kernels  66.5 us (27%)
  other arithmetic  48.5 us (19%)
  starting transfers between devices  46.5 us (19%)
  waiting for transfers between devices  38.7 us (15%)
  local copies, waits for them, and re-layouts  35 us (14%)
  between operations  7.93 us (3%)
  matrix products  3.04 us (1%)
    pallas_call x1, Pallas kernels, diffuse(): pl.pallas_call(diffusion_kernel, grid=(blocks,), in_specs=[smem, smem, pl...  66.5 us
    ppermute x14, waiting for transfers between devices, whole_grid(): other = lax.ppermute(x, axis, [(j, j ^ distance) for j in range(size)])  35.2 us
    ppermute x14, starting transfers between devices, whole_grid(): other = lax.ppermute(x, axis, [(j, j ^ distance) for j in range(size)])  17.6 us
    reduce_sum x3, other arithmetic, body(): alpha = norm_now / jnp.sum(direction * image)  10.8 us
    ppermute x1, starting transfers between devices, diffuse(): lax.ppermute(field[:, rows - HALO:, cols - HALO:], both, pairs(-1, -1))  8.59 us
    unnamed x24, local copies, waits for them, and re-layouts  8.03 us
    reduce_sum x2, other arithmetic, body(): norm_next = jnp.sum(residual * residual)  7.5 us
    mul x3, other arithmetic, grid_operator(): padded = jnp.pad(maskf * vector, 1)  5.52 us
  transfers between devices with their start and end apart: 23, of which 12 were waited for; matrix products, arithmetic and copies ran while one was open for 16% of the time, Pallas kernels for 0%

profile of v3, /device:TPU:6, one launch (start us, length us, event | category | flops | bytes accessed | tf_op | source)
XLA Modules:
  0.0 246.1 jit_solution(13134246595776738990)
XLA Ops:
  0.6 2.9 %fusion.50 = (f32[128,4,4]{2,1,0:T(4,128)}, f32[128,4,4]{2,1,0:T(4,128)}, f32[128,4,4]{2,1,0:T(4,128)}, f32[128,4,4]{2,1,0:T(4,128)}) fusion(f32[128,32,512]{2,1,0:T(8,128)} %core_ref.1), kind=kLoop, calls=%fused_computation.133 | loop fusion | bytes 65536 | tf_op jit(solution)/shard_map/slice | solution.py:146
  3.6 1.3 collective-permute-start.3
  4.8 4.1 %fusion.49 = (f32[128,4,512]{2,1,0:T(4,128)}, f32[128,4,512]{2,1,0:T(4,128)}) fusion(f32[128,32,512]{2,1,0:T(8,128)} %core_ref.1), kind=kLoop, calls=%fused_computation.132 | loop fusion | bytes 4194304 | tf_op jit(solution)/shard_map/slice | solution.py:142
  8.9 2.7 %collective-permute-start.2 = (f32[128,4,512]{2,1,0:T(4,128)}, f32[128,4,512]{2,1,0:T(4,128)S(1)}, u32[]{:S(2)}, u32[]{:S(2)}) collective-permute-start(f32[128,4,512]{2,1,0:T(4,128)} %get-tuple-element.28), channel_id=1, source_target_pairs={{1,0},{2,1},{3,2},{4,3},{5,4},{6,5},{7,6},{8,7},{9,8},{10,9},{11,1... | collective-permute-start | bytes 3145736 | tf_op jit(solution)/shard_map/ppermute | solution.py:142
  11.7 5.2 %collective-permute-start.5 = (f32[128,4,512]{2,1,0:T(4,128)}, f32[128,4,512]{2,1,0:T(4,128)}, u32[]{:S(2)}, u32[]{:S(2)}) collective-permute-start(f32[128,4,512]{2,1,0:T(4,128)} %get-tuple-element.29), channel_id=1, source_target_pairs={{0,1},{1,2},{2,3},{3,4},{4,5},{5,6},{6,7},{7,8},{8,9},{9,10},{10,1... | collective-permute-start | bytes 3145736 | tf_op jit(solution)/shard_map/ppermute | solution.py:143
  16.9 4.3 %fusion.51 = (f32[128,32,4]{2,1,0:T(8,128)S(1)}, f32[128,32,4]{2,1,0:T(8,128)}) fusion(f32[128,32,512]{2,1,0:T(8,128)} %core_ref.1), kind=kLoop, calls=%fused_computation.134 | loop fusion | bytes 262144 | tf_op jit(solution)/shard_map/slice | solution.py:144
  21.2 3.3 %copy.143 = f32[128,32,4]{0,1,2:T(8,128)} copy(f32[128,32,4]{2,1,0:T(8,128)} %get-tuple-element.35) | data formatting | bytes 131072
  24.5 2.9 %collective-permute-start.1 = (f32[128,32,4]{0,1,2:T(8,128)}, f32[128,32,4]{0,1,2:T(8,128)S(1)}, u32[]{:S(2)}, u32[]{:S(2)}) collective-permute-start(f32[128,32,4]{0,1,2:T(8,128)} %copy.143), channel_id=1, source_target_pairs={{0,16},{16,32},{32,48},{48,64},{64,80},{80,96},{96,112},{1,17},{17... | collective-permute-start | bytes 196616 | tf_op jit(solution)/shard_map/ppermute | solution.py:145
  27.4 1.9 copy.142
  29.3 1.3 collective-permute-start
  32.0 0.7 copy.122
  32.7 1.6 reshape.262
  34.5 0.7 broadcast_compare_fusion
  36.7 1.4 and_convert_fusion.mask_ref
  38.2 3.2 %collective-permute-start.4 = (f32[128,4,4]{2,1,0:T(4,128)}, f32[128,4,4]{2,1,0:T(4,128)}, u32[]{:S(2)}, u32[]{:S(2)}) collective-permute-start(f32[128,4,4]{2,1,0:T(4,128)} %get-tuple-element.31), channel_id=1, source_target_pairs={{1,16},{2,17},{3,18},{4,19},{5,20},{6,21},{7,22},{8,23},{9,24},{10... | collective-permute-start | bytes 24584 | tf_op jit(solution)/shard_map/ppermute | solution.py:147
  41.4 2.7 %copy.119 = f32[128,32,4]{2,1,0:T(8,128)S(1)} copy(f32[128,32,4]{0,1,2:T(8,128)} %collective-permute-done) | data formatting | bytes 131072 | tf_op jit(solution)/shard_map/ppermute | solution.py:144
  44.2 1.3 collective-permute-start.6
  45.5 2.9 %copy.120 = f32[128,32,4]{2,1,0:T(8,128)} copy(f32[128,32,4]{0,1,2:T(8,128)S(1)} %collective-permute-done.1) | data formatting | bytes 131072 | tf_op jit(solution)/shard_map/ppermute | solution.py:145
  48.3 8.6 %collective-permute-start.7 = (f32[128,4,4]{2,1,0:T(4,128)}, f32[128,4,4]{2,1,0:T(4,128)S(1)}, u32[]{:S(2)}, u32[]{:S(2)}) collective-permute-start(f32[128,4,4]{2,1,0:T(4,128)} %get-tuple-element.33), channel_id=1, source_target_pairs={{0,17},{1,18},{2,19},{3,20},{4,21},{5,22},{6,23},{7,24},{8,25},{9,... | collective-permute-start | bytes 24584 | tf_op jit(solution)/shard_map/ppermute | solution.py:149
  56.9 3.5 %pad_maximum_fusion.lanes_ref = f32[128,32,128]{2,1,0:T(8,128)} fusion(f32[128,32,4]{2,1,0:T(8,128)} %copy.120, f32[128,32,4]{2,1,0:T(8,128)S(1)} %copy.119, f32[128]{0:T(128)S(1)} %pad.78.clone), kind=kLoop, calls=%fused_computation.34 | loop fusion | flops 1048576 | bytes 2228736 | tf_op jit(solution)/shard_map/concatenate | solution.py:151
  60.5 2.9 %collective-permute-done.7 = f32[128,4,4]{2,1,0:T(4,128)S(1)} collective-permute-done((f32[128,4,4]{2,1,0:T(4,128)}, f32[128,4,4]{2,1,0:T(4,128)S(1)}, u32[]{:S(2)}, u32[]{:S(2)}) %collective-permute-start.7) | collective-permute-done | bytes 8224 | tf_op jit(solution)/shard_map/ppermute | solution.py:149
  63.4 3.8 %maximum_maximum_fusion.rows_ref = f32[128,8,640]{2,1,0:T(8,128)} fusion(f32[128,4,4]{2,1,0:T(4,128)S(1)} %collective-permute-done.7, f32[128,4,120]{2,1,0:T(4,128)S(1)} %broadcast_in_dim.52, f32[128,4,4]{2,1,0:T(4,128)} %collective-permute-done.6, f32[128,4,512]{2,1,0:T(4,128)} %collective-permute-done.5, f32[128,4,4]{2,1,0:T(4,128)} %collective-permute-done.4, ...), kind=kLoop, calls=%fused_computation.3 | loop fusion | flops 4587520 | bytes 4997120 | tf_op jit(solution)/shard_map/concatenate | solution.py:153
  67.2 66.5 %shard_map.111 = (f32[128,32,512]{2,1,0:T(8,128)}, f32[4,32,512]{2,1,0:T(8,128)}) custom-call(f32[128]{0:T(128)} %kappa_ref.1, f32[4,128]{1,0:T(4,128)} %weight_ref.1, f32[128,32,512]{2,1,0:T(8,128)} %core_ref.1, f32[128,32,128]{2,1,0:T(8,128)} %pad_maximum_fusion.lanes_ref, f32[128,8,640]{2,1,0:T(8,128)} %maximum_maximum_fusion.rows_ref, ...), custom_call_target="tpu_custom_call" | custom-call | flops 131072000 | bytes 16777216 | tf_op jit(solution)/shard_map/pallas_call | solution.py:171
  133.7 1.0 convert_element_type.47
  135.6 2.4 collective-permute-start.8
  138.3 0.8 gather_fusion
  139.6 0.7 gather_fusion.2
  140.4 3.0 %convolution_bitcast_fusion = f32[4,32,128]{2,0,1:T(4,128)S(1)} fusion(bf16[32,4,128,128]{3,2,1,0:T(8,128)(2,1)} %param.13, bf16[32,4,4,128]{3,2,1,0:T(4,128)(2,1)S(1)} %bitcast.85, bf16[32,4,4,128]{3,2,1,0:T(4,128)(2,1)S(1)} %bitcast.86, pred[32,4]{1,0:T(8,128)(4,1)S(1)} %and.145, pred[32,4]{1,0:T(8,128)(4,1)S(1)} %and.141), kind=kOutput, calls=%fused_computation.50 | convolution fusion | flops 16908288 | bytes 4522240 | tf_op jit(solution)/shard_map/bkij,bkcj->cbi/dot_general | solution.py:257
  143.7 5.2 %collective-permute-done.9 = f32[1,16,256]{2,1,0:T(8,128)S(1)} collective-permute-done((f32[1,16,256]{2,1,0:T(8,128)S(1)}, f32[1,16,256]{2,1,0:T(8,128)S(1)}, u32[]{:S(2)}, u32[]{:S(2)}) %collective-permute-start.9) | collective-permute-done | bytes 16416 | tf_op jit(solution)/shard_map/ppermute | solution.py:62
  148.9 3.2 %collective-permute-start.10 = (f32[2,16,256]{2,1,0:T(8,128)S(1)}, f32[2,16,256]{2,1,0:T(8,128)S(1)}, u32[]{:S(2)}, u32[]{:S(2)}) collective-permute-start(f32[2,16,256]{2,1,0:T(8,128)S(1)} %maximum_select_fusion.12), channel_id=1, source_target_pairs={{0,8},{1,9},{2,10},{3,11},{4,12},{5,13},{6,14},{7,15},{8,0},{9,1},... | collective-permute-start | bytes 98312 | tf_op jit(solution)/shard_map/ppermute | solution.py:62
  152.1 2.2 collective-permute-done.10
  154.3 2.5 %collective-permute-start.11 = (f32[4,16,256]{2,1,0:T(8,128)S(1)}, f32[4,16,256]{2,1,0:T(8,128)S(1)}, u32[]{:S(2)}, u32[]{:S(2)}) collective-permute-start(f32[4,16,256]{2,1,0:T(8,128)S(1)} %maximum_select_fusion.10), channel_id=1, source_target_pairs={{0,64},{16,80},{32,96},{48,112},{64,0},{80,16},{96,32},{112,48},{1... | collective-permute-start | bytes 196616 | tf_op jit(solution)/shard_map/ppermute | solution.py:62
  157.3 2.8 %collective-permute-start.17 = (f32[2,16,256]{2,1,0:T(8,128)S(1)}, f32[2,16,256]{2,1,0:T(8,128)S(1)}, u32[]{:S(2)}, u32[]{:S(2)}) collective-permute-start(f32[2,16,256]{2,1,0:T(8,128)S(1)} %maximum_select_fusion.13), channel_id=1, source_target_pairs={{0,8},{1,9},{2,10},{3,11},{4,12},{5,13},{6,14},{7,15},{8,0},{9,1},... | collective-permute-start | bytes 98312 | tf_op jit(solution)/shard_map/ppermute | solution.py:62
  160.2 0.8 collective-permute-start.12
  161.0 1.8 collective-permute-done.17
  162.8 2.4 collective-permute-start.18
  165.3 1.7 collective-permute-start.13
  166.9 1.7 collective-permute-done.18
  168.8 4.8 %collective-permute-done.19 = f32[8,16,256]{2,1,0:T(8,128)S(1)} collective-permute-done((f32[8,16,256]{2,1,0:T(8,128)S(1)}, f32[8,16,256]{2,1,0:T(8,128)S(1)}, u32[]{:S(2)}, u32[]{:S(2)}) %collective-permute-start.19) | collective-permute-done | bytes 131104 | tf_op jit(solution)/shard_map/ppermute | solution.py:62
  173.7 1.2 collective-permute-start.20
  175.0 1.1 collective-permute-start.14
  176.1 4.0 %collective-permute-done.20 = f32[16,16,256]{2,1,0:T(8,128)S(1)} collective-permute-done((f32[16,16,256]{2,1,0:T(8,128)S(1)}, f32[16,16,256]{2,1,0:T(8,128)S(1)}, u32[]{:S(2)}, u32[]{:S(2)}) %collective-permute-start.20) | collective-permute-done | bytes 262176 | tf_op jit(solution)/shard_map/ppermute | solution.py:62
  180.2 1.2 collective-permute-start.21
  181.4 8.5 %collective-permute-done.14 = f32[32,16,256]{2,1,0:T(8,128)S(1)} collective-permute-done((f32[32,16,256]{2,1,0:T(8,128)S(1)}, f32[32,16,256]{2,1,0:T(8,128)S(1)}, u32[]{:S(2)}, u32[]{:S(2)}) %collective-permute-start.14) | collective-permute-done | bytes 524320 | tf_op jit(solution)/shard_map/ppermute | solution.py:62
  190.1 6.2 %collective-permute-done.21 = f32[32,16,256]{2,1,0:T(8,128)} collective-permute-done((f32[32,16,256]{2,1,0:T(8,128)S(1)}, f32[32,16,256]{2,1,0:T(8,128)}, u32[]{:S(2)}, u32[]{:S(2)}) %collective-permute-start.21) | collective-permute-done | bytes 524320 | tf_op jit(solution)/shard_map/ppermute | solution.py:62
  196.3 1.4 maximum_select_fusion.3
  198.0 0.6 reshape.264
  198.7 1.9 maximum_select_fusion
  200.8 1.6 copy.136
  202.4 0.9 copy.144
  203.3 1.1 multiply_reduce_fusion.5
  204.5 1.9 fusion.19
  206.6 1.6 copy.140
  208.2 0.9 copy.146
  209.1 2.8 %fusion.18 = pred[128,16,256]{2,1,0:T(8,128)(4,1)S(1)} fusion(f32[64,16,256]{2,1,0:T(8,128)S(1)} %maximum_select_fusion.3, f32[64,16,256]{2,1,0:T(8,128)} %collective-permute-done.22, pred[]{:T(512)S(6)} %eq.105), kind=kLoop, calls=%fused_computation.48 | loop fusion | flops 2097152 | bytes 2621441 | tf_op jit(solution)/shard_map/ge | solution.py:208
  213.0 3.5 %multiply_reduce_fusion.4 = (f32[]{:T(128)}, f32[256,2048]{1,0:T(8,128)}) fusion(f32[256,2048]{1,0:T(8,128)S(1)} %bitcast.58, pred[256,2048]{1,0:T(8,128)(4,1)S(1)} %bitcast.67, f32[256,2048]{1,0:T(8,128)S(1)} %broadcast_select_fusion.2, f32[256,2048]{1,0:T(8,128)S(1)} %bitcast.63), kind=kLoop, calls=%fused_computation.45 | loop fusion | flops 6291455 | bytes 8912900 | tf_op jit(solution)/shard_map/reduce_sum | solution.py:269
  217.9 2.7 %multiply_reduce_fusion.3 = f32[]{:T(128)} fusion(f32[256,2048]{1,0:T(8,128)S(1)} %bitcast.59, f32[256,2048]{1,0:T(8,128)} %get-tuple-element.21, f32[]{:T(128)S(6)} %div.31), kind=kLoop, calls=%fused_computation.43 | loop fusion | flops 2097151 | bytes 4194312 | tf_op jit(solution)/shard_map/reduce_sum | solution.py:272
  222.0 2.3 broadcast_select_fusion.1
  224.4 3.8 %multiply_reduce_fusion.2 = (f32[]{:T(128)}, f32[256,2048]{1,0:T(8,128)}) fusion(f32[256,2048]{1,0:T(8,128)S(1)} %get-tuple-element.19, pred[256,2048]{1,0:T(8,128)(4,1)S(1)} %bitcast.69, f32[256,2048]{1,0:T(8,128)S(1)} %get-tuple-element.18, f32[256,2048]{1,0:T(8,128)S(1)} %bitcast.64), kind=kLoop, calls=%fused_computation.41 | loop fusion | flops 6291455 | bytes 8912900 | tf_op jit(solution)/shard_map/reduce_sum | solution.py:269
  229.5 4.8 %multiply_reduce_fusion.1 = (f32[]{:T(128)}, f32[256,2048]{1,0:T(8,128)}) fusion(f32[256,2048]{1,0:T(8,128)} %get-tuple-element.17, f32[]{:T(128)S(6)} %div.33, f32[256,2048]{1,0:T(8,128)S(1)} %bitcast.61, f32[256,2048]{1,0:T(8,128)} %get-tuple-element.21, f32[]{:T(128)S(6)} %div.31), kind=kLoop, calls=%fused_computation.39 | loop fusion | flops 3145727 | bytes 8388620 | tf_op jit(solution)/shard_map/reduce_sum | solution.py:272
  235.6 2.9 %broadcast_select_fusion = (f32[256,2048]{1,0:T(8,128)S(1)}, f32[256,2048]{1,0:T(8,128)S(1)}) fusion(pred[256,2048]{1,0:T(8,128)(4,1)S(1)} %bitcast.70, f32[256,2048]{1,0:T(8,128)} %get-tuple-element.15, f32[256,2048]{1,0:T(8,128)} %copy-done.3, f32[]{:T(128)S(6)} %div.34), kind=kLoop, calls=%fused_computation.53 | loop fusion | flops 1572864 | bytes 8912900 | tf_op jit(solution)/shard_map/mul | solution.py:82
  238.6 3.5 %multiply_reduce_fusion = (f32[]{:T(128)}, f32[256,2048]{1,0:T(8,128)}) fusion(f32[256,2048]{1,0:T(8,128)S(1)} %get-tuple-element.13, pred[256,2048]{1,0:T(8,128)(4,1)S(1)} %bitcast.71, f32[256,2048]{1,0:T(8,128)S(1)} %get-tuple-element.12, f32[256,2048]{1,0:T(8,128)S(1)} %bitcast.65), kind=kLoop, calls=%fused_computation.37 | loop fusion | flops 6291455 | bytes 8912900 | tf_op jit(solution)/shard_map/reduce_sum | solution.py:269
  243.4 1.4 fusion.31
  244.8 1.3 dynamic-slice_subtract_fusion
  (91 shorter events, 7.9 us)
Async XLA Ops:
  3.6 44.8 %collective-permute-start.3 = (f32[128,4,4]{2,1,0:T(4,128)}, f32[128,4,4]{2,1,0:T(4,128)S(1)}, u32[]{:S(2)}, u32[]{:S(2)}) collective-permute-start(f32[128,4,4]{2,1,0:T(4,128)} %get-tuple-element.30), channel_id=1, source_target_pairs={{17,0},{18,1},{19,2},{20,3},{21,4},{22,5},{23,6},{24,7},{25,8},{26... | collective-permute-start | bytes 24584 | tf_op jit(solution)/shard_map/ppermute | solution.py:146
  8.9 54.4 %collective-permute-start.2 = (f32[128,4,512]{2,1,0:T(4,128)}, f32[128,4,512]{2,1,0:T(4,128)S(1)}, u32[]{:S(2)}, u32[]{:S(2)}) collective-permute-start(f32[128,4,512]{2,1,0:T(4,128)} %get-tuple-element.28), channel_id=1, source_target_pairs={{1,0},{2,1},{3,2},{4,3},{5,4},{6,5},{7,6},{8,7},{9,8},{10,9},{11,1... | collective-permute-start | bytes 3145736 | tf_op jit(solution)/shard_map/ppermute | solution.py:142
  11.7 51.7 %collective-permute-start.5 = (f32[128,4,512]{2,1,0:T(4,128)}, f32[128,4,512]{2,1,0:T(4,128)}, u32[]{:S(2)}, u32[]{:S(2)}) collective-permute-start(f32[128,4,512]{2,1,0:T(4,128)} %get-tuple-element.29), channel_id=1, source_target_pairs={{0,1},{1,2},{2,3},{3,4},{4,5},{5,6},{6,7},{7,8},{8,9},{9,10},{10,1... | collective-permute-start | bytes 3145736 | tf_op jit(solution)/shard_map/ppermute | solution.py:143
  21.2 10.7 %copy-start.6 = (s32[4096]{0:T(1024)S(1)}, s32[4096]{0:T(1024)}, u32[]{:S(2)}) copy-start(s32[4096]{0:T(1024)} %param.12) | copy-start | bytes 49156
  21.2 10.8 %copy-start.5 = (s32[4096,4]{0,1:T(4,128)S(1)}, s32[4096,4]{0,1:T(4,128)}, u32[]{:S(2)}) copy-start(s32[4096,4]{0,1:T(4,128)} %param.11) | copy-start | bytes 196612
  24.5 19.7 %collective-permute-start.1 = (f32[128,32,4]{0,1,2:T(8,128)}, f32[128,32,4]{0,1,2:T(8,128)S(1)}, u32[]{:S(2)}, u32[]{:S(2)}) collective-permute-start(f32[128,32,4]{0,1,2:T(8,128)} %copy.143), channel_id=1, source_target_pairs={{0,16},{16,32},{32,48},{48,64},{64,80},{80,96},{96,112},{1,17},{17... | collective-permute-start | bytes 196616 | tf_op jit(solution)/shard_map/ppermute | solution.py:145
  29.3 8.9 %collective-permute-start = (f32[128,32,4]{0,1,2:T(8,128)}, f32[128,32,4]{0,1,2:T(8,128)}, u32[]{:S(2)}, u32[]{:S(2)}) collective-permute-start(f32[128,32,4]{0,1,2:T(8,128)} %copy.142), channel_id=1, source_target_pairs={{16,0},{32,16},{48,32},{64,48},{80,64},{96,80},{112,96},{17,1},{33... | collective-permute-start | bytes 196616 | tf_op jit(solution)/shard_map/ppermute | solution.py:144
  38.2 22.3 %collective-permute-start.4 = (f32[128,4,4]{2,1,0:T(4,128)}, f32[128,4,4]{2,1,0:T(4,128)}, u32[]{:S(2)}, u32[]{:S(2)}) collective-permute-start(f32[128,4,4]{2,1,0:T(4,128)} %get-tuple-element.31), channel_id=1, source_target_pairs={{1,16},{2,17},{3,18},{4,19},{5,20},{6,21},{7,22},{8,23},{9,24},{10... | collective-permute-start | bytes 24584 | tf_op jit(solution)/shard_map/ppermute | solution.py:147
  44.2 16.3 %collective-permute-start.6 = (f32[128,4,4]{2,1,0:T(4,128)}, f32[128,4,4]{2,1,0:T(4,128)}, u32[]{:S(2)}, u32[]{:S(2)}) collective-permute-start(f32[128,4,4]{2,1,0:T(4,128)} %get-tuple-element.32), channel_id=1, source_target_pairs={{16,1},{17,2},{18,3},{19,4},{20,5},{21,6},{22,7},{23,8},{24,9},{25... | collective-permute-start | bytes 24584 | tf_op jit(solution)/shard_map/ppermute | solution.py:148
  48.3 15.0 %collective-permute-start.7 = (f32[128,4,4]{2,1,0:T(4,128)}, f32[128,4,4]{2,1,0:T(4,128)S(1)}, u32[]{:S(2)}, u32[]{:S(2)}) collective-permute-start(f32[128,4,4]{2,1,0:T(4,128)} %get-tuple-element.33), channel_id=1, source_target_pairs={{0,17},{1,18},{2,19},{3,20},{4,21},{5,22},{6,23},{7,24},{8,25},{9,... | collective-permute-start | bytes 24584 | tf_op jit(solution)/shard_map/ppermute | solution.py:149
  135.6 4.0 %collective-permute-start.8 = (bf16[32,4,128]{2,1,0:T(4,128)(2,1)S(1)}, bf16[32,4,128]{2,1,0:T(4,128)(2,1)S(1)}, u32[]{:S(2)}, u32[]{:S(2)}) collective-permute-start(bf16[32,4,128]{2,1,0:T(4,128)(2,1)S(1)} %broadcast_multiply_fusion), channel_id=1, source_target_pairs={{0,112},{16,0},{32,16},{48,32},{64,48},{80,64},{96,80},{112,96},{1... | collective-permute-start | bytes 98312 | tf_op jit(solution)/shard_map/ppermute | solution.py:27
  140.4 3.1 %copy-start.7 = (s32[16,256]{1,0:T(8,128)S(1)}, s32[16,256]{1,0:T(8,128)}, u32[]{:S(2)}) copy-start(s32[16,256]{1,0:T(8,128)} %param.14) | copy-start | bytes 49156
  140.4 3.1 %copy-start.8 = (f32[16,256]{1,0:T(8,128)S(1)}, f32[16,256]{1,0:T(8,128)}, u32[]{:S(2)}) copy-start(f32[16,256]{1,0:T(8,128)} %param.15) | copy-start | bytes 49156
  143.6 5.3 %collective-permute-start.9 = (f32[1,16,256]{2,1,0:T(8,128)S(1)}, f32[1,16,256]{2,1,0:T(8,128)S(1)}, u32[]{:S(2)}, u32[]{:S(2)}) collective-permute-start(f32[1,16,256]{2,1,0:T(8,128)S(1)} %get-tuple-element.42), channel_id=1, source_target_pairs={{0,2},{1,3},{2,0},{3,1},{4,6},{5,7},{6,4},{7,5},{8,10},{9,11},{10,... | collective-permute-start | bytes 49160 | tf_op jit(solution)/shard_map/ppermute | solution.py:62
  148.9 5.4 %collective-permute-start.10 = (f32[2,16,256]{2,1,0:T(8,128)S(1)}, f32[2,16,256]{2,1,0:T(8,128)S(1)}, u32[]{:S(2)}, u32[]{:S(2)}) collective-permute-start(f32[2,16,256]{2,1,0:T(8,128)S(1)} %maximum_select_fusion.12), channel_id=1, source_target_pairs={{0,8},{1,9},{2,10},{3,11},{4,12},{5,13},{6,14},{7,15},{8,0},{9,1},... | collective-permute-start | bytes 98312 | tf_op jit(solution)/shard_map/ppermute | solution.py:62
  152.1 5.2 %collective-permute-start.16 = (f32[1,16,256]{2,1,0:T(8,128)S(1)}, f32[1,16,256]{2,1,0:T(8,128)S(1)}, u32[]{:S(2)}, u32[]{:S(2)}) collective-permute-start(f32[1,16,256]{2,1,0:T(8,128)S(1)} %get-tuple-element.43), channel_id=1, source_target_pairs={{0,2},{1,3},{2,0},{3,1},{4,6},{5,7},{6,4},{7,5},{8,10},{9,11},{10,... | collective-permute-start | bytes 49160 | tf_op jit(solution)/shard_map/ppermute | solution.py:62
  154.3 5.8 %collective-permute-start.11 = (f32[4,16,256]{2,1,0:T(8,128)S(1)}, f32[4,16,256]{2,1,0:T(8,128)S(1)}, u32[]{:S(2)}, u32[]{:S(2)}) collective-permute-start(f32[4,16,256]{2,1,0:T(8,128)S(1)} %maximum_select_fusion.10), channel_id=1, source_target_pairs={{0,64},{16,80},{32,96},{48,112},{64,0},{80,16},{96,32},{112,48},{1... | collective-permute-start | bytes 196616 | tf_op jit(solution)/shard_map/ppermute | solution.py:62
  157.3 5.4 %collective-permute-start.17 = (f32[2,16,256]{2,1,0:T(8,128)S(1)}, f32[2,16,256]{2,1,0:T(8,128)S(1)}, u32[]{:S(2)}, u32[]{:S(2)}) collective-permute-start(f32[2,16,256]{2,1,0:T(8,128)S(1)} %maximum_select_fusion.13), channel_id=1, source_target_pairs={{0,8},{1,9},{2,10},{3,11},{4,12},{5,13},{6,14},{7,15},{8,0},{9,1},... | collective-permute-start | bytes 98312 | tf_op jit(solution)/shard_map/ppermute | solution.py:62
  160.2 5.0 %collective-permute-start.12 = (f32[8,16,256]{2,1,0:T(8,128)S(1)}, f32[8,16,256]{2,1,0:T(8,128)S(1)}, u32[]{:S(2)}, u32[]{:S(2)}) collective-permute-start(f32[8,16,256]{2,1,0:T(8,128)S(1)} %maximum_select_fusion.8), channel_id=1, source_target_pairs={{0,1},{1,0},{2,3},{3,2},{4,5},{5,4},{6,7},{7,6},{8,9},{9,8},{10,11... | collective-permute-start | bytes 393224 | tf_op jit(solution)/shard_map/ppermute | solution.py:62
  162.8 5.8 %collective-permute-start.18 = (f32[4,16,256]{2,1,0:T(8,128)S(1)}, f32[4,16,256]{2,1,0:T(8,128)S(1)}, u32[]{:S(2)}, u32[]{:S(2)}) collective-permute-start(f32[4,16,256]{2,1,0:T(8,128)S(1)} %maximum_select_fusion.11), channel_id=1, source_target_pairs={{0,64},{16,80},{32,96},{48,112},{64,0},{80,16},{96,32},{112,48},{1... | collective-permute-start | bytes 196616 | tf_op jit(solution)/shard_map/ppermute | solution.py:62
  165.3 9.7 %collective-permute-start.13 = (f32[16,16,256]{2,1,0:T(8,128)S(1)}, f32[16,16,256]{2,1,0:T(8,128)S(1)}, u32[]{:S(2)}, u32[]{:S(2)}) collective-permute-start(f32[16,16,256]{2,1,0:T(8,128)S(1)} %maximum_select_fusion.6), channel_id=1, source_target_pairs={{0,4},{1,5},{2,6},{3,7},{4,0},{5,1},{6,2},{7,3},{8,12},{9,13},{10,... | collective-permute-start | bytes 786440 | tf_op jit(solution)/shard_map/ppermute | solution.py:62
  168.6 5.0 %collective-permute-start.19 = (f32[8,16,256]{2,1,0:T(8,128)S(1)}, f32[8,16,256]{2,1,0:T(8,128)S(1)}, u32[]{:S(2)}, u32[]{:S(2)}) collective-permute-start(f32[8,16,256]{2,1,0:T(8,128)S(1)} %maximum_select_fusion.9), channel_id=1, source_target_pairs={{0,1},{1,0},{2,3},{3,2},{4,5},{5,4},{6,7},{7,6},{8,9},{9,8},{10,11... | collective-permute-start | bytes 393224 | tf_op jit(solution)/shard_map/ppermute | solution.py:62
  173.7 6.5 %collective-permute-start.20 = (f32[16,16,256]{2,1,0:T(8,128)S(1)}, f32[16,16,256]{2,1,0:T(8,128)S(1)}, u32[]{:S(2)}, u32[]{:S(2)}) collective-permute-start(f32[16,16,256]{2,1,0:T(8,128)S(1)} %maximum_select_fusion.7), channel_id=1, source_target_pairs={{0,4},{1,5},{2,6},{3,7},{4,0},{5,1},{6,2},{7,3},{8,12},{9,13},{10,... | collective-permute-start | bytes 786440 | tf_op jit(solution)/shard_map/ppermute | solution.py:62
  175.0 14.9 %collective-permute-start.14 = (f32[32,16,256]{2,1,0:T(8,128)S(1)}, f32[32,16,256]{2,1,0:T(8,128)S(1)}, u32[]{:S(2)}, u32[]{:S(2)}) collective-permute-start(f32[32,16,256]{2,1,0:T(8,128)S(1)} %maximum_select_fusion.4), channel_id=1, source_target_pairs={{0,32},{16,48},{32,0},{48,16},{64,96},{80,112},{96,64},{112,80},{1... | collective-permute-start | bytes 1572872 | tf_op jit(solution)/shard_map/ppermute | solution.py:62
  180.2 16.1 %collective-permute-start.21 = (f32[32,16,256]{2,1,0:T(8,128)S(1)}, f32[32,16,256]{2,1,0:T(8,128)}, u32[]{:S(2)}, u32[]{:S(2)}) collective-permute-start(f32[32,16,256]{2,1,0:T(8,128)S(1)} %maximum_select_fusion.5), channel_id=1, source_target_pairs={{0,32},{16,48},{32,0},{48,16},{64,96},{80,112},{96,64},{112,80},{1... | collective-permute-start | bytes 1572872 | tf_op jit(solution)/shard_map/ppermute | solution.py:62
  190.1 8.6 %collective-permute-start.15 = (f32[64,16,256]{2,1,0:T(8,128)S(1)}, f32[64,16,256]{2,1,0:T(8,128)}, u32[]{:S(2)}, u32[]{:S(2)}) collective-permute-start(f32[64,16,256]{2,1,0:T(8,128)S(1)} %maximum_select_fusion.2), channel_id=1, source_target_pairs={{0,16},{16,0},{32,48},{48,32},{64,80},{80,64},{96,112},{112,96},{1... | collective-permute-start | bytes 3145736 | tf_op jit(solution)/shard_map/ppermute | solution.py:62
  197.7 6.8 %collective-permute-start.22 = (f32[64,16,256]{2,1,0:T(8,128)S(1)}, f32[64,16,256]{2,1,0:T(8,128)}, u32[]{:S(2)}, u32[]{:S(2)}) collective-permute-start(f32[64,16,256]{2,1,0:T(8,128)S(1)} %maximum_select_fusion.3), channel_id=1, source_target_pairs={{0,16},{16,0},{32,48},{48,32},{64,80},{80,64},{96,112},{112,96},{1... | collective-permute-start | bytes 3145736 | tf_op jit(solution)/shard_map/ppermute | solution.py:62
  209.1 3.9 %copy-start = (f32[32,8,8,256]{3,1,2,0:T(8,128)}, f32[32,8,8,256]{3,1,2,0:T(8,128)S(1)}, u32[]{:S(2)}) copy-start(f32[32,8,8,256]{3,1,2,0:T(8,128)S(1)} %copy.146) | copy-start | bytes 6291460
  222.0 2.4 copy-start.1
  224.4 3.8 %copy-start.3 = (f32[256,2048]{1,0:T(8,128)}, f32[256,2048]{1,0:T(8,128)S(1)}, u32[]{:S(2)}) copy-start(f32[256,2048]{1,0:T(8,128)S(1)} %get-tuple-element.19) | copy-start | bytes 6291460
  235.6 3.0 %copy-start.2 = (f32[32,8,8,256]{3,1,2,0:T(8,128)S(1)}, f32[32,8,8,256]{3,1,2,0:T(8,128)}, u32[]{:S(2)}) copy-start(f32[32,8,8,256]{3,1,2,0:T(8,128)} %copy-done) | copy-start | bytes 6291460
  238.5 3.5 %copy-start.4 = (f32[256,2048]{1,0:T(8,128)}, f32[256,2048]{1,0:T(8,128)S(1)}, u32[]{:S(2)}) copy-start(f32[256,2048]{1,0:T(8,128)S(1)} %get-tuple-element.13) | copy-start | bytes 6291460

commit v4 on v3

--- a/solution.py
+++ b/solution.py
@@ -118,7 +118,7 @@
             flux_ref[c] += weight_ref[c, lev] * core
         return carry
 
-    lax.fori_loop(0, levels, level, 0)
+    lax.fori_loop(0, levels, level, 0, unroll=2)
 
 
 def diffuse(field, atm_kappa, vert_weight):
@@ -197,6 +197,89 @@
     return out, flux
 
 
+def strip_sum(acc):
+    return acc.sum(axis=0, keepdims=True).sum(axis=1, keepdims=True)
+
+
+def cg_kernel(rhs_ref, coded_ref, height_ref, residual_ref, pad_ref, dir_ref, img_ref):
+    rows, cols = rhs_ref.shape
+    strips = rows // 8
+    zeros = jnp.zeros((8, cols), jnp.float32)
+    pad_ref[0:8, :] = zeros
+    pad_ref[rows + 8 : rows + 16, :] = zeros
+    row = lax.broadcasted_iota(jnp.int32, (8, cols), 0)
+    col = lax.broadcasted_iota(jnp.int32, (8, cols), 1)
+
+    def at(k, offset=0):
+        return pl.ds(pl.multiple_of(k * 8 + offset, 8), 8)
+
+    def init(k, acc):
+        v = rhs_ref[at(k), :]
+        m = (coded_ref[at(k), :] >= 0.0).astype(jnp.float32)
+        residual_ref[at(k), :] = v
+        dir_ref[at(k), :] = v
+        height_ref[at(k), :] = jnp.zeros_like(v)
+        pad_ref[at(k, 8), :] = m * v
+        return acc + v * v
+
+    def image(k, acc):
+        prev = pad_ref[at(k), :]
+        cur = pad_ref[at(k, 8), :]
+        nxt = pad_ref[at(k, 16), :]
+        south = jnp.where(row == 7, pltpu.roll(nxt, 7, 0), pltpu.roll(cur, 7, 0))
+        north = jnp.where(row == 0, pltpu.roll(prev, 1, 0), pltpu.roll(cur, 1, 0))
+        east = jnp.where(col == cols - 1, 0.0, pltpu.roll(cur, cols - 1, 1))
+        west = jnp.where(col == 0, 0.0, pltpu.roll(cur, 1, 1))
+        beside = south + north + east + west
+        ot = coded_ref[at(k), :]
+        m = (ot >= 0.0).astype(jnp.float32)
+        v = dir_ref[at(k), :]
+        w = m * ((4.0 + ot) * v - beside) + (1.0 - m) * v
+        img_ref[at(k), :] = w
+        return acc + v * w
+
+    norm_now = strip_sum(lax.fori_loop(0, strips, init, zeros))
+    for step in range(ITERS):
+        alpha = norm_now / strip_sum(lax.fori_loop(0, strips, image, zeros))
+
+        def update(k, acc):
+            v = dir_ref[at(k), :]
+            height_ref[at(k), :] = height_ref[at(k), :] + alpha * v
+            r = residual_ref[at(k), :] - alpha * img_ref[at(k), :]
+            residual_ref[at(k), :] = r
+            return acc + r * r
+
+        norm_next = strip_sum(lax.fori_loop(0, strips, update, zeros))
+        beta = norm_next / norm_now
+
+        def direct(k, carry):
+            d = residual_ref[at(k), :] + beta * dir_ref[at(k), :]
+            dir_ref[at(k), :] = d
+            m = (coded_ref[at(k), :] >= 0.0).astype(jnp.float32)
+            pad_ref[at(k, 8), :] = m * d
+            return carry
+
+        if step < ITERS - 1:
+            lax.fori_loop(0, strips, direct, 0)
+        norm_now = norm_next
+
+
+def solve_grid(rhs, coded):
+    rows, cols = rhs.shape
+    whole = pl.BlockSpec(memory_space=pltpu.VMEM)
+    return pl.pallas_call(
+        cg_kernel,
+        in_specs=[whole, whole],
+        out_specs=[whole, whole],
+        out_shape=[jax.ShapeDtypeStruct(rhs.shape, jnp.float32)] * 2,
+        scratch_shapes=[
+            pltpu.VMEM((rows + 16, cols), jnp.float32),
+            pltpu.VMEM((rows, cols), jnp.float32),
+            pltpu.VMEM((rows, cols), jnp.float32),
+        ],
+    )(rhs, coded)
+
+
 def body(
     atm_state, atm_kappa, vert_weight, remap_src, remap_count, remap_weight, land_mask, ocean_term
 ):
@@ -205,7 +288,6 @@
     count_gx = lax.axis_size("gx")
     count_gy = lax.axis_size("gy")
     coded_all = whole_grid(jnp.where(land_mask != 0, ocean_term, -1.0))
-    maskf = (coded_all >= 0.0).astype(jnp.float32)
     field, flux = diffuse(atm_state, atm_kappa, vert_weight)
     flux = flux.reshape(flux.shape[0], tile_lat * tile_lon)
     ocean_blocks, lists, width, _ = remap_weight.shape
@@ -260,18 +342,7 @@
     ocean_flux = remapped.reshape(comps, ocean_rows, ocean_cols)
     rhs_tile = land_mask.astype(jnp.float32) * (ocean_flux[0] + ocean_flux[1])
     rhs = whole_grid(rhs_tile)
-    height = jnp.zeros_like(rhs)
-    residual = rhs
-    direction = rhs
-    norm_now = jnp.sum(residual * residual)
-    for step in range(ITERS):
-        image = grid_operator(direction, maskf, coded_all)
-        alpha = norm_now / jnp.sum(direction * image)
-        height = height + alpha * direction
-        residual = residual - alpha * image
-        norm_next = jnp.sum(residual * residual)
-        direction = residual + norm_next / norm_now * direction
-        norm_now = norm_next
+    height, residual = solve_grid(rhs, coded_all)
     height = lax.dynamic_slice(height, (gy_index * ocean_rows, gx_index * ocean_cols), (ocean_rows, ocean_cols))
     residual = lax.dynamic_slice(residual, (gy_index * ocean_rows, gx_index * ocean_cols), (ocean_rows, ocean_cols))
     return (field, ocean_flux, height, residual)

time: 250 us -> 236 us (0.944)
  other arithmetic: 48.5 us -> 18 us
  Pallas kernels: 66.5 us -> 80 us
  local copies, waits for them, and re-layouts: 35 us -> 47.1 us
  between operations: 7.93 us -> 1.11 us
  waiting for transfers between devices: 38.7 us -> 34.8 us
    reduce_sum x6 -> x0, other arithmetic: 19.5 us -> none  [the longest x3 10.8 us: body(): alpha = norm_now / jnp.sum(direction * image)]
    pallas_call x0 -> x1, Pallas kernels: none -> 19.4 us  [solve_grid(): pl.pallas_call(cg_kernel, in_specs=[whole, whole], out_specs=[whole, whol...]
    pallas_call x1, Pallas kernels: 66.5 us -> 60.6 us  [diffuse(): pl.pallas_call(diffusion_kernel, grid=(blocks,), in_specs=[smem, smem, pl...]
    mul x3 -> x0, other arithmetic: 5.52 us -> none  [grid_operator(): padded = jnp.pad(maskf * vector, 1)]
    unnamed x24 -> x13, local copies, waits for them, and re-layouts: 8.03 us -> 13.5 us
    reshape x0 -> x2, local copies, waits for them, and re-layouts: none -> 4.93 us  [whole_grid(): x = x.reshape(count_gy, count_gx, rows, cols).transpose(0, 2, 1, 3)]
    ppermute x14, waiting for transfers between devices: 35.2 us -> 31.3 us  [whole_grid(): other = lax.ppermute(x, axis, [(j, j ^ distance) for j in range(size)])]
    add x2 -> x0, other arithmetic: 3.29 us -> none  [the longest x1 1.93 us: grid_operator(): 4.0 + ocean_term]
  transfers between devices with their start and end apart: 23 -> 23, of which waited for: 12 -> 13; matrix products, arithmetic and copies ran while one was open for 16% -> 19% of each run, Pallas kernels for 0% -> 0%
where the time goes in v4:
time: 236 us; the launch traced here: 232 us
  Pallas kernels  80 us (34%)
  starting transfers between devices  47.9 us (20%)
  local copies, waits for them, and re-layouts  47.1 us (20%)
  waiting for transfers between devices  34.8 us (15%)
  other arithmetic  18 us (8%)
  matrix products  3.04 us (1%)
    pallas_call x1, Pallas kernels, diffuse(): pl.pallas_call(diffusion_kernel, grid=(blocks,), in_specs=[smem, smem, pl...  60.6 us
    ppermute x14, waiting for transfers between devices, whole_grid(): other = lax.ppermute(x, axis, [(j, j ^ distance) for j in range(size)])  31.3 us
    pallas_call x1, Pallas kernels, solve_grid(): pl.pallas_call(cg_kernel, in_specs=[whole, whole], out_specs=[whole, whol...  19.4 us
    ppermute x14, starting transfers between devices, whole_grid(): other = lax.ppermute(x, axis, [(j, j ^ distance) for j in range(size)])  18.9 us
    unnamed x13, local copies, waits for them, and re-layouts  13.5 us
    ppermute x1, starting transfers between devices, diffuse(): lax.ppermute(field[:, rows - HALO:, cols - HALO:], both, pairs(-1, -1))  8.58 us
    select_n x14, other arithmetic, whole_grid(): x = jnp.where(index & distance == 0, low, high)  5.47 us
    ppermute x1, starting transfers between devices, diffuse(): north = lax.ppermute(field[:, rows - HALO:, :], 'gy', up_gy)  5.22 us
  transfers between devices with their start and end apart: 23, of which 13 were waited for; matrix products, arithmetic and copies ran while one was open for 19% of the time, Pallas kernels for 0%

profile of v4, /device:TPU:6, one launch (start us, length us, event | category | flops | bytes accessed | tf_op | source)
XLA Modules:
  0.0 231.9 jit_solution(6748423824420772329)
XLA Ops:
  0.6 2.9 %fusion.25 = (f32[128,4,4]{2,1,0:T(4,128)}, f32[128,4,4]{2,1,0:T(4,128)}, f32[128,4,4]{2,1,0:T(4,128)}, f32[128,4,4]{2,1,0:T(4,128)}) fusion(f32[128,32,512]{2,1,0:T(8,128)} %core_ref.1), kind=kLoop, calls=%fused_computation.80 | loop fusion | bytes 65536 | tf_op jit(solution)/shard_map/slice | solution.py:146
  3.5 1.3 collective-permute-start.3
  4.8 4.1 %fusion.24 = (f32[128,4,512]{2,1,0:T(4,128)}, f32[128,4,512]{2,1,0:T(4,128)}) fusion(f32[128,32,512]{2,1,0:T(8,128)} %core_ref.1), kind=kLoop, calls=%fused_computation.79 | loop fusion | bytes 4194304 | tf_op jit(solution)/shard_map/slice | solution.py:142
  8.9 2.7 %collective-permute-start.2 = (f32[128,4,512]{2,1,0:T(4,128)}, f32[128,4,512]{2,1,0:T(4,128)S(1)}, u32[]{:S(2)}, u32[]{:S(2)}) collective-permute-start(f32[128,4,512]{2,1,0:T(4,128)} %get-tuple-element.20), channel_id=1, source_target_pairs={{1,0},{2,1},{3,2},{4,3},{5,4},{6,5},{7,6},{8,7},{9,8},{10,9},{11,1... | collective-permute-start | bytes 3145736 | tf_op jit(solution)/shard_map/ppermute | solution.py:142
  11.7 5.2 %collective-permute-start.5 = (f32[128,4,512]{2,1,0:T(4,128)}, f32[128,4,512]{2,1,0:T(4,128)}, u32[]{:S(2)}, u32[]{:S(2)}) collective-permute-start(f32[128,4,512]{2,1,0:T(4,128)} %get-tuple-element.21), channel_id=1, source_target_pairs={{0,1},{1,2},{2,3},{3,4},{4,5},{5,6},{6,7},{7,8},{8,9},{9,10},{10,1... | collective-permute-start | bytes 3145736 | tf_op jit(solution)/shard_map/ppermute | solution.py:143
  16.9 4.3 %fusion.26 = (f32[128,32,4]{2,1,0:T(8,128)S(1)}, f32[128,32,4]{2,1,0:T(8,128)}) fusion(f32[128,32,512]{2,1,0:T(8,128)} %core_ref.1), kind=kLoop, calls=%fused_computation.81 | loop fusion | bytes 262144 | tf_op jit(solution)/shard_map/slice | solution.py:144
  21.1 3.3 %copy.96 = f32[128,32,4]{0,1,2:T(8,128)} copy(f32[128,32,4]{2,1,0:T(8,128)} %get-tuple-element.27) | data formatting | bytes 131072
  24.5 2.9 %collective-permute-start.1 = (f32[128,32,4]{0,1,2:T(8,128)}, f32[128,32,4]{0,1,2:T(8,128)S(1)}, u32[]{:S(2)}, u32[]{:S(2)}) collective-permute-start(f32[128,32,4]{0,1,2:T(8,128)} %copy.96), channel_id=1, source_target_pairs={{0,16},{16,32},{32,48},{48,64},{64,80},{80,96},{96,112},{1,17},{17... | collective-permute-start | bytes 196616 | tf_op jit(solution)/shard_map/ppermute | solution.py:145
  27.4 1.9 copy.95
  29.3 1.3 collective-permute-start
  30.6 0.6 fusion.17
  31.2 0.6 lt.137
  32.0 0.7 copy.79
  32.6 1.6 reshape.258
  34.5 0.7 broadcast_compare_fusion
  36.7 1.4 and_convert_fusion.mask_ref
  38.2 3.2 %collective-permute-start.4 = (f32[128,4,4]{2,1,0:T(4,128)}, f32[128,4,4]{2,1,0:T(4,128)}, u32[]{:S(2)}, u32[]{:S(2)}) collective-permute-start(f32[128,4,4]{2,1,0:T(4,128)} %get-tuple-element.23), channel_id=1, source_target_pairs={{1,16},{2,17},{3,18},{4,19},{5,20},{6,21},{7,22},{8,23},{9,24},{10... | collective-permute-start | bytes 24584 | tf_op jit(solution)/shard_map/ppermute | solution.py:147
  41.4 2.7 %copy.76 = f32[128,32,4]{2,1,0:T(8,128)S(1)} copy(f32[128,32,4]{0,1,2:T(8,128)} %collective-permute-done) | data formatting | bytes 131072 | tf_op jit(solution)/shard_map/ppermute | solution.py:144
  44.2 1.3 collective-permute-start.6
  45.5 2.9 %copy.77 = f32[128,32,4]{2,1,0:T(8,128)} copy(f32[128,32,4]{0,1,2:T(8,128)S(1)} %collective-permute-done.1) | data formatting | bytes 131072 | tf_op jit(solution)/shard_map/ppermute | solution.py:145
  48.3 8.6 %collective-permute-start.7 = (f32[128,4,4]{2,1,0:T(4,128)}, f32[128,4,4]{2,1,0:T(4,128)S(1)}, u32[]{:S(2)}, u32[]{:S(2)}) collective-permute-start(f32[128,4,4]{2,1,0:T(4,128)} %get-tuple-element.25), channel_id=1, source_target_pairs={{0,17},{1,18},{2,19},{3,20},{4,21},{5,22},{6,23},{7,24},{8,25},{9,... | collective-permute-start | bytes 24584 | tf_op jit(solution)/shard_map/ppermute | solution.py:149
  56.9 3.5 %pad_maximum_fusion.lanes_ref = f32[128,32,128]{2,1,0:T(8,128)} fusion(f32[128,32,4]{2,1,0:T(8,128)} %copy.77, f32[128,32,4]{2,1,0:T(8,128)S(1)} %copy.76, f32[128]{0:T(128)S(1)} %pad.65.clone), kind=kLoop, calls=%fused_computation.4 | loop fusion | flops 1048576 | bytes 2228736 | tf_op jit(solution)/shard_map/concatenate | solution.py:151
  60.5 2.9 %collective-permute-done.7 = f32[128,4,4]{2,1,0:T(4,128)S(1)} collective-permute-done((f32[128,4,4]{2,1,0:T(4,128)}, f32[128,4,4]{2,1,0:T(4,128)S(1)}, u32[]{:S(2)}, u32[]{:S(2)}) %collective-permute-start.7) | collective-permute-done | bytes 8224 | tf_op jit(solution)/shard_map/ppermute | solution.py:149
  63.4 3.8 %maximum_maximum_fusion.rows_ref = f32[128,8,640]{2,1,0:T(8,128)} fusion(f32[128,4,4]{2,1,0:T(4,128)S(1)} %collective-permute-done.7, f32[128,4,120]{2,1,0:T(4,128)S(1)} %broadcast_in_dim.52, f32[128,4,4]{2,1,0:T(4,128)} %collective-permute-done.6, f32[128,4,512]{2,1,0:T(4,128)} %collective-permute-done.5, f32[128,4,4]{2,1,0:T(4,128)} %collective-permute-done.4, ...), kind=kLoop, calls=%fused_computation.3 | loop fusion | flops 4587520 | bytes 4997120 | tf_op jit(solution)/shard_map/concatenate | solution.py:153
  67.2 60.6 %shard_map.111 = (f32[128,32,512]{2,1,0:T(8,128)}, f32[4,32,512]{2,1,0:T(8,128)}) custom-call(f32[128]{0:T(128)} %kappa_ref.1, f32[4,128]{1,0:T(4,128)} %weight_ref.1, f32[128,32,512]{2,1,0:T(8,128)} %core_ref.1, f32[128,32,128]{2,1,0:T(8,128)} %pad_maximum_fusion.lanes_ref, f32[128,8,640]{2,1,0:T(8,128)} %maximum_maximum_fusion.rows_ref, ...), custom_call_target="tpu_custom_call" | custom-call | flops 131072000 | bytes 16777216 | tf_op jit(solution)/shard_map/pallas_call | solution.py:171
  127.8 1.0 convert_element_type.40
  129.0 0.6 gather_fusion.1
  129.7 2.4 %collective-permute-start.8 = (bf16[32,4,128]{2,1,0:T(4,128)(2,1)S(1)}, bf16[32,4,128]{2,1,0:T(4,128)(2,1)S(1)}, u32[]{:S(2)}, u32[]{:S(2)}) collective-permute-start(bf16[32,4,128]{2,1,0:T(4,128)(2,1)S(1)} %broadcast_multiply_fusion), channel_id=1, source_target_pairs={{0,112},{16,0},{32,16},{48,32},{64,48},{80,64},{96,80},{112,96},{1... | collective-permute-start | bytes 98312 | tf_op jit(solution)/shard_map/ppermute | solution.py:27
  132.3 0.8 gather_fusion
  133.1 0.6 collective-permute-done.8
  133.7 0.7 gather_fusion.2
  134.5 3.0 %convolution_bitcast_fusion = f32[4,32,128]{2,0,1:T(4,128)S(1)} fusion(bf16[32,4,128,128]{3,2,1,0:T(8,128)(2,1)} %param.13, bf16[32,4,4,128]{3,2,1,0:T(4,128)(2,1)S(1)} %bitcast.57, bf16[32,4,4,128]{3,2,1,0:T(4,128)(2,1)S(1)} %bitcast.58, pred[32,4]{1,0:T(8,128)(4,1)S(1)} %and.145, pred[32,4]{1,0:T(8,128)(4,1)S(1)} %and.141), kind=kOutput, calls=%fused_computation.7 | convolution fusion | flops 16908288 | bytes 4522240 | tf_op jit(solution)/shard_map/bkij,bkcj->cbi/dot_general | solution.py:339
  137.7 3.5 %collective-permute-start.9 = (f32[1,16,256]{2,1,0:T(8,128)S(1)}, f32[1,16,256]{2,1,0:T(8,128)S(1)}, u32[]{:S(2)}, u32[]{:S(2)}) collective-permute-start(f32[1,16,256]{2,1,0:T(8,128)S(1)} %get-tuple-element.35), channel_id=1, source_target_pairs={{0,2},{1,3},{2,0},{3,1},{4,6},{5,7},{6,4},{7,5},{8,10},{9,11},{10,... | collective-permute-start | bytes 49160 | tf_op jit(solution)/shard_map/ppermute | solution.py:62
  141.2 1.7 collective-permute-done.16
  142.9 3.2 %collective-permute-start.17 = (f32[2,16,256]{2,1,0:T(8,128)S(1)}, f32[2,16,256]{2,1,0:T(8,128)S(1)}, u32[]{:S(2)}, u32[]{:S(2)}) collective-permute-start(f32[2,16,256]{2,1,0:T(8,128)S(1)} %maximum_select_fusion.13), channel_id=1, source_target_pairs={{0,8},{1,9},{2,10},{3,11},{4,12},{5,13},{6,14},{7,15},{8,0},{9,1},... | collective-permute-start | bytes 98312 | tf_op jit(solution)/shard_map/ppermute | solution.py:62
  146.1 0.4 collective-permute-start.10
  146.6 1.8 collective-permute-done.17
  148.4 2.5 %collective-permute-start.18 = (f32[4,16,256]{2,1,0:T(8,128)S(1)}, f32[4,16,256]{2,1,0:T(8,128)S(1)}, u32[]{:S(2)}, u32[]{:S(2)}) collective-permute-start(f32[4,16,256]{2,1,0:T(8,128)S(1)} %maximum_select_fusion.11), channel_id=1, source_target_pairs={{0,64},{16,80},{32,96},{48,112},{64,0},{80,16},{96,32},{112,48},{1... | collective-permute-start | bytes 196616 | tf_op jit(solution)/shard_map/ppermute | solution.py:62
  150.9 0.8 collective-permute-done.10
  151.7 2.4 %collective-permute-start.11 = (f32[4,16,256]{2,1,0:T(8,128)S(1)}, f32[4,16,256]{2,1,0:T(8,128)S(1)}, u32[]{:S(2)}, u32[]{:S(2)}) collective-permute-start(f32[4,16,256]{2,1,0:T(8,128)S(1)} %maximum_select_fusion.10), channel_id=1, source_target_pairs={{0,64},{16,80},{32,96},{48,112},{64,0},{80,16},{96,32},{112,48},{1... | collective-permute-start | bytes 196616 | tf_op jit(solution)/shard_map/ppermute | solution.py:62
  154.2 0.8 collective-permute-start.19
  155.0 2.5 %collective-permute-done.11 = f32[4,16,256]{2,1,0:T(8,128)S(1)} collective-permute-done((f32[4,16,256]{2,1,0:T(8,128)S(1)}, f32[4,16,256]{2,1,0:T(8,128)S(1)}, u32[]{:S(2)}, u32[]{:S(2)}) %collective-permute-start.11) | collective-permute-done | bytes 65568 | tf_op jit(solution)/shard_map/ppermute | solution.py:62
  157.6 2.9 %collective-permute-done.19 = f32[8,16,256]{2,1,0:T(8,128)S(1)} collective-permute-done((f32[8,16,256]{2,1,0:T(8,128)S(1)}, f32[8,16,256]{2,1,0:T(8,128)S(1)}, u32[]{:S(2)}, u32[]{:S(2)}) %collective-permute-start.19) | collective-permute-done | bytes 131104 | tf_op jit(solution)/shard_map/ppermute | solution.py:62
  160.5 1.8 collective-permute-start.20
  162.6 1.2 collective-permute-start.13
  163.8 5.2 %collective-permute-done.20 = f32[16,16,256]{2,1,0:T(8,128)S(1)} collective-permute-done((f32[16,16,256]{2,1,0:T(8,128)S(1)}, f32[16,16,256]{2,1,0:T(8,128)S(1)}, u32[]{:S(2)}, u32[]{:S(2)}) %collective-permute-start.20) | collective-permute-done | bytes 262176 | tf_op jit(solution)/shard_map/ppermute | solution.py:62
  169.0 1.3 collective-permute-start.21
  170.3 1.4 collective-permute-done.13
  171.8 1.3 collective-permute-start.14
  173.1 9.1 %collective-permute-done.21 = f32[32,16,256]{2,1,0:T(8,128)S(1)} collective-permute-done((f32[32,16,256]{2,1,0:T(8,128)S(1)}, f32[32,16,256]{2,1,0:T(8,128)S(1)}, u32[]{:S(2)}, u32[]{:S(2)}) %collective-permute-start.21) | collective-permute-done | bytes 524320 | tf_op jit(solution)/shard_map/ppermute | solution.py:62
  182.5 5.5 %collective-permute-done.14 = f32[32,16,256]{2,1,0:T(8,128)} collective-permute-done((f32[32,16,256]{2,1,0:T(8,128)S(1)}, f32[32,16,256]{2,1,0:T(8,128)}, u32[]{:S(2)}, u32[]{:S(2)}) %collective-permute-start.14) | collective-permute-done | bytes 524320 | tf_op jit(solution)/shard_map/ppermute | solution.py:62
  188.0 1.4 maximum_select_fusion.2
  189.7 0.6 reshape.260
  190.3 1.9 maximum_select_fusion.1
  192.2 1.6 copy.93
  193.9 2.5 %reshape.263 = f32[16,8,16,256]{3,1,2,0:T(8,128)} reshape(f32[2,2,2,2,2,2,2,16,256]{8,6,5,4,7,3,2,1,0:T(2,128)S(1)} %copy.93) | data formatting | bytes 4194304 | tf_op jit(solution)/shard_map/reshape | solution.py:77
  196.3 3.8 %copy.98 = f32[32,8,8,256]{3,1,2,0:T(8,128)} copy(f32[32,8,8,256]{3,2,1,0:T(8,128)} %bitcast.52) | data formatting | bytes 4194304
  200.1 1.9 maximum_select_fusion
  202.0 1.6 copy.92
  203.7 2.5 %reshape.261 = f32[16,8,16,256]{3,1,2,0:T(8,128)} reshape(f32[2,2,2,2,2,2,2,16,256]{8,6,5,4,7,3,2,1,0:T(2,128)S(1)} %copy.92) | data formatting | bytes 4194304 | tf_op jit(solution)/shard_map/reshape | solution.py:77
  206.1 3.8 %copy.97 = f32[32,8,8,256]{3,1,2,0:T(8,128)} copy(f32[32,8,8,256]{3,2,1,0:T(8,128)} %bitcast.53) | data formatting | bytes 4194304
  209.9 19.4 %shard_map.112 = (f32[256,2048]{1,0:T(8,128)}, f32[256,2048]{1,0:T(8,128)}) custom-call(f32[256,2048]{1,0:T(8,128)} %bitcast.49, f32[256,2048]{1,0:T(8,128)} %bitcast.48), custom_call_target="tpu_custom_call" | custom-call | tf_op jit(solution)/shard_map/pallas_call | solution.py:270
  229.3 1.3 dynamic_slice.30
  230.6 1.3 dynamic_slice.31
  (69 shorter events, 3.7 us)
Async XLA Ops:
  3.5 44.8 %collective-permute-start.3 = (f32[128,4,4]{2,1,0:T(4,128)}, f32[128,4,4]{2,1,0:T(4,128)S(1)}, u32[]{:S(2)}, u32[]{:S(2)}) collective-permute-start(f32[128,4,4]{2,1,0:T(4,128)} %get-tuple-element.22), channel_id=1, source_target_pairs={{17,0},{18,1},{19,2},{20,3},{21,4},{22,5},{23,6},{24,7},{25,8},{26... | collective-permute-start | bytes 24584 | tf_op jit(solution)/shard_map/ppermute | solution.py:146
  8.9 54.4 %collective-permute-start.2 = (f32[128,4,512]{2,1,0:T(4,128)}, f32[128,4,512]{2,1,0:T(4,128)S(1)}, u32[]{:S(2)}, u32[]{:S(2)}) collective-permute-start(f32[128,4,512]{2,1,0:T(4,128)} %get-tuple-element.20), channel_id=1, source_target_pairs={{1,0},{2,1},{3,2},{4,3},{5,4},{6,5},{7,6},{8,7},{9,8},{10,9},{11,1... | collective-permute-start | bytes 3145736 | tf_op jit(solution)/shard_map/ppermute | solution.py:142
  11.7 51.7 %collective-permute-start.5 = (f32[128,4,512]{2,1,0:T(4,128)}, f32[128,4,512]{2,1,0:T(4,128)}, u32[]{:S(2)}, u32[]{:S(2)}) collective-permute-start(f32[128,4,512]{2,1,0:T(4,128)} %get-tuple-element.21), channel_id=1, source_target_pairs={{0,1},{1,2},{2,3},{3,4},{4,5},{5,6},{6,7},{7,8},{8,9},{9,10},{10,1... | collective-permute-start | bytes 3145736 | tf_op jit(solution)/shard_map/ppermute | solution.py:143
  21.1 10.7 %copy-start.1 = (s32[4096]{0:T(1024)S(1)}, s32[4096]{0:T(1024)}, u32[]{:S(2)}) copy-start(s32[4096]{0:T(1024)} %param.12) | copy-start | bytes 49156
  21.1 10.8 %copy-start = (s32[4096,4]{0,1:T(4,128)S(1)}, s32[4096,4]{0,1:T(4,128)}, u32[]{:S(2)}) copy-start(s32[4096,4]{0,1:T(4,128)} %param.11) | copy-start | bytes 196612
  24.5 19.7 %collective-permute-start.1 = (f32[128,32,4]{0,1,2:T(8,128)}, f32[128,32,4]{0,1,2:T(8,128)S(1)}, u32[]{:S(2)}, u32[]{:S(2)}) collective-permute-start(f32[128,32,4]{0,1,2:T(8,128)} %copy.96), channel_id=1, source_target_pairs={{0,16},{16,32},{32,48},{48,64},{64,80},{80,96},{96,112},{1,17},{17... | collective-permute-start | bytes 196616 | tf_op jit(solution)/shard_map/ppermute | solution.py:145
  29.3 8.9 %collective-permute-start = (f32[128,32,4]{0,1,2:T(8,128)}, f32[128,32,4]{0,1,2:T(8,128)}, u32[]{:S(2)}, u32[]{:S(2)}) collective-permute-start(f32[128,32,4]{0,1,2:T(8,128)} %copy.95), channel_id=1, source_target_pairs={{16,0},{32,16},{48,32},{64,48},{80,64},{96,80},{112,96},{17,1},{33... | collective-permute-start | bytes 196616 | tf_op jit(solution)/shard_map/ppermute | solution.py:144
  38.2 22.3 %collective-permute-start.4 = (f32[128,4,4]{2,1,0:T(4,128)}, f32[128,4,4]{2,1,0:T(4,128)}, u32[]{:S(2)}, u32[]{:S(2)}) collective-permute-start(f32[128,4,4]{2,1,0:T(4,128)} %get-tuple-element.23), channel_id=1, source_target_pairs={{1,16},{2,17},{3,18},{4,19},{5,20},{6,21},{7,22},{8,23},{9,24},{10... | collective-permute-start | bytes 24584 | tf_op jit(solution)/shard_map/ppermute | solution.py:147
  44.2 16.3 %collective-permute-start.6 = (f32[128,4,4]{2,1,0:T(4,128)}, f32[128,4,4]{2,1,0:T(4,128)}, u32[]{:S(2)}, u32[]{:S(2)}) collective-permute-start(f32[128,4,4]{2,1,0:T(4,128)} %get-tuple-element.24), channel_id=1, source_target_pairs={{16,1},{17,2},{18,3},{19,4},{20,5},{21,6},{22,7},{23,8},{24,9},{25... | collective-permute-start | bytes 24584 | tf_op jit(solution)/shard_map/ppermute | solution.py:148
  48.3 15.0 %collective-permute-start.7 = (f32[128,4,4]{2,1,0:T(4,128)}, f32[128,4,4]{2,1,0:T(4,128)S(1)}, u32[]{:S(2)}, u32[]{:S(2)}) collective-permute-start(f32[128,4,4]{2,1,0:T(4,128)} %get-tuple-element.25), channel_id=1, source_target_pairs={{0,17},{1,18},{2,19},{3,20},{4,21},{5,22},{6,23},{7,24},{8,25},{9,... | collective-permute-start | bytes 24584 | tf_op jit(solution)/shard_map/ppermute | solution.py:149
  129.7 4.0 %collective-permute-start.8 = (bf16[32,4,128]{2,1,0:T(4,128)(2,1)S(1)}, bf16[32,4,128]{2,1,0:T(4,128)(2,1)S(1)}, u32[]{:S(2)}, u32[]{:S(2)}) collective-permute-start(bf16[32,4,128]{2,1,0:T(4,128)(2,1)S(1)} %broadcast_multiply_fusion), channel_id=1, source_target_pairs={{0,112},{16,0},{32,16},{48,32},{64,48},{80,64},{96,80},{112,96},{1... | collective-permute-start | bytes 98312 | tf_op jit(solution)/shard_map/ppermute | solution.py:27
  134.4 3.1 %copy-start.2 = (f32[16,256]{1,0:T(8,128)S(1)}, f32[16,256]{1,0:T(8,128)}, u32[]{:S(2)}) copy-start(f32[16,256]{1,0:T(8,128)} %param.15) | copy-start | bytes 49156
  134.4 3.1 %copy-start.3 = (s32[16,256]{1,0:T(8,128)S(1)}, s32[16,256]{1,0:T(8,128)}, u32[]{:S(2)}) copy-start(s32[16,256]{1,0:T(8,128)} %param.14) | copy-start | bytes 49156
  137.6 5.3 %collective-permute-start.16 = (f32[1,16,256]{2,1,0:T(8,128)S(1)}, f32[1,16,256]{2,1,0:T(8,128)S(1)}, u32[]{:S(2)}, u32[]{:S(2)}) collective-permute-start(f32[1,16,256]{2,1,0:T(8,128)S(1)} %get-tuple-element.34), channel_id=1, source_target_pairs={{0,2},{1,3},{2,0},{3,1},{4,6},{5,7},{6,4},{7,5},{8,10},{9,11},{10,... | collective-permute-start | bytes 49160 | tf_op jit(solution)/shard_map/ppermute | solution.py:62
  137.7 8.4 %collective-permute-start.9 = (f32[1,16,256]{2,1,0:T(8,128)S(1)}, f32[1,16,256]{2,1,0:T(8,128)S(1)}, u32[]{:S(2)}, u32[]{:S(2)}) collective-permute-start(f32[1,16,256]{2,1,0:T(8,128)S(1)} %get-tuple-element.35), channel_id=1, source_target_pairs={{0,2},{1,3},{2,0},{3,1},{4,6},{5,7},{6,4},{7,5},{8,10},{9,11},{10,... | collective-permute-start | bytes 49160 | tf_op jit(solution)/shard_map/ppermute | solution.py:62
  142.9 5.4 %collective-permute-start.17 = (f32[2,16,256]{2,1,0:T(8,128)S(1)}, f32[2,16,256]{2,1,0:T(8,128)S(1)}, u32[]{:S(2)}, u32[]{:S(2)}) collective-permute-start(f32[2,16,256]{2,1,0:T(8,128)S(1)} %maximum_select_fusion.13), channel_id=1, source_target_pairs={{0,8},{1,9},{2,10},{3,11},{4,12},{5,13},{6,14},{7,15},{8,0},{9,1},... | collective-permute-start | bytes 98312 | tf_op jit(solution)/shard_map/ppermute | solution.py:62
  146.1 5.5 %collective-permute-start.10 = (f32[2,16,256]{2,1,0:T(8,128)S(1)}, f32[2,16,256]{2,1,0:T(8,128)S(1)}, u32[]{:S(2)}, u32[]{:S(2)}) collective-permute-start(f32[2,16,256]{2,1,0:T(8,128)S(1)} %maximum_select_fusion.12), channel_id=1, source_target_pairs={{0,8},{1,9},{2,10},{3,11},{4,12},{5,13},{6,14},{7,15},{8,0},{9,1},... | collective-permute-start | bytes 98312 | tf_op jit(solution)/shard_map/ppermute | solution.py:62
  148.4 5.8 %collective-permute-start.18 = (f32[4,16,256]{2,1,0:T(8,128)S(1)}, f32[4,16,256]{2,1,0:T(8,128)S(1)}, u32[]{:S(2)}, u32[]{:S(2)}) collective-permute-start(f32[4,16,256]{2,1,0:T(8,128)S(1)} %maximum_select_fusion.11), channel_id=1, source_target_pairs={{0,64},{16,80},{32,96},{48,112},{64,0},{80,16},{96,32},{112,48},{1... | collective-permute-start | bytes 196616 | tf_op jit(solution)/shard_map/ppermute | solution.py:62
  151.7 5.8 %collective-permute-start.11 = (f32[4,16,256]{2,1,0:T(8,128)S(1)}, f32[4,16,256]{2,1,0:T(8,128)S(1)}, u32[]{:S(2)}, u32[]{:S(2)}) collective-permute-start(f32[4,16,256]{2,1,0:T(8,128)S(1)} %maximum_select_fusion.10), channel_id=1, source_target_pairs={{0,64},{16,80},{32,96},{48,112},{64,0},{80,16},{96,32},{112,48},{1... | collective-permute-start | bytes 196616 | tf_op jit(solution)/shard_map/ppermute | solution.py:62
  154.2 6.3 %collective-permute-start.19 = (f32[8,16,256]{2,1,0:T(8,128)S(1)}, f32[8,16,256]{2,1,0:T(8,128)S(1)}, u32[]{:S(2)}, u32[]{:S(2)}) collective-permute-start(f32[8,16,256]{2,1,0:T(8,128)S(1)} %maximum_select_fusion.9), channel_id=1, source_target_pairs={{0,1},{1,0},{2,3},{3,2},{4,5},{5,4},{6,7},{7,6},{8,9},{9,8},{10,11... | collective-permute-start | bytes 393224 | tf_op jit(solution)/shard_map/ppermute | solution.py:62
  157.5 5.0 %collective-permute-start.12 = (f32[8,16,256]{2,1,0:T(8,128)S(1)}, f32[8,16,256]{2,1,0:T(8,128)S(1)}, u32[]{:S(2)}, u32[]{:S(2)}) collective-permute-start(f32[8,16,256]{2,1,0:T(8,128)S(1)} %maximum_select_fusion.8), channel_id=1, source_target_pairs={{0,1},{1,0},{2,3},{3,2},{4,5},{5,4},{6,7},{7,6},{8,9},{9,8},{10,11... | collective-permute-start | bytes 393224 | tf_op jit(solution)/shard_map/ppermute | solution.py:62
  160.5 8.4 %collective-permute-start.20 = (f32[16,16,256]{2,1,0:T(8,128)S(1)}, f32[16,16,256]{2,1,0:T(8,128)S(1)}, u32[]{:S(2)}, u32[]{:S(2)}) collective-permute-start(f32[16,16,256]{2,1,0:T(8,128)S(1)} %maximum_select_fusion.7), channel_id=1, source_target_pairs={{0,4},{1,5},{2,6},{3,7},{4,0},{5,1},{6,2},{7,3},{8,12},{9,13},{10,... | collective-permute-start | bytes 786440 | tf_op jit(solution)/shard_map/ppermute | solution.py:62
  162.6 9.2 %collective-permute-start.13 = (f32[16,16,256]{2,1,0:T(8,128)S(1)}, f32[16,16,256]{2,1,0:T(8,128)S(1)}, u32[]{:S(2)}, u32[]{:S(2)}) collective-permute-start(f32[16,16,256]{2,1,0:T(8,128)S(1)} %maximum_select_fusion.6), channel_id=1, source_target_pairs={{0,4},{1,5},{2,6},{3,7},{4,0},{5,1},{6,2},{7,3},{8,12},{9,13},{10,... | collective-permute-start | bytes 786440 | tf_op jit(solution)/shard_map/ppermute | solution.py:62
  169.0 13.3 %collective-permute-start.21 = (f32[32,16,256]{2,1,0:T(8,128)S(1)}, f32[32,16,256]{2,1,0:T(8,128)S(1)}, u32[]{:S(2)}, u32[]{:S(2)}) collective-permute-start(f32[32,16,256]{2,1,0:T(8,128)S(1)} %maximum_select_fusion.5), channel_id=1, source_target_pairs={{0,32},{16,48},{32,0},{48,16},{64,96},{80,112},{96,64},{112,80},{1... | collective-permute-start | bytes 1572872 | tf_op jit(solution)/shard_map/ppermute | solution.py:62
  171.8 16.2 %collective-permute-start.14 = (f32[32,16,256]{2,1,0:T(8,128)S(1)}, f32[32,16,256]{2,1,0:T(8,128)}, u32[]{:S(2)}, u32[]{:S(2)}) collective-permute-start(f32[32,16,256]{2,1,0:T(8,128)S(1)} %maximum_select_fusion.4), channel_id=1, source_target_pairs={{0,32},{16,48},{32,0},{48,16},{64,96},{80,112},{96,64},{112,80},{1... | collective-permute-start | bytes 1572872 | tf_op jit(solution)/shard_map/ppermute | solution.py:62
  182.4 7.9 %collective-permute-start.22 = (f32[64,16,256]{2,1,0:T(8,128)S(1)}, f32[64,16,256]{2,1,0:T(8,128)}, u32[]{:S(2)}, u32[]{:S(2)}) collective-permute-start(f32[64,16,256]{2,1,0:T(8,128)S(1)} %maximum_select_fusion.3), channel_id=1, source_target_pairs={{0,16},{16,0},{32,48},{48,32},{64,80},{80,64},{96,112},{112,96},{1... | collective-permute-start | bytes 3145736 | tf_op jit(solution)/shard_map/ppermute | solution.py:62
  189.3 10.8 %collective-permute-start.15 = (f32[64,16,256]{2,1,0:T(8,128)S(1)}, f32[64,16,256]{2,1,0:T(8,128)}, u32[]{:S(2)}, u32[]{:S(2)}) collective-permute-start(f32[64,16,256]{2,1,0:T(8,128)S(1)} %maximum_select_fusion.2), channel_id=1, source_target_pairs={{0,16},{16,0},{32,48},{48,32},{64,80},{80,64},{96,112},{112,96},{1... | collective-permute-start | bytes 3145736 | tf_op jit(solution)/shard_map/ppermute | solution.py:62

commit v5 on v4

--- a/solution.py
+++ b/solution.py
@@ -1,3 +1,5 @@
+import functools
+
 import jax
 import jax.numpy as jnp
 from jax import lax
@@ -52,30 +54,13 @@
     return far + near
 
 
-def whole_grid(tile):
-    rows, cols = tile.shape
-    rounds = gather_rounds()
+def stack_gather(tile, rounds):
     x = tile[None]
     for axis, distance in rounds:
         size = lax.axis_size(axis)
-        index = lax.axis_index(axis)
         other = lax.ppermute(x, axis, [(j, j ^ distance) for j in range(size)])
-        low = jnp.concatenate([x, other], axis=0)
-        high = jnp.concatenate([other, x], axis=0)
-        x = jnp.where((index & distance) == 0, low, high)
-    count = len(rounds)
-    x = x.reshape((2,) * count + (rows, cols))
-    order = []
-    for axis in ("gy", "gx"):
-        d = lax.axis_size(axis) // 2
-        while d >= 1:
-            order.append(count - 1 - rounds.index((axis, d)))
-            d //= 2
-    x = x.transpose(order + [count, count + 1])
-    count_gy = lax.axis_size("gy")
-    count_gx = lax.axis_size("gx")
-    x = x.reshape(count_gy, count_gx, rows, cols).transpose(0, 2, 1, 3)
-    return x.reshape(count_gy * rows, count_gx * cols)
+        x = jnp.concatenate([x, other], axis=0)
+    return x
 
 
 def grid_operator(vector, maskf, ocean_term):
@@ -201,8 +186,31 @@
     return acc.sum(axis=0, keepdims=True).sum(axis=1, keepdims=True)
 
 
-def cg_kernel(rhs_ref, coded_ref, height_ref, residual_ref, pad_ref, dir_ref, img_ref):
+def cg_kernel(
+    rounds, index_ref, rhs_stack, coded_stack, height_out, residual_out,
+    rhs_ref, coded_ref, height_ref, residual_ref, pad_ref, dir_ref, img_ref,
+):
     rows, cols = rhs_ref.shape
+    tile_rows, tile_cols = height_out.shape
+    gy = index_ref[0]
+    gx = index_ref[1]
+
+    def place(k, carry):
+        gy_off = 0
+        gx_off = 0
+        for bit, (axis, distance) in enumerate(rounds):
+            flag = lax.shift_right_logical(k, bit) & 1
+            if axis == "gy":
+                gy_off = gy_off + flag * distance
+            else:
+                gx_off = gx_off + flag * distance
+        r0 = pl.multiple_of(lax.bitwise_xor(gy, gy_off) * tile_rows, tile_rows)
+        c0 = pl.multiple_of(lax.bitwise_xor(gx, gx_off) * tile_cols, tile_cols)
+        rhs_ref[pl.ds(r0, tile_rows), pl.ds(c0, tile_cols)] = rhs_stack[k]
+        coded_ref[pl.ds(r0, tile_rows), pl.ds(c0, tile_cols)] = coded_stack[k]
+        return carry
+
+    lax.fori_loop(0, rhs_stack.shape[0], place, 0)
     strips = rows // 8
     zeros = jnp.zeros((8, cols), jnp.float32)
     pad_ref[0:8, :] = zeros
@@ -262,22 +270,26 @@
         if step < ITERS - 1:
             lax.fori_loop(0, strips, direct, 0)
         norm_now = norm_next
-
-
-def solve_grid(rhs, coded):
-    rows, cols = rhs.shape
+    r0 = pl.multiple_of(gy * tile_rows, tile_rows)
+    c0 = pl.multiple_of(gx * tile_cols, tile_cols)
+    height_out[...] = height_ref[pl.ds(r0, tile_rows), pl.ds(c0, tile_cols)]
+    residual_out[...] = residual_ref[pl.ds(r0, tile_rows), pl.ds(c0, tile_cols)]
+
+
+def solve_grid(rhs_stack, coded_stack, rounds):
+    parts, tile_rows, tile_cols = rhs_stack.shape
+    rows = lax.axis_size("gy") * tile_rows
+    cols = lax.axis_size("gx") * tile_cols
+    index = jnp.stack([lax.axis_index("gy"), lax.axis_index("gx")]).astype(jnp.int32)
     whole = pl.BlockSpec(memory_space=pltpu.VMEM)
+    grid = pltpu.VMEM((rows, cols), jnp.float32)
     return pl.pallas_call(
-        cg_kernel,
-        in_specs=[whole, whole],
+        functools.partial(cg_kernel, rounds),
+        in_specs=[pl.BlockSpec(memory_space=pltpu.SMEM), whole, whole],
         out_specs=[whole, whole],
-        out_shape=[jax.ShapeDtypeStruct(rhs.shape, jnp.float32)] * 2,
-        scratch_shapes=[
-            pltpu.VMEM((rows + 16, cols), jnp.float32),
-            pltpu.VMEM((rows, cols), jnp.float32),
-            pltpu.VMEM((rows, cols), jnp.float32),
-        ],
-    )(rhs, coded)
+        out_shape=[jax.ShapeDtypeStruct((tile_rows, tile_cols), jnp.float32)] * 2,
+        scratch_shapes=[grid, grid, grid, grid, pltpu.VMEM((rows + 16, cols), jnp.float32), grid, grid],
+    )(index, rhs_stack, coded_stack)
 
 
 def body(
@@ -287,7 +299,8 @@
     kappa = atm_kappa[:, None, None]
     count_gx = lax.axis_size("gx")
     count_gy = lax.axis_size("gy")
-    coded_all = whole_grid(jnp.where(land_mask != 0, ocean_term, -1.0))
+    rounds = gather_rounds()
+    coded_all = stack_gather(jnp.where(land_mask != 0, ocean_term, -1.0), rounds)
     field, flux = diffuse(atm_state, atm_kappa, vert_weight)
     flux = flux.reshape(flux.shape[0], tile_lat * tile_lon)
     ocean_blocks, lists, width, _ = remap_weight.shape
@@ -341,10 +354,8 @@
     )
     ocean_flux = remapped.reshape(comps, ocean_rows, ocean_cols)
     rhs_tile = land_mask.astype(jnp.float32) * (ocean_flux[0] + ocean_flux[1])
-    rhs = whole_grid(rhs_tile)
-    height, residual = solve_grid(rhs, coded_all)
-    height = lax.dynamic_slice(height, (gy_index * ocean_rows, gx_index * ocean_cols), (ocean_rows, ocean_cols))
-    residual = lax.dynamic_slice(residual, (gy_index * ocean_rows, gx_index * ocean_cols), (ocean_rows, ocean_cols))
+    rhs = stack_gather(rhs_tile, rounds)
+    height, residual = solve_grid(rhs, coded_all, rounds)
     return (field, ocean_flux, height, residual)
 
 

time: 236 us -> 224 us (0.949)
  local copies, waits for them, and re-layouts: 47.1 us -> 40.5 us
  waiting for transfers between devices: 34.8 us -> 40.3 us
  other arithmetic: 18 us -> 13.1 us
  starting transfers between devices: 47.9 us -> 43.5 us
    ppermute x14, waiting for transfers between devices: 31.3 us -> 24.2 us  [stack_gather(): other = lax.ppermute(x, axis, [(j, j ^ distance) for j in range(size)])]
    ppermute x1, waiting for transfers between devices: 0.01 us -> 7.07 us  [diffuse(): south_east = lax.ppermute(field[:, :HALO, :HALO], both, pairs(1, 1))]
    select_n x14 -> x0, other arithmetic: 5.47 us -> none  [whole_grid(): x = jnp.where(index & distance == 0, low, high)]
    reshape x2 -> x0, local copies, waits for them, and re-layouts: 4.93 us -> none  [whole_grid(): x = x.reshape(count_gy, count_gx, rows, cols).transpose(0, 2, 1, 3)]
    concatenate x0 -> x4, local copies, waits for them, and re-layouts: none -> 4.19 us  [stack_gather(): x = jnp.concatenate([x, other], axis=0)]
    ppermute x1, waiting for transfers between devices: 0.01 us -> 3.96 us  [diffuse(): south_west = lax.ppermute(field[:, :HALO, cols - HALO:], both, pairs(-1, 1))]
    transpose x2 -> x0, local copies, waits for them, and re-layouts: 3.24 us -> none  [whole_grid(): x = x.transpose(order + [count, count + 1])]
    ppermute x1, starting transfers between devices: 8.58 us -> 5.35 us  [diffuse(): lax.ppermute(field[:, rows - HALO:, cols - HALO:], both, pairs(-1, -1))]
  transfers between devices with their start and end apart: 23 -> 23, of which waited for: 13 -> 13; matrix products, arithmetic and copies ran while one was open for 19% -> 16% of each run, Pallas kernels for 0% -> 0%
where the time goes in v5:
time: 224 us; the launch traced here: 222 us
  Pallas kernels  80.5 us (36%)
  starting transfers between devices  43.5 us (19%)
  local copies, waits for them, and re-layouts  40.5 us (18%)
  waiting for transfers between devices  40.3 us (18%)
  other arithmetic  13.1 us (6%)
  matrix products  3.04 us (1%)
    pallas_call x1, Pallas kernels, diffuse(): pl.pallas_call(diffusion_kernel, grid=(blocks,), in_specs=[smem, smem, pl...  60.6 us
    ppermute x14, waiting for transfers between devices, stack_gather(): other = lax.ppermute(x, axis, [(j, j ^ distance) for j in range(size)])  24.2 us
    ppermute x14, starting transfers between devices, stack_gather(): other = lax.ppermute(x, axis, [(j, j ^ distance) for j in range(size)])  20.9 us
    pallas_call x1, Pallas kernels, solve_grid(): pl.pallas_call(functools.partial(cg_kernel, rounds), in_specs=[pl.BlockSp...  19.9 us
    unnamed x27, local copies, waits for them, and re-layouts  13.8 us
    ppermute x1, waiting for transfers between devices, diffuse(): south_east = lax.ppermute(field[:, :HALO, :HALO], both, pairs(1, 1))  7.07 us
    ppermute x1, starting transfers between devices, diffuse(): lax.ppermute(field[:, rows - HALO:, cols - HALO:], both, pairs(-1, -1))  5.35 us
    ppermute x1, starting transfers between devices, diffuse(): south_west = lax.ppermute(field[:, :HALO, cols - HALO:], both, pairs(-1, 1))  4.98 us
  transfers between devices with their start and end apart: 23, of which 13 were waited for; matrix products, arithmetic and copies ran while one was open for 16% of the time, Pallas kernels for 0%

profile of v5, /device:TPU:6, one launch (start us, length us, event | category | flops | bytes accessed | tf_op | source)
XLA Modules:
  0.0 222.0 jit_solution(17652525295256243496)
XLA Ops:
  0.6 4.3 %fusion.26 = (f32[128,32,4]{2,1,0:T(8,128)S(1)}, f32[128,32,4]{2,1,0:T(8,128)}) fusion(f32[128,32,512]{2,1,0:T(8,128)} %core_ref.1), kind=kLoop, calls=%fused_computation.126 | loop fusion | bytes 262144 | tf_op jit(solution)/shard_map/slice | solution.py:129
  4.9 3.3 %copy.86 = f32[128,32,4]{0,1,2:T(8,128)} copy(f32[128,32,4]{2,1,0:T(8,128)} %get-tuple-element.31) | data formatting | bytes 131072
  8.2 2.4 %collective-permute-start.1 = (f32[128,32,4]{0,1,2:T(8,128)}, f32[128,32,4]{0,1,2:T(8,128)}, u32[]{:S(2)}, u32[]{:S(2)}) collective-permute-start(f32[128,32,4]{0,1,2:T(8,128)} %copy.86), channel_id=1, source_target_pairs={{0,16},{16,32},{32,48},{48,64},{64,80},{80,96},{96,112},{1,17},{17... | collective-permute-start | bytes 196616 | tf_op jit(solution)/shard_map/ppermute | solution.py:130
  10.5 1.9 copy.85
  12.5 1.3 collective-permute-start
  13.8 2.9 %fusion.25 = (f32[128,4,4]{2,1,0:T(4,128)}, f32[128,4,4]{2,1,0:T(4,128)}, f32[128,4,4]{2,1,0:T(4,128)}, f32[128,4,4]{2,1,0:T(4,128)}) fusion(f32[128,32,512]{2,1,0:T(8,128)} %core_ref.1), kind=kLoop, calls=%fused_computation.125 | loop fusion | bytes 65536 | tf_op jit(solution)/shard_map/slice | solution.py:131
  16.6 5.3 %collective-permute-start.7 = (f32[128,4,4]{2,1,0:T(4,128)}, f32[128,4,4]{2,1,0:T(4,128)S(1)}, u32[]{:S(2)}, u32[]{:S(2)}) collective-permute-start(f32[128,4,4]{2,1,0:T(4,128)} %get-tuple-element.29), channel_id=1, source_target_pairs={{0,17},{1,18},{2,19},{3,20},{4,21},{5,22},{6,23},{7,24},{8,25},{9,... | collective-permute-start | bytes 24584 | tf_op jit(solution)/shard_map/ppermute | solution.py:134
  22.0 4.1 %fusion.24 = (f32[128,4,512]{2,1,0:T(4,128)}, f32[128,4,512]{2,1,0:T(4,128)}) fusion(f32[128,32,512]{2,1,0:T(8,128)} %core_ref.1), kind=kLoop, calls=%fused_computation.124 | loop fusion | bytes 4194304 | tf_op jit(solution)/shard_map/slice | solution.py:127
  26.1 3.4 %collective-permute-start.5 = (f32[128,4,512]{2,1,0:T(4,128)}, f32[128,4,512]{2,1,0:T(4,128)S(1)}, u32[]{:S(2)}, u32[]{:S(2)}) collective-permute-start(f32[128,4,512]{2,1,0:T(4,128)} %get-tuple-element.25), channel_id=1, source_target_pairs={{0,1},{1,2},{2,3},{3,4},{4,5},{5,6},{6,7},{7,8},{8,9},{9,10},{10,1... | collective-permute-start | bytes 3145736 | tf_op jit(solution)/shard_map/ppermute | solution.py:128
  29.5 2.4 %collective-permute-start.2 = (f32[128,4,512]{2,1,0:T(4,128)}, f32[128,4,512]{2,1,0:T(4,128)}, u32[]{:S(2)}, u32[]{:S(2)}) collective-permute-start(f32[128,4,512]{2,1,0:T(4,128)} %get-tuple-element.24), channel_id=1, source_target_pairs={{1,0},{2,1},{3,2},{4,3},{5,4},{6,5},{7,6},{8,7},{9,8},{10,9},{11,1... | collective-permute-start | bytes 3145736 | tf_op jit(solution)/shard_map/ppermute | solution.py:127
  32.5 0.6 copy.71
  33.2 1.6 reshape.236
  37.0 1.4 and_convert_fusion.mask_ref
  38.5 1.3 collective-permute-start.6
  39.7 2.7 %copy.69 = f32[128,32,4]{2,1,0:T(8,128)S(1)} copy(f32[128,32,4]{0,1,2:T(8,128)} %collective-permute-done.1) | data formatting | bytes 131072 | tf_op jit(solution)/shard_map/ppermute | solution.py:130
  42.5 5.0 %collective-permute-start.4 = (f32[128,4,4]{2,1,0:T(4,128)}, f32[128,4,4]{2,1,0:T(4,128)}, u32[]{:S(2)}, u32[]{:S(2)}) collective-permute-start(f32[128,4,4]{2,1,0:T(4,128)} %get-tuple-element.27), channel_id=1, source_target_pairs={{1,16},{2,17},{3,18},{4,19},{5,20},{6,21},{7,22},{8,23},{9,24},{10... | collective-permute-start | bytes 24584 | tf_op jit(solution)/shard_map/ppermute | solution.py:132
  47.5 2.9 %copy.68 = f32[128,32,4]{2,1,0:T(8,128)} copy(f32[128,32,4]{0,1,2:T(8,128)S(1)} %collective-permute-done) | data formatting | bytes 131072 | tf_op jit(solution)/shard_map/ppermute | solution.py:129
  50.3 1.5 collective-permute-start.3
  51.8 3.5 %pad_maximum_fusion.lanes_ref = f32[128,32,128]{2,1,0:T(8,128)} fusion(f32[128,32,4]{2,1,0:T(8,128)S(1)} %copy.69, f32[128,32,4]{2,1,0:T(8,128)} %copy.68, f32[128]{0:T(128)S(1)} %pad.29.clone), kind=kLoop, calls=%fused_computation.4 | loop fusion | flops 1048576 | bytes 2228736 | tf_op jit(solution)/shard_map/concatenate | solution.py:136
  55.3 1.8 collective-permute-done.6
  57.1 4.0 %collective-permute-done.4 = f32[128,4,4]{2,1,0:T(4,128)} collective-permute-done((f32[128,4,4]{2,1,0:T(4,128)}, f32[128,4,4]{2,1,0:T(4,128)}, u32[]{:S(2)}, u32[]{:S(2)}) %collective-permute-start.4) | collective-permute-done | bytes 8224 | tf_op jit(solution)/shard_map/ppermute | solution.py:132
  61.1 7.1 %collective-permute-done.3 = f32[128,4,4]{2,1,0:T(4,128)S(1)} collective-permute-done((f32[128,4,4]{2,1,0:T(4,128)}, f32[128,4,4]{2,1,0:T(4,128)S(1)}, u32[]{:S(2)}, u32[]{:S(2)}) %collective-permute-start.3) | collective-permute-done | bytes 8224 | tf_op jit(solution)/shard_map/ppermute | solution.py:131
  68.2 3.9 %maximum_maximum_fusion.rows_ref = f32[128,8,640]{2,1,0:T(8,128)} fusion(f32[128,4,4]{2,1,0:T(4,128)S(1)} %collective-permute-done.7, f32[128,4,120]{2,1,0:T(4,128)S(1)} %broadcast_in_dim.52, f32[128,4,4]{2,1,0:T(4,128)} %collective-permute-done.6, f32[128,4,512]{2,1,0:T(4,128)S(1)} %collective-permute-done.5, f32[128,4,4]{2,1,0:T(4,128)} %collective-permute-done.4, ...), kind=kLoop, calls=%fused_computation.3 | loop fusion | flops 4587520 | bytes 4997120 | tf_op jit(solution)/shard_map/concatenate | solution.py:138
  72.1 60.6 %shard_map.111 = (f32[128,32,512]{2,1,0:T(8,128)}, f32[4,32,512]{2,1,0:T(8,128)}) custom-call(f32[128]{0:T(128)} %kappa_ref.1, f32[4,128]{1,0:T(4,128)} %weight_ref.1, f32[128,32,512]{2,1,0:T(8,128)} %core_ref.1, f32[128,32,128]{2,1,0:T(8,128)} %pad_maximum_fusion.lanes_ref, f32[128,8,640]{2,1,0:T(8,128)} %maximum_maximum_fusion.rows_ref, ...), custom_call_target="tpu_custom_call" | custom-call | flops 131072000 | bytes 16777216 | tf_op jit(solution)/shard_map/pallas_call | solution.py:156
  132.7 1.0 convert_element_type.40
  133.8 0.6 gather_fusion.1
  134.8 0.7 gather_fusion
  135.6 3.3 %collective-permute-done.8 = bf16[32,4,128]{2,1,0:T(4,128)(2,1)S(1)} collective-permute-done((bf16[32,4,128]{2,1,0:T(4,128)(2,1)S(1)}, bf16[32,4,128]{2,1,0:T(4,128)(2,1)S(1)}, u32[]{:S(2)}, u32[]{:S(2)}) %collective-permute-start.8) | collective-permute-done | bytes 32800 | tf_op jit(solution)/shard_map/ppermute | solution.py:29
  138.9 0.7 gather_fusion.2
  139.7 3.0 %convolution_bitcast_fusion = f32[4,32,128]{2,0,1:T(4,128)S(1)} fusion(bf16[32,4,128,128]{3,2,1,0:T(8,128)(2,1)} %param.13, bf16[32,4,4,128]{3,2,1,0:T(4,128)(2,1)S(1)} %bitcast.37, bf16[32,4,4,128]{3,2,1,0:T(4,128)(2,1)S(1)} %bitcast.38, pred[32,4]{1,0:T(8,128)(4,1)S(1)} %and.117, pred[32,4]{1,0:T(8,128)(4,1)S(1)} %and.113), kind=kOutput, calls=%fused_computation.5 | convolution fusion | flops 16908288 | bytes 4522240 | tf_op jit(solution)/shard_map/bkij,bkcj->cbi/dot_general | solution.py:352
  142.8 0.6 constant_dynamic-update-slice_fusion.43
  143.5 3.5 %collective-permute-start.16 = (f32[1,16,256]{2,1,0:T(8,128)S(1)}, f32[1,16,256]{2,1,0:T(8,128)S(1)}, u32[]{:S(2)}, u32[]{:S(2)}) collective-permute-start(f32[1,16,256]{2,1,0:T(8,128)S(1)} %get-tuple-element.15), channel_id=1, source_target_pairs={{0,2},{1,3},{2,0},{3,1},{4,6},{5,7},{6,4},{7,5},{8,10},{9,11},{10,... | collective-permute-start | bytes 49160 | tf_op jit(solution)/shard_map/ppermute | solution.py:61
  147.0 1.7 collective-permute-done.9
  148.7 2.9 %collective-permute-start.10 = (f32[2,16,256]{2,1,0:T(8,128)S(1)}, f32[2,16,256]{2,1,0:T(8,128)S(1)}, u32[]{:S(2)}, u32[]{:S(2)}) collective-permute-start(f32[2,16,256]{2,1,0:T(8,128)S(1)} %pad_maximum_fusion.5), channel_id=1, source_target_pairs={{0,8},{1,9},{2,10},{3,11},{4,12},{5,13},{6,14},{7,15},{8,0},{9,1},... | collective-permute-start | bytes 98312 | tf_op jit(solution)/shard_map/ppermute | solution.py:61
  151.6 0.6 collective-permute-start.17
  152.2 0.6 constant_dynamic-update-slice_fusion.16
  152.8 0.6 constant_dynamic-update-slice_fusion.42
  153.5 0.7 collective-permute-done.10
  154.1 4.4 %collective-permute-start.11 = (f32[4,16,256]{2,1,0:T(8,128)S(1)}, f32[4,16,256]{2,1,0:T(8,128)S(1)}, u32[]{:S(2)}, u32[]{:S(2)}) collective-permute-start(f32[4,16,256]{2,1,0:T(8,128)S(1)} %pad_maximum_fusion.3), channel_id=1, source_target_pairs={{0,64},{16,80},{32,96},{48,112},{64,0},{80,16},{96,32},{112,48},{1... | collective-permute-start | bytes 196616 | tf_op jit(solution)/shard_map/ppermute | solution.py:61
  158.5 2.7 %collective-permute-start.18 = (f32[4,16,256]{2,1,0:T(8,128)S(1)}, f32[4,16,256]{2,1,0:T(8,128)S(1)}, u32[]{:S(2)}, u32[]{:S(2)}) collective-permute-start(f32[4,16,256]{2,1,0:T(8,128)S(1)} %pad_maximum_fusion.4), channel_id=1, source_target_pairs={{0,64},{16,80},{32,96},{48,112},{64,0},{80,16},{96,32},{112,48},{1... | collective-permute-start | bytes 196616 | tf_op jit(solution)/shard_map/ppermute | solution.py:61
  161.2 0.6 constant_dynamic-update-slice_fusion.15
  161.8 0.6 constant_dynamic-update-slice_fusion.41
  162.6 1.8 collective-permute-done.18
  164.7 0.6 constant_dynamic-update-slice_fusion.14
  165.3 2.2 collective-permute-done.12
  167.5 0.7 constant_dynamic-update-slice_fusion.13
  168.7 0.6 constant_dynamic-update-slice_fusion.40
  169.4 0.7 constant_dynamic-update-slice_fusion.39
  170.1 1.4 collective-permute-start.20
  171.6 3.8 %collective-permute-done.13 = f32[16,16,256]{2,1,0:T(8,128)S(1)} collective-permute-done((f32[16,16,256]{2,1,0:T(8,128)S(1)}, f32[16,16,256]{2,1,0:T(8,128)S(1)}, u32[]{:S(2)}, u32[]{:S(2)}) %collective-permute-start.13) | collective-permute-done | bytes 262176 | tf_op jit(solution)/shard_map/ppermute | solution.py:61
  175.4 0.8 constant_dynamic-update-slice_fusion.12
  176.1 2.4 %collective-permute-start.14 = (f32[32,16,256]{2,1,0:T(8,128)S(1)}, f32[32,16,256]{2,1,0:T(8,128)S(1)}, u32[]{:S(2)}, u32[]{:S(2)}) collective-permute-start(f32[32,16,256]{2,1,0:T(8,128)S(1)} %get-tuple-element.41), channel_id=1, source_target_pairs={{0,32},{16,48},{32,0},{48,16},{64,96},{80,112},{96,64},{112,80},{1... | collective-permute-start | bytes 1572872 | tf_op jit(solution)/shard_map/ppermute | solution.py:61
  178.6 0.8 constant_dynamic-update-slice_fusion.38
  179.3 2.0 collective-permute-start.21
  181.4 8.5 %collective-permute-done.14 = f32[32,16,256]{2,1,0:T(8,128)S(1)} collective-permute-done((f32[32,16,256]{2,1,0:T(8,128)S(1)}, f32[32,16,256]{2,1,0:T(8,128)S(1)}, u32[]{:S(2)}, u32[]{:S(2)}) %collective-permute-start.14) | collective-permute-done | bytes 524320 | tf_op jit(solution)/shard_map/ppermute | solution.py:61
  189.8 0.9 constant_dynamic-update-slice_fusion.11
  190.7 4.7 %collective-permute-done.21 = f32[32,16,256]{2,1,0:T(8,128)S(1)} collective-permute-done((f32[32,16,256]{2,1,0:T(8,128)S(1)}, f32[32,16,256]{2,1,0:T(8,128)S(1)}, u32[]{:S(2)}, u32[]{:S(2)}) %collective-permute-start.21) | collective-permute-done | bytes 524320 | tf_op jit(solution)/shard_map/ppermute | solution.py:61
  195.4 0.9 constant_dynamic-update-slice_fusion.37
  197.0 0.6 reshape.238
  197.6 1.1 constant_dynamic-update-slice_fusion.18.rhs_stack
  198.7 0.7 collective-permute-done.22
  199.4 1.3 constant_dynamic-update-slice_fusion.44.coded_stack
  200.7 1.3 copy-done
  202.0 19.9 %shard_map.112 = (f32[16,256]{1,0:T(8,128)}, f32[16,256]{1,0:T(8,128)}) custom-call(s32[2]{0:T(128)} %pad_add_fusion.index_ref, f32[128,16,256]{2,1,0:T(8,128)} %constant_dynamic-update-slice_fusion.18.rhs_stack, f32[128,16,256]{2,1,0:T(8,128)} %copy-done), custom_call_target="tpu_custom_call" | custom-call | tf_op jit(solution)/shard_map/pallas_call | solution.py:286
  (74 shorter events, 5.0 us)
Async XLA Ops:
  8.2 30.3 %collective-permute-start.1 = (f32[128,32,4]{0,1,2:T(8,128)}, f32[128,32,4]{0,1,2:T(8,128)}, u32[]{:S(2)}, u32[]{:S(2)}) collective-permute-start(f32[128,32,4]{0,1,2:T(8,128)} %copy.86), channel_id=1, source_target_pairs={{0,16},{16,32},{32,48},{48,64},{64,80},{80,96},{96,112},{1,17},{17... | collective-permute-start | bytes 196616 | tf_op jit(solution)/shard_map/ppermute | solution.py:130
  12.5 30.0 %collective-permute-start = (f32[128,32,4]{0,1,2:T(8,128)}, f32[128,32,4]{0,1,2:T(8,128)S(1)}, u32[]{:S(2)}, u32[]{:S(2)}) collective-permute-start(f32[128,32,4]{0,1,2:T(8,128)} %copy.85), channel_id=1, source_target_pairs={{16,0},{32,16},{48,32},{64,48},{80,64},{96,80},{112,96},{17,1},{33... | collective-permute-start | bytes 196616 | tf_op jit(solution)/shard_map/ppermute | solution.py:129
  16.6 15.9 %copy-start.2 = (s32[4096,4]{0,1:T(4,128)S(1)}, s32[4096,4]{0,1:T(4,128)}, u32[]{:S(2)}) copy-start(s32[4096,4]{0,1:T(4,128)} %param.11) | copy-start | bytes 196612
  16.6 33.7 %collective-permute-start.7 = (f32[128,4,4]{2,1,0:T(4,128)}, f32[128,4,4]{2,1,0:T(4,128)S(1)}, u32[]{:S(2)}, u32[]{:S(2)}) collective-permute-start(f32[128,4,4]{2,1,0:T(4,128)} %get-tuple-element.29), channel_id=1, source_target_pairs={{0,17},{1,18},{2,19},{3,20},{4,21},{5,22},{6,23},{7,24},{8,25},{9,... | collective-permute-start | bytes 24584 | tf_op jit(solution)/shard_map/ppermute | solution.py:134
  26.1 42.1 %collective-permute-start.5 = (f32[128,4,512]{2,1,0:T(4,128)}, f32[128,4,512]{2,1,0:T(4,128)S(1)}, u32[]{:S(2)}, u32[]{:S(2)}) collective-permute-start(f32[128,4,512]{2,1,0:T(4,128)} %get-tuple-element.25), channel_id=1, source_target_pairs={{0,1},{1,2},{2,3},{3,4},{4,5},{5,6},{6,7},{7,8},{8,9},{9,10},{10,1... | collective-permute-start | bytes 3145736 | tf_op jit(solution)/shard_map/ppermute | solution.py:128
  29.5 38.7 %collective-permute-start.2 = (f32[128,4,512]{2,1,0:T(4,128)}, f32[128,4,512]{2,1,0:T(4,128)}, u32[]{:S(2)}, u32[]{:S(2)}) collective-permute-start(f32[128,4,512]{2,1,0:T(4,128)} %get-tuple-element.24), channel_id=1, source_target_pairs={{1,0},{2,1},{3,2},{4,3},{5,4},{6,5},{7,6},{8,7},{9,8},{10,9},{11,1... | collective-permute-start | bytes 3145736 | tf_op jit(solution)/shard_map/ppermute | solution.py:127
  32.5 2.5 %copy-start.3 = (s32[4096]{0:T(1024)S(1)}, s32[4096]{0:T(1024)}, u32[]{:S(2)}) copy-start(s32[4096]{0:T(1024)} %param.12) | copy-start | bytes 49156
  38.5 18.7 %collective-permute-start.6 = (f32[128,4,4]{2,1,0:T(4,128)}, f32[128,4,4]{2,1,0:T(4,128)}, u32[]{:S(2)}, u32[]{:S(2)}) collective-permute-start(f32[128,4,4]{2,1,0:T(4,128)} %get-tuple-element.28), channel_id=1, source_target_pairs={{16,1},{17,2},{18,3},{19,4},{20,5},{21,6},{22,7},{23,8},{24,9},{25... | collective-permute-start | bytes 24584 | tf_op jit(solution)/shard_map/ppermute | solution.py:133
  42.5 18.6 %collective-permute-start.4 = (f32[128,4,4]{2,1,0:T(4,128)}, f32[128,4,4]{2,1,0:T(4,128)}, u32[]{:S(2)}, u32[]{:S(2)}) collective-permute-start(f32[128,4,4]{2,1,0:T(4,128)} %get-tuple-element.27), channel_id=1, source_target_pairs={{1,16},{2,17},{3,18},{4,19},{5,20},{6,21},{7,22},{8,23},{9,24},{10... | collective-permute-start | bytes 24584 | tf_op jit(solution)/shard_map/ppermute | solution.py:132
  50.3 17.8 %collective-permute-start.3 = (f32[128,4,4]{2,1,0:T(4,128)}, f32[128,4,4]{2,1,0:T(4,128)S(1)}, u32[]{:S(2)}, u32[]{:S(2)}) collective-permute-start(f32[128,4,4]{2,1,0:T(4,128)} %get-tuple-element.26), channel_id=1, source_target_pairs={{17,0},{18,1},{19,2},{20,3},{21,4},{22,5},{23,6},{24,7},{25,8},{26... | collective-permute-start | bytes 24584 | tf_op jit(solution)/shard_map/ppermute | solution.py:131
  134.6 4.4 %collective-permute-start.8 = (bf16[32,4,128]{2,1,0:T(4,128)(2,1)S(1)}, bf16[32,4,128]{2,1,0:T(4,128)(2,1)S(1)}, u32[]{:S(2)}, u32[]{:S(2)}) collective-permute-start(bf16[32,4,128]{2,1,0:T(4,128)(2,1)S(1)} %broadcast_multiply_fusion), channel_id=1, source_target_pairs={{0,112},{16,0},{32,16},{48,32},{64,48},{80,64},{96,80},{112,96},{1... | collective-permute-start | bytes 98312 | tf_op jit(solution)/shard_map/ppermute | solution.py:29
  139.7 3.1 %copy-start.4 = (f32[16,256]{1,0:T(8,128)S(1)}, f32[16,256]{1,0:T(8,128)}, u32[]{:S(2)}) copy-start(f32[16,256]{1,0:T(8,128)} %param.15) | copy-start | bytes 49156
  139.7 3.1 %copy-start.5 = (s32[16,256]{1,0:T(8,128)S(1)}, s32[16,256]{1,0:T(8,128)}, u32[]{:S(2)}) copy-start(s32[16,256]{1,0:T(8,128)} %param.14) | copy-start | bytes 49156
  143.5 5.2 %collective-permute-start.9 = (f32[1,16,256]{2,1,0:T(8,128)S(1)}, f32[1,16,256]{2,1,0:T(8,128)S(1)}, u32[]{:S(2)}, u32[]{:S(2)}) collective-permute-start(f32[1,16,256]{2,1,0:T(8,128)S(1)} %get-tuple-element.80), channel_id=1, source_target_pairs={{0,2},{1,3},{2,0},{3,1},{4,6},{5,7},{6,4},{7,5},{8,10},{9,11},{10,... | collective-permute-start | bytes 49160 | tf_op jit(solution)/shard_map/ppermute | solution.py:61
  143.5 8.1 %collective-permute-start.16 = (f32[1,16,256]{2,1,0:T(8,128)S(1)}, f32[1,16,256]{2,1,0:T(8,128)S(1)}, u32[]{:S(2)}, u32[]{:S(2)}) collective-permute-start(f32[1,16,256]{2,1,0:T(8,128)S(1)} %get-tuple-element.15), channel_id=1, source_target_pairs={{0,2},{1,3},{2,0},{3,1},{4,6},{5,7},{6,4},{7,5},{8,10},{9,11},{10,... | collective-permute-start | bytes 49160 | tf_op jit(solution)/shard_map/ppermute | solution.py:61
  148.7 5.4 %collective-permute-start.10 = (f32[2,16,256]{2,1,0:T(8,128)S(1)}, f32[2,16,256]{2,1,0:T(8,128)S(1)}, u32[]{:S(2)}, u32[]{:S(2)}) collective-permute-start(f32[2,16,256]{2,1,0:T(8,128)S(1)} %pad_maximum_fusion.5), channel_id=1, source_target_pairs={{0,8},{1,9},{2,10},{3,11},{4,12},{5,13},{6,14},{7,15},{8,0},{9,1},... | collective-permute-start | bytes 98312 | tf_op jit(solution)/shard_map/ppermute | solution.py:61
  151.6 6.9 %collective-permute-start.17 = (f32[2,16,256]{2,1,0:T(8,128)S(1)}, f32[2,16,256]{2,1,0:T(8,128)S(1)}, u32[]{:S(2)}, u32[]{:S(2)}) collective-permute-start(f32[2,16,256]{2,1,0:T(8,128)S(1)} %pad_maximum_fusion.6), channel_id=1, source_target_pairs={{0,8},{1,9},{2,10},{3,11},{4,12},{5,13},{6,14},{7,15},{8,0},{9,1},... | collective-permute-start | bytes 98312 | tf_op jit(solution)/shard_map/ppermute | solution.py:61
  154.1 8.3 %collective-permute-start.11 = (f32[4,16,256]{2,1,0:T(8,128)S(1)}, f32[4,16,256]{2,1,0:T(8,128)S(1)}, u32[]{:S(2)}, u32[]{:S(2)}) collective-permute-start(f32[4,16,256]{2,1,0:T(8,128)S(1)} %pad_maximum_fusion.3), channel_id=1, source_target_pairs={{0,64},{16,80},{32,96},{48,112},{64,0},{80,16},{96,32},{112,48},{1... | collective-permute-start | bytes 196616 | tf_op jit(solution)/shard_map/ppermute | solution.py:61
  158.5 5.8 %collective-permute-start.18 = (f32[4,16,256]{2,1,0:T(8,128)S(1)}, f32[4,16,256]{2,1,0:T(8,128)S(1)}, u32[]{:S(2)}, u32[]{:S(2)}) collective-permute-start(f32[4,16,256]{2,1,0:T(8,128)S(1)} %pad_maximum_fusion.4), channel_id=1, source_target_pairs={{0,64},{16,80},{32,96},{48,112},{64,0},{80,16},{96,32},{112,48},{1... | collective-permute-start | bytes 196616 | tf_op jit(solution)/shard_map/ppermute | solution.py:61
  162.5 5.0 %collective-permute-start.12 = (f32[8,16,256]{2,1,0:T(8,128)S(1)}, f32[8,16,256]{2,1,0:T(8,128)S(1)}, u32[]{:S(2)}, u32[]{:S(2)}) collective-permute-start(f32[8,16,256]{2,1,0:T(8,128)S(1)} %pad_maximum_fusion.1), channel_id=1, source_target_pairs={{0,1},{1,0},{2,3},{3,2},{4,5},{5,4},{6,7},{7,6},{8,9},{9,8},{10,11... | collective-permute-start | bytes 393224 | tf_op jit(solution)/shard_map/ppermute | solution.py:61
  164.4 5.0 %collective-permute-start.19 = (f32[8,16,256]{2,1,0:T(8,128)S(1)}, f32[8,16,256]{2,1,0:T(8,128)S(1)}, u32[]{:S(2)}, u32[]{:S(2)}) collective-permute-start(f32[8,16,256]{2,1,0:T(8,128)S(1)} %pad_maximum_fusion.2), channel_id=1, source_target_pairs={{0,1},{1,0},{2,3},{3,2},{4,5},{5,4},{6,7},{7,6},{8,9},{9,8},{10,11... | collective-permute-start | bytes 393224 | tf_op jit(solution)/shard_map/ppermute | solution.py:61
  168.2 7.2 %collective-permute-start.13 = (f32[16,16,256]{2,1,0:T(8,128)S(1)}, f32[16,16,256]{2,1,0:T(8,128)S(1)}, u32[]{:S(2)}, u32[]{:S(2)}) collective-permute-start(f32[16,16,256]{2,1,0:T(8,128)S(1)} %get-tuple-element.49), channel_id=1, source_target_pairs={{0,4},{1,5},{2,6},{3,7},{4,0},{5,1},{6,2},{7,3},{8,12},{9,13},{10,... | collective-permute-start | bytes 786440 | tf_op jit(solution)/shard_map/ppermute | solution.py:61
  170.1 8.4 %collective-permute-start.20 = (f32[16,16,256]{2,1,0:T(8,128)S(1)}, f32[16,16,256]{2,1,0:T(8,128)S(1)}, u32[]{:S(2)}, u32[]{:S(2)}) collective-permute-start(f32[16,16,256]{2,1,0:T(8,128)S(1)} %get-tuple-element.45), channel_id=1, source_target_pairs={{0,4},{1,5},{2,6},{3,7},{4,0},{5,1},{6,2},{7,3},{8,12},{9,13},{10,... | collective-permute-start | bytes 786440 | tf_op jit(solution)/shard_map/ppermute | solution.py:61
  176.1 13.7 %collective-permute-start.14 = (f32[32,16,256]{2,1,0:T(8,128)S(1)}, f32[32,16,256]{2,1,0:T(8,128)S(1)}, u32[]{:S(2)}, u32[]{:S(2)}) collective-permute-start(f32[32,16,256]{2,1,0:T(8,128)S(1)} %get-tuple-element.41), channel_id=1, source_target_pairs={{0,32},{16,48},{32,0},{48,16},{64,96},{80,112},{96,64},{112,80},{1... | collective-permute-start | bytes 1572872 | tf_op jit(solution)/shard_map/ppermute | solution.py:61
  179.3 16.1 %collective-permute-start.21 = (f32[32,16,256]{2,1,0:T(8,128)S(1)}, f32[32,16,256]{2,1,0:T(8,128)S(1)}, u32[]{:S(2)}, u32[]{:S(2)}) collective-permute-start(f32[32,16,256]{2,1,0:T(8,128)S(1)} %get-tuple-element.38), channel_id=1, source_target_pairs={{0,32},{16,48},{32,0},{48,16},{64,96},{80,112},{96,64},{112,80},{1... | collective-permute-start | bytes 1572872 | tf_op jit(solution)/shard_map/ppermute | solution.py:61
  190.7 5.7 %copy-start.1 = (f32[128,16,256]{2,1,0:T(8,128)}, f32[128,16,256]{2,1,0:T(8,128)S(1)}, u32[]{:S(2)}) copy-start(f32[128,16,256]{2,1,0:T(8,128)S(1)} %get-tuple-element.35) | copy-start | bytes 6291460
  190.7 6.9 %collective-permute-start.15 = (f32[64,16,256]{2,1,0:T(8,128)}, f32[64,16,256]{2,1,0:T(8,128)S(1)}, u32[]{:S(2)}, u32[]{:S(2)}) collective-permute-start(f32[64,16,256]{2,1,0:T(8,128)} %get-tuple-element.34), channel_id=1, source_target_pairs={{0,16},{16,0},{32,48},{48,32},{64,80},{80,64},{96,112},{112,96},{1... | collective-permute-start | bytes 3145736 | tf_op jit(solution)/shard_map/ppermute | solution.py:61
  196.4 3.0 %collective-permute-start.22 = (f32[64,16,256]{2,1,0:T(8,128)}, f32[64,16,256]{2,1,0:T(8,128)}, u32[]{:S(2)}, u32[]{:S(2)}) collective-permute-start(f32[64,16,256]{2,1,0:T(8,128)} %get-tuple-element.32), channel_id=1, source_target_pairs={{0,16},{16,0},{32,48},{48,32},{64,80},{80,64},{96,112},{112,96},{1... | collective-permute-start | bytes 3145736 | tf_op jit(solution)/shard_map/ppermute | solution.py:61
  200.7 1.3 copy-start

commit v6 on v5

--- a/solution.py
+++ b/solution.py
@@ -187,7 +187,7 @@
 
 
 def cg_kernel(
-    rounds, index_ref, rhs_stack, coded_stack, height_out, residual_out,
+    rounds, index_ref, both_stack, height_out, residual_out,
     rhs_ref, coded_ref, height_ref, residual_ref, pad_ref, dir_ref, img_ref,
 ):
     rows, cols = rhs_ref.shape
@@ -206,11 +206,11 @@
                 gx_off = gx_off + flag * distance
         r0 = pl.multiple_of(lax.bitwise_xor(gy, gy_off) * tile_rows, tile_rows)
         c0 = pl.multiple_of(lax.bitwise_xor(gx, gx_off) * tile_cols, tile_cols)
-        rhs_ref[pl.ds(r0, tile_rows), pl.ds(c0, tile_cols)] = rhs_stack[k]
-        coded_ref[pl.ds(r0, tile_rows), pl.ds(c0, tile_cols)] = coded_stack[k]
+        rhs_ref[pl.ds(r0, tile_rows), pl.ds(c0, tile_cols)] = both_stack[k, 1]
+        coded_ref[pl.ds(r0, tile_rows), pl.ds(c0, tile_cols)] = both_stack[k, 0]
         return carry
 
-    lax.fori_loop(0, rhs_stack.shape[0], place, 0)
+    lax.fori_loop(0, both_stack.shape[0], place, 0)
     strips = rows // 8
     zeros = jnp.zeros((8, cols), jnp.float32)
     pad_ref[0:8, :] = zeros
@@ -276,8 +276,8 @@
     residual_out[...] = residual_ref[pl.ds(r0, tile_rows), pl.ds(c0, tile_cols)]
 
 
-def solve_grid(rhs_stack, coded_stack, rounds):
-    parts, tile_rows, tile_cols = rhs_stack.shape
+def solve_grid(both_stack, rounds):
+    parts, _, tile_rows, tile_cols = both_stack.shape
     rows = lax.axis_size("gy") * tile_rows
     cols = lax.axis_size("gx") * tile_cols
     index = jnp.stack([lax.axis_index("gy"), lax.axis_index("gx")]).astype(jnp.int32)
@@ -285,11 +285,11 @@
     grid = pltpu.VMEM((rows, cols), jnp.float32)
     return pl.pallas_call(
         functools.partial(cg_kernel, rounds),
-        in_specs=[pl.BlockSpec(memory_space=pltpu.SMEM), whole, whole],
+        in_specs=[pl.BlockSpec(memory_space=pltpu.SMEM), whole],
         out_specs=[whole, whole],
         out_shape=[jax.ShapeDtypeStruct((tile_rows, tile_cols), jnp.float32)] * 2,
         scratch_shapes=[grid, grid, grid, grid, pltpu.VMEM((rows + 16, cols), jnp.float32), grid, grid],
-    )(index, rhs_stack, coded_stack)
+    )(index, both_stack)
 
 
 def body(
@@ -300,7 +300,7 @@
     count_gx = lax.axis_size("gx")
     count_gy = lax.axis_size("gy")
     rounds = gather_rounds()
-    coded_all = stack_gather(jnp.where(land_mask != 0, ocean_term, -1.0), rounds)
+    coded = jnp.where(land_mask != 0, ocean_term, -1.0)
     field, flux = diffuse(atm_state, atm_kappa, vert_weight)
     flux = flux.reshape(flux.shape[0], tile_lat * tile_lon)
     ocean_blocks, lists, width, _ = remap_weight.shape
@@ -354,8 +354,8 @@
     )
     ocean_flux = remapped.reshape(comps, ocean_rows, ocean_cols)
     rhs_tile = land_mask.astype(jnp.float32) * (ocean_flux[0] + ocean_flux[1])
-    rhs = stack_gather(rhs_tile, rounds)
-    height, residual = solve_grid(rhs, coded_all, rounds)
+    both = stack_gather(jnp.stack([coded, rhs_tile]), rounds)
+    height, residual = solve_grid(both, rounds)
     return (field, ocean_flux, height, residual)
 
 

time: 224 us -> 235 us (1.049)
  waiting for transfers between devices: 40.3 us -> 66.2 us
  starting transfers between devices: 43.5 us -> 33.4 us
  local copies, waits for them, and re-layouts: 40.5 us -> 35.5 us
    ppermute x14 -> x7, waiting for transfers between devices: 24.2 us -> 50.1 us  [stack_gather(): other = lax.ppermute(x, axis, [(j, j ^ distance) for j in range(size)])]
    ppermute x14 -> x7, starting transfers between devices: 20.9 us -> 10.7 us  [stack_gather(): other = lax.ppermute(x, axis, [(j, j ^ distance) for j in range(size)])]
    unnamed x27 -> x16, local copies, waits for them, and re-layouts: 13.8 us -> 9.95 us
  transfers between devices with their start and end apart: 23 -> 16, of which waited for: 13 -> 11; matrix products, arithmetic and copies ran while one was open for 16% -> 13% of each run, Pallas kernels for 0% -> 0%
where the time goes in v6:
time: 235 us; the launch traced here: 233 us
  Pallas kernels  80.3 us (34%)
  waiting for transfers between devices  66.2 us (28%)
  local copies, waits for them, and re-layouts  35.5 us (15%)
  starting transfers between devices  33.4 us (14%)
  other arithmetic  13.2 us (6%)
  matrix products  3.04 us (1%)
    pallas_call x1, Pallas kernels, diffuse(): pl.pallas_call(diffusion_kernel, grid=(blocks,), in_specs=[smem, smem, pl...  60.6 us
    ppermute x7, waiting for transfers between devices, stack_gather(): other = lax.ppermute(x, axis, [(j, j ^ distance) for j in range(size)])  50.1 us
    pallas_call x1, Pallas kernels, solve_grid(): pl.pallas_call(functools.partial(cg_kernel, rounds), in_specs=[pl.BlockSp...  19.8 us
    ppermute x7, starting transfers between devices, stack_gather(): other = lax.ppermute(x, axis, [(j, j ^ distance) for j in range(size)])  10.7 us
    unnamed x16, local copies, waits for them, and re-layouts  9.95 us
    ppermute x1, waiting for transfers between devices, diffuse(): south_east = lax.ppermute(field[:, :HALO, :HALO], both, pairs(1, 1))  7.07 us
    ppermute x1, starting transfers between devices, diffuse(): lax.ppermute(field[:, rows - HALO:, cols - HALO:], both, pairs(-1, -1))  5.36 us
    ppermute x1, starting transfers between devices, diffuse(): south_west = lax.ppermute(field[:, :HALO, cols - HALO:], both, pairs(-1, 1))  4.99 us
  transfers between devices with their start and end apart: 16, of which 11 were waited for; matrix products, arithmetic and copies ran while one was open for 13% of the time, Pallas kernels for 0%

profile of v6, /device:TPU:6, one launch (start us, length us, event | category | flops | bytes accessed | tf_op | source)
XLA Modules:
  0.0 232.8 jit_solution(15513777989003299542)
XLA Ops:
  0.6 4.3 %fusion.26 = (f32[128,32,4]{2,1,0:T(8,128)S(1)}, f32[128,32,4]{2,1,0:T(8,128)}) fusion(f32[128,32,512]{2,1,0:T(8,128)} %core_ref.1), kind=kLoop, calls=%fused_computation.98 | loop fusion | bytes 262144 | tf_op jit(solution)/shard_map/slice | solution.py:129
  4.9 3.3 %copy.86 = f32[128,32,4]{0,1,2:T(8,128)} copy(f32[128,32,4]{2,1,0:T(8,128)} %get-tuple-element.27) | data formatting | bytes 131072
  8.2 2.3 %collective-permute-start.1 = (f32[128,32,4]{0,1,2:T(8,128)}, f32[128,32,4]{0,1,2:T(8,128)}, u32[]{:S(2)}, u32[]{:S(2)}) collective-permute-start(f32[128,32,4]{0,1,2:T(8,128)} %copy.86), channel_id=1, source_target_pairs={{0,16},{16,32},{32,48},{48,64},{64,80},{80,96},{96,112},{1,17},{17... | collective-permute-start | bytes 196616 | tf_op jit(solution)/shard_map/ppermute | solution.py:130
  10.5 1.9 copy.85
  12.5 1.3 collective-permute-start
  13.8 2.9 %fusion.25 = (f32[128,4,4]{2,1,0:T(4,128)}, f32[128,4,4]{2,1,0:T(4,128)}, f32[128,4,4]{2,1,0:T(4,128)}, f32[128,4,4]{2,1,0:T(4,128)}) fusion(f32[128,32,512]{2,1,0:T(8,128)} %core_ref.1), kind=kLoop, calls=%fused_computation.97 | loop fusion | bytes 65536 | tf_op jit(solution)/shard_map/slice | solution.py:131
  16.7 5.4 %collective-permute-start.7 = (f32[128,4,4]{2,1,0:T(4,128)}, f32[128,4,4]{2,1,0:T(4,128)S(1)}, u32[]{:S(2)}, u32[]{:S(2)}) collective-permute-start(f32[128,4,4]{2,1,0:T(4,128)} %get-tuple-element.25), channel_id=1, source_target_pairs={{0,17},{1,18},{2,19},{3,20},{4,21},{5,22},{6,23},{7,24},{8,25},{9,... | collective-permute-start | bytes 24584 | tf_op jit(solution)/shard_map/ppermute | solution.py:134
  22.0 4.1 %fusion.24 = (f32[128,4,512]{2,1,0:T(4,128)}, f32[128,4,512]{2,1,0:T(4,128)}) fusion(f32[128,32,512]{2,1,0:T(8,128)} %core_ref.1), kind=kLoop, calls=%fused_computation.96 | loop fusion | bytes 4194304 | tf_op jit(solution)/shard_map/slice | solution.py:127
  26.1 3.5 %collective-permute-start.5 = (f32[128,4,512]{2,1,0:T(4,128)}, f32[128,4,512]{2,1,0:T(4,128)S(1)}, u32[]{:S(2)}, u32[]{:S(2)}) collective-permute-start(f32[128,4,512]{2,1,0:T(4,128)} %get-tuple-element.21), channel_id=1, source_target_pairs={{0,1},{1,2},{2,3},{3,4},{4,5},{5,6},{6,7},{7,8},{8,9},{9,10},{10,1... | collective-permute-start | bytes 3145736 | tf_op jit(solution)/shard_map/ppermute | solution.py:128
  29.7 2.4 %collective-permute-start.2 = (f32[128,4,512]{2,1,0:T(4,128)}, f32[128,4,512]{2,1,0:T(4,128)}, u32[]{:S(2)}, u32[]{:S(2)}) collective-permute-start(f32[128,4,512]{2,1,0:T(4,128)} %get-tuple-element.20), channel_id=1, source_target_pairs={{1,0},{2,1},{3,2},{4,3},{5,4},{6,5},{7,6},{8,7},{9,8},{10,9},{11,1... | collective-permute-start | bytes 3145736 | tf_op jit(solution)/shard_map/ppermute | solution.py:127
  32.1 0.6 fusion.17
  32.7 0.6 copy.71
  33.4 1.6 reshape.236
  35.3 0.1 lt.129
  35.6 0.2 fusion.22
  35.9 0.2 reduce-window.13
  36.1 0.1 add_reduce_fusion
  36.2 0.2 dynamic-slice_reduce_fusion
  36.4 0.2 fusion.4
  36.6 0.1 copy.81
  36.7 0.2 reduce-window.14
  36.9 0.1 select_reduce_fusion
  37.1 1.4 and_convert_fusion.mask_ref
  38.6 1.3 collective-permute-start.6
  39.9 2.7 %copy.69 = f32[128,32,4]{2,1,0:T(8,128)S(1)} copy(f32[128,32,4]{0,1,2:T(8,128)} %collective-permute-done.1) | data formatting | bytes 131072 | tf_op jit(solution)/shard_map/ppermute | solution.py:130
  42.7 5.0 %collective-permute-start.4 = (f32[128,4,4]{2,1,0:T(4,128)}, f32[128,4,4]{2,1,0:T(4,128)}, u32[]{:S(2)}, u32[]{:S(2)}) collective-permute-start(f32[128,4,4]{2,1,0:T(4,128)} %get-tuple-element.23), channel_id=1, source_target_pairs={{1,16},{2,17},{3,18},{4,19},{5,20},{6,21},{7,22},{8,23},{9,24},{10... | collective-permute-start | bytes 24584 | tf_op jit(solution)/shard_map/ppermute | solution.py:132
  47.7 2.9 %copy.68 = f32[128,32,4]{2,1,0:T(8,128)} copy(f32[128,32,4]{0,1,2:T(8,128)S(1)} %collective-permute-done) | data formatting | bytes 131072 | tf_op jit(solution)/shard_map/ppermute | solution.py:129
  50.5 1.5 collective-permute-start.3
  52.0 3.5 %pad_maximum_fusion.lanes_ref = f32[128,32,128]{2,1,0:T(8,128)} fusion(f32[128,32,4]{2,1,0:T(8,128)S(1)} %copy.69, f32[128,32,4]{2,1,0:T(8,128)} %copy.68, f32[128]{0:T(128)S(1)} %pad.22.clone), kind=kLoop, calls=%fused_computation.4 | loop fusion | flops 1048576 | bytes 2228736 | tf_op jit(solution)/shard_map/concatenate | solution.py:136
  55.5 1.8 collective-permute-done.6
  57.3 4.0 %collective-permute-done.4 = f32[128,4,4]{2,1,0:T(4,128)} collective-permute-done((f32[128,4,4]{2,1,0:T(4,128)}, f32[128,4,4]{2,1,0:T(4,128)}, u32[]{:S(2)}, u32[]{:S(2)}) %collective-permute-start.4) | collective-permute-done | bytes 8224 | tf_op jit(solution)/shard_map/ppermute | solution.py:132
  61.3 7.1 %collective-permute-done.3 = f32[128,4,4]{2,1,0:T(4,128)S(1)} collective-permute-done((f32[128,4,4]{2,1,0:T(4,128)}, f32[128,4,4]{2,1,0:T(4,128)S(1)}, u32[]{:S(2)}, u32[]{:S(2)}) %collective-permute-start.3) | collective-permute-done | bytes 8224 | tf_op jit(solution)/shard_map/ppermute | solution.py:131
  68.4 3.9 %maximum_maximum_fusion.rows_ref = f32[128,8,640]{2,1,0:T(8,128)} fusion(f32[128,4,4]{2,1,0:T(4,128)S(1)} %collective-permute-done.7, f32[128,4,120]{2,1,0:T(4,128)S(1)} %broadcast_in_dim.49, f32[128,4,4]{2,1,0:T(4,128)} %collective-permute-done.6, f32[128,4,512]{2,1,0:T(4,128)S(1)} %collective-permute-done.5, f32[128,4,4]{2,1,0:T(4,128)} %collective-permute-done.4, ...), kind=kLoop, calls=%fused_computation.3 | loop fusion | flops 4587520 | bytes 4997120 | tf_op jit(solution)/shard_map/concatenate | solution.py:138
  72.2 60.6 %shard_map.111 = (f32[128,32,512]{2,1,0:T(8,128)}, f32[4,32,512]{2,1,0:T(8,128)}) custom-call(f32[128]{0:T(128)} %kappa_ref.1, f32[4,128]{1,0:T(4,128)} %weight_ref.1, f32[128,32,512]{2,1,0:T(8,128)} %core_ref.1, f32[128,32,128]{2,1,0:T(8,128)} %pad_maximum_fusion.lanes_ref, f32[128,8,640]{2,1,0:T(8,128)} %maximum_maximum_fusion.rows_ref, ...), custom_call_target="tpu_custom_call" | custom-call | flops 131072000 | bytes 16777216 | tf_op jit(solution)/shard_map/pallas_call | solution.py:156
  132.8 1.0 convert_element_type.40
  134.0 0.6 gather_fusion.1
  134.8 0.1 and.117
  134.9 0.1 and.113
  135.0 0.7 gather_fusion
  135.8 3.3 %collective-permute-done.8 = bf16[32,4,128]{2,1,0:T(4,128)(2,1)S(1)} collective-permute-done((bf16[32,4,128]{2,1,0:T(4,128)(2,1)S(1)}, bf16[32,4,128]{2,1,0:T(4,128)(2,1)S(1)}, u32[]{:S(2)}, u32[]{:S(2)}) %collective-permute-start.8) | collective-permute-done | bytes 32800 | tf_op jit(solution)/shard_map/ppermute | solution.py:29
  139.1 0.7 gather_fusion.2
  139.8 3.0 %convolution_bitcast_fusion = f32[4,32,128]{2,0,1:T(4,128)S(1)} fusion(bf16[32,4,128,128]{3,2,1,0:T(8,128)(2,1)} %param.13, bf16[32,4,4,128]{3,2,1,0:T(4,128)(2,1)S(1)} %bitcast.45, bf16[32,4,4,128]{3,2,1,0:T(4,128)(2,1)S(1)} %bitcast.46, pred[32,4]{1,0:T(8,128)(4,1)S(1)} %and.117, pred[32,4]{1,0:T(8,128)(4,1)S(1)} %and.113), kind=kOutput, calls=%fused_computation.5 | convolution fusion | flops 16908288 | bytes 4522240 | tf_op jit(solution)/shard_map/bkij,bkcj->cbi/dot_general | solution.py:352
  143.1 5.4 %collective-permute-done.9 = f32[1,2,16,256]{3,2,1,0:T(8,128)S(1)} collective-permute-done((f32[1,2,16,256]{3,2,1,0:T(8,128)S(1)}, f32[1,2,16,256]{3,2,1,0:T(8,128)S(1)}, u32[]{:S(2)}, u32[]{:S(2)}) %collective-permute-start.9) | collective-permute-done | bytes 32800 | tf_op jit(solution)/shard_map/ppermute | solution.py:61
  148.5 2.9 %collective-permute-start.10 = (f32[2,2,16,256]{3,2,1,0:T(8,128)S(1)}, f32[2,2,16,256]{3,2,1,0:T(8,128)S(1)}, u32[]{:S(2)}, u32[]{:S(2)}) collective-permute-start(f32[2,2,16,256]{3,2,1,0:T(8,128)S(1)} %pad_maximum_fusion.3), channel_id=1, source_target_pairs={{0,8},{1,9},{2,10},{3,11},{4,12},{5,13},{6,14},{7,15},{8,0},{9,1},... | collective-permute-start | bytes 196616 | tf_op jit(solution)/shard_map/ppermute | solution.py:61
  151.4 3.1 %collective-permute-done.10 = f32[2,2,16,256]{3,2,1,0:T(8,128)S(1)} collective-permute-done((f32[2,2,16,256]{3,2,1,0:T(8,128)S(1)}, f32[2,2,16,256]{3,2,1,0:T(8,128)S(1)}, u32[]{:S(2)}, u32[]{:S(2)}) %collective-permute-start.10) | collective-permute-done | bytes 65568 | tf_op jit(solution)/shard_map/ppermute | solution.py:61
  154.5 4.0 %collective-permute-start.11 = (f32[4,2,16,256]{3,2,1,0:T(8,128)S(1)}, f32[4,2,16,256]{3,2,1,0:T(8,128)S(1)}, u32[]{:S(2)}, u32[]{:S(2)}) collective-permute-start(f32[4,2,16,256]{3,2,1,0:T(8,128)S(1)} %pad_maximum_fusion.2), channel_id=1, source_target_pairs={{0,64},{16,80},{32,96},{48,112},{64,0},{80,16},{96,32},{112,48},{1... | collective-permute-start | bytes 393224 | tf_op jit(solution)/shard_map/ppermute | solution.py:61
  158.6 0.6 constant_dynamic-update-slice_fusion.17
  159.2 2.6 %collective-permute-done.11 = f32[4,2,16,256]{3,2,1,0:T(8,128)S(1)} collective-permute-done((f32[4,2,16,256]{3,2,1,0:T(8,128)S(1)}, f32[4,2,16,256]{3,2,1,0:T(8,128)S(1)}, u32[]{:S(2)}, u32[]{:S(2)}) %collective-permute-start.11) | collective-permute-done | bytes 131104 | tf_op jit(solution)/shard_map/ppermute | solution.py:61
  161.9 0.6 constant_dynamic-update-slice_fusion.16
  162.5 0.7 constant_dynamic-update-slice_fusion.15
  163.2 0.7 constant_dynamic-update-slice_fusion.14
  163.9 5.2 %collective-permute-done.12 = f32[8,2,16,256]{3,2,1,0:T(8,128)S(1)} collective-permute-done((f32[8,2,16,256]{3,2,1,0:T(8,128)S(1)}, f32[8,2,16,256]{3,2,1,0:T(8,128)S(1)}, u32[]{:S(2)}, u32[]{:S(2)}) %collective-permute-start.12) | collective-permute-done | bytes 262176 | tf_op jit(solution)/shard_map/ppermute | solution.py:61
  169.1 0.9 constant_dynamic-update-slice_fusion.13
  170.0 1.6 collective-permute-start.13
  171.6 10.3 %collective-permute-done.13 = f32[16,2,16,256]{3,2,1,0:T(8,128)S(1)} collective-permute-done((f32[16,2,16,256]{3,2,1,0:T(8,128)S(1)}, f32[16,2,16,256]{3,2,1,0:T(8,128)S(1)}, u32[]{:S(2)}, u32[]{:S(2)}) %collective-permute-start.13) | collective-permute-done | bytes 524320 | tf_op jit(solution)/shard_map/ppermute | solution.py:61
  181.9 1.2 constant_dynamic-update-slice_fusion.12
  183.0 2.1 collective-permute-start.14
  185.1 20.4 %collective-permute-done.14 = f32[32,2,16,256]{3,2,1,0:T(8,128)S(1)} collective-permute-done((f32[32,2,16,256]{3,2,1,0:T(8,128)S(1)}, f32[32,2,16,256]{3,2,1,0:T(8,128)S(1)}, u32[]{:S(2)}, u32[]{:S(2)}) %collective-permute-start.14) | collective-permute-done | bytes 1048608 | tf_op jit(solution)/shard_map/ppermute | solution.py:61
  205.5 1.6 constant_dynamic-update-slice_fusion.11
  207.1 0.6 pad_add_fusion.index_ref
  207.8 0.6 reshape.238
  208.4 3.1 %collective-permute-done.15 = f32[64,2,16,256]{3,2,1,0:T(8,128)S(1)} collective-permute-done((f32[64,2,16,256]{3,2,1,0:T(8,128)}, f32[64,2,16,256]{3,2,1,0:T(8,128)S(1)}, u32[]{:S(2)}, u32[]{:S(2)}) %collective-permute-start.15) | collective-permute-done | bytes 2097184 | tf_op jit(solution)/shard_map/ppermute | solution.py:61
  211.5 1.5 constant_dynamic-update-slice_fusion.18.both_stack
  213.0 19.8 %shard_map.112 = (f32[16,256]{1,0:T(8,128)}, f32[16,256]{1,0:T(8,128)}) custom-call(s32[2]{0:T(128)} %pad_add_fusion.index_ref, f32[128,2,16,256]{3,2,1,0:T(8,128)} %constant_dynamic-update-slice_fusion.18.both_stack), custom_call_target="tpu_custom_call" | custom-call | tf_op jit(solution)/shard_map/pallas_call | solution.py:286
  (46 shorter events, 1.4 us)
Async XLA Ops:
  8.2 30.5 %collective-permute-start.1 = (f32[128,32,4]{0,1,2:T(8,128)}, f32[128,32,4]{0,1,2:T(8,128)}, u32[]{:S(2)}, u32[]{:S(2)}) collective-permute-start(f32[128,32,4]{0,1,2:T(8,128)} %copy.86), channel_id=1, source_target_pairs={{0,16},{16,32},{32,48},{48,64},{64,80},{80,96},{96,112},{1,17},{17... | collective-permute-start | bytes 196616 | tf_op jit(solution)/shard_map/ppermute | solution.py:130
  12.5 30.2 %collective-permute-start = (f32[128,32,4]{0,1,2:T(8,128)}, f32[128,32,4]{0,1,2:T(8,128)S(1)}, u32[]{:S(2)}, u32[]{:S(2)}) collective-permute-start(f32[128,32,4]{0,1,2:T(8,128)} %copy.85), channel_id=1, source_target_pairs={{16,0},{32,16},{48,32},{64,48},{80,64},{96,80},{112,96},{17,1},{33... | collective-permute-start | bytes 196616 | tf_op jit(solution)/shard_map/ppermute | solution.py:129
  16.7 16.0 %copy-start = (s32[4096,4]{0,1:T(4,128)S(1)}, s32[4096,4]{0,1:T(4,128)}, u32[]{:S(2)}) copy-start(s32[4096,4]{0,1:T(4,128)} %param.11) | copy-start | bytes 196612
  16.7 33.9 %collective-permute-start.7 = (f32[128,4,4]{2,1,0:T(4,128)}, f32[128,4,4]{2,1,0:T(4,128)S(1)}, u32[]{:S(2)}, u32[]{:S(2)}) collective-permute-start(f32[128,4,4]{2,1,0:T(4,128)} %get-tuple-element.25), channel_id=1, source_target_pairs={{0,17},{1,18},{2,19},{3,20},{4,21},{5,22},{6,23},{7,24},{8,25},{9,... | collective-permute-start | bytes 24584 | tf_op jit(solution)/shard_map/ppermute | solution.py:134
  26.1 9.0 %copy-start.1 = (s32[4096]{0:T(1024)S(1)}, s32[4096]{0:T(1024)}, u32[]{:S(2)}) copy-start(s32[4096]{0:T(1024)} %param.12) | copy-start | bytes 49156
  26.1 42.2 %collective-permute-start.5 = (f32[128,4,512]{2,1,0:T(4,128)}, f32[128,4,512]{2,1,0:T(4,128)S(1)}, u32[]{:S(2)}, u32[]{:S(2)}) collective-permute-start(f32[128,4,512]{2,1,0:T(4,128)} %get-tuple-element.21), channel_id=1, source_target_pairs={{0,1},{1,2},{2,3},{3,4},{4,5},{5,6},{6,7},{7,8},{8,9},{9,10},{10,1... | collective-permute-start | bytes 3145736 | tf_op jit(solution)/shard_map/ppermute | solution.py:128
  29.7 38.7 %collective-permute-start.2 = (f32[128,4,512]{2,1,0:T(4,128)}, f32[128,4,512]{2,1,0:T(4,128)}, u32[]{:S(2)}, u32[]{:S(2)}) collective-permute-start(f32[128,4,512]{2,1,0:T(4,128)} %get-tuple-element.20), channel_id=1, source_target_pairs={{1,0},{2,1},{3,2},{4,3},{5,4},{6,5},{7,6},{8,7},{9,8},{10,9},{11,1... | collective-permute-start | bytes 3145736 | tf_op jit(solution)/shard_map/ppermute | solution.py:127
  38.6 18.7 %collective-permute-start.6 = (f32[128,4,4]{2,1,0:T(4,128)}, f32[128,4,4]{2,1,0:T(4,128)}, u32[]{:S(2)}, u32[]{:S(2)}) collective-permute-start(f32[128,4,4]{2,1,0:T(4,128)} %get-tuple-element.24), channel_id=1, source_target_pairs={{16,1},{17,2},{18,3},{19,4},{20,5},{21,6},{22,7},{23,8},{24,9},{25... | collective-permute-start | bytes 24584 | tf_op jit(solution)/shard_map/ppermute | solution.py:133
  42.7 18.6 %collective-permute-start.4 = (f32[128,4,4]{2,1,0:T(4,128)}, f32[128,4,4]{2,1,0:T(4,128)}, u32[]{:S(2)}, u32[]{:S(2)}) collective-permute-start(f32[128,4,4]{2,1,0:T(4,128)} %get-tuple-element.23), channel_id=1, source_target_pairs={{1,16},{2,17},{3,18},{4,19},{5,20},{6,21},{7,22},{8,23},{9,24},{10... | collective-permute-start | bytes 24584 | tf_op jit(solution)/shard_map/ppermute | solution.py:132
  50.5 17.8 %collective-permute-start.3 = (f32[128,4,4]{2,1,0:T(4,128)}, f32[128,4,4]{2,1,0:T(4,128)S(1)}, u32[]{:S(2)}, u32[]{:S(2)}) collective-permute-start(f32[128,4,4]{2,1,0:T(4,128)} %get-tuple-element.22), channel_id=1, source_target_pairs={{17,0},{18,1},{19,2},{20,3},{21,4},{22,5},{23,6},{24,7},{25,8},{26... | collective-permute-start | bytes 24584 | tf_op jit(solution)/shard_map/ppermute | solution.py:131
  134.7 4.4 %collective-permute-start.8 = (bf16[32,4,128]{2,1,0:T(4,128)(2,1)S(1)}, bf16[32,4,128]{2,1,0:T(4,128)(2,1)S(1)}, u32[]{:S(2)}, u32[]{:S(2)}) collective-permute-start(bf16[32,4,128]{2,1,0:T(4,128)(2,1)S(1)} %broadcast_multiply_fusion), channel_id=1, source_target_pairs={{0,112},{16,0},{32,16},{48,32},{64,48},{80,64},{96,80},{112,96},{1... | collective-permute-start | bytes 98312 | tf_op jit(solution)/shard_map/ppermute | solution.py:29
  135.8 7.2 %copy-start.2 = (f32[16,256]{1,0:T(8,128)S(1)}, f32[16,256]{1,0:T(8,128)}, u32[]{:S(2)}) copy-start(f32[16,256]{1,0:T(8,128)} %param.15) | copy-start | bytes 49156
  135.8 7.2 %copy-start.3 = (s32[16,256]{1,0:T(8,128)S(1)}, s32[16,256]{1,0:T(8,128)}, u32[]{:S(2)}) copy-start(s32[16,256]{1,0:T(8,128)} %param.14) | copy-start | bytes 49156
  143.0 5.5 %collective-permute-start.9 = (f32[1,2,16,256]{3,2,1,0:T(8,128)S(1)}, f32[1,2,16,256]{3,2,1,0:T(8,128)S(1)}, u32[]{:S(2)}, u32[]{:S(2)}) collective-permute-start(f32[1,2,16,256]{3,2,1,0:T(8,128)S(1)} %maximum_bitcast_fusion), channel_id=1, source_target_pairs={{0,2},{1,3},{2,0},{3,1},{4,6},{5,7},{6,4},{7,5},{8,10},{9,11},{10,... | collective-permute-start | bytes 98312 | tf_op jit(solution)/shard_map/ppermute | solution.py:61
  148.5 6.0 %collective-permute-start.10 = (f32[2,2,16,256]{3,2,1,0:T(8,128)S(1)}, f32[2,2,16,256]{3,2,1,0:T(8,128)S(1)}, u32[]{:S(2)}, u32[]{:S(2)}) collective-permute-start(f32[2,2,16,256]{3,2,1,0:T(8,128)S(1)} %pad_maximum_fusion.3), channel_id=1, source_target_pairs={{0,8},{1,9},{2,10},{3,11},{4,12},{5,13},{6,14},{7,15},{8,0},{9,1},... | collective-permute-start | bytes 196616 | tf_op jit(solution)/shard_map/ppermute | solution.py:61
  154.5 7.3 %collective-permute-start.11 = (f32[4,2,16,256]{3,2,1,0:T(8,128)S(1)}, f32[4,2,16,256]{3,2,1,0:T(8,128)S(1)}, u32[]{:S(2)}, u32[]{:S(2)}) collective-permute-start(f32[4,2,16,256]{3,2,1,0:T(8,128)S(1)} %pad_maximum_fusion.2), channel_id=1, source_target_pairs={{0,64},{16,80},{32,96},{48,112},{64,0},{80,16},{96,32},{112,48},{1... | collective-permute-start | bytes 393224 | tf_op jit(solution)/shard_map/ppermute | solution.py:61
  161.8 7.3 %collective-permute-start.12 = (f32[8,2,16,256]{3,2,1,0:T(8,128)S(1)}, f32[8,2,16,256]{3,2,1,0:T(8,128)S(1)}, u32[]{:S(2)}, u32[]{:S(2)}) collective-permute-start(f32[8,2,16,256]{3,2,1,0:T(8,128)S(1)} %pad_maximum_fusion.1), channel_id=1, source_target_pairs={{0,1},{1,0},{2,3},{3,2},{4,5},{5,4},{6,7},{7,6},{8,9},{9,8},{10,11... | collective-permute-start | bytes 786440 | tf_op jit(solution)/shard_map/ppermute | solution.py:61
  170.0 11.9 %collective-permute-start.13 = (f32[16,2,16,256]{3,2,1,0:T(8,128)S(1)}, f32[16,2,16,256]{3,2,1,0:T(8,128)S(1)}, u32[]{:S(2)}, u32[]{:S(2)}) collective-permute-start(f32[16,2,16,256]{3,2,1,0:T(8,128)S(1)} %get-tuple-element.36), channel_id=1, source_target_pairs={{0,4},{1,5},{2,6},{3,7},{4,0},{5,1},{6,2},{7,3},{8,12},{9,13},{10,... | collective-permute-start | bytes 1572872 | tf_op jit(solution)/shard_map/ppermute | solution.py:61
  183.0 22.5 %collective-permute-start.14 = (f32[32,2,16,256]{3,2,1,0:T(8,128)S(1)}, f32[32,2,16,256]{3,2,1,0:T(8,128)S(1)}, u32[]{:S(2)}, u32[]{:S(2)}) collective-permute-start(f32[32,2,16,256]{3,2,1,0:T(8,128)S(1)} %get-tuple-element.32), channel_id=1, source_target_pairs={{0,32},{16,48},{32,0},{48,16},{64,96},{80,112},{96,64},{112,80},{1... | collective-permute-start | bytes 3145736 | tf_op jit(solution)/shard_map/ppermute | solution.py:61
  207.1 4.4 %collective-permute-start.15 = (f32[64,2,16,256]{3,2,1,0:T(8,128)}, f32[64,2,16,256]{3,2,1,0:T(8,128)S(1)}, u32[]{:S(2)}, u32[]{:S(2)}) collective-permute-start(f32[64,2,16,256]{3,2,1,0:T(8,128)} %get-tuple-element.28), channel_id=1, source_target_pairs={{0,16},{16,0},{32,48},{48,32},{64,80},{80,64},{96,112},{112,96},{1... | collective-permute-start | bytes 6291464 | tf_op jit(solution)/shard_map/ppermute | solution.py:61

commit v7 on v5

--- a/solution.py
+++ b/solution.py
@@ -73,37 +73,66 @@
 LEVEL_BLOCK = 8
 
 
-def diffusion_kernel(kappa_ref, weight_ref, core_ref, lanes_ref, rows_ref, mask_ref, out_ref, flux_ref):
+def diffusion_kernel(kappa_ref, weight_ref, core_ref, lanes_ref, rows_ref, mask_ref, out_ref, flux_ref, buf_a, buf_b):
     block = pl.program_id(0)
-    levels, rows, cols = core_ref.shape
+    height, levels, width = buf_a.shape
+    rows = height - 2 * HALO
+    cols = flux_ref.shape[2]
 
     @pl.when(block == 0)
     def _():
         flux_ref[...] = jnp.zeros_like(flux_ref)
 
-    mask = mask_ref[...]
-
-    def level(l, carry):
-        lev = block * levels + l
-        kappa = kappa_ref[lev]
-        top = jnp.concatenate([core_ref[l], lanes_ref[l]], axis=1)
-        f = jnp.concatenate([top, rows_ref[l]], axis=0)
-        height, width = f.shape
-        for step in range(STEPS):
-            beside = (
-                pltpu.roll(f, height - 1, 0)
-                + pltpu.roll(f, 1, 0)
-                + pltpu.roll(f, width - 1, 1)
-                + pltpu.roll(f, 1, 1)
-            )
-            f = (f + kappa * (beside - 4.0 * f)) * mask
-        core = f[:rows, :cols]
-        out_ref[l] = core
-        for c in range(flux_ref.shape[0]):
-            flux_ref[c] += weight_ref[c, lev] * core
+    kappa = kappa_ref[...]
+    weight = weight_ref[0]
+
+    chunks = cols // 128
+    wide = width // 128
+
+    def load_core(q, carry):
+        r = q - HALO
+        pieces = [core_ref[pl.ds(r * chunks + k, levels, stride=rows * chunks), :] for k in range(chunks)]
+        pieces.append(lanes_ref[pl.ds(r, levels, stride=rows), :])
+        buf_a[q] = jnp.concatenate(pieces, axis=1)
         return carry
 
-    lax.fori_loop(0, levels, level, 0, unroll=2)
+    lax.fori_loop(HALO, HALO + rows, load_core, 0)
+    for h in range(2 * HALO):
+        q = rows + HALO + h if h < HALO else h - HALO
+        buf_a[q] = jnp.concatenate(
+            [rows_ref[pl.ds(h * wide + k, levels, stride=2 * HALO * wide), :] for k in range(wide)], axis=1
+        )
+
+    def advance(src, q):
+        cur = src[q]
+        beside = (
+            src[q + 1]
+            + src[q - 1]
+            + pltpu.roll(cur, width - 1, 1)
+            + pltpu.roll(cur, 1, 1)
+        )
+        return (cur + kappa * (beside - 4.0 * cur)) * mask_ref[q]
+
+    for step in range(1, STEPS):
+        src, dst = (buf_a, buf_b) if step % 2 == 1 else (buf_b, buf_a)
+
+        def one(q, carry, src=src, dst=dst):
+            dst[q] = advance(src, q)
+            return carry
+
+        lax.fori_loop(step, height - step, one, 0, unroll=2)
+
+    last = buf_b if STEPS % 2 == 0 else buf_a
+
+    def final(q, carry):
+        f = advance(last, q)[:, :cols]
+        r = q - HALO
+        for k in range(chunks):
+            out_ref[pl.ds(r * chunks + k, levels, stride=rows * chunks), :] = f[:, k * 128 : (k + 1) * 128]
+        flux_ref[r] += jnp.dot(weight, f, precision=lax.Precision.HIGHEST, preferred_element_type=jnp.float32)
+        return carry
+
+    lax.fori_loop(HALO, HALO + rows, final, 0, unroll=2)
 
 
 def diffuse(field, atm_kappa, vert_weight):
@@ -146,39 +175,51 @@
     width = cols + 128
     r = jnp.arange(height, dtype=jnp.int32)
     c = jnp.arange(width, dtype=jnp.int32)
-    global_r = gy_index * rows + jnp.where(r < rows + HALO, r, r - height)
+    global_r = gy_index * rows + r - HALO
     global_c = gx_index * cols + jnp.where(c < cols + HALO, c, c - width)
     inside_r = (global_r >= 0) & (global_r < count_gy * rows)
     inside_c = (global_c >= 0) & (global_c < count_gx * cols) & ((c < cols + HALO) | (c >= width - HALO))
     mask = (inside_r[:, None] & inside_c[None, :]).astype(jnp.float32)
+    mask = jnp.broadcast_to(mask[:, None, :], (height, LEVEL_BLOCK, width))
     blocks = levels // LEVEL_BLOCK
-    smem = pl.BlockSpec(memory_space=pltpu.SMEM)
+    kappa = jnp.broadcast_to(atm_kappa[:, None], (levels, width))
+    weight = vert_weight.reshape(comps, blocks, LEVEL_BLOCK).transpose(1, 0, 2)
     out, flux = pl.pallas_call(
         diffusion_kernel,
         grid=(blocks,),
         in_specs=[
-            smem,
-            smem,
-            pl.BlockSpec((LEVEL_BLOCK, rows, cols), lambda b: (b, 0, 0)),
-            pl.BlockSpec((LEVEL_BLOCK, rows, 128), lambda b: (b, 0, 0)),
-            pl.BlockSpec((LEVEL_BLOCK, 2 * HALO, width), lambda b: (b, 0, 0)),
-            pl.BlockSpec((height, width), lambda b: (0, 0)),
+            pl.BlockSpec((LEVEL_BLOCK, width), lambda b: (b, 0)),
+            pl.BlockSpec((1, comps, LEVEL_BLOCK), lambda b: (b, 0, 0)),
+            pl.BlockSpec((LEVEL_BLOCK * rows * cols // 128, 128), lambda b: (b, 0)),
+            pl.BlockSpec((LEVEL_BLOCK * rows, 128), lambda b: (b, 0)),
+            pl.BlockSpec((LEVEL_BLOCK * 2 * HALO * width // 128, 128), lambda b: (b, 0)),
+            pl.BlockSpec((height, LEVEL_BLOCK, width), lambda b: (0, 0, 0)),
         ],
         out_specs=[
-            pl.BlockSpec((LEVEL_BLOCK, rows, cols), lambda b: (b, 0, 0)),
-            pl.BlockSpec((comps, rows, cols), lambda b: (0, 0, 0)),
+            pl.BlockSpec((LEVEL_BLOCK * rows * cols // 128, 128), lambda b: (b, 0)),
+            pl.BlockSpec((rows, comps, cols), lambda b: (0, 0, 0)),
         ],
         out_shape=[
-            jax.ShapeDtypeStruct(field.shape, field.dtype),
-            jax.ShapeDtypeStruct((comps, rows, cols), jnp.float32),
+            jax.ShapeDtypeStruct((levels * rows * cols // 128, 128), field.dtype),
+            jax.ShapeDtypeStruct((rows, comps, cols), jnp.float32),
         ],
+        scratch_shapes=[pltpu.VMEM((height, LEVEL_BLOCK, width), jnp.float32)] * 2,
         compiler_params=pltpu.CompilerParams(dimension_semantics=("arbitrary",)),
         cost_estimate=pl.CostEstimate(
             flops=levels * height * width * STEPS * 10,
             transcendentals=0,
             bytes_accessed=2 * field.size * 4,
         ),
-    )(atm_kappa, vert_weight, field, lanes, halo_rows, mask)
+    )(
+        kappa,
+        weight,
+        field.reshape(levels * rows * cols // 128, 128),
+        lanes.reshape(levels * rows, 128),
+        halo_rows.reshape(levels * 2 * HALO * width // 128, 128),
+        mask,
+    )
+    out = out.reshape(levels, rows, cols)
+    flux = flux.transpose(1, 0, 2)
     return out, flux
 
 

time: 224 us -> 345 us (1.54)
  Pallas kernels: 80.5 us -> 182 us
  local copies, waits for them, and re-layouts: 40.5 us -> 68.1 us
  other arithmetic: 13.1 us -> 9.6 us
    pallas_call x1, Pallas kernels: 60.6 us -> 162 us  [diffuse(): pl.pallas_call(diffusion_kernel, grid=(blocks,), in_specs=[pl.BlockSpec((...]
    reshape x0 -> x5, local copies, waits for them, and re-layouts: none -> 20.7 us  [the longest x1 9.32 us: diffuse(): out = out.reshape(levels, rows, cols)]
    ppermute x14, waiting for transfers between devices: 24.2 us -> 29.4 us  [stack_gather(): other = lax.ppermute(x, axis, [(j, j ^ distance) for j in range(size)])]
    unnamed x27 -> x41, local copies, waits for them, and re-layouts: 13.8 us -> 18.4 us
    ppermute x1, waiting for transfers between devices: 3.96 us -> 0.01 us  [diffuse(): south_west = lax.ppermute(field[:, :HALO, cols - HALO:], both, pairs(-1, 1))]
    ppermute x14, starting transfers between devices: 20.9 us -> 17.2 us  [stack_gather(): other = lax.ppermute(x, axis, [(j, j ^ distance) for j in range(size)])]
  transfers between devices with their start and end apart: 23 -> 23, of which waited for: 13 -> 11; matrix products, arithmetic and copies ran while one was open for 16% -> 17% of each run, Pallas kernels for 0% -> 0%
where the time goes in v7:
time: 345 us; the launch traced here: 342 us
  Pallas kernels  182 us (53%)
  local copies, waits for them, and re-layouts  68.1 us (20%)
  starting transfers between devices  40.3 us (12%)
  waiting for transfers between devices  38 us (11%)
  other arithmetic  9.6 us (3%)
    pallas_call x1, Pallas kernels, diffuse(): pl.pallas_call(diffusion_kernel, grid=(blocks,), in_specs=[pl.BlockSpec((...  162 us
    ppermute x14, waiting for transfers between devices, stack_gather(): other = lax.ppermute(x, axis, [(j, j ^ distance) for j in range(size)])  29.4 us
    pallas_call x1, Pallas kernels, solve_grid(): pl.pallas_call(functools.partial(cg_kernel, rounds), in_specs=[pl.BlockSp...  19.9 us
    unnamed x41, local copies, waits for them, and re-layouts  18.4 us
    ppermute x14, starting transfers between devices, stack_gather(): other = lax.ppermute(x, axis, [(j, j ^ distance) for j in range(size)])  17.2 us
    reshape x1, local copies, waits for them, and re-layouts, diffuse(): out = out.reshape(levels, rows, cols)  9.32 us
    reshape x1, local copies, waits for them, and re-layouts, diffuse(): field.reshape(levels * rows * cols // 128, 128)  9 us
  transfers between devices with their start and end apart: 23, of which 11 were waited for; matrix products, arithmetic and copies ran while one was open for 17% of the time, Pallas kernels for 0%

profile of v7, /device:TPU:6, one launch (start us, length us, event | category | flops | bytes accessed | tf_op | source)
XLA Modules:
  0.0 342.4 jit_solution(14623082509067113258)
XLA Ops:
  0.6 4.3 %fusion.25 = (f32[128,32,4]{2,1,0:T(8,128)S(1)}, f32[128,32,4]{2,1,0:T(8,128)}) fusion(f32[128,32,512]{2,1,0:T(8,128)} %param.8), kind=kLoop, calls=%fused_computation.124 | loop fusion | bytes 262144 | tf_op jit(solution)/shard_map/slice | solution.py:158
  4.9 3.3 copy.106
  8.2 2.3 collective-permute-start.1
  10.5 1.9 copy.105
  12.5 1.3 collective-permute-start
  13.8 2.7 fusion.24
  16.4 0.7 copy.112
  17.2 5.9 %collective-permute-start.7 = (f32[128,4,4]{2,0,1:T(8,128)}, f32[128,4,4]{2,0,1:T(8,128)}, u32[]{:S(2)}, u32[]{:S(2)}) collective-permute-start(f32[128,4,4]{2,0,1:T(8,128)} %copy.112), channel_id=1, source_target_pairs={{0,17},{1,18},{2,19},{3,20},{4,21},{5,22},{6,23},{7,24},{8,25},{9,... | collective-permute-start | bytes 24584 | tf_op jit(solution)/shard_map/ppermute | solution.py:163
  23.1 2.7 fusion.23
  26.2 3.4 collective-permute-start.5
  29.6 1.3 copy.107
  30.9 2.4 collective-permute-start.2
  33.4 0.6 copy.90
  34.1 1.7 reshape.277
  38.0 9.0 %reshape.273.core_ref = f32[16384,128]{1,0:T(8,128)} reshape(f32[128,32,512]{2,1,0:T(8,128)} %param.8) | data formatting | bytes 16777216 | tf_op jit(solution)/shard_map/reshape | solution.py:216
  47.7 0.7 copy.111
  48.4 0.7 copy.109
  49.1 0.7 copy.108
  49.9 1.3 collective-permute-start.6
  51.2 2.7 copy.81
  54.0 5.0 %collective-permute-start.4 = (f32[128,4,4]{2,0,1:T(8,128)}, f32[128,4,4]{2,0,1:T(8,128)}, u32[]{:S(2)}, u32[]{:S(2)}) collective-permute-start(f32[128,4,4]{2,0,1:T(8,128)} %copy.109), channel_id=1, source_target_pairs={{1,16},{2,17},{3,18},{4,19},{5,20},{6,21},{7,22},{8,23},{9,24},{10... | collective-permute-start | bytes 24584 | tf_op jit(solution)/shard_map/ppermute | solution.py:161
  58.9 3.7 %copy.80 = f32[128,32,4]{2,1,0:T(8,128)} copy(f32[128,32,4]{0,1,2:T(8,128)} %collective-permute-done) | data formatting | bytes 131072 | tf_op jit(solution)/shard_map/ppermute | solution.py:158
  62.6 1.5 collective-permute-start.3
  64.1 3.6 %pad_maximum_fusion = f32[128,32,128]{2,1,0:T(8,128)} fusion(f32[128,32,4]{2,1,0:T(8,128)S(1)} %copy.81, f32[128,32,4]{2,1,0:T(8,128)} %copy.80, f32[128]{0:T(128)S(1)} %pad.29.clone), kind=kLoop, calls=%fused_computation.4 | loop fusion | flops 1048576 | bytes 2228736 | tf_op jit(solution)/shard_map/concatenate | solution.py:165
  67.7 6.9 %collective-permute-done.3 = f32[128,4,4]{2,0,1:T(8,128)S(1)} collective-permute-done((f32[128,4,4]{2,0,1:T(8,128)}, f32[128,4,4]{2,0,1:T(8,128)S(1)}, u32[]{:S(2)}, u32[]{:S(2)}) %collective-permute-start.3) | collective-permute-done | bytes 8224 | tf_op jit(solution)/shard_map/ppermute | solution.py:160
  74.7 2.2 maximum_maximum_fusion
  76.8 1.5 copy.88
  78.4 1.7 reshape.275.rows_ref
  80.1 0.8 broadcast_in_dim.63.kappa_ref
  80.9 0.9 broadcast_in_dim.66.mask_ref
  81.8 162.3 %shard_map.111 = (f32[16384,128]{1,0:T(8,128)}, f32[32,4,512]{2,1,0:T(4,128)}) custom-call(f32[128,640]{1,0:T(8,128)} %broadcast_in_dim.63.kappa_ref, f32[16,4,8]{2,1,0:T(4,128)} %bitcast.44, f32[16384,128]{1,0:T(8,128)} %reshape.273.core_ref, f32[4096,128]{1,0:T(8,128)} %bitcast.40, f32[5120,128]{1,0:T(8,128)} %reshape.275.rows_ref, ...), custom_call_target="tpu_custom_call" | custom-call | flops 131072000 | bytes 16777216 | tf_op jit(solution)/shard_map/pallas_call | solution.py:187
  244.1 1.0 convert_element_type.47
  246.1 0.7 gather_fusion
  246.8 1.7 collective-permute-done.8
  248.6 0.7 gather_fusion.2
  249.3 3.0 convolution_bitcast_fusion
  253.1 3.5 %collective-permute-start.16 = (f32[1,16,256]{2,1,0:T(8,128)S(1)}, f32[1,16,256]{2,1,0:T(8,128)S(1)}, u32[]{:S(2)}, u32[]{:S(2)}) collective-permute-start(f32[1,16,256]{2,1,0:T(8,128)S(1)} %get-tuple-element.15), channel_id=1, source_target_pairs={{0,2},{1,3},{2,0},{3,1},{4,6},{5,7},{6,4},{7,5},{8,10},{9,11},{10,... | collective-permute-start | bytes 49160 | tf_op jit(solution)/shard_map/ppermute | solution.py:61
  256.6 1.7 collective-permute-done.9
  258.3 2.9 collective-permute-start.10
  263.1 0.7 collective-permute-done.10
  263.8 4.4 %collective-permute-start.11 = (f32[4,16,256]{2,1,0:T(8,128)S(1)}, f32[4,16,256]{2,1,0:T(8,128)S(1)}, u32[]{:S(2)}, u32[]{:S(2)}) collective-permute-start(f32[4,16,256]{2,1,0:T(8,128)S(1)} %pad_maximum_fusion.3), channel_id=1, source_target_pairs={{0,64},{16,80},{32,96},{48,112},{64,0},{80,16},{96,32},{112,48},{1... | collective-permute-start | bytes 196616 | tf_op jit(solution)/shard_map/ppermute | solution.py:61
  268.1 2.7 collective-permute-start.18
  272.1 1.9 collective-permute-done.18
  274.0 1.0 collective-permute-start.19
  275.0 0.6 constant_dynamic-update-slice_fusion.14
  275.7 2.8 collective-permute-done.12
  278.5 0.7 constant_dynamic-update-slice_fusion.13
  279.2 0.6 constant_dynamic-update-slice_fusion.40
  279.9 0.7 constant_dynamic-update-slice_fusion.39
  280.6 2.0 collective-permute-start.20
  282.5 4.9 %collective-permute-done.13 = f32[16,16,256]{2,1,0:T(8,128)S(1)} collective-permute-done((f32[16,16,256]{2,1,0:T(8,128)S(1)}, f32[16,16,256]{2,1,0:T(8,128)S(1)}, u32[]{:S(2)}, u32[]{:S(2)}) %collective-permute-start.13) | collective-permute-done | bytes 262176 | tf_op jit(solution)/shard_map/ppermute | solution.py:61
  287.5 0.8 constant_dynamic-update-slice_fusion.12
  288.3 2.0 collective-permute-done.20
  290.3 0.8 constant_dynamic-update-slice_fusion.38
  291.1 10.6 %collective-permute-done.14 = f32[32,16,256]{2,1,0:T(8,128)S(1)} collective-permute-done((f32[32,16,256]{2,1,0:T(8,128)S(1)}, f32[32,16,256]{2,1,0:T(8,128)S(1)}, u32[]{:S(2)}, u32[]{:S(2)}) %collective-permute-start.14) | collective-permute-done | bytes 524320 | tf_op jit(solution)/shard_map/ppermute | solution.py:61
  301.7 0.9 constant_dynamic-update-slice_fusion.11
  302.6 4.7 %collective-permute-done.21 = f32[32,16,256]{2,1,0:T(8,128)S(1)} collective-permute-done((f32[32,16,256]{2,1,0:T(8,128)S(1)}, f32[32,16,256]{2,1,0:T(8,128)S(1)}, u32[]{:S(2)}, u32[]{:S(2)}) %collective-permute-start.21) | collective-permute-done | bytes 524320 | tf_op jit(solution)/shard_map/ppermute | solution.py:61
  307.3 0.9 constant_dynamic-update-slice_fusion.37
  308.8 9.3 %reshape.276 = f32[128,32,512]{2,1,0:T(8,128)} reshape(f32[16384,128]{1,0:T(8,128)} %get-tuple-element.8) | data formatting | bytes 16777216 | tf_op jit(solution)/shard_map/reshape | solution.py:221
  318.1 0.6 reshape.279
  318.8 1.1 constant_dynamic-update-slice_fusion.18.rhs_stack
  319.8 1.3 constant_dynamic-update-slice_fusion.44.coded_stack
  321.1 1.3 copy-done
  322.5 19.9 %shard_map.112 = (f32[16,256]{1,0:T(8,128)}, f32[16,256]{1,0:T(8,128)}) custom-call(s32[2]{0:T(128)} %pad_add_fusion.index_ref, f32[128,16,256]{2,1,0:T(8,128)} %constant_dynamic-update-slice_fusion.18.rhs_stack, f32[128,16,256]{2,1,0:T(8,128)} %copy-done), custom_call_target="tpu_custom_call" | custom-call | tf_op jit(solution)/shard_map/pallas_call | solution.py:327
  (94 shorter events, 8.8 us)
Async XLA Ops:
  8.2 41.8 %collective-permute-start.1 = (f32[128,32,4]{0,1,2:T(8,128)}, f32[128,32,4]{0,1,2:T(8,128)}, u32[]{:S(2)}, u32[]{:S(2)}) collective-permute-start(f32[128,32,4]{0,1,2:T(8,128)} %copy.106), channel_id=1, source_target_pairs={{0,16},{16,32},{32,48},{48,64},{64,80},{80,96},{96,112},{1,17},{17... | collective-permute-start | bytes 196616 | tf_op jit(solution)/shard_map/ppermute | solution.py:159
  12.5 41.5 %collective-permute-start = (f32[128,32,4]{0,1,2:T(8,128)}, f32[128,32,4]{0,1,2:T(8,128)}, u32[]{:S(2)}, u32[]{:S(2)}) collective-permute-start(f32[128,32,4]{0,1,2:T(8,128)} %copy.105), channel_id=1, source_target_pairs={{16,0},{32,16},{48,32},{64,48},{80,64},{96,80},{112,96},{17,1},{33... | collective-permute-start | bytes 196616 | tf_op jit(solution)/shard_map/ppermute | solution.py:158
  17.2 45.5 %collective-permute-start.7 = (f32[128,4,4]{2,0,1:T(8,128)}, f32[128,4,4]{2,0,1:T(8,128)}, u32[]{:S(2)}, u32[]{:S(2)}) collective-permute-start(f32[128,4,4]{2,0,1:T(8,128)} %copy.112), channel_id=1, source_target_pairs={{0,17},{1,18},{2,19},{3,20},{4,21},{5,22},{6,23},{7,24},{8,25},{9,... | collective-permute-start | bytes 24584 | tf_op jit(solution)/shard_map/ppermute | solution.py:163
  25.8 7.6 %copy-start.4 = (s32[4096,4]{0,1:T(4,128)S(1)}, s32[4096,4]{0,1:T(4,128)}, u32[]{:S(2)}) copy-start(s32[4096,4]{0,1:T(4,128)} %param.11) | copy-start | bytes 196612
  26.2 48.4 %collective-permute-start.5 = (f32[128,4,512]{2,0,1:T(8,128)S(1)}, f32[128,4,512]{2,0,1:T(8,128)}, u32[]{:S(2)}, u32[]{:S(2)}) collective-permute-start(f32[128,4,512]{2,0,1:T(8,128)S(1)} %copy.110), channel_id=1, source_target_pairs={{0,1},{1,2},{2,3},{3,4},{4,5},{5,6},{6,7},{7,8},{8,9},{9,10},{10,1... | collective-permute-start | bytes 3145736 | tf_op jit(solution)/shard_map/ppermute | solution.py:157
  30.9 43.7 %collective-permute-start.2 = (f32[128,4,512]{2,0,1:T(8,128)}, f32[128,4,512]{2,0,1:T(8,128)}, u32[]{:S(2)}, u32[]{:S(2)}) collective-permute-start(f32[128,4,512]{2,0,1:T(8,128)} %copy.107), channel_id=1, source_target_pairs={{1,0},{2,1},{3,2},{4,3},{5,4},{6,5},{7,6},{8,7},{9,8},{10,9},{11,1... | collective-permute-start | bytes 3145736 | tf_op jit(solution)/shard_map/ppermute | solution.py:156
  33.4 2.5 copy-start.5
  37.9 9.0 %copy-start.8 = (f32[4,128]{1,0:T(4,128)S(1)}, f32[4,128]{1,0:T(4,128)}, u32[]{:S(2)}) copy-start(f32[4,128]{1,0:T(4,128)} %param.10) | copy-start | bytes 6148
  37.9 9.7 %copy-start.3 = (f32[128,4,4]{2,1,0:T(4,128)S(1)}, f32[128,4,4]{2,1,0:T(4,128)}, u32[]{:S(2)}) copy-start(f32[128,4,4]{2,1,0:T(4,128)} %get-tuple-element.28) | copy-start | bytes 24580
  38.0 10.4 %copy-start.2 = (f32[128,4,4]{2,1,0:T(4,128)S(1)}, f32[128,4,4]{2,1,0:T(4,128)}, u32[]{:S(2)}) copy-start(f32[128,4,4]{2,1,0:T(4,128)} %get-tuple-element.27) | copy-start | bytes 24580
  49.9 17.8 %collective-permute-start.6 = (f32[128,4,4]{2,0,1:T(8,128)}, f32[128,4,4]{2,0,1:T(8,128)S(1)}, u32[]{:S(2)}, u32[]{:S(2)}) collective-permute-start(f32[128,4,4]{2,0,1:T(8,128)} %copy.111), channel_id=1, source_target_pairs={{16,1},{17,2},{18,3},{19,4},{20,5},{21,6},{22,7},{23,8},{24,9},{25... | collective-permute-start | bytes 24584 | tf_op jit(solution)/shard_map/ppermute | solution.py:162
  54.0 13.8 %collective-permute-start.4 = (f32[128,4,4]{2,0,1:T(8,128)}, f32[128,4,4]{2,0,1:T(8,128)}, u32[]{:S(2)}, u32[]{:S(2)}) collective-permute-start(f32[128,4,4]{2,0,1:T(8,128)} %copy.109), channel_id=1, source_target_pairs={{1,16},{2,17},{3,18},{4,19},{5,20},{6,21},{7,22},{8,23},{9,24},{10... | collective-permute-start | bytes 24584 | tf_op jit(solution)/shard_map/ppermute | solution.py:161
  62.6 12.0 %collective-permute-start.3 = (f32[128,4,4]{2,0,1:T(8,128)}, f32[128,4,4]{2,0,1:T(8,128)S(1)}, u32[]{:S(2)}, u32[]{:S(2)}) collective-permute-start(f32[128,4,4]{2,0,1:T(8,128)} %copy.108), channel_id=1, source_target_pairs={{17,0},{18,1},{19,2},{20,3},{21,4},{22,5},{23,6},{24,7},{25,8},{26... | collective-permute-start | bytes 24584 | tf_op jit(solution)/shard_map/ppermute | solution.py:160
  78.4 1.7 copy-start.9
  245.8 2.8 collective-permute-start.8
  249.3 3.1 copy-start.6
  249.3 3.1 copy-start.7
  253.1 5.2 %collective-permute-start.9 = (f32[1,16,256]{2,1,0:T(8,128)S(1)}, f32[1,16,256]{2,1,0:T(8,128)S(1)}, u32[]{:S(2)}, u32[]{:S(2)}) collective-permute-start(f32[1,16,256]{2,1,0:T(8,128)S(1)} %get-tuple-element.80), channel_id=1, source_target_pairs={{0,2},{1,3},{2,0},{3,1},{4,6},{5,7},{6,4},{7,5},{8,10},{9,11},{10,... | collective-permute-start | bytes 49160 | tf_op jit(solution)/shard_map/ppermute | solution.py:61
  253.1 8.1 %collective-permute-start.16 = (f32[1,16,256]{2,1,0:T(8,128)S(1)}, f32[1,16,256]{2,1,0:T(8,128)S(1)}, u32[]{:S(2)}, u32[]{:S(2)}) collective-permute-start(f32[1,16,256]{2,1,0:T(8,128)S(1)} %get-tuple-element.15), channel_id=1, source_target_pairs={{0,2},{1,3},{2,0},{3,1},{4,6},{5,7},{6,4},{7,5},{8,10},{9,11},{10,... | collective-permute-start | bytes 49160 | tf_op jit(solution)/shard_map/ppermute | solution.py:61
  258.3 5.4 %collective-permute-start.10 = (f32[2,16,256]{2,1,0:T(8,128)S(1)}, f32[2,16,256]{2,1,0:T(8,128)S(1)}, u32[]{:S(2)}, u32[]{:S(2)}) collective-permute-start(f32[2,16,256]{2,1,0:T(8,128)S(1)} %pad_maximum_fusion.5), channel_id=1, source_target_pairs={{0,8},{1,9},{2,10},{3,11},{4,12},{5,13},{6,14},{7,15},{8,0},{9,1},... | collective-permute-start | bytes 98312 | tf_op jit(solution)/shard_map/ppermute | solution.py:61
  261.2 6.9 %collective-permute-start.17 = (f32[2,16,256]{2,1,0:T(8,128)S(1)}, f32[2,16,256]{2,1,0:T(8,128)S(1)}, u32[]{:S(2)}, u32[]{:S(2)}) collective-permute-start(f32[2,16,256]{2,1,0:T(8,128)S(1)} %pad_maximum_fusion.6), channel_id=1, source_target_pairs={{0,8},{1,9},{2,10},{3,11},{4,12},{5,13},{6,14},{7,15},{8,0},{9,1},... | collective-permute-start | bytes 98312 | tf_op jit(solution)/shard_map/ppermute | solution.py:61
  263.8 8.3 %collective-permute-start.11 = (f32[4,16,256]{2,1,0:T(8,128)S(1)}, f32[4,16,256]{2,1,0:T(8,128)S(1)}, u32[]{:S(2)}, u32[]{:S(2)}) collective-permute-start(f32[4,16,256]{2,1,0:T(8,128)S(1)} %pad_maximum_fusion.3), channel_id=1, source_target_pairs={{0,64},{16,80},{32,96},{48,112},{64,0},{80,16},{96,32},{112,48},{1... | collective-permute-start | bytes 196616 | tf_op jit(solution)/shard_map/ppermute | solution.py:61
  268.1 5.8 %collective-permute-start.18 = (f32[4,16,256]{2,1,0:T(8,128)S(1)}, f32[4,16,256]{2,1,0:T(8,128)S(1)}, u32[]{:S(2)}, u32[]{:S(2)}) collective-permute-start(f32[4,16,256]{2,1,0:T(8,128)S(1)} %pad_maximum_fusion.4), channel_id=1, source_target_pairs={{0,64},{16,80},{32,96},{48,112},{64,0},{80,16},{96,32},{112,48},{1... | collective-permute-start | bytes 196616 | tf_op jit(solution)/shard_map/ppermute | solution.py:61
  272.0 6.5 %collective-permute-start.12 = (f32[8,16,256]{2,1,0:T(8,128)S(1)}, f32[8,16,256]{2,1,0:T(8,128)S(1)}, u32[]{:S(2)}, u32[]{:S(2)}) collective-permute-start(f32[8,16,256]{2,1,0:T(8,128)S(1)} %pad_maximum_fusion.1), channel_id=1, source_target_pairs={{0,1},{1,0},{2,3},{3,2},{4,5},{5,4},{6,7},{7,6},{8,9},{9,8},{10,11... | collective-permute-start | bytes 393224 | tf_op jit(solution)/shard_map/ppermute | solution.py:61
  274.0 5.9 %collective-permute-start.19 = (f32[8,16,256]{2,1,0:T(8,128)S(1)}, f32[8,16,256]{2,1,0:T(8,128)S(1)}, u32[]{:S(2)}, u32[]{:S(2)}) collective-permute-start(f32[8,16,256]{2,1,0:T(8,128)S(1)} %pad_maximum_fusion.2), channel_id=1, source_target_pairs={{0,1},{1,0},{2,3},{3,2},{4,5},{5,4},{6,7},{7,6},{8,9},{9,8},{10,11... | collective-permute-start | bytes 393224 | tf_op jit(solution)/shard_map/ppermute | solution.py:61
  279.2 8.3 %collective-permute-start.13 = (f32[16,16,256]{2,1,0:T(8,128)S(1)}, f32[16,16,256]{2,1,0:T(8,128)S(1)}, u32[]{:S(2)}, u32[]{:S(2)}) collective-permute-start(f32[16,16,256]{2,1,0:T(8,128)S(1)} %get-tuple-element.49), channel_id=1, source_target_pairs={{0,4},{1,5},{2,6},{3,7},{4,0},{5,1},{6,2},{7,3},{8,12},{9,13},{10,... | collective-permute-start | bytes 786440 | tf_op jit(solution)/shard_map/ppermute | solution.py:61
  280.6 9.7 %collective-permute-start.20 = (f32[16,16,256]{2,1,0:T(8,128)S(1)}, f32[16,16,256]{2,1,0:T(8,128)S(1)}, u32[]{:S(2)}, u32[]{:S(2)}) collective-permute-start(f32[16,16,256]{2,1,0:T(8,128)S(1)} %get-tuple-element.45), channel_id=1, source_target_pairs={{0,4},{1,5},{2,6},{3,7},{4,0},{5,1},{6,2},{7,3},{8,12},{9,13},{10,... | collective-permute-start | bytes 786440 | tf_op jit(solution)/shard_map/ppermute | solution.py:61
  288.3 13.4 %collective-permute-start.14 = (f32[32,16,256]{2,1,0:T(8,128)S(1)}, f32[32,16,256]{2,1,0:T(8,128)S(1)}, u32[]{:S(2)}, u32[]{:S(2)}) collective-permute-start(f32[32,16,256]{2,1,0:T(8,128)S(1)} %get-tuple-element.41), channel_id=1, source_target_pairs={{0,32},{16,48},{32,0},{48,16},{64,96},{80,112},{96,64},{112,80},{1... | collective-permute-start | bytes 1572872 | tf_op jit(solution)/shard_map/ppermute | solution.py:61
  291.0 16.3 %collective-permute-start.21 = (f32[32,16,256]{2,1,0:T(8,128)S(1)}, f32[32,16,256]{2,1,0:T(8,128)S(1)}, u32[]{:S(2)}, u32[]{:S(2)}) collective-permute-start(f32[32,16,256]{2,1,0:T(8,128)S(1)} %get-tuple-element.38), channel_id=1, source_target_pairs={{0,32},{16,48},{32,0},{48,16},{64,96},{80,112},{96,64},{112,80},{1... | collective-permute-start | bytes 1572872 | tf_op jit(solution)/shard_map/ppermute | solution.py:61
  302.5 5.7 %copy-start.1 = (f32[128,16,256]{2,1,0:T(8,128)}, f32[128,16,256]{2,1,0:T(8,128)S(1)}, u32[]{:S(2)}) copy-start(f32[128,16,256]{2,1,0:T(8,128)S(1)} %get-tuple-element.35) | copy-start | bytes 6291460
  302.6 16.2 %collective-permute-start.15 = (f32[64,16,256]{2,1,0:T(8,128)}, f32[64,16,256]{2,1,0:T(8,128)S(1)}, u32[]{:S(2)}, u32[]{:S(2)}) collective-permute-start(f32[64,16,256]{2,1,0:T(8,128)} %get-tuple-element.34), channel_id=1, source_target_pairs={{0,16},{16,0},{32,48},{48,32},{64,80},{80,64},{96,112},{112,96},{1... | collective-permute-start | bytes 3145736 | tf_op jit(solution)/shard_map/ppermute | solution.py:61
  308.2 11.6 %collective-permute-start.22 = (f32[64,16,256]{2,1,0:T(8,128)}, f32[64,16,256]{2,1,0:T(8,128)}, u32[]{:S(2)}, u32[]{:S(2)}) collective-permute-start(f32[64,16,256]{2,1,0:T(8,128)} %get-tuple-element.32), channel_id=1, source_target_pairs={{0,16},{16,0},{32,48},{48,32},{64,80},{80,64},{96,112},{112,96},{1... | collective-permute-start | bytes 3145736 | tf_op jit(solution)/shard_map/ppermute | solution.py:61
  321.1 1.3 copy-start

commit v8 on v5

--- a/solution.py
+++ b/solution.py
@@ -70,7 +70,7 @@
 
 
 HALO = 4
-LEVEL_BLOCK = 8
+LEVEL_BLOCK = 16
 
 
 def diffusion_kernel(kappa_ref, weight_ref, core_ref, lanes_ref, rows_ref, mask_ref, out_ref, flux_ref):
@@ -82,6 +82,8 @@
         flux_ref[...] = jnp.zeros_like(flux_ref)
 
     mask = mask_ref[...]
+    mask_side = mask[:rows, cols:]
+    mask_low = mask[rows:, :]
 
     def level(l, carry):
         lev = block * levels + l
@@ -96,7 +98,9 @@
                 + pltpu.roll(f, width - 1, 1)
                 + pltpu.roll(f, 1, 1)
             )
-            f = (f + kappa * (beside - 4.0 * f)) * mask
+            f = f + kappa * (beside - 4.0 * f)
+            top = jnp.concatenate([f[:rows, :cols], f[:rows, cols:] * mask_side], axis=1)
+            f = jnp.concatenate([top, f[rows:, :] * mask_low], axis=0)
         core = f[:rows, :cols]
         out_ref[l] = core
         for c in range(flux_ref.shape[0]):

time: 224 us -> 222 us (level)
  no operation moved by 1% of the time
where the time goes in v8:
time: 222 us; the launch traced here: 220 us
  Pallas kernels  78.5 us (35%)
  starting transfers between devices  43.5 us (20%)
  local copies, waits for them, and re-layouts  40.5 us (18%)
  waiting for transfers between devices  40.3 us (18%)
  other arithmetic  13.1 us (6%)
  matrix products  3.04 us (1%)
    pallas_call x1, Pallas kernels, diffuse(): pl.pallas_call(diffusion_kernel, grid=(blocks,), in_specs=[smem, smem, pl...  58.5 us
    ppermute x14, waiting for transfers between devices, stack_gather(): other = lax.ppermute(x, axis, [(j, j ^ distance) for j in range(size)])  24.2 us
    ppermute x14, starting transfers between devices, stack_gather(): other = lax.ppermute(x, axis, [(j, j ^ distance) for j in range(size)])  20.9 us
    pallas_call x1, Pallas kernels, solve_grid(): pl.pallas_call(functools.partial(cg_kernel, rounds), in_specs=[pl.BlockSp...  19.9 us
    unnamed x27, local copies, waits for them, and re-layouts  13.8 us
    ppermute x1, waiting for transfers between devices, diffuse(): south_east = lax.ppermute(field[:, :HALO, :HALO], both, pairs(1, 1))  7.07 us
    ppermute x1, starting transfers between devices, diffuse(): lax.ppermute(field[:, rows - HALO:, cols - HALO:], both, pairs(-1, -1))  5.35 us
    ppermute x1, starting transfers between devices, diffuse(): south_west = lax.ppermute(field[:, :HALO, cols - HALO:], both, pairs(-1, 1))  4.98 us
  transfers between devices with their start and end apart: 23, of which 13 were waited for; matrix products, arithmetic and copies ran while one was open for 16% of the time, Pallas kernels for 0%

profile of v8, /device:TPU:6, one launch (start us, length us, event | category | flops | bytes accessed | tf_op | source)
XLA Modules:
  0.0 219.9 jit_solution(2423947629859668628)
XLA Ops:
  0.6 4.3 %fusion.26 = (f32[128,32,4]{2,1,0:T(8,128)S(1)}, f32[128,32,4]{2,1,0:T(8,128)}) fusion(f32[128,32,512]{2,1,0:T(8,128)} %core_ref.1), kind=kLoop, calls=%fused_computation.126 | loop fusion | bytes 262144 | tf_op jit(solution)/shard_map/slice | solution.py:133
  4.9 3.3 %copy.86 = f32[128,32,4]{0,1,2:T(8,128)} copy(f32[128,32,4]{2,1,0:T(8,128)} %get-tuple-element.31) | data formatting | bytes 131072
  8.2 2.4 %collective-permute-start.1 = (f32[128,32,4]{0,1,2:T(8,128)}, f32[128,32,4]{0,1,2:T(8,128)}, u32[]{:S(2)}, u32[]{:S(2)}) collective-permute-start(f32[128,32,4]{0,1,2:T(8,128)} %copy.86), channel_id=1, source_target_pairs={{0,16},{16,32},{32,48},{48,64},{64,80},{80,96},{96,112},{1,17},{17... | collective-permute-start | bytes 196616 | tf_op jit(solution)/shard_map/ppermute | solution.py:134
  10.5 1.9 copy.85
  12.5 1.3 collective-permute-start
  13.8 2.9 %fusion.25 = (f32[128,4,4]{2,1,0:T(4,128)}, f32[128,4,4]{2,1,0:T(4,128)}, f32[128,4,4]{2,1,0:T(4,128)}, f32[128,4,4]{2,1,0:T(4,128)}) fusion(f32[128,32,512]{2,1,0:T(8,128)} %core_ref.1), kind=kLoop, calls=%fused_computation.125 | loop fusion | bytes 65536 | tf_op jit(solution)/shard_map/slice | solution.py:135
  16.6 5.3 %collective-permute-start.7 = (f32[128,4,4]{2,1,0:T(4,128)}, f32[128,4,4]{2,1,0:T(4,128)S(1)}, u32[]{:S(2)}, u32[]{:S(2)}) collective-permute-start(f32[128,4,4]{2,1,0:T(4,128)} %get-tuple-element.29), channel_id=1, source_target_pairs={{0,17},{1,18},{2,19},{3,20},{4,21},{5,22},{6,23},{7,24},{8,25},{9,... | collective-permute-start | bytes 24584 | tf_op jit(solution)/shard_map/ppermute | solution.py:138
  22.0 4.1 %fusion.24 = (f32[128,4,512]{2,1,0:T(4,128)}, f32[128,4,512]{2,1,0:T(4,128)}) fusion(f32[128,32,512]{2,1,0:T(8,128)} %core_ref.1), kind=kLoop, calls=%fused_computation.124 | loop fusion | bytes 4194304 | tf_op jit(solution)/shard_map/slice | solution.py:131
  26.1 3.4 %collective-permute-start.5 = (f32[128,4,512]{2,1,0:T(4,128)}, f32[128,4,512]{2,1,0:T(4,128)S(1)}, u32[]{:S(2)}, u32[]{:S(2)}) collective-permute-start(f32[128,4,512]{2,1,0:T(4,128)} %get-tuple-element.25), channel_id=1, source_target_pairs={{0,1},{1,2},{2,3},{3,4},{4,5},{5,6},{6,7},{7,8},{8,9},{9,10},{10,1... | collective-permute-start | bytes 3145736 | tf_op jit(solution)/shard_map/ppermute | solution.py:132
  29.5 2.4 %collective-permute-start.2 = (f32[128,4,512]{2,1,0:T(4,128)}, f32[128,4,512]{2,1,0:T(4,128)}, u32[]{:S(2)}, u32[]{:S(2)}) collective-permute-start(f32[128,4,512]{2,1,0:T(4,128)} %get-tuple-element.24), channel_id=1, source_target_pairs={{1,0},{2,1},{3,2},{4,3},{5,4},{6,5},{7,6},{8,7},{9,8},{10,9},{11,1... | collective-permute-start | bytes 3145736 | tf_op jit(solution)/shard_map/ppermute | solution.py:131
  32.5 0.6 copy.71
  33.2 1.6 reshape.236
  37.0 1.4 and_convert_fusion.mask_ref
  38.5 1.3 collective-permute-start.6
  39.7 2.7 %copy.69 = f32[128,32,4]{2,1,0:T(8,128)S(1)} copy(f32[128,32,4]{0,1,2:T(8,128)} %collective-permute-done.1) | data formatting | bytes 131072 | tf_op jit(solution)/shard_map/ppermute | solution.py:134
  42.5 5.0 %collective-permute-start.4 = (f32[128,4,4]{2,1,0:T(4,128)}, f32[128,4,4]{2,1,0:T(4,128)}, u32[]{:S(2)}, u32[]{:S(2)}) collective-permute-start(f32[128,4,4]{2,1,0:T(4,128)} %get-tuple-element.27), channel_id=1, source_target_pairs={{1,16},{2,17},{3,18},{4,19},{5,20},{6,21},{7,22},{8,23},{9,24},{10... | collective-permute-start | bytes 24584 | tf_op jit(solution)/shard_map/ppermute | solution.py:136
  47.5 2.9 %copy.68 = f32[128,32,4]{2,1,0:T(8,128)} copy(f32[128,32,4]{0,1,2:T(8,128)S(1)} %collective-permute-done) | data formatting | bytes 131072 | tf_op jit(solution)/shard_map/ppermute | solution.py:133
  50.3 1.5 collective-permute-start.3
  51.8 3.5 %pad_maximum_fusion.lanes_ref = f32[128,32,128]{2,1,0:T(8,128)} fusion(f32[128,32,4]{2,1,0:T(8,128)S(1)} %copy.69, f32[128,32,4]{2,1,0:T(8,128)} %copy.68, f32[128]{0:T(128)S(1)} %pad.29.clone), kind=kLoop, calls=%fused_computation.4 | loop fusion | flops 1048576 | bytes 2228736 | tf_op jit(solution)/shard_map/concatenate | solution.py:140
  55.3 1.8 collective-permute-done.6
  57.1 4.0 %collective-permute-done.4 = f32[128,4,4]{2,1,0:T(4,128)} collective-permute-done((f32[128,4,4]{2,1,0:T(4,128)}, f32[128,4,4]{2,1,0:T(4,128)}, u32[]{:S(2)}, u32[]{:S(2)}) %collective-permute-start.4) | collective-permute-done | bytes 8224 | tf_op jit(solution)/shard_map/ppermute | solution.py:136
  61.1 7.1 %collective-permute-done.3 = f32[128,4,4]{2,1,0:T(4,128)S(1)} collective-permute-done((f32[128,4,4]{2,1,0:T(4,128)}, f32[128,4,4]{2,1,0:T(4,128)S(1)}, u32[]{:S(2)}, u32[]{:S(2)}) %collective-permute-start.3) | collective-permute-done | bytes 8224 | tf_op jit(solution)/shard_map/ppermute | solution.py:135
  68.2 3.9 %maximum_maximum_fusion.rows_ref = f32[128,8,640]{2,1,0:T(8,128)} fusion(f32[128,4,4]{2,1,0:T(4,128)S(1)} %collective-permute-done.7, f32[128,4,120]{2,1,0:T(4,128)S(1)} %broadcast_in_dim.52, f32[128,4,4]{2,1,0:T(4,128)} %collective-permute-done.6, f32[128,4,512]{2,1,0:T(4,128)S(1)} %collective-permute-done.5, f32[128,4,4]{2,1,0:T(4,128)} %collective-permute-done.4, ...), kind=kLoop, calls=%fused_computation.3 | loop fusion | flops 4587520 | bytes 4997120 | tf_op jit(solution)/shard_map/concatenate | solution.py:142
  72.1 58.5 %shard_map.111 = (f32[128,32,512]{2,1,0:T(8,128)}, f32[4,32,512]{2,1,0:T(8,128)}) custom-call(f32[128]{0:T(128)} %kappa_ref.1, f32[4,128]{1,0:T(4,128)} %weight_ref.1, f32[128,32,512]{2,1,0:T(8,128)} %core_ref.1, f32[128,32,128]{2,1,0:T(8,128)} %pad_maximum_fusion.lanes_ref, f32[128,8,640]{2,1,0:T(8,128)} %maximum_maximum_fusion.rows_ref, ...), custom_call_target="tpu_custom_call" | custom-call | flops 131072000 | bytes 16777216 | tf_op jit(solution)/shard_map/pallas_call | solution.py:160
  130.6 1.0 convert_element_type.40
  131.8 0.6 gather_fusion.1
  132.8 0.7 gather_fusion
  133.5 3.3 %collective-permute-done.8 = bf16[32,4,128]{2,1,0:T(4,128)(2,1)S(1)} collective-permute-done((bf16[32,4,128]{2,1,0:T(4,128)(2,1)S(1)}, bf16[32,4,128]{2,1,0:T(4,128)(2,1)S(1)}, u32[]{:S(2)}, u32[]{:S(2)}) %collective-permute-start.8) | collective-permute-done | bytes 32800 | tf_op jit(solution)/shard_map/ppermute | solution.py:29
  136.9 0.7 gather_fusion.2
  137.6 3.0 %convolution_bitcast_fusion = f32[4,32,128]{2,0,1:T(4,128)S(1)} fusion(bf16[32,4,128,128]{3,2,1,0:T(8,128)(2,1)} %param.13, bf16[32,4,4,128]{3,2,1,0:T(4,128)(2,1)S(1)} %bitcast.37, bf16[32,4,4,128]{3,2,1,0:T(4,128)(2,1)S(1)} %bitcast.38, pred[32,4]{1,0:T(8,128)(4,1)S(1)} %and.117, pred[32,4]{1,0:T(8,128)(4,1)S(1)} %and.113), kind=kOutput, calls=%fused_computation.5 | convolution fusion | flops 16908288 | bytes 4522240 | tf_op jit(solution)/shard_map/bkij,bkcj->cbi/dot_general | solution.py:356
  140.8 0.6 constant_dynamic-update-slice_fusion.43
  141.4 3.5 %collective-permute-start.16 = (f32[1,16,256]{2,1,0:T(8,128)S(1)}, f32[1,16,256]{2,1,0:T(8,128)S(1)}, u32[]{:S(2)}, u32[]{:S(2)}) collective-permute-start(f32[1,16,256]{2,1,0:T(8,128)S(1)} %get-tuple-element.15), channel_id=1, source_target_pairs={{0,2},{1,3},{2,0},{3,1},{4,6},{5,7},{6,4},{7,5},{8,10},{9,11},{10,... | collective-permute-start | bytes 49160 | tf_op jit(solution)/shard_map/ppermute | solution.py:61
  144.9 1.7 collective-permute-done.9
  146.7 2.9 %collective-permute-start.10 = (f32[2,16,256]{2,1,0:T(8,128)S(1)}, f32[2,16,256]{2,1,0:T(8,128)S(1)}, u32[]{:S(2)}, u32[]{:S(2)}) collective-permute-start(f32[2,16,256]{2,1,0:T(8,128)S(1)} %pad_maximum_fusion.5), channel_id=1, source_target_pairs={{0,8},{1,9},{2,10},{3,11},{4,12},{5,13},{6,14},{7,15},{8,0},{9,1},... | collective-permute-start | bytes 98312 | tf_op jit(solution)/shard_map/ppermute | solution.py:61
  149.6 0.6 collective-permute-start.17
  150.2 0.6 constant_dynamic-update-slice_fusion.16
  150.8 0.6 constant_dynamic-update-slice_fusion.42
  151.4 0.7 collective-permute-done.10
  152.1 4.4 %collective-permute-start.11 = (f32[4,16,256]{2,1,0:T(8,128)S(1)}, f32[4,16,256]{2,1,0:T(8,128)S(1)}, u32[]{:S(2)}, u32[]{:S(2)}) collective-permute-start(f32[4,16,256]{2,1,0:T(8,128)S(1)} %pad_maximum_fusion.3), channel_id=1, source_target_pairs={{0,64},{16,80},{32,96},{48,112},{64,0},{80,16},{96,32},{112,48},{1... | collective-permute-start | bytes 196616 | tf_op jit(solution)/shard_map/ppermute | solution.py:61
  156.5 2.7 %collective-permute-start.18 = (f32[4,16,256]{2,1,0:T(8,128)S(1)}, f32[4,16,256]{2,1,0:T(8,128)S(1)}, u32[]{:S(2)}, u32[]{:S(2)}) collective-permute-start(f32[4,16,256]{2,1,0:T(8,128)S(1)} %pad_maximum_fusion.4), channel_id=1, source_target_pairs={{0,64},{16,80},{32,96},{48,112},{64,0},{80,16},{96,32},{112,48},{1... | collective-permute-start | bytes 196616 | tf_op jit(solution)/shard_map/ppermute | solution.py:61
  159.2 0.6 constant_dynamic-update-slice_fusion.15
  159.8 0.6 constant_dynamic-update-slice_fusion.41
  160.5 1.8 collective-permute-done.18
  162.6 0.6 constant_dynamic-update-slice_fusion.14
  163.3 2.2 %collective-permute-done.12 = f32[8,16,256]{2,1,0:T(8,128)S(1)} collective-permute-done((f32[8,16,256]{2,1,0:T(8,128)S(1)}, f32[8,16,256]{2,1,0:T(8,128)S(1)}, u32[]{:S(2)}, u32[]{:S(2)}) %collective-permute-start.12) | collective-permute-done | bytes 131104 | tf_op jit(solution)/shard_map/ppermute | solution.py:61
  165.5 0.7 constant_dynamic-update-slice_fusion.13
  166.7 0.6 constant_dynamic-update-slice_fusion.40
  167.4 0.7 constant_dynamic-update-slice_fusion.39
  168.1 1.4 collective-permute-start.20
  169.5 3.8 %collective-permute-done.13 = f32[16,16,256]{2,1,0:T(8,128)S(1)} collective-permute-done((f32[16,16,256]{2,1,0:T(8,128)S(1)}, f32[16,16,256]{2,1,0:T(8,128)S(1)}, u32[]{:S(2)}, u32[]{:S(2)}) %collective-permute-start.13) | collective-permute-done | bytes 262176 | tf_op jit(solution)/shard_map/ppermute | solution.py:61
  173.3 0.8 constant_dynamic-update-slice_fusion.12
  174.1 2.4 %collective-permute-start.14 = (f32[32,16,256]{2,1,0:T(8,128)S(1)}, f32[32,16,256]{2,1,0:T(8,128)S(1)}, u32[]{:S(2)}, u32[]{:S(2)}) collective-permute-start(f32[32,16,256]{2,1,0:T(8,128)S(1)} %get-tuple-element.41), channel_id=1, source_target_pairs={{0,32},{16,48},{32,0},{48,16},{64,96},{80,112},{96,64},{112,80},{1... | collective-permute-start | bytes 1572872 | tf_op jit(solution)/shard_map/ppermute | solution.py:61
  176.5 0.8 constant_dynamic-update-slice_fusion.38
  177.3 2.0 collective-permute-start.21
  179.3 8.5 %collective-permute-done.14 = f32[32,16,256]{2,1,0:T(8,128)S(1)} collective-permute-done((f32[32,16,256]{2,1,0:T(8,128)S(1)}, f32[32,16,256]{2,1,0:T(8,128)S(1)}, u32[]{:S(2)}, u32[]{:S(2)}) %collective-permute-start.14) | collective-permute-done | bytes 524320 | tf_op jit(solution)/shard_map/ppermute | solution.py:61
  187.8 0.9 constant_dynamic-update-slice_fusion.11
  188.7 4.7 %collective-permute-done.21 = f32[32,16,256]{2,1,0:T(8,128)S(1)} collective-permute-done((f32[32,16,256]{2,1,0:T(8,128)S(1)}, f32[32,16,256]{2,1,0:T(8,128)S(1)}, u32[]{:S(2)}, u32[]{:S(2)}) %collective-permute-start.21) | collective-permute-done | bytes 524320 | tf_op jit(solution)/shard_map/ppermute | solution.py:61
  193.4 0.9 constant_dynamic-update-slice_fusion.37
  194.9 0.6 reshape.238
  195.6 1.1 constant_dynamic-update-slice_fusion.18.rhs_stack
  196.7 0.7 collective-permute-done.22
  197.3 1.3 constant_dynamic-update-slice_fusion.44.coded_stack
  198.7 1.3 copy-done
  200.0 19.9 %shard_map.112 = (f32[16,256]{1,0:T(8,128)}, f32[16,256]{1,0:T(8,128)}) custom-call(s32[2]{0:T(128)} %pad_add_fusion.index_ref, f32[128,16,256]{2,1,0:T(8,128)} %constant_dynamic-update-slice_fusion.18.rhs_stack, f32[128,16,256]{2,1,0:T(8,128)} %copy-done), custom_call_target="tpu_custom_call" | custom-call | tf_op jit(solution)/shard_map/pallas_call | solution.py:290
  (74 shorter events, 5.0 us)
Async XLA Ops:
  8.2 30.3 %collective-permute-start.1 = (f32[128,32,4]{0,1,2:T(8,128)}, f32[128,32,4]{0,1,2:T(8,128)}, u32[]{:S(2)}, u32[]{:S(2)}) collective-permute-start(f32[128,32,4]{0,1,2:T(8,128)} %copy.86), channel_id=1, source_target_pairs={{0,16},{16,32},{32,48},{48,64},{64,80},{80,96},{96,112},{1,17},{17... | collective-permute-start | bytes 196616 | tf_op jit(solution)/shard_map/ppermute | solution.py:134
  12.5 30.0 %collective-permute-start = (f32[128,32,4]{0,1,2:T(8,128)}, f32[128,32,4]{0,1,2:T(8,128)S(1)}, u32[]{:S(2)}, u32[]{:S(2)}) collective-permute-start(f32[128,32,4]{0,1,2:T(8,128)} %copy.85), channel_id=1, source_target_pairs={{16,0},{32,16},{48,32},{64,48},{80,64},{96,80},{112,96},{17,1},{33... | collective-permute-start | bytes 196616 | tf_op jit(solution)/shard_map/ppermute | solution.py:133
  16.6 15.9 %copy-start.2 = (s32[4096,4]{0,1:T(4,128)S(1)}, s32[4096,4]{0,1:T(4,128)}, u32[]{:S(2)}) copy-start(s32[4096,4]{0,1:T(4,128)} %param.11) | copy-start | bytes 196612
  16.6 33.7 %collective-permute-start.7 = (f32[128,4,4]{2,1,0:T(4,128)}, f32[128,4,4]{2,1,0:T(4,128)S(1)}, u32[]{:S(2)}, u32[]{:S(2)}) collective-permute-start(f32[128,4,4]{2,1,0:T(4,128)} %get-tuple-element.29), channel_id=1, source_target_pairs={{0,17},{1,18},{2,19},{3,20},{4,21},{5,22},{6,23},{7,24},{8,25},{9,... | collective-permute-start | bytes 24584 | tf_op jit(solution)/shard_map/ppermute | solution.py:138
  26.1 42.1 %collective-permute-start.5 = (f32[128,4,512]{2,1,0:T(4,128)}, f32[128,4,512]{2,1,0:T(4,128)S(1)}, u32[]{:S(2)}, u32[]{:S(2)}) collective-permute-start(f32[128,4,512]{2,1,0:T(4,128)} %get-tuple-element.25), channel_id=1, source_target_pairs={{0,1},{1,2},{2,3},{3,4},{4,5},{5,6},{6,7},{7,8},{8,9},{9,10},{10,1... | collective-permute-start | bytes 3145736 | tf_op jit(solution)/shard_map/ppermute | solution.py:132
  29.5 38.7 %collective-permute-start.2 = (f32[128,4,512]{2,1,0:T(4,128)}, f32[128,4,512]{2,1,0:T(4,128)}, u32[]{:S(2)}, u32[]{:S(2)}) collective-permute-start(f32[128,4,512]{2,1,0:T(4,128)} %get-tuple-element.24), channel_id=1, source_target_pairs={{1,0},{2,1},{3,2},{4,3},{5,4},{6,5},{7,6},{8,7},{9,8},{10,9},{11,1... | collective-permute-start | bytes 3145736 | tf_op jit(solution)/shard_map/ppermute | solution.py:131
  32.5 2.5 %copy-start.3 = (s32[4096]{0:T(1024)S(1)}, s32[4096]{0:T(1024)}, u32[]{:S(2)}) copy-start(s32[4096]{0:T(1024)} %param.12) | copy-start | bytes 49156
  38.5 18.7 %collective-permute-start.6 = (f32[128,4,4]{2,1,0:T(4,128)}, f32[128,4,4]{2,1,0:T(4,128)}, u32[]{:S(2)}, u32[]{:S(2)}) collective-permute-start(f32[128,4,4]{2,1,0:T(4,128)} %get-tuple-element.28), channel_id=1, source_target_pairs={{16,1},{17,2},{18,3},{19,4},{20,5},{21,6},{22,7},{23,8},{24,9},{25... | collective-permute-start | bytes 24584 | tf_op jit(solution)/shard_map/ppermute | solution.py:137
  42.5 18.6 %collective-permute-start.4 = (f32[128,4,4]{2,1,0:T(4,128)}, f32[128,4,4]{2,1,0:T(4,128)}, u32[]{:S(2)}, u32[]{:S(2)}) collective-permute-start(f32[128,4,4]{2,1,0:T(4,128)} %get-tuple-element.27), channel_id=1, source_target_pairs={{1,16},{2,17},{3,18},{4,19},{5,20},{6,21},{7,22},{8,23},{9,24},{10... | collective-permute-start | bytes 24584 | tf_op jit(solution)/shard_map/ppermute | solution.py:136
  50.3 17.8 %collective-permute-start.3 = (f32[128,4,4]{2,1,0:T(4,128)}, f32[128,4,4]{2,1,0:T(4,128)S(1)}, u32[]{:S(2)}, u32[]{:S(2)}) collective-permute-start(f32[128,4,4]{2,1,0:T(4,128)} %get-tuple-element.26), channel_id=1, source_target_pairs={{17,0},{18,1},{19,2},{20,3},{21,4},{22,5},{23,6},{24,7},{25,8},{26... | collective-permute-start | bytes 24584 | tf_op jit(solution)/shard_map/ppermute | solution.py:135
  132.5 4.4 %collective-permute-start.8 = (bf16[32,4,128]{2,1,0:T(4,128)(2,1)S(1)}, bf16[32,4,128]{2,1,0:T(4,128)(2,1)S(1)}, u32[]{:S(2)}, u32[]{:S(2)}) collective-permute-start(bf16[32,4,128]{2,1,0:T(4,128)(2,1)S(1)} %broadcast_multiply_fusion), channel_id=1, source_target_pairs={{0,112},{16,0},{32,16},{48,32},{64,48},{80,64},{96,80},{112,96},{1... | collective-permute-start | bytes 98312 | tf_op jit(solution)/shard_map/ppermute | solution.py:29
  137.6 3.1 %copy-start.4 = (f32[16,256]{1,0:T(8,128)S(1)}, f32[16,256]{1,0:T(8,128)}, u32[]{:S(2)}) copy-start(f32[16,256]{1,0:T(8,128)} %param.15) | copy-start | bytes 49156
  137.6 3.1 %copy-start.5 = (s32[16,256]{1,0:T(8,128)S(1)}, s32[16,256]{1,0:T(8,128)}, u32[]{:S(2)}) copy-start(s32[16,256]{1,0:T(8,128)} %param.14) | copy-start | bytes 49156
  141.4 5.2 %collective-permute-start.9 = (f32[1,16,256]{2,1,0:T(8,128)S(1)}, f32[1,16,256]{2,1,0:T(8,128)S(1)}, u32[]{:S(2)}, u32[]{:S(2)}) collective-permute-start(f32[1,16,256]{2,1,0:T(8,128)S(1)} %get-tuple-element.80), channel_id=1, source_target_pairs={{0,2},{1,3},{2,0},{3,1},{4,6},{5,7},{6,4},{7,5},{8,10},{9,11},{10,... | collective-permute-start | bytes 49160 | tf_op jit(solution)/shard_map/ppermute | solution.py:61
  141.4 8.1 %collective-permute-start.16 = (f32[1,16,256]{2,1,0:T(8,128)S(1)}, f32[1,16,256]{2,1,0:T(8,128)S(1)}, u32[]{:S(2)}, u32[]{:S(2)}) collective-permute-start(f32[1,16,256]{2,1,0:T(8,128)S(1)} %get-tuple-element.15), channel_id=1, source_target_pairs={{0,2},{1,3},{2,0},{3,1},{4,6},{5,7},{6,4},{7,5},{8,10},{9,11},{10,... | collective-permute-start | bytes 49160 | tf_op jit(solution)/shard_map/ppermute | solution.py:61
  146.7 5.4 %collective-permute-start.10 = (f32[2,16,256]{2,1,0:T(8,128)S(1)}, f32[2,16,256]{2,1,0:T(8,128)S(1)}, u32[]{:S(2)}, u32[]{:S(2)}) collective-permute-start(f32[2,16,256]{2,1,0:T(8,128)S(1)} %pad_maximum_fusion.5), channel_id=1, source_target_pairs={{0,8},{1,9},{2,10},{3,11},{4,12},{5,13},{6,14},{7,15},{8,0},{9,1},... | collective-permute-start | bytes 98312 | tf_op jit(solution)/shard_map/ppermute | solution.py:61
  149.6 6.9 %collective-permute-start.17 = (f32[2,16,256]{2,1,0:T(8,128)S(1)}, f32[2,16,256]{2,1,0:T(8,128)S(1)}, u32[]{:S(2)}, u32[]{:S(2)}) collective-permute-start(f32[2,16,256]{2,1,0:T(8,128)S(1)} %pad_maximum_fusion.6), channel_id=1, source_target_pairs={{0,8},{1,9},{2,10},{3,11},{4,12},{5,13},{6,14},{7,15},{8,0},{9,1},... | collective-permute-start | bytes 98312 | tf_op jit(solution)/shard_map/ppermute | solution.py:61
  152.1 8.3 %collective-permute-start.11 = (f32[4,16,256]{2,1,0:T(8,128)S(1)}, f32[4,16,256]{2,1,0:T(8,128)S(1)}, u32[]{:S(2)}, u32[]{:S(2)}) collective-permute-start(f32[4,16,256]{2,1,0:T(8,128)S(1)} %pad_maximum_fusion.3), channel_id=1, source_target_pairs={{0,64},{16,80},{32,96},{48,112},{64,0},{80,16},{96,32},{112,48},{1... | collective-permute-start | bytes 196616 | tf_op jit(solution)/shard_map/ppermute | solution.py:61
  156.5 5.8 %collective-permute-start.18 = (f32[4,16,256]{2,1,0:T(8,128)S(1)}, f32[4,16,256]{2,1,0:T(8,128)S(1)}, u32[]{:S(2)}, u32[]{:S(2)}) collective-permute-start(f32[4,16,256]{2,1,0:T(8,128)S(1)} %pad_maximum_fusion.4), channel_id=1, source_target_pairs={{0,64},{16,80},{32,96},{48,112},{64,0},{80,16},{96,32},{112,48},{1... | collective-permute-start | bytes 196616 | tf_op jit(solution)/shard_map/ppermute | solution.py:61
  160.4 5.0 %collective-permute-start.12 = (f32[8,16,256]{2,1,0:T(8,128)S(1)}, f32[8,16,256]{2,1,0:T(8,128)S(1)}, u32[]{:S(2)}, u32[]{:S(2)}) collective-permute-start(f32[8,16,256]{2,1,0:T(8,128)S(1)} %pad_maximum_fusion.1), channel_id=1, source_target_pairs={{0,1},{1,0},{2,3},{3,2},{4,5},{5,4},{6,7},{7,6},{8,9},{9,8},{10,11... | collective-permute-start | bytes 393224 | tf_op jit(solution)/shard_map/ppermute | solution.py:61
  162.4 5.0 %collective-permute-start.19 = (f32[8,16,256]{2,1,0:T(8,128)S(1)}, f32[8,16,256]{2,1,0:T(8,128)S(1)}, u32[]{:S(2)}, u32[]{:S(2)}) collective-permute-start(f32[8,16,256]{2,1,0:T(8,128)S(1)} %pad_maximum_fusion.2), channel_id=1, source_target_pairs={{0,1},{1,0},{2,3},{3,2},{4,5},{5,4},{6,7},{7,6},{8,9},{9,8},{10,11... | collective-permute-start | bytes 393224 | tf_op jit(solution)/shard_map/ppermute | solution.py:61
  166.2 7.2 %collective-permute-start.13 = (f32[16,16,256]{2,1,0:T(8,128)S(1)}, f32[16,16,256]{2,1,0:T(8,128)S(1)}, u32[]{:S(2)}, u32[]{:S(2)}) collective-permute-start(f32[16,16,256]{2,1,0:T(8,128)S(1)} %get-tuple-element.49), channel_id=1, source_target_pairs={{0,4},{1,5},{2,6},{3,7},{4,0},{5,1},{6,2},{7,3},{8,12},{9,13},{10,... | collective-permute-start | bytes 786440 | tf_op jit(solution)/shard_map/ppermute | solution.py:61
  168.1 8.4 %collective-permute-start.20 = (f32[16,16,256]{2,1,0:T(8,128)S(1)}, f32[16,16,256]{2,1,0:T(8,128)S(1)}, u32[]{:S(2)}, u32[]{:S(2)}) collective-permute-start(f32[16,16,256]{2,1,0:T(8,128)S(1)} %get-tuple-element.45), channel_id=1, source_target_pairs={{0,4},{1,5},{2,6},{3,7},{4,0},{5,1},{6,2},{7,3},{8,12},{9,13},{10,... | collective-permute-start | bytes 786440 | tf_op jit(solution)/shard_map/ppermute | solution.py:61
  174.1 13.7 %collective-permute-start.14 = (f32[32,16,256]{2,1,0:T(8,128)S(1)}, f32[32,16,256]{2,1,0:T(8,128)S(1)}, u32[]{:S(2)}, u32[]{:S(2)}) collective-permute-start(f32[32,16,256]{2,1,0:T(8,128)S(1)} %get-tuple-element.41), channel_id=1, source_target_pairs={{0,32},{16,48},{32,0},{48,16},{64,96},{80,112},{96,64},{112,80},{1... | collective-permute-start | bytes 1572872 | tf_op jit(solution)/shard_map/ppermute | solution.py:61
  177.3 16.1 %collective-permute-start.21 = (f32[32,16,256]{2,1,0:T(8,128)S(1)}, f32[32,16,256]{2,1,0:T(8,128)S(1)}, u32[]{:S(2)}, u32[]{:S(2)}) collective-permute-start(f32[32,16,256]{2,1,0:T(8,128)S(1)} %get-tuple-element.38), channel_id=1, source_target_pairs={{0,32},{16,48},{32,0},{48,16},{64,96},{80,112},{96,64},{112,80},{1... | collective-permute-start | bytes 1572872 | tf_op jit(solution)/shard_map/ppermute | solution.py:61
  188.7 5.7 %copy-start.1 = (f32[128,16,256]{2,1,0:T(8,128)}, f32[128,16,256]{2,1,0:T(8,128)S(1)}, u32[]{:S(2)}) copy-start(f32[128,16,256]{2,1,0:T(8,128)S(1)} %get-tuple-element.35) | copy-start | bytes 6291460
  188.7 6.9 %collective-permute-start.15 = (f32[64,16,256]{2,1,0:T(8,128)}, f32[64,16,256]{2,1,0:T(8,128)S(1)}, u32[]{:S(2)}, u32[]{:S(2)}) collective-permute-start(f32[64,16,256]{2,1,0:T(8,128)} %get-tuple-element.34), channel_id=1, source_target_pairs={{0,16},{16,0},{32,48},{48,32},{64,80},{80,64},{96,112},{112,96},{1... | collective-permute-start | bytes 3145736 | tf_op jit(solution)/shard_map/ppermute | solution.py:61
  194.3 3.0 %collective-permute-start.22 = (f32[64,16,256]{2,1,0:T(8,128)}, f32[64,16,256]{2,1,0:T(8,128)}, u32[]{:S(2)}, u32[]{:S(2)}) collective-permute-start(f32[64,16,256]{2,1,0:T(8,128)} %get-tuple-element.32), channel_id=1, source_target_pairs={{0,16},{16,0},{32,48},{48,32},{64,80},{80,64},{96,112},{112,96},{1... | collective-permute-start | bytes 3145736 | tf_op jit(solution)/shard_map/ppermute | solution.py:61
  198.6 1.3 copy-start

commit v9 on v8

--- a/solution.py
+++ b/solution.py
@@ -110,7 +110,7 @@
     lax.fori_loop(0, levels, level, 0, unroll=2)
 
 
-def diffuse(field, atm_kappa, vert_weight):
+def diffuse(field, core, atm_kappa, vert_weight):
     levels, rows, cols = field.shape
     comps = vert_weight.shape[0]
     count_gx = lax.axis_size("gx")
@@ -182,7 +182,7 @@
             transcendentals=0,
             bytes_accessed=2 * field.size * 4,
         ),
-    )(atm_kappa, vert_weight, field, lanes, halo_rows, mask)
+    )(atm_kappa, vert_weight, core, lanes, halo_rows, mask)
     return out, flux
 
 
@@ -305,7 +305,8 @@
     count_gy = lax.axis_size("gy")
     rounds = gather_rounds()
     coded_all = stack_gather(jnp.where(land_mask != 0, ocean_term, -1.0), rounds)
-    field, flux = diffuse(atm_state, atm_kappa, vert_weight)
+    core, coded_all = lax.optimization_barrier((atm_state, coded_all))
+    field, flux = diffuse(atm_state, core, atm_kappa, vert_weight)
     flux = flux.reshape(flux.shape[0], tile_lat * tile_lon)
     ocean_blocks, lists, width, _ = remap_weight.shape
     comps = vert_weight.shape[0]

time: 222 us -> 262 us (1.18)
  waiting for transfers between devices: 40.3 us -> 61.9 us
  starting transfers between devices: 43.5 us -> 60.5 us
    ppermute x14, waiting for transfers between devices: 24.2 us -> 51.2 us  [stack_gather(): other = lax.ppermute(x, axis, [(j, j ^ distance) for j in range(size)])]
    ppermute x14, starting transfers between devices: 20.9 us -> 41.7 us  [stack_gather(): other = lax.ppermute(x, axis, [(j, j ^ distance) for j in range(size)])]
    ppermute x1, starting transfers between devices: 5.35 us -> 1.29 us  [diffuse(): lax.ppermute(field[:, rows - HALO:, cols - HALO:], both, pairs(-1, -1))]
    unnamed x27 -> x31, local copies, waits for them, and re-layouts: 13.8 us -> 14.8 us
  transfers between devices with their start and end apart: 23 -> 23, of which waited for: 13 -> 15; matrix products, arithmetic and copies ran while one was open for 16% -> 17% of each run, Pallas kernels for 0% -> 0%
where the time goes in v9:
time: 262 us; the launch traced here: 260 us
  Pallas kernels  79.2 us (30%)
  waiting for transfers between devices  61.9 us (24%)
  starting transfers between devices  60.5 us (23%)
  local copies, waits for them, and re-layouts  40.7 us (16%)
  other arithmetic  13.5 us (5%)
  matrix products  3.04 us (1%)
    pallas_call x1, Pallas kernels, diffuse(): pl.pallas_call(diffusion_kernel, grid=(blocks,), in_specs=[smem, smem, pl...  59.3 us
    ppermute x14, waiting for transfers between devices, stack_gather(): other = lax.ppermute(x, axis, [(j, j ^ distance) for j in range(size)])  51.2 us
    ppermute x14, starting transfers between devices, stack_gather(): other = lax.ppermute(x, axis, [(j, j ^ distance) for j in range(size)])  41.7 us
    pallas_call x1, Pallas kernels, solve_grid(): pl.pallas_call(functools.partial(cg_kernel, rounds), in_specs=[pl.BlockSp...  19.9 us
    unnamed x31, local copies, waits for them, and re-layouts  14.8 us
    ppermute x1, waiting for transfers between devices, diffuse(): south_east = lax.ppermute(field[:, :HALO, :HALO], both, pairs(1, 1))  5.66 us
  transfers between devices with their start and end apart: 23, of which 15 were waited for; matrix products, arithmetic and copies ran while one was open for 17% of the time, Pallas kernels for 0%

profile of v9, /device:TPU:6, one launch (start us, length us, event | category | flops | bytes accessed | tf_op | source)
XLA Modules:
  0.0 260.0 jit_solution(5830830726831503340)
XLA Ops:
  0.6 1.3 constant_dynamic-update-slice_fusion.17
  2.0 1.4 collective-permute-start
  3.4 4.3 %fusion.26 = (f32[128,32,4]{2,1,0:T(8,128)S(1)}, f32[128,32,4]{2,1,0:T(8,128)}) fusion(f32[128,32,512]{2,1,0:T(8,128)} %core_ref), kind=kLoop, calls=%fused_computation.126 | loop fusion | bytes 262144 | tf_op jit(solution)/shard_map/slice | solution.py:133
  7.6 2.7 %copy.86 = f32[128,32,4]{0,1,2:T(8,128)S(1)} copy(f32[128,32,4]{2,1,0:T(8,128)} %get-tuple-element.35) | data formatting | bytes 131072
  10.3 1.5 collective-permute-start.8
  11.7 2.0 copy.85
  13.7 1.4 collective-permute-start.7
  15.1 4.1 %fusion.24 = (f32[128,4,512]{2,1,0:T(4,128)}, f32[128,4,512]{2,1,0:T(4,128)}) fusion(f32[128,32,512]{2,1,0:T(8,128)} %core_ref), kind=kLoop, calls=%fused_computation.124 | loop fusion | bytes 4194304 | tf_op jit(solution)/shard_map/slice | solution.py:131
  19.2 5.0 %collective-permute-start.12 = (f32[128,4,512]{2,1,0:T(4,128)}, f32[128,4,512]{2,1,0:T(4,128)}, u32[]{:S(2)}, u32[]{:S(2)}) collective-permute-start(f32[128,4,512]{2,1,0:T(4,128)} %get-tuple-element.29), channel_id=1, source_target_pairs={{0,1},{1,2},{2,3},{3,4},{4,5},{5,6},{6,7},{7,8},{8,9},{9,10},{10,1... | collective-permute-start | bytes 3145736 | tf_op jit(solution)/shard_map/ppermute | solution.py:132
  24.2 1.9 collective-permute-start.9
  26.2 0.6 copy.71
  26.9 1.6 reshape.236
  29.7 0.6 constant_dynamic-update-slice_fusion.10
  30.5 3.0 %collective-permute-start.1 = (f32[2,16,256]{2,1,0:T(8,128)S(1)}, f32[2,16,256]{2,1,0:T(8,128)S(1)}, u32[]{:S(2)}, u32[]{:S(2)}) collective-permute-start(f32[2,16,256]{2,1,0:T(8,128)S(1)} %pad_maximum_fusion.5), channel_id=1, source_target_pairs={{0,8},{1,9},{2,10},{3,11},{4,12},{5,13},{6,14},{7,15},{8,0},{9,1},... | collective-permute-start | bytes 98312 | tf_op jit(solution)/shard_map/ppermute | solution.py:61
  33.6 2.4 collective-permute-done.1
  36.0 6.7 %collective-permute-start.2 = (f32[4,16,256]{2,1,0:T(8,128)S(1)}, f32[4,16,256]{2,1,0:T(8,128)S(1)}, u32[]{:S(2)}, u32[]{:S(2)}) collective-permute-start(f32[4,16,256]{2,1,0:T(8,128)S(1)} %pad_maximum_fusion.3), channel_id=1, source_target_pairs={{0,64},{16,80},{32,96},{48,112},{64,0},{80,16},{96,32},{112,48},{1... | collective-permute-start | bytes 196616 | tf_op jit(solution)/shard_map/ppermute | solution.py:61
  43.3 1.6 collective-permute-done.2
  45.1 0.6 constant_dynamic-update-slice_fusion.15
  45.7 0.7 constant_dynamic-update-slice_fusion.14
  46.4 4.1 %collective-permute-done.3 = f32[8,16,256]{2,1,0:T(8,128)S(1)} collective-permute-done((f32[8,16,256]{2,1,0:T(8,128)S(1)}, f32[8,16,256]{2,1,0:T(8,128)S(1)}, u32[]{:S(2)}, u32[]{:S(2)}) %collective-permute-start.3) | collective-permute-done | bytes 131104 | tf_op jit(solution)/shard_map/ppermute | solution.py:61
  50.5 0.8 constant_dynamic-update-slice_fusion.13
  51.3 19.8 %collective-permute-start.4 = (f32[16,16,256]{2,1,0:T(8,128)S(1)}, f32[16,16,256]{2,1,0:T(8,128)S(1)}, u32[]{:S(2)}, u32[]{:S(2)}) collective-permute-start(f32[16,16,256]{2,1,0:T(8,128)S(1)} %get-tuple-element.53), channel_id=1, source_target_pairs={{0,4},{1,5},{2,6},{3,7},{4,0},{5,1},{6,2},{7,3},{8,12},{9,13},{10,... | collective-permute-start | bytes 786440 | tf_op jit(solution)/shard_map/ppermute | solution.py:61
  71.0 4.8 %collective-permute-done.4 = f32[16,16,256]{2,1,0:T(8,128)S(1)} collective-permute-done((f32[16,16,256]{2,1,0:T(8,128)S(1)}, f32[16,16,256]{2,1,0:T(8,128)S(1)}, u32[]{:S(2)}, u32[]{:S(2)}) %collective-permute-start.4) | collective-permute-done | bytes 262176 | tf_op jit(solution)/shard_map/ppermute | solution.py:61
  75.8 0.9 constant_dynamic-update-slice_fusion.12
  76.7 1.4 collective-permute-start.5
  78.1 0.7 and_convert_fusion.mask_ref
  79.1 9.3 %collective-permute-done.5 = f32[32,16,256]{2,1,0:T(8,128)S(1)} collective-permute-done((f32[32,16,256]{2,1,0:T(8,128)}, f32[32,16,256]{2,1,0:T(8,128)S(1)}, u32[]{:S(2)}, u32[]{:S(2)}) %collective-permute-start.5) | collective-permute-done | bytes 524320 | tf_op jit(solution)/shard_map/ppermute | solution.py:61
  88.4 0.9 constant_dynamic-update-slice_fusion.11
  89.5 3.5 %fusion.25 = (f32[128,4,4]{2,1,0:T(4,128)}, f32[128,4,4]{2,1,0:T(4,128)}, f32[128,4,4]{2,1,0:T(4,128)}, f32[128,4,4]{2,1,0:T(4,128)}) fusion(f32[128,32,512]{2,1,0:T(8,128)} %core_ref), kind=kLoop, calls=%fused_computation.125 | loop fusion | bytes 65536 | tf_op jit(solution)/shard_map/slice | solution.py:135
  93.2 0.6 copy-done.5
  93.8 1.3 collective-permute-start.14
  95.1 1.5 collective-permute-start.13
  96.7 2.7 %copy.69 = f32[128,32,4]{2,1,0:T(8,128)S(1)} copy(f32[128,32,4]{0,1,2:T(8,128)} %copy-done.5) | data formatting | bytes 131072 | tf_op jit(solution)/shard_map/ppermute | solution.py:134
  99.5 3.7 %copy.68 = f32[128,32,4]{2,1,0:T(8,128)} copy(f32[128,32,4]{0,1,2:T(8,128)} %collective-permute-done.7) | data formatting | bytes 131072 | tf_op jit(solution)/shard_map/ppermute | solution.py:133
  103.2 4.9 %collective-permute-start.11 = (f32[128,4,4]{2,1,0:T(4,128)}, f32[128,4,4]{2,1,0:T(4,128)S(1)}, u32[]{:S(2)}, u32[]{:S(2)}) collective-permute-start(f32[128,4,4]{2,1,0:T(4,128)} %get-tuple-element.31), channel_id=1, source_target_pairs={{1,16},{2,17},{3,18},{4,19},{5,20},{6,21},{7,22},{8,23},{9,24},{10... | collective-permute-start | bytes 24584 | tf_op jit(solution)/shard_map/ppermute | solution.py:136
  108.1 1.3 collective-permute-start.10
  109.4 3.6 %pad_maximum_fusion.lanes_ref = f32[128,32,128]{2,1,0:T(8,128)} fusion(f32[128,32,4]{2,1,0:T(8,128)S(1)} %copy.69, f32[128,32,4]{2,1,0:T(8,128)} %copy.68, f32[128]{0:T(128)S(1)} %pad.20.clone), kind=kLoop, calls=%fused_computation.4 | loop fusion | flops 1048576 | bytes 2228736 | tf_op jit(solution)/shard_map/concatenate | solution.py:140
  112.9 2.0 collective-permute-done.11
  114.9 5.7 %collective-permute-done.10 = f32[128,4,4]{2,1,0:T(4,128)S(1)} collective-permute-done((f32[128,4,4]{2,1,0:T(4,128)}, f32[128,4,4]{2,1,0:T(4,128)S(1)}, u32[]{:S(2)}, u32[]{:S(2)}) %collective-permute-start.10) | collective-permute-done | bytes 8224 | tf_op jit(solution)/shard_map/ppermute | solution.py:135
  120.7 4.2 %maximum_maximum_fusion.rows_ref = f32[128,8,640]{2,1,0:T(8,128)} fusion(f32[128,4,4]{2,1,0:T(4,128)S(1)} %collective-permute-done.14, f32[128,4,120]{2,1,0:T(4,128)S(1)} %broadcast_in_dim.54, f32[128,4,4]{2,1,0:T(4,128)} %collective-permute-done.13, f32[128,4,512]{2,1,0:T(4,128)} %collective-permute-done.12, f32[128,4,4]{2,1,0:T(4,128)S(1)} %collective-permute-done.11, ...), kind=kLoop, calls=%fused_computation.3 | loop fusion | flops 4587520 | bytes 4997120 | tf_op jit(solution)/shard_map/concatenate | solution.py:142
  125.0 59.3 %shard_map.111 = (f32[128,32,512]{2,1,0:T(8,128)}, f32[4,32,512]{2,1,0:T(8,128)}) custom-call(f32[128]{0:T(128)} %kappa_ref.1, f32[4,128]{1,0:T(4,128)} %weight_ref.1, f32[128,32,512]{2,1,0:T(8,128)} %core_ref, f32[128,32,128]{2,1,0:T(8,128)} %pad_maximum_fusion.lanes_ref, f32[128,8,640]{2,1,0:T(8,128)} %maximum_maximum_fusion.rows_ref, ...), custom_call_target="tpu_custom_call" | custom-call | flops 131072000 | bytes 16777216 | tf_op jit(solution)/shard_map/pallas_call | solution.py:160
  184.3 1.0 convert_element_type.40
  186.5 0.7 gather_fusion
  187.2 3.1 %collective-permute-done.15 = bf16[32,4,128]{2,1,0:T(4,128)(2,1)S(1)} collective-permute-done((bf16[32,4,128]{2,1,0:T(4,128)(2,1)S(1)}, bf16[32,4,128]{2,1,0:T(4,128)(2,1)S(1)}, u32[]{:S(2)}, u32[]{:S(2)}) %collective-permute-start.15) | collective-permute-done | bytes 32800 | tf_op jit(solution)/shard_map/ppermute | solution.py:29
  190.3 0.7 gather_fusion.2
  191.0 3.0 %convolution_bitcast_fusion = f32[4,32,128]{2,0,1:T(4,128)S(1)} fusion(bf16[32,4,128,128]{3,2,1,0:T(8,128)(2,1)} %param.13, bf16[32,4,4,128]{3,2,1,0:T(4,128)(2,1)S(1)} %bitcast.37, bf16[32,4,4,128]{3,2,1,0:T(4,128)(2,1)S(1)} %bitcast.38, pred[32,4]{1,0:T(8,128)(4,1)S(1)} %and.117, pred[32,4]{1,0:T(8,128)(4,1)S(1)} %and.113), kind=kOutput, calls=%fused_computation.5 | convolution fusion | flops 16908288 | bytes 4522240 | tf_op jit(solution)/shard_map/bkij,bkcj->cbi/dot_general | solution.py:357
  195.1 4.8 %collective-permute-done.16 = f32[1,16,256]{2,1,0:T(8,128)S(1)} collective-permute-done((f32[1,16,256]{2,1,0:T(8,128)S(1)}, f32[1,16,256]{2,1,0:T(8,128)S(1)}, u32[]{:S(2)}, u32[]{:S(2)}) %collective-permute-start.16) | collective-permute-done | bytes 16416 | tf_op jit(solution)/shard_map/ppermute | solution.py:61
  200.0 1.8 collective-permute-start.17
  201.8 3.6 %collective-permute-done.17 = f32[2,16,256]{2,1,0:T(8,128)S(1)} collective-permute-done((f32[2,16,256]{2,1,0:T(8,128)S(1)}, f32[2,16,256]{2,1,0:T(8,128)S(1)}, u32[]{:S(2)}, u32[]{:S(2)}) %collective-permute-start.17) | collective-permute-done | bytes 32800 | tf_op jit(solution)/shard_map/ppermute | solution.py:61
  205.4 3.8 %collective-permute-start.18 = (f32[4,16,256]{2,1,0:T(8,128)S(1)}, f32[4,16,256]{2,1,0:T(8,128)S(1)}, u32[]{:S(2)}, u32[]{:S(2)}) collective-permute-start(f32[4,16,256]{2,1,0:T(8,128)S(1)} %pad_maximum_fusion.4), channel_id=1, source_target_pairs={{0,64},{16,80},{32,96},{48,112},{64,0},{80,16},{96,32},{112,48},{1... | collective-permute-start | bytes 196616 | tf_op jit(solution)/shard_map/ppermute | solution.py:61
  209.8 1.6 collective-permute-done.18
  212.2 0.6 constant_dynamic-update-slice_fusion.40
  212.8 3.7 %collective-permute-done.19 = f32[8,16,256]{2,1,0:T(8,128)S(1)} collective-permute-done((f32[8,16,256]{2,1,0:T(8,128)S(1)}, f32[8,16,256]{2,1,0:T(8,128)S(1)}, u32[]{:S(2)}, u32[]{:S(2)}) %collective-permute-start.19) | collective-permute-done | bytes 131104 | tf_op jit(solution)/shard_map/ppermute | solution.py:61
  216.5 0.7 constant_dynamic-update-slice_fusion.39
  217.2 1.1 collective-permute-start.20
  218.3 5.3 %collective-permute-done.20 = f32[16,16,256]{2,1,0:T(8,128)S(1)} collective-permute-done((f32[16,16,256]{2,1,0:T(8,128)S(1)}, f32[16,16,256]{2,1,0:T(8,128)S(1)}, u32[]{:S(2)}, u32[]{:S(2)}) %collective-permute-start.20) | collective-permute-done | bytes 262176 | tf_op jit(solution)/shard_map/ppermute | solution.py:61
  223.6 0.8 constant_dynamic-update-slice_fusion.38
  224.4 2.3 collective-permute-start.21
  226.7 8.2 %collective-permute-done.21 = f32[32,16,256]{2,1,0:T(8,128)S(1)} collective-permute-done((f32[32,16,256]{2,1,0:T(8,128)S(1)}, f32[32,16,256]{2,1,0:T(8,128)S(1)}, u32[]{:S(2)}, u32[]{:S(2)}) %collective-permute-start.21) | collective-permute-done | bytes 524320 | tf_op jit(solution)/shard_map/ppermute | solution.py:61
  234.9 0.9 constant_dynamic-update-slice_fusion.37
  236.4 0.6 reshape.238
  237.0 1.6 collective-permute-done.22
  238.7 1.3 copy-done.3
  240.1 19.9 %shard_map.112 = (f32[16,256]{1,0:T(8,128)}, f32[16,256]{1,0:T(8,128)}) custom-call(s32[2]{0:T(128)} %pad_add_fusion.index_ref, f32[128,16,256]{2,1,0:T(8,128)} %copy-done.3, f32[128,16,256]{2,1,0:T(8,128)} %copy-done.2), custom_call_target="tpu_custom_call" | custom-call | tf_op jit(solution)/shard_map/pallas_call | solution.py:290
  (79 shorter events, 7.2 us)
Async XLA Ops:
  2.0 28.5 %collective-permute-start = (f32[1,16,256]{2,1,0:T(8,128)S(1)}, f32[1,16,256]{2,1,0:T(8,128)S(1)}, u32[]{:S(2)}, u32[]{:S(2)}) collective-permute-start(f32[1,16,256]{2,1,0:T(8,128)S(1)} %get-tuple-element.27), channel_id=1, source_target_pairs={{0,2},{1,3},{2,0},{3,1},{4,6},{5,7},{6,4},{7,5},{8,10},{9,11},{10,... | collective-permute-start | bytes 49160 | tf_op jit(solution)/shard_map/ppermute | solution.py:61
  10.3 82.9 %collective-permute-start.8 = (f32[128,32,4]{0,1,2:T(8,128)S(1)}, f32[128,32,4]{0,1,2:T(8,128)S(1)}, u32[]{:S(2)}, u32[]{:S(2)}) collective-permute-start(f32[128,32,4]{0,1,2:T(8,128)S(1)} %copy.86), channel_id=1, source_target_pairs={{0,16},{16,32},{32,48},{48,64},{64,80},{80,96},{96,112},{1,17},{17... | collective-permute-start | bytes 196616 | tf_op jit(solution)/shard_map/ppermute | solution.py:134
  13.7 12.5 %copy-start.4 = (s32[4096,4]{0,1:T(4,128)S(1)}, s32[4096,4]{0,1:T(4,128)}, u32[]{:S(2)}) copy-start(s32[4096,4]{0,1:T(4,128)} %param.11) | copy-start | bytes 196612
  13.7 81.4 %collective-permute-start.7 = (f32[128,32,4]{0,1,2:T(8,128)}, f32[128,32,4]{0,1,2:T(8,128)}, u32[]{:S(2)}, u32[]{:S(2)}) collective-permute-start(f32[128,32,4]{0,1,2:T(8,128)} %copy.85), channel_id=1, source_target_pairs={{16,0},{32,16},{48,32},{64,48},{80,64},{96,80},{112,96},{17,1},{33... | collective-permute-start | bytes 196616 | tf_op jit(solution)/shard_map/ppermute | solution.py:133
  19.2 101.4 %collective-permute-start.12 = (f32[128,4,512]{2,1,0:T(4,128)}, f32[128,4,512]{2,1,0:T(4,128)}, u32[]{:S(2)}, u32[]{:S(2)}) collective-permute-start(f32[128,4,512]{2,1,0:T(4,128)} %get-tuple-element.29), channel_id=1, source_target_pairs={{0,1},{1,2},{2,3},{3,4},{4,5},{5,6},{6,7},{7,8},{8,9},{9,10},{10,1... | collective-permute-start | bytes 3145736 | tf_op jit(solution)/shard_map/ppermute | solution.py:132
  24.2 96.4 %collective-permute-start.9 = (f32[128,4,512]{2,1,0:T(4,128)}, f32[128,4,512]{2,1,0:T(4,128)}, u32[]{:S(2)}, u32[]{:S(2)}) collective-permute-start(f32[128,4,512]{2,1,0:T(4,128)} %get-tuple-element.28), channel_id=1, source_target_pairs={{1,0},{2,1},{3,2},{4,3},{5,4},{6,5},{7,6},{8,7},{9,8},{10,9},{11,1... | collective-permute-start | bytes 3145736 | tf_op jit(solution)/shard_map/ppermute | solution.py:131
  26.2 2.5 copy-start.7
  30.5 5.5 %collective-permute-start.1 = (f32[2,16,256]{2,1,0:T(8,128)S(1)}, f32[2,16,256]{2,1,0:T(8,128)S(1)}, u32[]{:S(2)}, u32[]{:S(2)}) collective-permute-start(f32[2,16,256]{2,1,0:T(8,128)S(1)} %pad_maximum_fusion.5), channel_id=1, source_target_pairs={{0,8},{1,9},{2,10},{3,11},{4,12},{5,13},{6,14},{7,15},{8,0},{9,1},... | collective-permute-start | bytes 98312 | tf_op jit(solution)/shard_map/ppermute | solution.py:61
  36.0 8.9 %collective-permute-start.2 = (f32[4,16,256]{2,1,0:T(8,128)S(1)}, f32[4,16,256]{2,1,0:T(8,128)S(1)}, u32[]{:S(2)}, u32[]{:S(2)}) collective-permute-start(f32[4,16,256]{2,1,0:T(8,128)S(1)} %pad_maximum_fusion.3), channel_id=1, source_target_pairs={{0,64},{16,80},{32,96},{48,112},{64,0},{80,16},{96,32},{112,48},{1... | collective-permute-start | bytes 196616 | tf_op jit(solution)/shard_map/ppermute | solution.py:61
  45.0 5.5 %collective-permute-start.3 = (f32[8,16,256]{2,1,0:T(8,128)S(1)}, f32[8,16,256]{2,1,0:T(8,128)S(1)}, u32[]{:S(2)}, u32[]{:S(2)}) collective-permute-start(f32[8,16,256]{2,1,0:T(8,128)S(1)} %pad_maximum_fusion.1), channel_id=1, source_target_pairs={{0,1},{1,0},{2,3},{3,2},{4,5},{5,4},{6,7},{7,6},{8,9},{9,8},{10,11... | collective-permute-start | bytes 393224 | tf_op jit(solution)/shard_map/ppermute | solution.py:61
  51.3 24.6 %collective-permute-start.4 = (f32[16,16,256]{2,1,0:T(8,128)S(1)}, f32[16,16,256]{2,1,0:T(8,128)S(1)}, u32[]{:S(2)}, u32[]{:S(2)}) collective-permute-start(f32[16,16,256]{2,1,0:T(8,128)S(1)} %get-tuple-element.53), channel_id=1, source_target_pairs={{0,4},{1,5},{2,6},{3,7},{4,0},{5,1},{6,2},{7,3},{8,12},{9,13},{10,... | collective-permute-start | bytes 786440 | tf_op jit(solution)/shard_map/ppermute | solution.py:61
  76.7 11.7 %collective-permute-start.5 = (f32[32,16,256]{2,1,0:T(8,128)}, f32[32,16,256]{2,1,0:T(8,128)S(1)}, u32[]{:S(2)}, u32[]{:S(2)}) collective-permute-start(f32[32,16,256]{2,1,0:T(8,128)} %get-tuple-element.45), channel_id=1, source_target_pairs={{0,32},{16,48},{32,0},{48,16},{64,96},{80,112},{96,64},{112,80},{1... | collective-permute-start | bytes 1572872 | tf_op jit(solution)/shard_map/ppermute | solution.py:61
  89.4 7.3 %copy-start = (f32[128,16,256]{2,1,0:T(8,128)}, f32[128,16,256]{2,1,0:T(8,128)S(1)}, u32[]{:S(2)}) copy-start(f32[128,16,256]{2,1,0:T(8,128)S(1)} %get-tuple-element.39) | copy-start | bytes 6291460
  89.4 35.5 %collective-permute-start.6 = (f32[64,16,256]{2,1,0:T(8,128)}, f32[64,16,256]{2,1,0:T(8,128)S(1)}, u32[]{:S(2)}, u32[]{:S(2)}) collective-permute-start(f32[64,16,256]{2,1,0:T(8,128)} %get-tuple-element.38), channel_id=1, source_target_pairs={{0,16},{16,0},{32,48},{48,32},{64,80},{80,64},{96,112},{112,96},{1... | collective-permute-start | bytes 3145736 | tf_op jit(solution)/shard_map/ppermute | solution.py:61
  93.2 0.6 copy-start.5
  93.8 9.4 %collective-permute-start.14 = (f32[128,4,4]{2,1,0:T(4,128)}, f32[128,4,4]{2,1,0:T(4,128)S(1)}, u32[]{:S(2)}, u32[]{:S(2)}) collective-permute-start(f32[128,4,4]{2,1,0:T(4,128)} %get-tuple-element.32), channel_id=1, source_target_pairs={{0,17},{1,18},{2,19},{3,20},{4,21},{5,22},{6,23},{7,24},{8,25},{9,... | collective-permute-start | bytes 24584 | tf_op jit(solution)/shard_map/ppermute | solution.py:138
  95.1 12.9 %collective-permute-start.13 = (f32[128,4,4]{2,1,0:T(4,128)}, f32[128,4,4]{2,1,0:T(4,128)}, u32[]{:S(2)}, u32[]{:S(2)}) collective-permute-start(f32[128,4,4]{2,1,0:T(4,128)} %get-tuple-element.33), channel_id=1, source_target_pairs={{16,1},{17,2},{18,3},{19,4},{20,5},{21,6},{22,7},{23,8},{24,9},{25... | collective-permute-start | bytes 24584 | tf_op jit(solution)/shard_map/ppermute | solution.py:137
  103.2 11.7 %collective-permute-start.11 = (f32[128,4,4]{2,1,0:T(4,128)}, f32[128,4,4]{2,1,0:T(4,128)S(1)}, u32[]{:S(2)}, u32[]{:S(2)}) collective-permute-start(f32[128,4,4]{2,1,0:T(4,128)} %get-tuple-element.31), channel_id=1, source_target_pairs={{1,16},{2,17},{3,18},{4,19},{5,20},{6,21},{7,22},{8,23},{9,24},{10... | collective-permute-start | bytes 24584 | tf_op jit(solution)/shard_map/ppermute | solution.py:136
  108.1 12.5 %collective-permute-start.10 = (f32[128,4,4]{2,1,0:T(4,128)}, f32[128,4,4]{2,1,0:T(4,128)S(1)}, u32[]{:S(2)}, u32[]{:S(2)}) collective-permute-start(f32[128,4,4]{2,1,0:T(4,128)} %get-tuple-element.30), channel_id=1, source_target_pairs={{17,0},{18,1},{19,2},{20,3},{21,4},{22,5},{23,6},{24,7},{25,8},{26... | collective-permute-start | bytes 24584 | tf_op jit(solution)/shard_map/ppermute | solution.py:135
  120.6 4.2 %copy-start.1 = (f32[128,16,256]{2,1,0:T(8,128)S(1)}, f32[128,16,256]{2,1,0:T(8,128)}, u32[]{:S(2)}) copy-start(f32[128,16,256]{2,1,0:T(8,128)} %copy-done) | copy-start | bytes 6291460
  125.0 59.3 %copy-start.2 = (f32[128,16,256]{2,1,0:T(8,128)}, f32[128,16,256]{2,1,0:T(8,128)S(1)}, u32[]{:S(2)}) copy-start(f32[128,16,256]{2,1,0:T(8,128)S(1)} %constant_dynamic-update-slice_fusion.18.coded_stack) | copy-start | bytes 6291460
  186.2 4.1 %collective-permute-start.15 = (bf16[32,4,128]{2,1,0:T(4,128)(2,1)S(1)}, bf16[32,4,128]{2,1,0:T(4,128)(2,1)S(1)}, u32[]{:S(2)}, u32[]{:S(2)}) collective-permute-start(bf16[32,4,128]{2,1,0:T(4,128)(2,1)S(1)} %broadcast_multiply_fusion), channel_id=1, source_target_pairs={{0,112},{16,0},{32,16},{48,32},{64,48},{80,64},{96,80},{112,96},{1... | collective-permute-start | bytes 98312 | tf_op jit(solution)/shard_map/ppermute | solution.py:29
  191.0 3.1 %copy-start.6 = (s32[16,256]{1,0:T(8,128)S(1)}, s32[16,256]{1,0:T(8,128)}, u32[]{:S(2)}) copy-start(s32[16,256]{1,0:T(8,128)} %param.14) | copy-start | bytes 49156
  194.7 5.2 %collective-permute-start.16 = (f32[1,16,256]{2,1,0:T(8,128)S(1)}, f32[1,16,256]{2,1,0:T(8,128)S(1)}, u32[]{:S(2)}, u32[]{:S(2)}) collective-permute-start(f32[1,16,256]{2,1,0:T(8,128)S(1)} %get-tuple-element.19), channel_id=1, source_target_pairs={{0,2},{1,3},{2,0},{3,1},{4,6},{5,7},{6,4},{7,5},{8,10},{9,11},{10,... | collective-permute-start | bytes 49160 | tf_op jit(solution)/shard_map/ppermute | solution.py:61
  200.0 5.4 %collective-permute-start.17 = (f32[2,16,256]{2,1,0:T(8,128)S(1)}, f32[2,16,256]{2,1,0:T(8,128)S(1)}, u32[]{:S(2)}, u32[]{:S(2)}) collective-permute-start(f32[2,16,256]{2,1,0:T(8,128)S(1)} %pad_maximum_fusion.6), channel_id=1, source_target_pairs={{0,8},{1,9},{2,10},{3,11},{4,12},{5,13},{6,14},{7,15},{8,0},{9,1},... | collective-permute-start | bytes 98312 | tf_op jit(solution)/shard_map/ppermute | solution.py:61
  205.4 6.0 %collective-permute-start.18 = (f32[4,16,256]{2,1,0:T(8,128)S(1)}, f32[4,16,256]{2,1,0:T(8,128)S(1)}, u32[]{:S(2)}, u32[]{:S(2)}) collective-permute-start(f32[4,16,256]{2,1,0:T(8,128)S(1)} %pad_maximum_fusion.4), channel_id=1, source_target_pairs={{0,64},{16,80},{32,96},{48,112},{64,0},{80,16},{96,32},{112,48},{1... | collective-permute-start | bytes 196616 | tf_op jit(solution)/shard_map/ppermute | solution.py:61
  211.5 5.0 %collective-permute-start.19 = (f32[8,16,256]{2,1,0:T(8,128)S(1)}, f32[8,16,256]{2,1,0:T(8,128)S(1)}, u32[]{:S(2)}, u32[]{:S(2)}) collective-permute-start(f32[8,16,256]{2,1,0:T(8,128)S(1)} %pad_maximum_fusion.2), channel_id=1, source_target_pairs={{0,1},{1,0},{2,3},{3,2},{4,5},{5,4},{6,7},{7,6},{8,9},{9,8},{10,11... | collective-permute-start | bytes 393224 | tf_op jit(solution)/shard_map/ppermute | solution.py:61
  217.2 6.4 %collective-permute-start.20 = (f32[16,16,256]{2,1,0:T(8,128)S(1)}, f32[16,16,256]{2,1,0:T(8,128)S(1)}, u32[]{:S(2)}, u32[]{:S(2)}) collective-permute-start(f32[16,16,256]{2,1,0:T(8,128)S(1)} %get-tuple-element.49), channel_id=1, source_target_pairs={{0,4},{1,5},{2,6},{3,7},{4,0},{5,1},{6,2},{7,3},{8,12},{9,13},{10,... | collective-permute-start | bytes 786440 | tf_op jit(solution)/shard_map/ppermute | solution.py:61
  224.4 10.5 %collective-permute-start.21 = (f32[32,16,256]{2,1,0:T(8,128)S(1)}, f32[32,16,256]{2,1,0:T(8,128)S(1)}, u32[]{:S(2)}, u32[]{:S(2)}) collective-permute-start(f32[32,16,256]{2,1,0:T(8,128)S(1)} %get-tuple-element.42), channel_id=1, source_target_pairs={{0,32},{16,48},{32,0},{48,16},{64,96},{80,112},{96,64},{112,80},{1... | collective-permute-start | bytes 1572872 | tf_op jit(solution)/shard_map/ppermute | solution.py:61
  235.8 2.9 %collective-permute-start.22 = (f32[64,16,256]{2,1,0:T(8,128)}, f32[64,16,256]{2,1,0:T(8,128)S(1)}, u32[]{:S(2)}, u32[]{:S(2)}) collective-permute-start(f32[64,16,256]{2,1,0:T(8,128)} %get-tuple-element.36), channel_id=1, source_target_pairs={{0,16},{16,0},{32,48},{48,32},{64,80},{80,64},{96,112},{112,96},{1... | collective-permute-start | bytes 3145736 | tf_op jit(solution)/shard_map/ppermute | solution.py:61
  238.7 1.3 copy-start.3

commit v10 on v8

--- a/solution.py
+++ b/solution.py
@@ -107,7 +107,7 @@
             flux_ref[c] += weight_ref[c, lev] * core
         return carry
 
-    lax.fori_loop(0, levels, level, 0, unroll=2)
+    lax.fori_loop(0, levels, level, 0, unroll=4)
 
 
 def diffuse(field, atm_kappa, vert_weight):
@@ -214,7 +214,7 @@
         coded_ref[pl.ds(r0, tile_rows), pl.ds(c0, tile_cols)] = coded_stack[k]
         return carry
 
-    lax.fori_loop(0, rhs_stack.shape[0], place, 0)
+    lax.fori_loop(0, rhs_stack.shape[0], place, 0, unroll=4)
     strips = rows // 8
     zeros = jnp.zeros((8, cols), jnp.float32)
     pad_ref[0:8, :] = zeros
@@ -250,9 +250,9 @@
         img_ref[at(k), :] = w
         return acc + v * w
 
-    norm_now = strip_sum(lax.fori_loop(0, strips, init, zeros))
+    norm_now = strip_sum(lax.fori_loop(0, strips, init, zeros, unroll=4))
     for step in range(ITERS):
-        alpha = norm_now / strip_sum(lax.fori_loop(0, strips, image, zeros))
+        alpha = norm_now / strip_sum(lax.fori_loop(0, strips, image, zeros, unroll=4))
 
         def update(k, acc):
             v = dir_ref[at(k), :]
@@ -261,7 +261,7 @@
             residual_ref[at(k), :] = r
             return acc + r * r
 
-        norm_next = strip_sum(lax.fori_loop(0, strips, update, zeros))
+        norm_next = strip_sum(lax.fori_loop(0, strips, update, zeros, unroll=4))
         beta = norm_next / norm_now
 
         def direct(k, carry):
@@ -272,7 +272,7 @@
             return carry
 
         if step < ITERS - 1:
-            lax.fori_loop(0, strips, direct, 0)
+            lax.fori_loop(0, strips, direct, 0, unroll=4)
         norm_now = norm_next
     r0 = pl.multiple_of(gy * tile_rows, tile_rows)
     c0 = pl.multiple_of(gx * tile_cols, tile_cols)

time: 222 us -> 215 us (0.968)
  Pallas kernels: 78.5 us -> 71.1 us
    pallas_call x1, Pallas kernels: 19.9 us -> 13.5 us  [solve_grid(): pl.pallas_call(functools.partial(cg_kernel, rounds), in_specs=[pl.BlockSp...]
  transfers between devices with their start and end apart: 23 -> 23, of which waited for: 13 -> 13; matrix products, arithmetic and copies ran while one was open for 16% -> 17% of each run, Pallas kernels for 0% -> 0%
where the time goes in v10:
time: 215 us; the launch traced here: 212 us
  Pallas kernels  71.1 us (33%)
  starting transfers between devices  43.5 us (20%)
  local copies, waits for them, and re-layouts  40.5 us (19%)
  waiting for transfers between devices  40.3 us (19%)
  other arithmetic  13.1 us (6%)
  matrix products  3.04 us (1%)
    pallas_call x1, Pallas kernels, diffuse(): pl.pallas_call(diffusion_kernel, grid=(blocks,), in_specs=[smem, smem, pl...  57.5 us
    ppermute x14, waiting for transfers between devices, stack_gather(): other = lax.ppermute(x, axis, [(j, j ^ distance) for j in range(size)])  24.2 us
    ppermute x14, starting transfers between devices, stack_gather(): other = lax.ppermute(x, axis, [(j, j ^ distance) for j in range(size)])  20.9 us
    unnamed x27, local copies, waits for them, and re-layouts  13.8 us
    pallas_call x1, Pallas kernels, solve_grid(): pl.pallas_call(functools.partial(cg_kernel, rounds), in_specs=[pl.BlockSp...  13.5 us
    ppermute x1, waiting for transfers between devices, diffuse(): south_east = lax.ppermute(field[:, :HALO, :HALO], both, pairs(1, 1))  7.07 us
    ppermute x1, starting transfers between devices, diffuse(): lax.ppermute(field[:, rows - HALO:, cols - HALO:], both, pairs(-1, -1))  5.35 us
    ppermute x1, starting transfers between devices, diffuse(): south_west = lax.ppermute(field[:, :HALO, cols - HALO:], both, pairs(-1, 1))  4.98 us
  transfers between devices with their start and end apart: 23, of which 13 were waited for; matrix products, arithmetic and copies ran while one was open for 17% of the time, Pallas kernels for 0%

profile of v10, /device:TPU:6, one launch (start us, length us, event | category | flops | bytes accessed | tf_op | source)
XLA Modules:
  0.0 212.5 jit_solution(1629028649152784604)
XLA Ops:
  0.6 4.3 %fusion.26 = (f32[128,32,4]{2,1,0:T(8,128)S(1)}, f32[128,32,4]{2,1,0:T(8,128)}) fusion(f32[128,32,512]{2,1,0:T(8,128)} %core_ref.1), kind=kLoop, calls=%fused_computation.126 | loop fusion | bytes 262144 | tf_op jit(solution)/shard_map/slice | solution.py:133
  4.9 3.3 %copy.86 = f32[128,32,4]{0,1,2:T(8,128)} copy(f32[128,32,4]{2,1,0:T(8,128)} %get-tuple-element.31) | data formatting | bytes 131072
  8.2 2.4 %collective-permute-start.1 = (f32[128,32,4]{0,1,2:T(8,128)}, f32[128,32,4]{0,1,2:T(8,128)}, u32[]{:S(2)}, u32[]{:S(2)}) collective-permute-start(f32[128,32,4]{0,1,2:T(8,128)} %copy.86), channel_id=1, source_target_pairs={{0,16},{16,32},{32,48},{48,64},{64,80},{80,96},{96,112},{1,17},{17... | collective-permute-start | bytes 196616 | tf_op jit(solution)/shard_map/ppermute | solution.py:134
  10.5 1.9 copy.85
  12.5 1.3 collective-permute-start
  13.8 2.9 %fusion.25 = (f32[128,4,4]{2,1,0:T(4,128)}, f32[128,4,4]{2,1,0:T(4,128)}, f32[128,4,4]{2,1,0:T(4,128)}, f32[128,4,4]{2,1,0:T(4,128)}) fusion(f32[128,32,512]{2,1,0:T(8,128)} %core_ref.1), kind=kLoop, calls=%fused_computation.125 | loop fusion | bytes 65536 | tf_op jit(solution)/shard_map/slice | solution.py:135
  16.6 5.3 %collective-permute-start.7 = (f32[128,4,4]{2,1,0:T(4,128)}, f32[128,4,4]{2,1,0:T(4,128)S(1)}, u32[]{:S(2)}, u32[]{:S(2)}) collective-permute-start(f32[128,4,4]{2,1,0:T(4,128)} %get-tuple-element.29), channel_id=1, source_target_pairs={{0,17},{1,18},{2,19},{3,20},{4,21},{5,22},{6,23},{7,24},{8,25},{9,... | collective-permute-start | bytes 24584 | tf_op jit(solution)/shard_map/ppermute | solution.py:138
  22.0 4.1 %fusion.24 = (f32[128,4,512]{2,1,0:T(4,128)}, f32[128,4,512]{2,1,0:T(4,128)}) fusion(f32[128,32,512]{2,1,0:T(8,128)} %core_ref.1), kind=kLoop, calls=%fused_computation.124 | loop fusion | bytes 4194304 | tf_op jit(solution)/shard_map/slice | solution.py:131
  26.1 3.4 %collective-permute-start.5 = (f32[128,4,512]{2,1,0:T(4,128)}, f32[128,4,512]{2,1,0:T(4,128)S(1)}, u32[]{:S(2)}, u32[]{:S(2)}) collective-permute-start(f32[128,4,512]{2,1,0:T(4,128)} %get-tuple-element.25), channel_id=1, source_target_pairs={{0,1},{1,2},{2,3},{3,4},{4,5},{5,6},{6,7},{7,8},{8,9},{9,10},{10,1... | collective-permute-start | bytes 3145736 | tf_op jit(solution)/shard_map/ppermute | solution.py:132
  29.5 2.4 %collective-permute-start.2 = (f32[128,4,512]{2,1,0:T(4,128)}, f32[128,4,512]{2,1,0:T(4,128)}, u32[]{:S(2)}, u32[]{:S(2)}) collective-permute-start(f32[128,4,512]{2,1,0:T(4,128)} %get-tuple-element.24), channel_id=1, source_target_pairs={{1,0},{2,1},{3,2},{4,3},{5,4},{6,5},{7,6},{8,7},{9,8},{10,9},{11,1... | collective-permute-start | bytes 3145736 | tf_op jit(solution)/shard_map/ppermute | solution.py:131
  32.5 0.6 copy.71
  33.2 1.6 reshape.236
  37.0 1.4 and_convert_fusion.mask_ref
  38.5 1.3 collective-permute-start.6
  39.7 2.7 %copy.69 = f32[128,32,4]{2,1,0:T(8,128)S(1)} copy(f32[128,32,4]{0,1,2:T(8,128)} %collective-permute-done.1) | data formatting | bytes 131072 | tf_op jit(solution)/shard_map/ppermute | solution.py:134
  42.5 5.0 %collective-permute-start.4 = (f32[128,4,4]{2,1,0:T(4,128)}, f32[128,4,4]{2,1,0:T(4,128)}, u32[]{:S(2)}, u32[]{:S(2)}) collective-permute-start(f32[128,4,4]{2,1,0:T(4,128)} %get-tuple-element.27), channel_id=1, source_target_pairs={{1,16},{2,17},{3,18},{4,19},{5,20},{6,21},{7,22},{8,23},{9,24},{10... | collective-permute-start | bytes 24584 | tf_op jit(solution)/shard_map/ppermute | solution.py:136
  47.5 2.9 %copy.68 = f32[128,32,4]{2,1,0:T(8,128)} copy(f32[128,32,4]{0,1,2:T(8,128)S(1)} %collective-permute-done) | data formatting | bytes 131072 | tf_op jit(solution)/shard_map/ppermute | solution.py:133
  50.3 1.5 collective-permute-start.3
  51.8 3.5 %pad_maximum_fusion.lanes_ref = f32[128,32,128]{2,1,0:T(8,128)} fusion(f32[128,32,4]{2,1,0:T(8,128)S(1)} %copy.69, f32[128,32,4]{2,1,0:T(8,128)} %copy.68, f32[128]{0:T(128)S(1)} %pad.29.clone), kind=kLoop, calls=%fused_computation.4 | loop fusion | flops 1048576 | bytes 2228736 | tf_op jit(solution)/shard_map/concatenate | solution.py:140
  55.3 1.8 collective-permute-done.6
  57.1 4.0 %collective-permute-done.4 = f32[128,4,4]{2,1,0:T(4,128)} collective-permute-done((f32[128,4,4]{2,1,0:T(4,128)}, f32[128,4,4]{2,1,0:T(4,128)}, u32[]{:S(2)}, u32[]{:S(2)}) %collective-permute-start.4) | collective-permute-done | bytes 8224 | tf_op jit(solution)/shard_map/ppermute | solution.py:136
  61.1 7.1 %collective-permute-done.3 = f32[128,4,4]{2,1,0:T(4,128)S(1)} collective-permute-done((f32[128,4,4]{2,1,0:T(4,128)}, f32[128,4,4]{2,1,0:T(4,128)S(1)}, u32[]{:S(2)}, u32[]{:S(2)}) %collective-permute-start.3) | collective-permute-done | bytes 8224 | tf_op jit(solution)/shard_map/ppermute | solution.py:135
  68.2 3.9 %maximum_maximum_fusion.rows_ref = f32[128,8,640]{2,1,0:T(8,128)} fusion(f32[128,4,4]{2,1,0:T(4,128)S(1)} %collective-permute-done.7, f32[128,4,120]{2,1,0:T(4,128)S(1)} %broadcast_in_dim.52, f32[128,4,4]{2,1,0:T(4,128)} %collective-permute-done.6, f32[128,4,512]{2,1,0:T(4,128)S(1)} %collective-permute-done.5, f32[128,4,4]{2,1,0:T(4,128)} %collective-permute-done.4, ...), kind=kLoop, calls=%fused_computation.3 | loop fusion | flops 4587520 | bytes 4997120 | tf_op jit(solution)/shard_map/concatenate | solution.py:142
  72.1 57.5 %shard_map.111 = (f32[128,32,512]{2,1,0:T(8,128)}, f32[4,32,512]{2,1,0:T(8,128)}) custom-call(f32[128]{0:T(128)} %kappa_ref.1, f32[4,128]{1,0:T(4,128)} %weight_ref.1, f32[128,32,512]{2,1,0:T(8,128)} %core_ref.1, f32[128,32,128]{2,1,0:T(8,128)} %pad_maximum_fusion.lanes_ref, f32[128,8,640]{2,1,0:T(8,128)} %maximum_maximum_fusion.rows_ref, ...), custom_call_target="tpu_custom_call" | custom-call | flops 131072000 | bytes 16777216 | tf_op jit(solution)/shard_map/pallas_call | solution.py:160
  129.6 1.0 convert_element_type.40
  130.8 0.6 gather_fusion.1
  131.8 0.7 gather_fusion
  132.5 3.3 %collective-permute-done.8 = bf16[32,4,128]{2,1,0:T(4,128)(2,1)S(1)} collective-permute-done((bf16[32,4,128]{2,1,0:T(4,128)(2,1)S(1)}, bf16[32,4,128]{2,1,0:T(4,128)(2,1)S(1)}, u32[]{:S(2)}, u32[]{:S(2)}) %collective-permute-start.8) | collective-permute-done | bytes 32800 | tf_op jit(solution)/shard_map/ppermute | solution.py:29
  135.9 0.7 gather_fusion.2
  136.6 3.0 %convolution_bitcast_fusion = f32[4,32,128]{2,0,1:T(4,128)S(1)} fusion(bf16[32,4,128,128]{3,2,1,0:T(8,128)(2,1)} %param.13, bf16[32,4,4,128]{3,2,1,0:T(4,128)(2,1)S(1)} %bitcast.37, bf16[32,4,4,128]{3,2,1,0:T(4,128)(2,1)S(1)} %bitcast.38, pred[32,4]{1,0:T(8,128)(4,1)S(1)} %and.117, pred[32,4]{1,0:T(8,128)(4,1)S(1)} %and.113), kind=kOutput, calls=%fused_computation.5 | convolution fusion | flops 16908288 | bytes 4522240 | tf_op jit(solution)/shard_map/bkij,bkcj->cbi/dot_general | solution.py:356
  139.8 0.6 constant_dynamic-update-slice_fusion.43
  140.4 3.5 %collective-permute-start.16 = (f32[1,16,256]{2,1,0:T(8,128)S(1)}, f32[1,16,256]{2,1,0:T(8,128)S(1)}, u32[]{:S(2)}, u32[]{:S(2)}) collective-permute-start(f32[1,16,256]{2,1,0:T(8,128)S(1)} %get-tuple-element.15), channel_id=1, source_target_pairs={{0,2},{1,3},{2,0},{3,1},{4,6},{5,7},{6,4},{7,5},{8,10},{9,11},{10,... | collective-permute-start | bytes 49160 | tf_op jit(solution)/shard_map/ppermute | solution.py:61
  143.9 1.7 collective-permute-done.9
  145.6 2.9 %collective-permute-start.10 = (f32[2,16,256]{2,1,0:T(8,128)S(1)}, f32[2,16,256]{2,1,0:T(8,128)S(1)}, u32[]{:S(2)}, u32[]{:S(2)}) collective-permute-start(f32[2,16,256]{2,1,0:T(8,128)S(1)} %pad_maximum_fusion.5), channel_id=1, source_target_pairs={{0,8},{1,9},{2,10},{3,11},{4,12},{5,13},{6,14},{7,15},{8,0},{9,1},... | collective-permute-start | bytes 98312 | tf_op jit(solution)/shard_map/ppermute | solution.py:61
  148.5 0.6 collective-permute-start.17
  149.2 0.6 constant_dynamic-update-slice_fusion.16
  149.8 0.6 constant_dynamic-update-slice_fusion.42
  150.4 0.7 collective-permute-done.10
  151.1 4.4 %collective-permute-start.11 = (f32[4,16,256]{2,1,0:T(8,128)S(1)}, f32[4,16,256]{2,1,0:T(8,128)S(1)}, u32[]{:S(2)}, u32[]{:S(2)}) collective-permute-start(f32[4,16,256]{2,1,0:T(8,128)S(1)} %pad_maximum_fusion.3), channel_id=1, source_target_pairs={{0,64},{16,80},{32,96},{48,112},{64,0},{80,16},{96,32},{112,48},{1... | collective-permute-start | bytes 196616 | tf_op jit(solution)/shard_map/ppermute | solution.py:61
  155.5 2.7 %collective-permute-start.18 = (f32[4,16,256]{2,1,0:T(8,128)S(1)}, f32[4,16,256]{2,1,0:T(8,128)S(1)}, u32[]{:S(2)}, u32[]{:S(2)}) collective-permute-start(f32[4,16,256]{2,1,0:T(8,128)S(1)} %pad_maximum_fusion.4), channel_id=1, source_target_pairs={{0,64},{16,80},{32,96},{48,112},{64,0},{80,16},{96,32},{112,48},{1... | collective-permute-start | bytes 196616 | tf_op jit(solution)/shard_map/ppermute | solution.py:61
  158.2 0.6 constant_dynamic-update-slice_fusion.15
  158.8 0.6 constant_dynamic-update-slice_fusion.41
  159.5 1.8 collective-permute-done.18
  161.6 0.6 constant_dynamic-update-slice_fusion.14
  162.2 2.2 %collective-permute-done.12 = f32[8,16,256]{2,1,0:T(8,128)S(1)} collective-permute-done((f32[8,16,256]{2,1,0:T(8,128)S(1)}, f32[8,16,256]{2,1,0:T(8,128)S(1)}, u32[]{:S(2)}, u32[]{:S(2)}) %collective-permute-start.12) | collective-permute-done | bytes 131104 | tf_op jit(solution)/shard_map/ppermute | solution.py:61
  164.4 0.7 constant_dynamic-update-slice_fusion.13
  165.7 0.6 constant_dynamic-update-slice_fusion.40
  166.4 0.7 constant_dynamic-update-slice_fusion.39
  167.1 1.4 collective-permute-start.20
  168.5 3.8 %collective-permute-done.13 = f32[16,16,256]{2,1,0:T(8,128)S(1)} collective-permute-done((f32[16,16,256]{2,1,0:T(8,128)S(1)}, f32[16,16,256]{2,1,0:T(8,128)S(1)}, u32[]{:S(2)}, u32[]{:S(2)}) %collective-permute-start.13) | collective-permute-done | bytes 262176 | tf_op jit(solution)/shard_map/ppermute | solution.py:61
  172.3 0.8 constant_dynamic-update-slice_fusion.12
  173.1 2.4 %collective-permute-start.14 = (f32[32,16,256]{2,1,0:T(8,128)S(1)}, f32[32,16,256]{2,1,0:T(8,128)S(1)}, u32[]{:S(2)}, u32[]{:S(2)}) collective-permute-start(f32[32,16,256]{2,1,0:T(8,128)S(1)} %get-tuple-element.41), channel_id=1, source_target_pairs={{0,32},{16,48},{32,0},{48,16},{64,96},{80,112},{96,64},{112,80},{1... | collective-permute-start | bytes 1572872 | tf_op jit(solution)/shard_map/ppermute | solution.py:61
  175.5 0.8 constant_dynamic-update-slice_fusion.38
  176.3 2.0 collective-permute-start.21
  178.3 8.5 %collective-permute-done.14 = f32[32,16,256]{2,1,0:T(8,128)S(1)} collective-permute-done((f32[32,16,256]{2,1,0:T(8,128)S(1)}, f32[32,16,256]{2,1,0:T(8,128)S(1)}, u32[]{:S(2)}, u32[]{:S(2)}) %collective-permute-start.14) | collective-permute-done | bytes 524320 | tf_op jit(solution)/shard_map/ppermute | solution.py:61
  186.8 0.9 constant_dynamic-update-slice_fusion.11
  187.7 4.7 %collective-permute-done.21 = f32[32,16,256]{2,1,0:T(8,128)S(1)} collective-permute-done((f32[32,16,256]{2,1,0:T(8,128)S(1)}, f32[32,16,256]{2,1,0:T(8,128)S(1)}, u32[]{:S(2)}, u32[]{:S(2)}) %collective-permute-start.21) | collective-permute-done | bytes 524320 | tf_op jit(solution)/shard_map/ppermute | solution.py:61
  192.4 0.9 constant_dynamic-update-slice_fusion.37
  193.9 0.6 reshape.238
  194.6 1.1 constant_dynamic-update-slice_fusion.18.rhs_stack
  195.6 0.7 collective-permute-done.22
  196.3 1.3 constant_dynamic-update-slice_fusion.44.coded_stack
  197.6 1.3 copy-done
  198.9 13.5 %shard_map.112 = (f32[16,256]{1,0:T(8,128)}, f32[16,256]{1,0:T(8,128)}) custom-call(s32[2]{0:T(128)} %pad_add_fusion.index_ref, f32[128,16,256]{2,1,0:T(8,128)} %constant_dynamic-update-slice_fusion.18.rhs_stack, f32[128,16,256]{2,1,0:T(8,128)} %copy-done), custom_call_target="tpu_custom_call" | custom-call | tf_op jit(solution)/shard_map/pallas_call | solution.py:290
  (74 shorter events, 5.0 us)
Async XLA Ops:
  8.2 30.3 %collective-permute-start.1 = (f32[128,32,4]{0,1,2:T(8,128)}, f32[128,32,4]{0,1,2:T(8,128)}, u32[]{:S(2)}, u32[]{:S(2)}) collective-permute-start(f32[128,32,4]{0,1,2:T(8,128)} %copy.86), channel_id=1, source_target_pairs={{0,16},{16,32},{32,48},{48,64},{64,80},{80,96},{96,112},{1,17},{17... | collective-permute-start | bytes 196616 | tf_op jit(solution)/shard_map/ppermute | solution.py:134
  12.5 30.0 %collective-permute-start = (f32[128,32,4]{0,1,2:T(8,128)}, f32[128,32,4]{0,1,2:T(8,128)S(1)}, u32[]{:S(2)}, u32[]{:S(2)}) collective-permute-start(f32[128,32,4]{0,1,2:T(8,128)} %copy.85), channel_id=1, source_target_pairs={{16,0},{32,16},{48,32},{64,48},{80,64},{96,80},{112,96},{17,1},{33... | collective-permute-start | bytes 196616 | tf_op jit(solution)/shard_map/ppermute | solution.py:133
  16.6 15.9 %copy-start.2 = (s32[4096,4]{0,1:T(4,128)S(1)}, s32[4096,4]{0,1:T(4,128)}, u32[]{:S(2)}) copy-start(s32[4096,4]{0,1:T(4,128)} %param.11) | copy-start | bytes 196612
  16.6 33.7 %collective-permute-start.7 = (f32[128,4,4]{2,1,0:T(4,128)}, f32[128,4,4]{2,1,0:T(4,128)S(1)}, u32[]{:S(2)}, u32[]{:S(2)}) collective-permute-start(f32[128,4,4]{2,1,0:T(4,128)} %get-tuple-element.29), channel_id=1, source_target_pairs={{0,17},{1,18},{2,19},{3,20},{4,21},{5,22},{6,23},{7,24},{8,25},{9,... | collective-permute-start | bytes 24584 | tf_op jit(solution)/shard_map/ppermute | solution.py:138
  26.1 42.1 %collective-permute-start.5 = (f32[128,4,512]{2,1,0:T(4,128)}, f32[128,4,512]{2,1,0:T(4,128)S(1)}, u32[]{:S(2)}, u32[]{:S(2)}) collective-permute-start(f32[128,4,512]{2,1,0:T(4,128)} %get-tuple-element.25), channel_id=1, source_target_pairs={{0,1},{1,2},{2,3},{3,4},{4,5},{5,6},{6,7},{7,8},{8,9},{9,10},{10,1... | collective-permute-start | bytes 3145736 | tf_op jit(solution)/shard_map/ppermute | solution.py:132
  29.5 38.7 %collective-permute-start.2 = (f32[128,4,512]{2,1,0:T(4,128)}, f32[128,4,512]{2,1,0:T(4,128)}, u32[]{:S(2)}, u32[]{:S(2)}) collective-permute-start(f32[128,4,512]{2,1,0:T(4,128)} %get-tuple-element.24), channel_id=1, source_target_pairs={{1,0},{2,1},{3,2},{4,3},{5,4},{6,5},{7,6},{8,7},{9,8},{10,9},{11,1... | collective-permute-start | bytes 3145736 | tf_op jit(solution)/shard_map/ppermute | solution.py:131
  32.5 2.5 %copy-start.3 = (s32[4096]{0:T(1024)S(1)}, s32[4096]{0:T(1024)}, u32[]{:S(2)}) copy-start(s32[4096]{0:T(1024)} %param.12) | copy-start | bytes 49156
  38.5 18.7 %collective-permute-start.6 = (f32[128,4,4]{2,1,0:T(4,128)}, f32[128,4,4]{2,1,0:T(4,128)}, u32[]{:S(2)}, u32[]{:S(2)}) collective-permute-start(f32[128,4,4]{2,1,0:T(4,128)} %get-tuple-element.28), channel_id=1, source_target_pairs={{16,1},{17,2},{18,3},{19,4},{20,5},{21,6},{22,7},{23,8},{24,9},{25... | collective-permute-start | bytes 24584 | tf_op jit(solution)/shard_map/ppermute | solution.py:137
  42.5 18.6 %collective-permute-start.4 = (f32[128,4,4]{2,1,0:T(4,128)}, f32[128,4,4]{2,1,0:T(4,128)}, u32[]{:S(2)}, u32[]{:S(2)}) collective-permute-start(f32[128,4,4]{2,1,0:T(4,128)} %get-tuple-element.27), channel_id=1, source_target_pairs={{1,16},{2,17},{3,18},{4,19},{5,20},{6,21},{7,22},{8,23},{9,24},{10... | collective-permute-start | bytes 24584 | tf_op jit(solution)/shard_map/ppermute | solution.py:136
  50.3 17.8 %collective-permute-start.3 = (f32[128,4,4]{2,1,0:T(4,128)}, f32[128,4,4]{2,1,0:T(4,128)S(1)}, u32[]{:S(2)}, u32[]{:S(2)}) collective-permute-start(f32[128,4,4]{2,1,0:T(4,128)} %get-tuple-element.26), channel_id=1, source_target_pairs={{17,0},{18,1},{19,2},{20,3},{21,4},{22,5},{23,6},{24,7},{25,8},{26... | collective-permute-start | bytes 24584 | tf_op jit(solution)/shard_map/ppermute | solution.py:135
  131.5 4.4 %collective-permute-start.8 = (bf16[32,4,128]{2,1,0:T(4,128)(2,1)S(1)}, bf16[32,4,128]{2,1,0:T(4,128)(2,1)S(1)}, u32[]{:S(2)}, u32[]{:S(2)}) collective-permute-start(bf16[32,4,128]{2,1,0:T(4,128)(2,1)S(1)} %broadcast_multiply_fusion), channel_id=1, source_target_pairs={{0,112},{16,0},{32,16},{48,32},{64,48},{80,64},{96,80},{112,96},{1... | collective-permute-start | bytes 98312 | tf_op jit(solution)/shard_map/ppermute | solution.py:29
  136.6 3.1 %copy-start.4 = (f32[16,256]{1,0:T(8,128)S(1)}, f32[16,256]{1,0:T(8,128)}, u32[]{:S(2)}) copy-start(f32[16,256]{1,0:T(8,128)} %param.15) | copy-start | bytes 49156
  136.6 3.1 %copy-start.5 = (s32[16,256]{1,0:T(8,128)S(1)}, s32[16,256]{1,0:T(8,128)}, u32[]{:S(2)}) copy-start(s32[16,256]{1,0:T(8,128)} %param.14) | copy-start | bytes 49156
  140.4 5.2 %collective-permute-start.9 = (f32[1,16,256]{2,1,0:T(8,128)S(1)}, f32[1,16,256]{2,1,0:T(8,128)S(1)}, u32[]{:S(2)}, u32[]{:S(2)}) collective-permute-start(f32[1,16,256]{2,1,0:T(8,128)S(1)} %get-tuple-element.80), channel_id=1, source_target_pairs={{0,2},{1,3},{2,0},{3,1},{4,6},{5,7},{6,4},{7,5},{8,10},{9,11},{10,... | collective-permute-start | bytes 49160 | tf_op jit(solution)/shard_map/ppermute | solution.py:61
  140.4 8.1 %collective-permute-start.16 = (f32[1,16,256]{2,1,0:T(8,128)S(1)}, f32[1,16,256]{2,1,0:T(8,128)S(1)}, u32[]{:S(2)}, u32[]{:S(2)}) collective-permute-start(f32[1,16,256]{2,1,0:T(8,128)S(1)} %get-tuple-element.15), channel_id=1, source_target_pairs={{0,2},{1,3},{2,0},{3,1},{4,6},{5,7},{6,4},{7,5},{8,10},{9,11},{10,... | collective-permute-start | bytes 49160 | tf_op jit(solution)/shard_map/ppermute | solution.py:61
  145.6 5.4 %collective-permute-start.10 = (f32[2,16,256]{2,1,0:T(8,128)S(1)}, f32[2,16,256]{2,1,0:T(8,128)S(1)}, u32[]{:S(2)}, u32[]{:S(2)}) collective-permute-start(f32[2,16,256]{2,1,0:T(8,128)S(1)} %pad_maximum_fusion.5), channel_id=1, source_target_pairs={{0,8},{1,9},{2,10},{3,11},{4,12},{5,13},{6,14},{7,15},{8,0},{9,1},... | collective-permute-start | bytes 98312 | tf_op jit(solution)/shard_map/ppermute | solution.py:61
  148.5 6.9 %collective-permute-start.17 = (f32[2,16,256]{2,1,0:T(8,128)S(1)}, f32[2,16,256]{2,1,0:T(8,128)S(1)}, u32[]{:S(2)}, u32[]{:S(2)}) collective-permute-start(f32[2,16,256]{2,1,0:T(8,128)S(1)} %pad_maximum_fusion.6), channel_id=1, source_target_pairs={{0,8},{1,9},{2,10},{3,11},{4,12},{5,13},{6,14},{7,15},{8,0},{9,1},... | collective-permute-start | bytes 98312 | tf_op jit(solution)/shard_map/ppermute | solution.py:61
  151.1 8.3 %collective-permute-start.11 = (f32[4,16,256]{2,1,0:T(8,128)S(1)}, f32[4,16,256]{2,1,0:T(8,128)S(1)}, u32[]{:S(2)}, u32[]{:S(2)}) collective-permute-start(f32[4,16,256]{2,1,0:T(8,128)S(1)} %pad_maximum_fusion.3), channel_id=1, source_target_pairs={{0,64},{16,80},{32,96},{48,112},{64,0},{80,16},{96,32},{112,48},{1... | collective-permute-start | bytes 196616 | tf_op jit(solution)/shard_map/ppermute | solution.py:61
  155.5 5.8 %collective-permute-start.18 = (f32[4,16,256]{2,1,0:T(8,128)S(1)}, f32[4,16,256]{2,1,0:T(8,128)S(1)}, u32[]{:S(2)}, u32[]{:S(2)}) collective-permute-start(f32[4,16,256]{2,1,0:T(8,128)S(1)} %pad_maximum_fusion.4), channel_id=1, source_target_pairs={{0,64},{16,80},{32,96},{48,112},{64,0},{80,16},{96,32},{112,48},{1... | collective-permute-start | bytes 196616 | tf_op jit(solution)/shard_map/ppermute | solution.py:61
  159.4 5.0 %collective-permute-start.12 = (f32[8,16,256]{2,1,0:T(8,128)S(1)}, f32[8,16,256]{2,1,0:T(8,128)S(1)}, u32[]{:S(2)}, u32[]{:S(2)}) collective-permute-start(f32[8,16,256]{2,1,0:T(8,128)S(1)} %pad_maximum_fusion.1), channel_id=1, source_target_pairs={{0,1},{1,0},{2,3},{3,2},{4,5},{5,4},{6,7},{7,6},{8,9},{9,8},{10,11... | collective-permute-start | bytes 393224 | tf_op jit(solution)/shard_map/ppermute | solution.py:61
  161.3 5.0 %collective-permute-start.19 = (f32[8,16,256]{2,1,0:T(8,128)S(1)}, f32[8,16,256]{2,1,0:T(8,128)S(1)}, u32[]{:S(2)}, u32[]{:S(2)}) collective-permute-start(f32[8,16,256]{2,1,0:T(8,128)S(1)} %pad_maximum_fusion.2), channel_id=1, source_target_pairs={{0,1},{1,0},{2,3},{3,2},{4,5},{5,4},{6,7},{7,6},{8,9},{9,8},{10,11... | collective-permute-start | bytes 393224 | tf_op jit(solution)/shard_map/ppermute | solution.py:61
  165.1 7.2 %collective-permute-start.13 = (f32[16,16,256]{2,1,0:T(8,128)S(1)}, f32[16,16,256]{2,1,0:T(8,128)S(1)}, u32[]{:S(2)}, u32[]{:S(2)}) collective-permute-start(f32[16,16,256]{2,1,0:T(8,128)S(1)} %get-tuple-element.49), channel_id=1, source_target_pairs={{0,4},{1,5},{2,6},{3,7},{4,0},{5,1},{6,2},{7,3},{8,12},{9,13},{10,... | collective-permute-start | bytes 786440 | tf_op jit(solution)/shard_map/ppermute | solution.py:61
  167.1 8.4 %collective-permute-start.20 = (f32[16,16,256]{2,1,0:T(8,128)S(1)}, f32[16,16,256]{2,1,0:T(8,128)S(1)}, u32[]{:S(2)}, u32[]{:S(2)}) collective-permute-start(f32[16,16,256]{2,1,0:T(8,128)S(1)} %get-tuple-element.45), channel_id=1, source_target_pairs={{0,4},{1,5},{2,6},{3,7},{4,0},{5,1},{6,2},{7,3},{8,12},{9,13},{10,... | collective-permute-start | bytes 786440 | tf_op jit(solution)/shard_map/ppermute | solution.py:61
  173.1 13.7 %collective-permute-start.14 = (f32[32,16,256]{2,1,0:T(8,128)S(1)}, f32[32,16,256]{2,1,0:T(8,128)S(1)}, u32[]{:S(2)}, u32[]{:S(2)}) collective-permute-start(f32[32,16,256]{2,1,0:T(8,128)S(1)} %get-tuple-element.41), channel_id=1, source_target_pairs={{0,32},{16,48},{32,0},{48,16},{64,96},{80,112},{96,64},{112,80},{1... | collective-permute-start | bytes 1572872 | tf_op jit(solution)/shard_map/ppermute | solution.py:61
  176.3 16.1 %collective-permute-start.21 = (f32[32,16,256]{2,1,0:T(8,128)S(1)}, f32[32,16,256]{2,1,0:T(8,128)S(1)}, u32[]{:S(2)}, u32[]{:S(2)}) collective-permute-start(f32[32,16,256]{2,1,0:T(8,128)S(1)} %get-tuple-element.38), channel_id=1, source_target_pairs={{0,32},{16,48},{32,0},{48,16},{64,96},{80,112},{96,64},{112,80},{1... | collective-permute-start | bytes 1572872 | tf_op jit(solution)/shard_map/ppermute | solution.py:61
  187.6 5.7 %copy-start.1 = (f32[128,16,256]{2,1,0:T(8,128)}, f32[128,16,256]{2,1,0:T(8,128)S(1)}, u32[]{:S(2)}) copy-start(f32[128,16,256]{2,1,0:T(8,128)S(1)} %get-tuple-element.35) | copy-start | bytes 6291460
  187.7 6.9 %collective-permute-start.15 = (f32[64,16,256]{2,1,0:T(8,128)}, f32[64,16,256]{2,1,0:T(8,128)S(1)}, u32[]{:S(2)}, u32[]{:S(2)}) collective-permute-start(f32[64,16,256]{2,1,0:T(8,128)} %get-tuple-element.34), channel_id=1, source_target_pairs={{0,16},{16,0},{32,48},{48,32},{64,80},{80,64},{96,112},{112,96},{1... | collective-permute-start | bytes 3145736 | tf_op jit(solution)/shard_map/ppermute | solution.py:61
  193.3 3.0 %collective-permute-start.22 = (f32[64,16,256]{2,1,0:T(8,128)}, f32[64,16,256]{2,1,0:T(8,128)}, u32[]{:S(2)}, u32[]{:S(2)}) collective-permute-start(f32[64,16,256]{2,1,0:T(8,128)} %get-tuple-element.32), channel_id=1, source_target_pairs={{0,16},{16,0},{32,48},{48,32},{64,80},{80,64},{96,112},{112,96},{1... | collective-permute-start | bytes 3145736 | tf_op jit(solution)/shard_map/ppermute | solution.py:61
  197.6 1.3 copy-start

commit v11 on v10

--- a/solution.py
+++ b/solution.py
@@ -107,7 +107,7 @@
             flux_ref[c] += weight_ref[c, lev] * core
         return carry
 
-    lax.fori_loop(0, levels, level, 0, unroll=4)
+    lax.fori_loop(0, levels, level, 0, unroll=8)
 
 
 def diffuse(field, atm_kappa, vert_weight):
@@ -250,9 +250,9 @@
         img_ref[at(k), :] = w
         return acc + v * w
 
-    norm_now = strip_sum(lax.fori_loop(0, strips, init, zeros, unroll=4))
+    norm_now = strip_sum(lax.fori_loop(0, strips, init, zeros, unroll=8))
     for step in range(ITERS):
-        alpha = norm_now / strip_sum(lax.fori_loop(0, strips, image, zeros, unroll=4))
+        alpha = norm_now / strip_sum(lax.fori_loop(0, strips, image, zeros, unroll=8))
 
         def update(k, acc):
             v = dir_ref[at(k), :]
@@ -261,7 +261,7 @@
             residual_ref[at(k), :] = r
             return acc + r * r
 
-        norm_next = strip_sum(lax.fori_loop(0, strips, update, zeros, unroll=4))
+        norm_next = strip_sum(lax.fori_loop(0, strips, update, zeros, unroll=8))
         beta = norm_next / norm_now
 
         def direct(k, carry):
@@ -272,7 +272,7 @@
             return carry
 
         if step < ITERS - 1:
-            lax.fori_loop(0, strips, direct, 0, unroll=4)
+            lax.fori_loop(0, strips, direct, 0, unroll=8)
         norm_now = norm_next
     r0 = pl.multiple_of(gy * tile_rows, tile_rows)
     c0 = pl.multiple_of(gx * tile_cols, tile_cols)

time: 215 us -> 214 us (level)
  no operation moved by 1% of the time
where the time goes in v11:
time: 214 us; the launch traced here: 212 us
  Pallas kernels  70.2 us (33%)
  starting transfers between devices  43.5 us (20%)
  local copies, waits for them, and re-layouts  40.5 us (19%)
  waiting for transfers between devices  40.3 us (19%)
  other arithmetic  13.1 us (6%)
  matrix products  3.04 us (1%)
    pallas_call x1, Pallas kernels, diffuse(): pl.pallas_call(diffusion_kernel, grid=(blocks,), in_specs=[smem, smem, pl...  57.1 us
    ppermute x14, waiting for transfers between devices, stack_gather(): other = lax.ppermute(x, axis, [(j, j ^ distance) for j in range(size)])  24.1 us
    ppermute x14, starting transfers between devices, stack_gather(): other = lax.ppermute(x, axis, [(j, j ^ distance) for j in range(size)])  20.9 us
    unnamed x27, local copies, waits for them, and re-layouts  13.8 us
    pallas_call x1, Pallas kernels, solve_grid(): pl.pallas_call(functools.partial(cg_kernel, rounds), in_specs=[pl.BlockSp...  13.1 us
    ppermute x1, waiting for transfers between devices, diffuse(): south_east = lax.ppermute(field[:, :HALO, :HALO], both, pairs(1, 1))  7.07 us
    ppermute x1, starting transfers between devices, diffuse(): lax.ppermute(field[:, rows - HALO:, cols - HALO:], both, pairs(-1, -1))  5.35 us
    ppermute x1, starting transfers between devices, diffuse(): south_west = lax.ppermute(field[:, :HALO, cols - HALO:], both, pairs(-1, 1))  4.98 us
  transfers between devices with their start and end apart: 23, of which 13 were waited for; matrix products, arithmetic and copies ran while one was open for 17% of the time, Pallas kernels for 0%

profile of v11, /device:TPU:6, one launch (start us, length us, event | category | flops | bytes accessed | tf_op | source)
XLA Modules:
  0.0 211.7 jit_solution(1674893280969533994)
XLA Ops:
  0.6 4.3 %fusion.26 = (f32[128,32,4]{2,1,0:T(8,128)S(1)}, f32[128,32,4]{2,1,0:T(8,128)}) fusion(f32[128,32,512]{2,1,0:T(8,128)} %core_ref.1), kind=kLoop, calls=%fused_computation.126 | loop fusion | bytes 262144 | tf_op jit(solution)/shard_map/slice | solution.py:133
  4.9 3.3 %copy.86 = f32[128,32,4]{0,1,2:T(8,128)} copy(f32[128,32,4]{2,1,0:T(8,128)} %get-tuple-element.31) | data formatting | bytes 131072
  8.2 2.4 %collective-permute-start.1 = (f32[128,32,4]{0,1,2:T(8,128)}, f32[128,32,4]{0,1,2:T(8,128)}, u32[]{:S(2)}, u32[]{:S(2)}) collective-permute-start(f32[128,32,4]{0,1,2:T(8,128)} %copy.86), channel_id=1, source_target_pairs={{0,16},{16,32},{32,48},{48,64},{64,80},{80,96},{96,112},{1,17},{17... | collective-permute-start | bytes 196616 | tf_op jit(solution)/shard_map/ppermute | solution.py:134
  10.5 1.9 copy.85
  12.5 1.3 collective-permute-start
  13.8 2.9 %fusion.25 = (f32[128,4,4]{2,1,0:T(4,128)}, f32[128,4,4]{2,1,0:T(4,128)}, f32[128,4,4]{2,1,0:T(4,128)}, f32[128,4,4]{2,1,0:T(4,128)}) fusion(f32[128,32,512]{2,1,0:T(8,128)} %core_ref.1), kind=kLoop, calls=%fused_computation.125 | loop fusion | bytes 65536 | tf_op jit(solution)/shard_map/slice | solution.py:135
  16.6 5.3 %collective-permute-start.7 = (f32[128,4,4]{2,1,0:T(4,128)}, f32[128,4,4]{2,1,0:T(4,128)S(1)}, u32[]{:S(2)}, u32[]{:S(2)}) collective-permute-start(f32[128,4,4]{2,1,0:T(4,128)} %get-tuple-element.29), channel_id=1, source_target_pairs={{0,17},{1,18},{2,19},{3,20},{4,21},{5,22},{6,23},{7,24},{8,25},{9,... | collective-permute-start | bytes 24584 | tf_op jit(solution)/shard_map/ppermute | solution.py:138
  22.0 4.1 %fusion.24 = (f32[128,4,512]{2,1,0:T(4,128)}, f32[128,4,512]{2,1,0:T(4,128)}) fusion(f32[128,32,512]{2,1,0:T(8,128)} %core_ref.1), kind=kLoop, calls=%fused_computation.124 | loop fusion | bytes 4194304 | tf_op jit(solution)/shard_map/slice | solution.py:131
  26.1 3.4 %collective-permute-start.5 = (f32[128,4,512]{2,1,0:T(4,128)}, f32[128,4,512]{2,1,0:T(4,128)S(1)}, u32[]{:S(2)}, u32[]{:S(2)}) collective-permute-start(f32[128,4,512]{2,1,0:T(4,128)} %get-tuple-element.25), channel_id=1, source_target_pairs={{0,1},{1,2},{2,3},{3,4},{4,5},{5,6},{6,7},{7,8},{8,9},{9,10},{10,1... | collective-permute-start | bytes 3145736 | tf_op jit(solution)/shard_map/ppermute | solution.py:132
  29.5 2.4 %collective-permute-start.2 = (f32[128,4,512]{2,1,0:T(4,128)}, f32[128,4,512]{2,1,0:T(4,128)}, u32[]{:S(2)}, u32[]{:S(2)}) collective-permute-start(f32[128,4,512]{2,1,0:T(4,128)} %get-tuple-element.24), channel_id=1, source_target_pairs={{1,0},{2,1},{3,2},{4,3},{5,4},{6,5},{7,6},{8,7},{9,8},{10,9},{11,1... | collective-permute-start | bytes 3145736 | tf_op jit(solution)/shard_map/ppermute | solution.py:131
  32.5 0.6 copy.71
  33.2 1.6 reshape.236
  37.0 1.4 and_convert_fusion.mask_ref
  38.5 1.3 collective-permute-start.6
  39.7 2.7 %copy.69 = f32[128,32,4]{2,1,0:T(8,128)S(1)} copy(f32[128,32,4]{0,1,2:T(8,128)} %collective-permute-done.1) | data formatting | bytes 131072 | tf_op jit(solution)/shard_map/ppermute | solution.py:134
  42.5 5.0 %collective-permute-start.4 = (f32[128,4,4]{2,1,0:T(4,128)}, f32[128,4,4]{2,1,0:T(4,128)}, u32[]{:S(2)}, u32[]{:S(2)}) collective-permute-start(f32[128,4,4]{2,1,0:T(4,128)} %get-tuple-element.27), channel_id=1, source_target_pairs={{1,16},{2,17},{3,18},{4,19},{5,20},{6,21},{7,22},{8,23},{9,24},{10... | collective-permute-start | bytes 24584 | tf_op jit(solution)/shard_map/ppermute | solution.py:136
  47.5 2.9 %copy.68 = f32[128,32,4]{2,1,0:T(8,128)} copy(f32[128,32,4]{0,1,2:T(8,128)S(1)} %collective-permute-done) | data formatting | bytes 131072 | tf_op jit(solution)/shard_map/ppermute | solution.py:133
  50.3 1.5 collective-permute-start.3
  51.8 3.5 %pad_maximum_fusion.lanes_ref = f32[128,32,128]{2,1,0:T(8,128)} fusion(f32[128,32,4]{2,1,0:T(8,128)S(1)} %copy.69, f32[128,32,4]{2,1,0:T(8,128)} %copy.68, f32[128]{0:T(128)S(1)} %pad.29.clone), kind=kLoop, calls=%fused_computation.4 | loop fusion | flops 1048576 | bytes 2228736 | tf_op jit(solution)/shard_map/concatenate | solution.py:140
  55.3 1.8 collective-permute-done.6
  57.1 4.0 %collective-permute-done.4 = f32[128,4,4]{2,1,0:T(4,128)} collective-permute-done((f32[128,4,4]{2,1,0:T(4,128)}, f32[128,4,4]{2,1,0:T(4,128)}, u32[]{:S(2)}, u32[]{:S(2)}) %collective-permute-start.4) | collective-permute-done | bytes 8224 | tf_op jit(solution)/shard_map/ppermute | solution.py:136
  61.1 7.1 %collective-permute-done.3 = f32[128,4,4]{2,1,0:T(4,128)S(1)} collective-permute-done((f32[128,4,4]{2,1,0:T(4,128)}, f32[128,4,4]{2,1,0:T(4,128)S(1)}, u32[]{:S(2)}, u32[]{:S(2)}) %collective-permute-start.3) | collective-permute-done | bytes 8224 | tf_op jit(solution)/shard_map/ppermute | solution.py:135
  68.2 3.9 %maximum_maximum_fusion.rows_ref = f32[128,8,640]{2,1,0:T(8,128)} fusion(f32[128,4,4]{2,1,0:T(4,128)S(1)} %collective-permute-done.7, f32[128,4,120]{2,1,0:T(4,128)S(1)} %broadcast_in_dim.52, f32[128,4,4]{2,1,0:T(4,128)} %collective-permute-done.6, f32[128,4,512]{2,1,0:T(4,128)S(1)} %collective-permute-done.5, f32[128,4,4]{2,1,0:T(4,128)} %collective-permute-done.4, ...), kind=kLoop, calls=%fused_computation.3 | loop fusion | flops 4587520 | bytes 4997120 | tf_op jit(solution)/shard_map/concatenate | solution.py:142
  72.1 57.1 %shard_map.111 = (f32[128,32,512]{2,1,0:T(8,128)}, f32[4,32,512]{2,1,0:T(8,128)}) custom-call(f32[128]{0:T(128)} %kappa_ref.1, f32[4,128]{1,0:T(4,128)} %weight_ref.1, f32[128,32,512]{2,1,0:T(8,128)} %core_ref.1, f32[128,32,128]{2,1,0:T(8,128)} %pad_maximum_fusion.lanes_ref, f32[128,8,640]{2,1,0:T(8,128)} %maximum_maximum_fusion.rows_ref, ...), custom_call_target="tpu_custom_call" | custom-call | flops 131072000 | bytes 16777216 | tf_op jit(solution)/shard_map/pallas_call | solution.py:160
  129.2 1.0 convert_element_type.40
  130.4 0.6 gather_fusion.1
  131.4 0.7 gather_fusion
  132.1 3.3 %collective-permute-done.8 = bf16[32,4,128]{2,1,0:T(4,128)(2,1)S(1)} collective-permute-done((bf16[32,4,128]{2,1,0:T(4,128)(2,1)S(1)}, bf16[32,4,128]{2,1,0:T(4,128)(2,1)S(1)}, u32[]{:S(2)}, u32[]{:S(2)}) %collective-permute-start.8) | collective-permute-done | bytes 32800 | tf_op jit(solution)/shard_map/ppermute | solution.py:29
  135.5 0.7 gather_fusion.2
  136.2 3.0 %convolution_bitcast_fusion = f32[4,32,128]{2,0,1:T(4,128)S(1)} fusion(bf16[32,4,128,128]{3,2,1,0:T(8,128)(2,1)} %param.13, bf16[32,4,4,128]{3,2,1,0:T(4,128)(2,1)S(1)} %bitcast.37, bf16[32,4,4,128]{3,2,1,0:T(4,128)(2,1)S(1)} %bitcast.38, pred[32,4]{1,0:T(8,128)(4,1)S(1)} %and.117, pred[32,4]{1,0:T(8,128)(4,1)S(1)} %and.113), kind=kOutput, calls=%fused_computation.5 | convolution fusion | flops 16908288 | bytes 4522240 | tf_op jit(solution)/shard_map/bkij,bkcj->cbi/dot_general | solution.py:356
  139.4 0.6 constant_dynamic-update-slice_fusion.43
  140.0 3.5 %collective-permute-start.16 = (f32[1,16,256]{2,1,0:T(8,128)S(1)}, f32[1,16,256]{2,1,0:T(8,128)S(1)}, u32[]{:S(2)}, u32[]{:S(2)}) collective-permute-start(f32[1,16,256]{2,1,0:T(8,128)S(1)} %get-tuple-element.15), channel_id=1, source_target_pairs={{0,2},{1,3},{2,0},{3,1},{4,6},{5,7},{6,4},{7,5},{8,10},{9,11},{10,... | collective-permute-start | bytes 49160 | tf_op jit(solution)/shard_map/ppermute | solution.py:61
  143.5 1.7 collective-permute-done.9
  145.3 2.9 %collective-permute-start.10 = (f32[2,16,256]{2,1,0:T(8,128)S(1)}, f32[2,16,256]{2,1,0:T(8,128)S(1)}, u32[]{:S(2)}, u32[]{:S(2)}) collective-permute-start(f32[2,16,256]{2,1,0:T(8,128)S(1)} %pad_maximum_fusion.5), channel_id=1, source_target_pairs={{0,8},{1,9},{2,10},{3,11},{4,12},{5,13},{6,14},{7,15},{8,0},{9,1},... | collective-permute-start | bytes 98312 | tf_op jit(solution)/shard_map/ppermute | solution.py:61
  148.2 0.6 collective-permute-start.17
  148.8 0.6 constant_dynamic-update-slice_fusion.16
  149.4 0.6 constant_dynamic-update-slice_fusion.42
  150.0 0.7 collective-permute-done.10
  150.7 4.4 %collective-permute-start.11 = (f32[4,16,256]{2,1,0:T(8,128)S(1)}, f32[4,16,256]{2,1,0:T(8,128)S(1)}, u32[]{:S(2)}, u32[]{:S(2)}) collective-permute-start(f32[4,16,256]{2,1,0:T(8,128)S(1)} %pad_maximum_fusion.3), channel_id=1, source_target_pairs={{0,64},{16,80},{32,96},{48,112},{64,0},{80,16},{96,32},{112,48},{1... | collective-permute-start | bytes 196616 | tf_op jit(solution)/shard_map/ppermute | solution.py:61
  155.1 2.7 %collective-permute-start.18 = (f32[4,16,256]{2,1,0:T(8,128)S(1)}, f32[4,16,256]{2,1,0:T(8,128)S(1)}, u32[]{:S(2)}, u32[]{:S(2)}) collective-permute-start(f32[4,16,256]{2,1,0:T(8,128)S(1)} %pad_maximum_fusion.4), channel_id=1, source_target_pairs={{0,64},{16,80},{32,96},{48,112},{64,0},{80,16},{96,32},{112,48},{1... | collective-permute-start | bytes 196616 | tf_op jit(solution)/shard_map/ppermute | solution.py:61
  157.8 0.6 constant_dynamic-update-slice_fusion.15
  158.4 0.6 constant_dynamic-update-slice_fusion.41
  159.1 1.8 collective-permute-done.18
  161.2 0.6 constant_dynamic-update-slice_fusion.14
  161.8 2.2 %collective-permute-done.12 = f32[8,16,256]{2,1,0:T(8,128)S(1)} collective-permute-done((f32[8,16,256]{2,1,0:T(8,128)S(1)}, f32[8,16,256]{2,1,0:T(8,128)S(1)}, u32[]{:S(2)}, u32[]{:S(2)}) %collective-permute-start.12) | collective-permute-done | bytes 131104 | tf_op jit(solution)/shard_map/ppermute | solution.py:61
  164.1 0.7 constant_dynamic-update-slice_fusion.13
  165.3 0.6 constant_dynamic-update-slice_fusion.40
  166.0 0.7 constant_dynamic-update-slice_fusion.39
  166.7 1.4 collective-permute-start.20
  168.1 3.8 %collective-permute-done.13 = f32[16,16,256]{2,1,0:T(8,128)S(1)} collective-permute-done((f32[16,16,256]{2,1,0:T(8,128)S(1)}, f32[16,16,256]{2,1,0:T(8,128)S(1)}, u32[]{:S(2)}, u32[]{:S(2)}) %collective-permute-start.13) | collective-permute-done | bytes 262176 | tf_op jit(solution)/shard_map/ppermute | solution.py:61
  171.9 0.8 constant_dynamic-update-slice_fusion.12
  172.7 2.4 %collective-permute-start.14 = (f32[32,16,256]{2,1,0:T(8,128)S(1)}, f32[32,16,256]{2,1,0:T(8,128)S(1)}, u32[]{:S(2)}, u32[]{:S(2)}) collective-permute-start(f32[32,16,256]{2,1,0:T(8,128)S(1)} %get-tuple-element.41), channel_id=1, source_target_pairs={{0,32},{16,48},{32,0},{48,16},{64,96},{80,112},{96,64},{112,80},{1... | collective-permute-start | bytes 1572872 | tf_op jit(solution)/shard_map/ppermute | solution.py:61
  175.1 0.8 constant_dynamic-update-slice_fusion.38
  175.9 2.0 collective-permute-start.21
  177.9 8.5 %collective-permute-done.14 = f32[32,16,256]{2,1,0:T(8,128)S(1)} collective-permute-done((f32[32,16,256]{2,1,0:T(8,128)S(1)}, f32[32,16,256]{2,1,0:T(8,128)S(1)}, u32[]{:S(2)}, u32[]{:S(2)}) %collective-permute-start.14) | collective-permute-done | bytes 524320 | tf_op jit(solution)/shard_map/ppermute | solution.py:61
  186.4 0.9 constant_dynamic-update-slice_fusion.11
  187.3 4.7 %collective-permute-done.21 = f32[32,16,256]{2,1,0:T(8,128)S(1)} collective-permute-done((f32[32,16,256]{2,1,0:T(8,128)S(1)}, f32[32,16,256]{2,1,0:T(8,128)S(1)}, u32[]{:S(2)}, u32[]{:S(2)}) %collective-permute-start.21) | collective-permute-done | bytes 524320 | tf_op jit(solution)/shard_map/ppermute | solution.py:61
  192.0 0.9 constant_dynamic-update-slice_fusion.37
  193.5 0.6 reshape.238
  194.2 1.1 constant_dynamic-update-slice_fusion.18.rhs_stack
  195.3 0.7 collective-permute-done.22
  195.9 1.3 constant_dynamic-update-slice_fusion.44.coded_stack
  197.2 1.3 copy-done
  198.6 13.1 %shard_map.112 = (f32[16,256]{1,0:T(8,128)}, f32[16,256]{1,0:T(8,128)}) custom-call(s32[2]{0:T(128)} %pad_add_fusion.index_ref, f32[128,16,256]{2,1,0:T(8,128)} %constant_dynamic-update-slice_fusion.18.rhs_stack, f32[128,16,256]{2,1,0:T(8,128)} %copy-done), custom_call_target="tpu_custom_call" | custom-call | tf_op jit(solution)/shard_map/pallas_call | solution.py:290
  (74 shorter events, 5.0 us)
Async XLA Ops:
  8.2 30.3 %collective-permute-start.1 = (f32[128,32,4]{0,1,2:T(8,128)}, f32[128,32,4]{0,1,2:T(8,128)}, u32[]{:S(2)}, u32[]{:S(2)}) collective-permute-start(f32[128,32,4]{0,1,2:T(8,128)} %copy.86), channel_id=1, source_target_pairs={{0,16},{16,32},{32,48},{48,64},{64,80},{80,96},{96,112},{1,17},{17... | collective-permute-start | bytes 196616 | tf_op jit(solution)/shard_map/ppermute | solution.py:134
  12.5 30.0 %collective-permute-start = (f32[128,32,4]{0,1,2:T(8,128)}, f32[128,32,4]{0,1,2:T(8,128)S(1)}, u32[]{:S(2)}, u32[]{:S(2)}) collective-permute-start(f32[128,32,4]{0,1,2:T(8,128)} %copy.85), channel_id=1, source_target_pairs={{16,0},{32,16},{48,32},{64,48},{80,64},{96,80},{112,96},{17,1},{33... | collective-permute-start | bytes 196616 | tf_op jit(solution)/shard_map/ppermute | solution.py:133
  16.6 15.9 %copy-start.2 = (s32[4096,4]{0,1:T(4,128)S(1)}, s32[4096,4]{0,1:T(4,128)}, u32[]{:S(2)}) copy-start(s32[4096,4]{0,1:T(4,128)} %param.11) | copy-start | bytes 196612
  16.6 33.7 %collective-permute-start.7 = (f32[128,4,4]{2,1,0:T(4,128)}, f32[128,4,4]{2,1,0:T(4,128)S(1)}, u32[]{:S(2)}, u32[]{:S(2)}) collective-permute-start(f32[128,4,4]{2,1,0:T(4,128)} %get-tuple-element.29), channel_id=1, source_target_pairs={{0,17},{1,18},{2,19},{3,20},{4,21},{5,22},{6,23},{7,24},{8,25},{9,... | collective-permute-start | bytes 24584 | tf_op jit(solution)/shard_map/ppermute | solution.py:138
  26.1 42.1 %collective-permute-start.5 = (f32[128,4,512]{2,1,0:T(4,128)}, f32[128,4,512]{2,1,0:T(4,128)S(1)}, u32[]{:S(2)}, u32[]{:S(2)}) collective-permute-start(f32[128,4,512]{2,1,0:T(4,128)} %get-tuple-element.25), channel_id=1, source_target_pairs={{0,1},{1,2},{2,3},{3,4},{4,5},{5,6},{6,7},{7,8},{8,9},{9,10},{10,1... | collective-permute-start | bytes 3145736 | tf_op jit(solution)/shard_map/ppermute | solution.py:132
  29.5 38.7 %collective-permute-start.2 = (f32[128,4,512]{2,1,0:T(4,128)}, f32[128,4,512]{2,1,0:T(4,128)}, u32[]{:S(2)}, u32[]{:S(2)}) collective-permute-start(f32[128,4,512]{2,1,0:T(4,128)} %get-tuple-element.24), channel_id=1, source_target_pairs={{1,0},{2,1},{3,2},{4,3},{5,4},{6,5},{7,6},{8,7},{9,8},{10,9},{11,1... | collective-permute-start | bytes 3145736 | tf_op jit(solution)/shard_map/ppermute | solution.py:131
  32.5 2.5 %copy-start.3 = (s32[4096]{0:T(1024)S(1)}, s32[4096]{0:T(1024)}, u32[]{:S(2)}) copy-start(s32[4096]{0:T(1024)} %param.12) | copy-start | bytes 49156
  38.5 18.7 %collective-permute-start.6 = (f32[128,4,4]{2,1,0:T(4,128)}, f32[128,4,4]{2,1,0:T(4,128)}, u32[]{:S(2)}, u32[]{:S(2)}) collective-permute-start(f32[128,4,4]{2,1,0:T(4,128)} %get-tuple-element.28), channel_id=1, source_target_pairs={{16,1},{17,2},{18,3},{19,4},{20,5},{21,6},{22,7},{23,8},{24,9},{25... | collective-permute-start | bytes 24584 | tf_op jit(solution)/shard_map/ppermute | solution.py:137
  42.5 18.6 %collective-permute-start.4 = (f32[128,4,4]{2,1,0:T(4,128)}, f32[128,4,4]{2,1,0:T(4,128)}, u32[]{:S(2)}, u32[]{:S(2)}) collective-permute-start(f32[128,4,4]{2,1,0:T(4,128)} %get-tuple-element.27), channel_id=1, source_target_pairs={{1,16},{2,17},{3,18},{4,19},{5,20},{6,21},{7,22},{8,23},{9,24},{10... | collective-permute-start | bytes 24584 | tf_op jit(solution)/shard_map/ppermute | solution.py:136
  50.3 17.8 %collective-permute-start.3 = (f32[128,4,4]{2,1,0:T(4,128)}, f32[128,4,4]{2,1,0:T(4,128)S(1)}, u32[]{:S(2)}, u32[]{:S(2)}) collective-permute-start(f32[128,4,4]{2,1,0:T(4,128)} %get-tuple-element.26), channel_id=1, source_target_pairs={{17,0},{18,1},{19,2},{20,3},{21,4},{22,5},{23,6},{24,7},{25,8},{26... | collective-permute-start | bytes 24584 | tf_op jit(solution)/shard_map/ppermute | solution.py:135
  131.1 4.4 %collective-permute-start.8 = (bf16[32,4,128]{2,1,0:T(4,128)(2,1)S(1)}, bf16[32,4,128]{2,1,0:T(4,128)(2,1)S(1)}, u32[]{:S(2)}, u32[]{:S(2)}) collective-permute-start(bf16[32,4,128]{2,1,0:T(4,128)(2,1)S(1)} %broadcast_multiply_fusion), channel_id=1, source_target_pairs={{0,112},{16,0},{32,16},{48,32},{64,48},{80,64},{96,80},{112,96},{1... | collective-permute-start | bytes 98312 | tf_op jit(solution)/shard_map/ppermute | solution.py:29
  136.2 3.1 %copy-start.4 = (f32[16,256]{1,0:T(8,128)S(1)}, f32[16,256]{1,0:T(8,128)}, u32[]{:S(2)}) copy-start(f32[16,256]{1,0:T(8,128)} %param.15) | copy-start | bytes 49156
  136.2 3.1 %copy-start.5 = (s32[16,256]{1,0:T(8,128)S(1)}, s32[16,256]{1,0:T(8,128)}, u32[]{:S(2)}) copy-start(s32[16,256]{1,0:T(8,128)} %param.14) | copy-start | bytes 49156
  140.0 5.2 %collective-permute-start.9 = (f32[1,16,256]{2,1,0:T(8,128)S(1)}, f32[1,16,256]{2,1,0:T(8,128)S(1)}, u32[]{:S(2)}, u32[]{:S(2)}) collective-permute-start(f32[1,16,256]{2,1,0:T(8,128)S(1)} %get-tuple-element.80), channel_id=1, source_target_pairs={{0,2},{1,3},{2,0},{3,1},{4,6},{5,7},{6,4},{7,5},{8,10},{9,11},{10,... | collective-permute-start | bytes 49160 | tf_op jit(solution)/shard_map/ppermute | solution.py:61
  140.0 8.1 %collective-permute-start.16 = (f32[1,16,256]{2,1,0:T(8,128)S(1)}, f32[1,16,256]{2,1,0:T(8,128)S(1)}, u32[]{:S(2)}, u32[]{:S(2)}) collective-permute-start(f32[1,16,256]{2,1,0:T(8,128)S(1)} %get-tuple-element.15), channel_id=1, source_target_pairs={{0,2},{1,3},{2,0},{3,1},{4,6},{5,7},{6,4},{7,5},{8,10},{9,11},{10,... | collective-permute-start | bytes 49160 | tf_op jit(solution)/shard_map/ppermute | solution.py:61
  145.3 5.4 %collective-permute-start.10 = (f32[2,16,256]{2,1,0:T(8,128)S(1)}, f32[2,16,256]{2,1,0:T(8,128)S(1)}, u32[]{:S(2)}, u32[]{:S(2)}) collective-permute-start(f32[2,16,256]{2,1,0:T(8,128)S(1)} %pad_maximum_fusion.5), channel_id=1, source_target_pairs={{0,8},{1,9},{2,10},{3,11},{4,12},{5,13},{6,14},{7,15},{8,0},{9,1},... | collective-permute-start | bytes 98312 | tf_op jit(solution)/shard_map/ppermute | solution.py:61
  148.2 6.9 %collective-permute-start.17 = (f32[2,16,256]{2,1,0:T(8,128)S(1)}, f32[2,16,256]{2,1,0:T(8,128)S(1)}, u32[]{:S(2)}, u32[]{:S(2)}) collective-permute-start(f32[2,16,256]{2,1,0:T(8,128)S(1)} %pad_maximum_fusion.6), channel_id=1, source_target_pairs={{0,8},{1,9},{2,10},{3,11},{4,12},{5,13},{6,14},{7,15},{8,0},{9,1},... | collective-permute-start | bytes 98312 | tf_op jit(solution)/shard_map/ppermute | solution.py:61
  150.7 8.3 %collective-permute-start.11 = (f32[4,16,256]{2,1,0:T(8,128)S(1)}, f32[4,16,256]{2,1,0:T(8,128)S(1)}, u32[]{:S(2)}, u32[]{:S(2)}) collective-permute-start(f32[4,16,256]{2,1,0:T(8,128)S(1)} %pad_maximum_fusion.3), channel_id=1, source_target_pairs={{0,64},{16,80},{32,96},{48,112},{64,0},{80,16},{96,32},{112,48},{1... | collective-permute-start | bytes 196616 | tf_op jit(solution)/shard_map/ppermute | solution.py:61
  155.1 5.8 %collective-permute-start.18 = (f32[4,16,256]{2,1,0:T(8,128)S(1)}, f32[4,16,256]{2,1,0:T(8,128)S(1)}, u32[]{:S(2)}, u32[]{:S(2)}) collective-permute-start(f32[4,16,256]{2,1,0:T(8,128)S(1)} %pad_maximum_fusion.4), channel_id=1, source_target_pairs={{0,64},{16,80},{32,96},{48,112},{64,0},{80,16},{96,32},{112,48},{1... | collective-permute-start | bytes 196616 | tf_op jit(solution)/shard_map/ppermute | solution.py:61
  159.0 5.0 %collective-permute-start.12 = (f32[8,16,256]{2,1,0:T(8,128)S(1)}, f32[8,16,256]{2,1,0:T(8,128)S(1)}, u32[]{:S(2)}, u32[]{:S(2)}) collective-permute-start(f32[8,16,256]{2,1,0:T(8,128)S(1)} %pad_maximum_fusion.1), channel_id=1, source_target_pairs={{0,1},{1,0},{2,3},{3,2},{4,5},{5,4},{6,7},{7,6},{8,9},{9,8},{10,11... | collective-permute-start | bytes 393224 | tf_op jit(solution)/shard_map/ppermute | solution.py:61
  160.9 5.0 %collective-permute-start.19 = (f32[8,16,256]{2,1,0:T(8,128)S(1)}, f32[8,16,256]{2,1,0:T(8,128)S(1)}, u32[]{:S(2)}, u32[]{:S(2)}) collective-permute-start(f32[8,16,256]{2,1,0:T(8,128)S(1)} %pad_maximum_fusion.2), channel_id=1, source_target_pairs={{0,1},{1,0},{2,3},{3,2},{4,5},{5,4},{6,7},{7,6},{8,9},{9,8},{10,11... | collective-permute-start | bytes 393224 | tf_op jit(solution)/shard_map/ppermute | solution.py:61
  164.8 7.2 %collective-permute-start.13 = (f32[16,16,256]{2,1,0:T(8,128)S(1)}, f32[16,16,256]{2,1,0:T(8,128)S(1)}, u32[]{:S(2)}, u32[]{:S(2)}) collective-permute-start(f32[16,16,256]{2,1,0:T(8,128)S(1)} %get-tuple-element.49), channel_id=1, source_target_pairs={{0,4},{1,5},{2,6},{3,7},{4,0},{5,1},{6,2},{7,3},{8,12},{9,13},{10,... | collective-permute-start | bytes 786440 | tf_op jit(solution)/shard_map/ppermute | solution.py:61
  166.7 8.4 %collective-permute-start.20 = (f32[16,16,256]{2,1,0:T(8,128)S(1)}, f32[16,16,256]{2,1,0:T(8,128)S(1)}, u32[]{:S(2)}, u32[]{:S(2)}) collective-permute-start(f32[16,16,256]{2,1,0:T(8,128)S(1)} %get-tuple-element.45), channel_id=1, source_target_pairs={{0,4},{1,5},{2,6},{3,7},{4,0},{5,1},{6,2},{7,3},{8,12},{9,13},{10,... | collective-permute-start | bytes 786440 | tf_op jit(solution)/shard_map/ppermute | solution.py:61
  172.7 13.7 %collective-permute-start.14 = (f32[32,16,256]{2,1,0:T(8,128)S(1)}, f32[32,16,256]{2,1,0:T(8,128)S(1)}, u32[]{:S(2)}, u32[]{:S(2)}) collective-permute-start(f32[32,16,256]{2,1,0:T(8,128)S(1)} %get-tuple-element.41), channel_id=1, source_target_pairs={{0,32},{16,48},{32,0},{48,16},{64,96},{80,112},{96,64},{112,80},{1... | collective-permute-start | bytes 1572872 | tf_op jit(solution)/shard_map/ppermute | solution.py:61
  175.9 16.1 %collective-permute-start.21 = (f32[32,16,256]{2,1,0:T(8,128)S(1)}, f32[32,16,256]{2,1,0:T(8,128)S(1)}, u32[]{:S(2)}, u32[]{:S(2)}) collective-permute-start(f32[32,16,256]{2,1,0:T(8,128)S(1)} %get-tuple-element.38), channel_id=1, source_target_pairs={{0,32},{16,48},{32,0},{48,16},{64,96},{80,112},{96,64},{112,80},{1... | collective-permute-start | bytes 1572872 | tf_op jit(solution)/shard_map/ppermute | solution.py:61
  187.3 5.7 %copy-start.1 = (f32[128,16,256]{2,1,0:T(8,128)}, f32[128,16,256]{2,1,0:T(8,128)S(1)}, u32[]{:S(2)}) copy-start(f32[128,16,256]{2,1,0:T(8,128)S(1)} %get-tuple-element.35) | copy-start | bytes 6291460
  187.3 6.9 %collective-permute-start.15 = (f32[64,16,256]{2,1,0:T(8,128)}, f32[64,16,256]{2,1,0:T(8,128)S(1)}, u32[]{:S(2)}, u32[]{:S(2)}) collective-permute-start(f32[64,16,256]{2,1,0:T(8,128)} %get-tuple-element.34), channel_id=1, source_target_pairs={{0,16},{16,0},{32,48},{48,32},{64,80},{80,64},{96,112},{112,96},{1... | collective-permute-start | bytes 3145736 | tf_op jit(solution)/shard_map/ppermute | solution.py:61
  192.9 3.0 %collective-permute-start.22 = (f32[64,16,256]{2,1,0:T(8,128)}, f32[64,16,256]{2,1,0:T(8,128)}, u32[]{:S(2)}, u32[]{:S(2)}) collective-permute-start(f32[64,16,256]{2,1,0:T(8,128)} %get-tuple-element.32), channel_id=1, source_target_pairs={{0,16},{16,0},{32,48},{48,32},{64,80},{80,64},{96,112},{112,96},{1... | collective-permute-start | bytes 3145736 | tf_op jit(solution)/shard_map/ppermute | solution.py:61
  197.2 1.3 copy-start

commit v12 on v11

--- a/solution.py
+++ b/solution.py
@@ -128,8 +128,13 @@
         if 0 <= i + di < count_gx and 0 <= j + dj < count_gy
     ]
     both = ("gx", "gy")
-    south = lax.ppermute(field[:, :HALO, :], "gy", down_gy)
-    north = lax.ppermute(field[:, rows - HALO :, :], "gy", up_gy)
+    half = levels // 2
+    south = jnp.concatenate(
+        [lax.ppermute(field[l : l + half, :HALO, :], "gy", down_gy) for l in (0, half)], axis=0
+    )
+    north = jnp.concatenate(
+        [lax.ppermute(field[l : l + half, rows - HALO :, :], "gy", up_gy) for l in (0, half)], axis=0
+    )
     east = lax.ppermute(field[:, :, :HALO], "gx", down_gx)
     west = lax.ppermute(field[:, :, cols - HALO :], "gx", up_gx)
     south_east = lax.ppermute(field[:, :HALO, :HALO], both, pairs(1, 1))

time: 214 us -> 230 us (1.075)
  starting transfers between devices: 43.5 us -> 51.4 us
  waiting for transfers between devices: 40.3 us -> 46.7 us
    ppermute x2 -> x4, starting transfers between devices: 5.83 us -> 11.7 us  [the longest x2 6.79 us: diffuse(): lax.ppermute(field[l:l + half, rows - HALO:, :], 'gy', up_gy)]
    ppermute x14, waiting for transfers between devices: 24.1 us -> 27.8 us  [stack_gather(): other = lax.ppermute(x, axis, [(j, j ^ distance) for j in range(size)])]
    ppermute x1, waiting for transfers between devices: 3.96 us -> 7.06 us  [diffuse(): south_west = lax.ppermute(field[:, :HALO, cols - HALO:], both, pairs(-1, 1))]
    ppermute x1, starting transfers between devices: 0.02 us -> 2.73 us  [shifted(): return lax.ppermute(x, axis, [(i, (i + by) % size) for i in range(size)])]
    unnamed x27 -> x33, local copies, waits for them, and re-layouts: 13.8 us -> 13.3 us
  transfers between devices with their start and end apart: 23 -> 25, of which waited for: 13 -> 13; matrix products, arithmetic and copies ran while one was open for 17% -> 17% of each run, Pallas kernels for 0% -> 0%
where the time goes in v12:
time: 230 us; the launch traced here: 226 us
  Pallas kernels  70.3 us (31%)
  starting transfers between devices  51.4 us (22%)
  waiting for transfers between devices  46.7 us (20%)
  local copies, waits for them, and re-layouts  39.3 us (17%)
  other arithmetic  14.7 us (6%)
  matrix products  3.04 us (1%)
    pallas_call x1, Pallas kernels, diffuse(): pl.pallas_call(diffusion_kernel, grid=(blocks,), in_specs=[smem, smem, pl...  57.2 us
    ppermute x14, waiting for transfers between devices, stack_gather(): other = lax.ppermute(x, axis, [(j, j ^ distance) for j in range(size)])  27.8 us
    ppermute x14, starting transfers between devices, stack_gather(): other = lax.ppermute(x, axis, [(j, j ^ distance) for j in range(size)])  19.5 us
    unnamed x33, local copies, waits for them, and re-layouts  13.3 us
    pallas_call x1, Pallas kernels, solve_grid(): pl.pallas_call(functools.partial(cg_kernel, rounds), in_specs=[pl.BlockSp...  13.1 us
    ppermute x1, waiting for transfers between devices, diffuse(): south_west = lax.ppermute(field[:, :HALO, cols - HALO:], both, pairs(-1, 1))  7.06 us
    ppermute x2, starting transfers between devices, diffuse(): lax.ppermute(field[l:l + half, rows - HALO:, :], 'gy', up_gy)  6.79 us
    ppermute x1, starting transfers between devices, diffuse(): south_west = lax.ppermute(field[:, :HALO, cols - HALO:], both, pairs(-1, 1))  6.38 us
  transfers between devices with their start and end apart: 25, of which 13 were waited for; matrix products, arithmetic and copies ran while one was open for 17% of the time, Pallas kernels for 0%

profile of v12, /device:TPU:6, one launch (start us, length us, event | category | flops | bytes accessed | tf_op | source)
XLA Modules:
  0.0 226.5 jit_solution(13966349704601472211)
XLA Ops:
  0.6 4.3 %fusion.26 = (f32[128,32,4]{2,1,0:T(8,128)}, f32[128,32,4]{2,1,0:T(8,128)S(1)}) fusion(f32[128,32,512]{2,1,0:T(8,128)} %core_ref.1), kind=kLoop, calls=%fused_computation.126 | loop fusion | bytes 262144 | tf_op jit(solution)/shard_map/slice | solution.py:138
  4.9 1.9 copy.86
  6.9 1.7 collective-permute-start.1
  8.6 2.9 %fusion.25 = (f32[128,4,4]{2,1,0:T(4,128)}, f32[128,4,4]{2,1,0:T(4,128)}, f32[128,4,4]{2,1,0:T(4,128)}, f32[128,4,4]{2,1,0:T(4,128)}) fusion(f32[128,32,512]{2,1,0:T(8,128)} %core_ref.1), kind=kLoop, calls=%fused_computation.125 | loop fusion | bytes 65536 | tf_op jit(solution)/shard_map/slice | solution.py:140
  11.5 5.2 %collective-permute-start.9 = (f32[128,4,4]{2,1,0:T(4,128)}, f32[128,4,4]{2,1,0:T(4,128)S(1)}, u32[]{:S(2)}, u32[]{:S(2)}) collective-permute-start(f32[128,4,4]{2,1,0:T(4,128)} %get-tuple-element.31), channel_id=1, source_target_pairs={{0,17},{1,18},{2,19},{3,20},{4,21},{5,22},{6,23},{7,24},{8,25},{9,... | collective-permute-start | bytes 24584 | tf_op jit(solution)/shard_map/ppermute | solution.py:143
  16.7 1.4 collective-permute-start.8
  18.2 3.8 %fusion.24 = (f32[64,4,512]{2,1,0:T(4,128)}, f32[64,4,512]{2,1,0:T(4,128)}, f32[64,4,512]{2,1,0:T(4,128)}, f32[64,4,512]{2,1,0:T(4,128)}) fusion(f32[128,32,512]{2,1,0:T(8,128)} %core_ref.1), kind=kLoop, calls=%fused_computation.124 | loop fusion | bytes 4194304 | tf_op jit(solution)/shard_map/slice | solution.py:133
  22.0 3.4 %collective-permute-start.7 = (f32[64,4,512]{2,1,0:T(4,128)}, f32[64,4,512]{2,1,0:T(4,128)S(1)}, u32[]{:S(2)}, u32[]{:S(2)}) collective-permute-start(f32[64,4,512]{2,1,0:T(4,128)} %get-tuple-element.25), channel_id=1, source_target_pairs={{0,1},{1,2},{2,3},{3,4},{4,5},{5,6},{6,7},{7,8},{8,9},{9,10},{10,1... | collective-permute-start | bytes 1572872 | tf_op jit(solution)/shard_map/ppermute | solution.py:136
  25.4 3.4 %collective-permute-start.6 = (f32[64,4,512]{2,1,0:T(4,128)}, f32[64,4,512]{2,1,0:T(4,128)S(1)}, u32[]{:S(2)}, u32[]{:S(2)}) collective-permute-start(f32[64,4,512]{2,1,0:T(4,128)} %get-tuple-element.26), channel_id=1, source_target_pairs={{0,1},{1,2},{2,3},{3,4},{4,5},{5,6},{6,7},{7,8},{8,9},{9,10},{10,1... | collective-permute-start | bytes 1572872 | tf_op jit(solution)/shard_map/ppermute | solution.py:136
  29.9 0.6 copy.71
  30.6 1.6 reshape.236
  33.7 1.4 and_convert_fusion.mask_ref
  35.4 2.4 %collective-permute-start.3 = (f32[64,4,512]{2,1,0:T(4,128)}, f32[64,4,512]{2,1,0:T(4,128)}, u32[]{:S(2)}, u32[]{:S(2)}) collective-permute-start(f32[64,4,512]{2,1,0:T(4,128)} %get-tuple-element.27), channel_id=1, source_target_pairs={{1,0},{2,1},{3,2},{4,3},{5,4},{6,5},{7,6},{8,7},{9,8},{10,9},{11,1... | collective-permute-start | bytes 1572872 | tf_op jit(solution)/shard_map/ppermute | solution.py:133
  37.9 2.4 %collective-permute-start.2 = (f32[64,4,512]{2,1,0:T(4,128)}, f32[64,4,512]{2,1,0:T(4,128)}, u32[]{:S(2)}, u32[]{:S(2)}) collective-permute-start(f32[64,4,512]{2,1,0:T(4,128)} %get-tuple-element.24), channel_id=1, source_target_pairs={{1,0},{2,1},{3,2},{4,3},{5,4},{6,5},{7,6},{8,7},{9,8},{10,9},{11,1... | collective-permute-start | bytes 1572872 | tf_op jit(solution)/shard_map/ppermute | solution.py:133
  40.3 0.6 fusion.5
  41.0 2.7 %copy.85 = f32[128,32,4]{0,1,2:T(8,128)S(1)} copy(f32[128,32,4]{2,1,0:T(8,128)} %get-tuple-element.32) | data formatting | bytes 131072
  43.6 1.3 collective-permute-start
  45.1 2.3 %collective-permute-done = f32[128,32,4]{0,1,2:T(8,128)S(1)} collective-permute-done((f32[128,32,4]{0,1,2:T(8,128)S(1)}, f32[128,32,4]{0,1,2:T(8,128)S(1)}, u32[]{:S(2)}, u32[]{:S(2)}) %collective-permute-start) | collective-permute-done | bytes 65568 | tf_op jit(solution)/shard_map/ppermute | solution.py:138
  47.4 6.4 %collective-permute-start.5 = (f32[128,4,4]{2,1,0:T(4,128)}, f32[128,4,4]{2,1,0:T(4,128)}, u32[]{:S(2)}, u32[]{:S(2)}) collective-permute-start(f32[128,4,4]{2,1,0:T(4,128)} %get-tuple-element.29), channel_id=1, source_target_pairs={{1,16},{2,17},{3,18},{4,19},{5,20},{6,21},{7,22},{8,23},{9,24},{10... | collective-permute-start | bytes 24584 | tf_op jit(solution)/shard_map/ppermute | solution.py:141
  54.9 1.9 copy.69
  56.8 2.9 %copy.68 = f32[128,32,4]{2,1,0:T(8,128)} copy(f32[128,32,4]{0,1,2:T(8,128)S(1)} %collective-permute-done) | data formatting | bytes 131072 | tf_op jit(solution)/shard_map/ppermute | solution.py:138
  59.6 7.1 %collective-permute-done.5 = f32[128,4,4]{2,1,0:T(4,128)} collective-permute-done((f32[128,4,4]{2,1,0:T(4,128)}, f32[128,4,4]{2,1,0:T(4,128)}, u32[]{:S(2)}, u32[]{:S(2)}) %collective-permute-start.5) | collective-permute-done | bytes 8224 | tf_op jit(solution)/shard_map/ppermute | solution.py:141
  66.7 1.5 collective-permute-start.4
  68.2 3.6 %pad_maximum_fusion.lanes_ref = f32[128,32,128]{2,1,0:T(8,128)} fusion(f32[128,32,4]{2,1,0:T(8,128)S(1)} %copy.69, f32[128,32,4]{2,1,0:T(8,128)} %copy.68, f32[128]{0:T(128)S(1)} %copy-done.8), kind=kLoop, calls=%fused_computation.4 | loop fusion | flops 1048576 | bytes 2228736 | tf_op jit(solution)/shard_map/concatenate | solution.py:145
  71.7 5.1 %collective-permute-done.4 = f32[128,4,4]{2,1,0:T(4,128)S(1)} collective-permute-done((f32[128,4,4]{2,1,0:T(4,128)}, f32[128,4,4]{2,1,0:T(4,128)S(1)}, u32[]{:S(2)}, u32[]{:S(2)}) %collective-permute-start.4) | collective-permute-done | bytes 8224 | tf_op jit(solution)/shard_map/ppermute | solution.py:140
  76.9 3.8 %maximum_maximum_fusion.rows_ref = f32[128,8,640]{2,1,0:T(8,128)} fusion(f32[128,4,4]{2,1,0:T(4,128)S(1)} %collective-permute-done.9, f32[128,4,120]{2,1,0:T(4,128)S(1)} %broadcast_in_dim.52, f32[128,4,4]{2,1,0:T(4,128)} %collective-permute-done.8, f32[64,4,512]{2,1,0:T(4,128)S(1)} %collective-permute-done.7, f32[64,4,512]{2,1,0:T(4,128)S(1)} %collective-permute-done.6, ...), kind=kLoop, calls=%fused_computation.3 | loop fusion | flops 5898240 | bytes 4997120 | tf_op jit(solution)/shard_map/concatenate | solution.py:147
  80.7 57.2 %shard_map.111 = (f32[128,32,512]{2,1,0:T(8,128)}, f32[4,32,512]{2,1,0:T(8,128)}) custom-call(f32[128]{0:T(128)} %kappa_ref.1, f32[4,128]{1,0:T(4,128)} %weight_ref.1, f32[128,32,512]{2,1,0:T(8,128)} %core_ref.1, f32[128,32,128]{2,1,0:T(8,128)} %pad_maximum_fusion.lanes_ref, f32[128,8,640]{2,1,0:T(8,128)} %maximum_maximum_fusion.rows_ref, ...), custom_call_target="tpu_custom_call" | custom-call | flops 131072000 | bytes 16777216 | tf_op jit(solution)/shard_map/pallas_call | solution.py:165
  137.9 1.0 convert_element_type.40
  139.8 2.7 %collective-permute-start.10 = (bf16[32,4,128]{2,1,0:T(4,128)(2,1)S(1)}, bf16[32,4,128]{2,1,0:T(4,128)(2,1)S(1)}, u32[]{:S(2)}, u32[]{:S(2)}) collective-permute-start(bf16[32,4,128]{2,1,0:T(4,128)(2,1)S(1)} %broadcast_multiply_fusion), channel_id=1, source_target_pairs={{0,112},{16,0},{32,16},{48,32},{64,48},{80,64},{96,80},{112,96},{1... | collective-permute-start | bytes 98312 | tf_op jit(solution)/shard_map/ppermute | solution.py:29
  142.8 0.7 gather_fusion
  143.5 4.5 %collective-permute-done.10 = bf16[32,4,128]{2,1,0:T(4,128)(2,1)S(1)} collective-permute-done((bf16[32,4,128]{2,1,0:T(4,128)(2,1)S(1)}, bf16[32,4,128]{2,1,0:T(4,128)(2,1)S(1)}, u32[]{:S(2)}, u32[]{:S(2)}) %collective-permute-start.10) | collective-permute-done | bytes 32800 | tf_op jit(solution)/shard_map/ppermute | solution.py:29
  148.0 0.7 gather_fusion.2
  148.8 3.0 %convolution_bitcast_fusion = f32[4,32,128]{2,0,1:T(4,128)S(1)} fusion(bf16[32,4,128,128]{3,2,1,0:T(8,128)(2,1)} %param.13, bf16[32,4,4,128]{3,2,1,0:T(4,128)(2,1)S(1)} %bitcast.37, bf16[32,4,4,128]{3,2,1,0:T(4,128)(2,1)S(1)} %bitcast.38, pred[32,4]{1,0:T(8,128)(4,1)S(1)} %and.117, pred[32,4]{1,0:T(8,128)(4,1)S(1)} %and.113), kind=kOutput, calls=%fused_computation.5 | convolution fusion | flops 16908288 | bytes 4522240 | tf_op jit(solution)/shard_map/bkij,bkcj->cbi/dot_general | solution.py:361
  152.5 3.5 %collective-permute-start.18 = (f32[1,16,256]{2,1,0:T(8,128)S(1)}, f32[1,16,256]{2,1,0:T(8,128)S(1)}, u32[]{:S(2)}, u32[]{:S(2)}) collective-permute-start(f32[1,16,256]{2,1,0:T(8,128)S(1)} %get-tuple-element.15), channel_id=1, source_target_pairs={{0,2},{1,3},{2,0},{3,1},{4,6},{5,7},{6,4},{7,5},{8,10},{9,11},{10,... | collective-permute-start | bytes 49160 | tf_op jit(solution)/shard_map/ppermute | solution.py:61
  156.1 1.7 collective-permute-done.11
  157.8 2.9 %collective-permute-start.12 = (f32[2,16,256]{2,1,0:T(8,128)S(1)}, f32[2,16,256]{2,1,0:T(8,128)S(1)}, u32[]{:S(2)}, u32[]{:S(2)}) collective-permute-start(f32[2,16,256]{2,1,0:T(8,128)S(1)} %pad_maximum_fusion.5), channel_id=1, source_target_pairs={{0,8},{1,9},{2,10},{3,11},{4,12},{5,13},{6,14},{7,15},{8,0},{9,1},... | collective-permute-start | bytes 98312 | tf_op jit(solution)/shard_map/ppermute | solution.py:61
  160.7 0.6 collective-permute-start.19
  162.5 0.7 collective-permute-done.12
  163.2 5.2 %collective-permute-start.13 = (f32[4,16,256]{2,1,0:T(8,128)S(1)}, f32[4,16,256]{2,1,0:T(8,128)S(1)}, u32[]{:S(2)}, u32[]{:S(2)}) collective-permute-start(f32[4,16,256]{2,1,0:T(8,128)S(1)} %pad_maximum_fusion.3), channel_id=1, source_target_pairs={{0,64},{16,80},{32,96},{48,112},{64,0},{80,16},{96,32},{112,48},{1... | collective-permute-start | bytes 196616 | tf_op jit(solution)/shard_map/ppermute | solution.py:61
  168.4 2.9 %collective-permute-start.20 = (f32[4,16,256]{2,1,0:T(8,128)S(1)}, f32[4,16,256]{2,1,0:T(8,128)S(1)}, u32[]{:S(2)}, u32[]{:S(2)}) collective-permute-start(f32[4,16,256]{2,1,0:T(8,128)S(1)} %pad_maximum_fusion.4), channel_id=1, source_target_pairs={{0,64},{16,80},{32,96},{48,112},{64,0},{80,16},{96,32},{112,48},{1... | collective-permute-start | bytes 196616 | tf_op jit(solution)/shard_map/ppermute | solution.py:61
  171.3 0.6 constant_dynamic-update-slice_fusion.15
  172.6 1.6 collective-permute-done.20
  174.7 0.7 constant_dynamic-update-slice_fusion.14
  175.4 2.6 %collective-permute-done.14 = f32[8,16,256]{2,1,0:T(8,128)S(1)} collective-permute-done((f32[8,16,256]{2,1,0:T(8,128)S(1)}, f32[8,16,256]{2,1,0:T(8,128)S(1)}, u32[]{:S(2)}, u32[]{:S(2)}) %collective-permute-start.14) | collective-permute-done | bytes 131104 | tf_op jit(solution)/shard_map/ppermute | solution.py:61
  178.0 0.7 constant_dynamic-update-slice_fusion.13
  179.1 0.6 constant_dynamic-update-slice_fusion.40
  179.8 0.7 constant_dynamic-update-slice_fusion.39
  180.5 1.6 collective-permute-start.22
  182.1 4.7 %collective-permute-done.15 = f32[16,16,256]{2,1,0:T(8,128)S(1)} collective-permute-done((f32[16,16,256]{2,1,0:T(8,128)S(1)}, f32[16,16,256]{2,1,0:T(8,128)S(1)}, u32[]{:S(2)}, u32[]{:S(2)}) %collective-permute-start.15) | collective-permute-done | bytes 262176 | tf_op jit(solution)/shard_map/ppermute | solution.py:61
  186.8 0.8 constant_dynamic-update-slice_fusion.12
  187.6 0.9 collective-permute-start.16
  188.4 1.1 collective-permute-done.22
  189.6 0.8 constant_dynamic-update-slice_fusion.38
  190.3 0.9 collective-permute-start.23
  191.2 10.0 %collective-permute-done.16 = f32[32,16,256]{2,1,0:T(8,128)S(1)} collective-permute-done((f32[32,16,256]{2,1,0:T(8,128)S(1)}, f32[32,16,256]{2,1,0:T(8,128)S(1)}, u32[]{:S(2)}, u32[]{:S(2)}) %collective-permute-start.16) | collective-permute-done | bytes 524320 | tf_op jit(solution)/shard_map/ppermute | solution.py:61
  201.2 0.9 constant_dynamic-update-slice_fusion.11
  202.1 4.7 %collective-permute-done.23 = f32[32,16,256]{2,1,0:T(8,128)S(1)} collective-permute-done((f32[32,16,256]{2,1,0:T(8,128)S(1)}, f32[32,16,256]{2,1,0:T(8,128)S(1)}, u32[]{:S(2)}, u32[]{:S(2)}) %collective-permute-start.23) | collective-permute-done | bytes 524320 | tf_op jit(solution)/shard_map/ppermute | solution.py:61
  206.8 0.9 constant_dynamic-update-slice_fusion.37
  208.4 0.6 reshape.238
  209.0 1.0 constant_dynamic-update-slice_fusion.18.rhs_stack
  210.1 0.7 collective-permute-done.24
  210.8 1.3 constant_dynamic-update-slice_fusion.44.coded_stack
  212.1 1.3 copy-done
  213.4 13.1 %shard_map.112 = (f32[16,256]{1,0:T(8,128)}, f32[16,256]{1,0:T(8,128)}) custom-call(s32[2]{0:T(128)} %pad_add_fusion.index_ref, f32[128,16,256]{2,1,0:T(8,128)} %constant_dynamic-update-slice_fusion.18.rhs_stack, f32[128,16,256]{2,1,0:T(8,128)} %copy-done), custom_call_target="tpu_custom_call" | custom-call | tf_op jit(solution)/shard_map/pallas_call | solution.py:295
  (84 shorter events, 9.5 us)
Async XLA Ops:
  6.9 36.8 %collective-permute-start.1 = (f32[128,32,4]{0,1,2:T(8,128)}, f32[128,32,4]{0,1,2:T(8,128)S(1)}, u32[]{:S(2)}, u32[]{:S(2)}) collective-permute-start(f32[128,32,4]{0,1,2:T(8,128)} %copy.86), channel_id=1, source_target_pairs={{0,16},{16,32},{32,48},{48,64},{64,80},{80,96},{96,112},{1,17},{17... | collective-permute-start | bytes 196616 | tf_op jit(solution)/shard_map/ppermute | solution.py:139
  11.5 23.9 %collective-permute-start.9 = (f32[128,4,4]{2,1,0:T(4,128)}, f32[128,4,4]{2,1,0:T(4,128)S(1)}, u32[]{:S(2)}, u32[]{:S(2)}) collective-permute-start(f32[128,4,4]{2,1,0:T(4,128)} %get-tuple-element.31), channel_id=1, source_target_pairs={{0,17},{1,18},{2,19},{3,20},{4,21},{5,22},{6,23},{7,24},{8,25},{9,... | collective-permute-start | bytes 24584 | tf_op jit(solution)/shard_map/ppermute | solution.py:143
  16.7 13.2 %copy-start.2 = (s32[4096,4]{0,1:T(4,128)S(1)}, s32[4096,4]{0,1:T(4,128)}, u32[]{:S(2)}) copy-start(s32[4096,4]{0,1:T(4,128)} %param.11) | copy-start | bytes 196612
  16.7 21.2 %collective-permute-start.8 = (f32[128,4,4]{2,1,0:T(4,128)}, f32[128,4,4]{2,1,0:T(4,128)}, u32[]{:S(2)}, u32[]{:S(2)}) collective-permute-start(f32[128,4,4]{2,1,0:T(4,128)} %get-tuple-element.30), channel_id=1, source_target_pairs={{16,1},{17,2},{18,3},{19,4},{20,5},{21,6},{22,7},{23,8},{24,9},{25... | collective-permute-start | bytes 24584 | tf_op jit(solution)/shard_map/ppermute | solution.py:142
  22.0 54.8 %collective-permute-start.7 = (f32[64,4,512]{2,1,0:T(4,128)}, f32[64,4,512]{2,1,0:T(4,128)S(1)}, u32[]{:S(2)}, u32[]{:S(2)}) collective-permute-start(f32[64,4,512]{2,1,0:T(4,128)} %get-tuple-element.25), channel_id=1, source_target_pairs={{0,1},{1,2},{2,3},{3,4},{4,5},{5,6},{6,7},{7,8},{8,9},{9,10},{10,1... | collective-permute-start | bytes 1572872 | tf_op jit(solution)/shard_map/ppermute | solution.py:136
  25.4 51.4 %collective-permute-start.6 = (f32[64,4,512]{2,1,0:T(4,128)}, f32[64,4,512]{2,1,0:T(4,128)S(1)}, u32[]{:S(2)}, u32[]{:S(2)}) collective-permute-start(f32[64,4,512]{2,1,0:T(4,128)} %get-tuple-element.26), channel_id=1, source_target_pairs={{0,1},{1,2},{2,3},{3,4},{4,5},{5,6},{6,7},{7,8},{8,9},{9,10},{10,1... | collective-permute-start | bytes 1572872 | tf_op jit(solution)/shard_map/ppermute | solution.py:136
  29.9 2.5 %copy-start.3 = (s32[4096]{0:T(1024)S(1)}, s32[4096]{0:T(1024)}, u32[]{:S(2)}) copy-start(s32[4096]{0:T(1024)} %param.12) | copy-start | bytes 49156
  35.4 41.4 %collective-permute-start.3 = (f32[64,4,512]{2,1,0:T(4,128)}, f32[64,4,512]{2,1,0:T(4,128)}, u32[]{:S(2)}, u32[]{:S(2)}) collective-permute-start(f32[64,4,512]{2,1,0:T(4,128)} %get-tuple-element.27), channel_id=1, source_target_pairs={{1,0},{2,1},{3,2},{4,3},{5,4},{6,5},{7,6},{8,7},{9,8},{10,9},{11,1... | collective-permute-start | bytes 1572872 | tf_op jit(solution)/shard_map/ppermute | solution.py:133
  37.9 38.9 %collective-permute-start.2 = (f32[64,4,512]{2,1,0:T(4,128)}, f32[64,4,512]{2,1,0:T(4,128)}, u32[]{:S(2)}, u32[]{:S(2)}) collective-permute-start(f32[64,4,512]{2,1,0:T(4,128)} %get-tuple-element.24), channel_id=1, source_target_pairs={{1,0},{2,1},{3,2},{4,3},{5,4},{6,5},{7,6},{8,7},{9,8},{10,9},{11,1... | collective-permute-start | bytes 1572872 | tf_op jit(solution)/shard_map/ppermute | solution.py:133
  43.6 3.8 %collective-permute-start = (f32[128,32,4]{0,1,2:T(8,128)S(1)}, f32[128,32,4]{0,1,2:T(8,128)S(1)}, u32[]{:S(2)}, u32[]{:S(2)}) collective-permute-start(f32[128,32,4]{0,1,2:T(8,128)S(1)} %copy.85), channel_id=1, source_target_pairs={{16,0},{32,16},{48,32},{64,48},{80,64},{96,80},{112,96},{17,1},{33... | collective-permute-start | bytes 196616 | tf_op jit(solution)/shard_map/ppermute | solution.py:138
  47.4 19.3 %collective-permute-start.5 = (f32[128,4,4]{2,1,0:T(4,128)}, f32[128,4,4]{2,1,0:T(4,128)}, u32[]{:S(2)}, u32[]{:S(2)}) collective-permute-start(f32[128,4,4]{2,1,0:T(4,128)} %get-tuple-element.29), channel_id=1, source_target_pairs={{1,16},{2,17},{3,18},{4,19},{5,20},{6,21},{7,22},{8,23},{9,24},{10... | collective-permute-start | bytes 24584 | tf_op jit(solution)/shard_map/ppermute | solution.py:141
  56.8 11.4 %copy-start.8 = (f32[128]{0:T(128)S(1)}, f32[128]{0:T(128)}, u32[]{:S(2)}) copy-start(f32[128]{0:T(128)} %pad.31.clone) | copy-start | bytes 1540
  66.7 10.1 %collective-permute-start.4 = (f32[128,4,4]{2,1,0:T(4,128)}, f32[128,4,4]{2,1,0:T(4,128)S(1)}, u32[]{:S(2)}, u32[]{:S(2)}) collective-permute-start(f32[128,4,4]{2,1,0:T(4,128)} %get-tuple-element.28), channel_id=1, source_target_pairs={{17,0},{18,1},{19,2},{20,3},{21,4},{22,5},{23,6},{24,7},{25,8},{26... | collective-permute-start | bytes 24584 | tf_op jit(solution)/shard_map/ppermute | solution.py:140
  80.7 59.0 %copy-start.7 = (bf16[32]{0:T(256)(128)(2,1)S(1)}, bf16[32]{0:T(256)(128)(2,1)}, u32[]{:S(2)}) copy-start(bf16[32]{0:T(256)(128)(2,1)} %convert_element_type.43) | copy-start | bytes 196
  80.7 61.8 %copy-start.6 = (s32[128]{0:T(128)S(1)}, s32[128]{0:T(128)}, u32[]{:S(2)}) copy-start(s32[128]{0:T(128)} %fusion.5) | copy-start | bytes 1540
  139.8 8.2 %collective-permute-start.10 = (bf16[32,4,128]{2,1,0:T(4,128)(2,1)S(1)}, bf16[32,4,128]{2,1,0:T(4,128)(2,1)S(1)}, u32[]{:S(2)}, u32[]{:S(2)}) collective-permute-start(bf16[32,4,128]{2,1,0:T(4,128)(2,1)S(1)} %broadcast_multiply_fusion), channel_id=1, source_target_pairs={{0,112},{16,0},{32,16},{48,32},{64,48},{80,64},{96,80},{112,96},{1... | collective-permute-start | bytes 98312 | tf_op jit(solution)/shard_map/ppermute | solution.py:29
  148.7 3.1 %copy-start.4 = (f32[16,256]{1,0:T(8,128)S(1)}, f32[16,256]{1,0:T(8,128)}, u32[]{:S(2)}) copy-start(f32[16,256]{1,0:T(8,128)} %param.15) | copy-start | bytes 49156
  148.7 3.1 %copy-start.5 = (s32[16,256]{1,0:T(8,128)S(1)}, s32[16,256]{1,0:T(8,128)}, u32[]{:S(2)}) copy-start(s32[16,256]{1,0:T(8,128)} %param.14) | copy-start | bytes 49156
  152.5 5.2 %collective-permute-start.11 = (f32[1,16,256]{2,1,0:T(8,128)S(1)}, f32[1,16,256]{2,1,0:T(8,128)S(1)}, u32[]{:S(2)}, u32[]{:S(2)}) collective-permute-start(f32[1,16,256]{2,1,0:T(8,128)S(1)} %get-tuple-element.82), channel_id=1, source_target_pairs={{0,2},{1,3},{2,0},{3,1},{4,6},{5,7},{6,4},{7,5},{8,10},{9,11},{10,... | collective-permute-start | bytes 49160 | tf_op jit(solution)/shard_map/ppermute | solution.py:61
  152.5 8.1 %collective-permute-start.18 = (f32[1,16,256]{2,1,0:T(8,128)S(1)}, f32[1,16,256]{2,1,0:T(8,128)S(1)}, u32[]{:S(2)}, u32[]{:S(2)}) collective-permute-start(f32[1,16,256]{2,1,0:T(8,128)S(1)} %get-tuple-element.15), channel_id=1, source_target_pairs={{0,2},{1,3},{2,0},{3,1},{4,6},{5,7},{6,4},{7,5},{8,10},{9,11},{10,... | collective-permute-start | bytes 49160 | tf_op jit(solution)/shard_map/ppermute | solution.py:61
  157.8 5.4 %collective-permute-start.12 = (f32[2,16,256]{2,1,0:T(8,128)S(1)}, f32[2,16,256]{2,1,0:T(8,128)S(1)}, u32[]{:S(2)}, u32[]{:S(2)}) collective-permute-start(f32[2,16,256]{2,1,0:T(8,128)S(1)} %pad_maximum_fusion.5), channel_id=1, source_target_pairs={{0,8},{1,9},{2,10},{3,11},{4,12},{5,13},{6,14},{7,15},{8,0},{9,1},... | collective-permute-start | bytes 98312 | tf_op jit(solution)/shard_map/ppermute | solution.py:61
  160.7 7.7 %collective-permute-start.19 = (f32[2,16,256]{2,1,0:T(8,128)S(1)}, f32[2,16,256]{2,1,0:T(8,128)S(1)}, u32[]{:S(2)}, u32[]{:S(2)}) collective-permute-start(f32[2,16,256]{2,1,0:T(8,128)S(1)} %pad_maximum_fusion.6), channel_id=1, source_target_pairs={{0,8},{1,9},{2,10},{3,11},{4,12},{5,13},{6,14},{7,15},{8,0},{9,1},... | collective-permute-start | bytes 98312 | tf_op jit(solution)/shard_map/ppermute | solution.py:61
  163.2 9.3 %collective-permute-start.13 = (f32[4,16,256]{2,1,0:T(8,128)S(1)}, f32[4,16,256]{2,1,0:T(8,128)S(1)}, u32[]{:S(2)}, u32[]{:S(2)}) collective-permute-start(f32[4,16,256]{2,1,0:T(8,128)S(1)} %pad_maximum_fusion.3), channel_id=1, source_target_pairs={{0,64},{16,80},{32,96},{48,112},{64,0},{80,16},{96,32},{112,48},{1... | collective-permute-start | bytes 196616 | tf_op jit(solution)/shard_map/ppermute | solution.py:61
  168.4 5.8 %collective-permute-start.20 = (f32[4,16,256]{2,1,0:T(8,128)S(1)}, f32[4,16,256]{2,1,0:T(8,128)S(1)}, u32[]{:S(2)}, u32[]{:S(2)}) collective-permute-start(f32[4,16,256]{2,1,0:T(8,128)S(1)} %pad_maximum_fusion.4), channel_id=1, source_target_pairs={{0,64},{16,80},{32,96},{48,112},{64,0},{80,16},{96,32},{112,48},{1... | collective-permute-start | bytes 196616 | tf_op jit(solution)/shard_map/ppermute | solution.py:61
  172.5 5.5 %collective-permute-start.14 = (f32[8,16,256]{2,1,0:T(8,128)S(1)}, f32[8,16,256]{2,1,0:T(8,128)S(1)}, u32[]{:S(2)}, u32[]{:S(2)}) collective-permute-start(f32[8,16,256]{2,1,0:T(8,128)S(1)} %pad_maximum_fusion.1), channel_id=1, source_target_pairs={{0,1},{1,0},{2,3},{3,2},{4,5},{5,4},{6,7},{7,6},{8,9},{9,8},{10,11... | collective-permute-start | bytes 393224 | tf_op jit(solution)/shard_map/ppermute | solution.py:61
  174.2 5.5 %collective-permute-start.21 = (f32[8,16,256]{2,1,0:T(8,128)S(1)}, f32[8,16,256]{2,1,0:T(8,128)S(1)}, u32[]{:S(2)}, u32[]{:S(2)}) collective-permute-start(f32[8,16,256]{2,1,0:T(8,128)S(1)} %pad_maximum_fusion.2), channel_id=1, source_target_pairs={{0,1},{1,0},{2,3},{3,2},{4,5},{5,4},{6,7},{7,6},{8,9},{9,8},{10,11... | collective-permute-start | bytes 393224 | tf_op jit(solution)/shard_map/ppermute | solution.py:61
  178.7 8.0 %collective-permute-start.15 = (f32[16,16,256]{2,1,0:T(8,128)S(1)}, f32[16,16,256]{2,1,0:T(8,128)S(1)}, u32[]{:S(2)}, u32[]{:S(2)}) collective-permute-start(f32[16,16,256]{2,1,0:T(8,128)S(1)} %get-tuple-element.51), channel_id=1, source_target_pairs={{0,4},{1,5},{2,6},{3,7},{4,0},{5,1},{6,2},{7,3},{8,12},{9,13},{10,... | collective-permute-start | bytes 786440 | tf_op jit(solution)/shard_map/ppermute | solution.py:61
  180.5 9.1 %collective-permute-start.22 = (f32[16,16,256]{2,1,0:T(8,128)S(1)}, f32[16,16,256]{2,1,0:T(8,128)S(1)}, u32[]{:S(2)}, u32[]{:S(2)}) collective-permute-start(f32[16,16,256]{2,1,0:T(8,128)S(1)} %get-tuple-element.47), channel_id=1, source_target_pairs={{0,4},{1,5},{2,6},{3,7},{4,0},{5,1},{6,2},{7,3},{8,12},{9,13},{10,... | collective-permute-start | bytes 786440 | tf_op jit(solution)/shard_map/ppermute | solution.py:61
  187.6 13.6 %collective-permute-start.16 = (f32[32,16,256]{2,1,0:T(8,128)S(1)}, f32[32,16,256]{2,1,0:T(8,128)S(1)}, u32[]{:S(2)}, u32[]{:S(2)}) collective-permute-start(f32[32,16,256]{2,1,0:T(8,128)S(1)} %get-tuple-element.43), channel_id=1, source_target_pairs={{0,32},{16,48},{32,0},{48,16},{64,96},{80,112},{96,64},{112,80},{1... | collective-permute-start | bytes 1572872 | tf_op jit(solution)/shard_map/ppermute | solution.py:61
  190.3 16.5 %collective-permute-start.23 = (f32[32,16,256]{2,1,0:T(8,128)S(1)}, f32[32,16,256]{2,1,0:T(8,128)S(1)}, u32[]{:S(2)}, u32[]{:S(2)}) collective-permute-start(f32[32,16,256]{2,1,0:T(8,128)S(1)} %get-tuple-element.40), channel_id=1, source_target_pairs={{0,32},{16,48},{32,0},{48,16},{64,96},{80,112},{96,64},{112,80},{1... | collective-permute-start | bytes 1572872 | tf_op jit(solution)/shard_map/ppermute | solution.py:61
  202.1 5.7 %copy-start.1 = (f32[128,16,256]{2,1,0:T(8,128)}, f32[128,16,256]{2,1,0:T(8,128)S(1)}, u32[]{:S(2)}) copy-start(f32[128,16,256]{2,1,0:T(8,128)S(1)} %get-tuple-element.37) | copy-start | bytes 6291460
  202.1 6.9 %collective-permute-start.17 = (f32[64,16,256]{2,1,0:T(8,128)}, f32[64,16,256]{2,1,0:T(8,128)S(1)}, u32[]{:S(2)}, u32[]{:S(2)}) collective-permute-start(f32[64,16,256]{2,1,0:T(8,128)} %get-tuple-element.36), channel_id=1, source_target_pairs={{0,16},{16,0},{32,48},{48,32},{64,80},{80,64},{96,112},{112,96},{1... | collective-permute-start | bytes 3145736 | tf_op jit(solution)/shard_map/ppermute | solution.py:61
  207.8 3.0 %collective-permute-start.24 = (f32[64,16,256]{2,1,0:T(8,128)}, f32[64,16,256]{2,1,0:T(8,128)}, u32[]{:S(2)}, u32[]{:S(2)}) collective-permute-start(f32[64,16,256]{2,1,0:T(8,128)} %get-tuple-element.34), channel_id=1, source_target_pairs={{0,16},{16,0},{32,48},{48,32},{64,80},{80,64},{96,112},{112,96},{1... | collective-permute-start | bytes 3145736 | tf_op jit(solution)/shard_map/ppermute | solution.py:61
  212.1 1.3 copy-start

commit v13 on v11

--- a/solution.py
+++ b/solution.py
@@ -70,7 +70,7 @@
 
 
 HALO = 4
-LEVEL_BLOCK = 16
+LEVEL_BLOCK = 32
 
 
 def diffusion_kernel(kappa_ref, weight_ref, core_ref, lanes_ref, rows_ref, mask_ref, out_ref, flux_ref):

time: 214 us -> 215 us (level)
  no operation moved by 1% of the time
where the time goes in v13:
time: 215 us; the launch traced here: 212 us
  Pallas kernels  70.9 us (33%)
  starting transfers between devices  43.5 us (20%)
  local copies, waits for them, and re-layouts  40.5 us (19%)
  waiting for transfers between devices  40.3 us (19%)
  other arithmetic  13.1 us (6%)
  matrix products  3.04 us (1%)
    pallas_call x1, Pallas kernels, diffuse(): pl.pallas_call(diffusion_kernel, grid=(blocks,), in_specs=[smem, smem, pl...  57.8 us
    ppermute x14, waiting for transfers between devices, stack_gather(): other = lax.ppermute(x, axis, [(j, j ^ distance) for j in range(size)])  24.2 us
    ppermute x14, starting transfers between devices, stack_gather(): other = lax.ppermute(x, axis, [(j, j ^ distance) for j in range(size)])  20.9 us
    unnamed x27, local copies, waits for them, and re-layouts  13.8 us
    pallas_call x1, Pallas kernels, solve_grid(): pl.pallas_call(functools.partial(cg_kernel, rounds), in_specs=[pl.BlockSp...  13.1 us
    ppermute x1, waiting for transfers between devices, diffuse(): south_east = lax.ppermute(field[:, :HALO, :HALO], both, pairs(1, 1))  7.07 us
    ppermute x1, starting transfers between devices, diffuse(): lax.ppermute(field[:, rows - HALO:, cols - HALO:], both, pairs(-1, -1))  5.35 us
    ppermute x1, starting transfers between devices, diffuse(): south_west = lax.ppermute(field[:, :HALO, cols - HALO:], both, pairs(-1, 1))  4.98 us
  transfers between devices with their start and end apart: 23, of which 13 were waited for; matrix products, arithmetic and copies ran while one was open for 17% of the time, Pallas kernels for 0%

profile of v13, /device:TPU:6, one launch (start us, length us, event | category | flops | bytes accessed | tf_op | source)
XLA Modules:
  0.0 212.4 jit_solution(6338903833047617303)
XLA Ops:
  0.6 4.3 %fusion.26 = (f32[128,32,4]{2,1,0:T(8,128)S(1)}, f32[128,32,4]{2,1,0:T(8,128)}) fusion(f32[128,32,512]{2,1,0:T(8,128)} %core_ref.1), kind=kLoop, calls=%fused_computation.126 | loop fusion | bytes 262144 | tf_op jit(solution)/shard_map/slice | solution.py:133
  4.9 3.3 %copy.86 = f32[128,32,4]{0,1,2:T(8,128)} copy(f32[128,32,4]{2,1,0:T(8,128)} %get-tuple-element.31) | data formatting | bytes 131072
  8.2 2.4 %collective-permute-start.1 = (f32[128,32,4]{0,1,2:T(8,128)}, f32[128,32,4]{0,1,2:T(8,128)}, u32[]{:S(2)}, u32[]{:S(2)}) collective-permute-start(f32[128,32,4]{0,1,2:T(8,128)} %copy.86), channel_id=1, source_target_pairs={{0,16},{16,32},{32,48},{48,64},{64,80},{80,96},{96,112},{1,17},{17... | collective-permute-start | bytes 196616 | tf_op jit(solution)/shard_map/ppermute | solution.py:134
  10.5 1.9 copy.85
  12.5 1.3 collective-permute-start
  13.8 2.9 %fusion.25 = (f32[128,4,4]{2,1,0:T(4,128)}, f32[128,4,4]{2,1,0:T(4,128)}, f32[128,4,4]{2,1,0:T(4,128)}, f32[128,4,4]{2,1,0:T(4,128)}) fusion(f32[128,32,512]{2,1,0:T(8,128)} %core_ref.1), kind=kLoop, calls=%fused_computation.125 | loop fusion | bytes 65536 | tf_op jit(solution)/shard_map/slice | solution.py:135
  16.6 5.3 %collective-permute-start.7 = (f32[128,4,4]{2,1,0:T(4,128)}, f32[128,4,4]{2,1,0:T(4,128)S(1)}, u32[]{:S(2)}, u32[]{:S(2)}) collective-permute-start(f32[128,4,4]{2,1,0:T(4,128)} %get-tuple-element.29), channel_id=1, source_target_pairs={{0,17},{1,18},{2,19},{3,20},{4,21},{5,22},{6,23},{7,24},{8,25},{9,... | collective-permute-start | bytes 24584 | tf_op jit(solution)/shard_map/ppermute | solution.py:138
  22.0 4.1 %fusion.24 = (f32[128,4,512]{2,1,0:T(4,128)}, f32[128,4,512]{2,1,0:T(4,128)}) fusion(f32[128,32,512]{2,1,0:T(8,128)} %core_ref.1), kind=kLoop, calls=%fused_computation.124 | loop fusion | bytes 4194304 | tf_op jit(solution)/shard_map/slice | solution.py:131
  26.1 3.4 %collective-permute-start.5 = (f32[128,4,512]{2,1,0:T(4,128)}, f32[128,4,512]{2,1,0:T(4,128)S(1)}, u32[]{:S(2)}, u32[]{:S(2)}) collective-permute-start(f32[128,4,512]{2,1,0:T(4,128)} %get-tuple-element.25), channel_id=1, source_target_pairs={{0,1},{1,2},{2,3},{3,4},{4,5},{5,6},{6,7},{7,8},{8,9},{9,10},{10,1... | collective-permute-start | bytes 3145736 | tf_op jit(solution)/shard_map/ppermute | solution.py:132
  29.5 2.4 %collective-permute-start.2 = (f32[128,4,512]{2,1,0:T(4,128)}, f32[128,4,512]{2,1,0:T(4,128)}, u32[]{:S(2)}, u32[]{:S(2)}) collective-permute-start(f32[128,4,512]{2,1,0:T(4,128)} %get-tuple-element.24), channel_id=1, source_target_pairs={{1,0},{2,1},{3,2},{4,3},{5,4},{6,5},{7,6},{8,7},{9,8},{10,9},{11,1... | collective-permute-start | bytes 3145736 | tf_op jit(solution)/shard_map/ppermute | solution.py:131
  32.5 0.6 copy.71
  33.2 1.6 reshape.236
  37.0 1.4 and_convert_fusion.mask_ref
  38.5 1.3 collective-permute-start.6
  39.7 2.7 %copy.69 = f32[128,32,4]{2,1,0:T(8,128)S(1)} copy(f32[128,32,4]{0,1,2:T(8,128)} %collective-permute-done.1) | data formatting | bytes 131072 | tf_op jit(solution)/shard_map/ppermute | solution.py:134
  42.5 5.0 %collective-permute-start.4 = (f32[128,4,4]{2,1,0:T(4,128)}, f32[128,4,4]{2,1,0:T(4,128)}, u32[]{:S(2)}, u32[]{:S(2)}) collective-permute-start(f32[128,4,4]{2,1,0:T(4,128)} %get-tuple-element.27), channel_id=1, source_target_pairs={{1,16},{2,17},{3,18},{4,19},{5,20},{6,21},{7,22},{8,23},{9,24},{10... | collective-permute-start | bytes 24584 | tf_op jit(solution)/shard_map/ppermute | solution.py:136
  47.5 2.9 %copy.68 = f32[128,32,4]{2,1,0:T(8,128)} copy(f32[128,32,4]{0,1,2:T(8,128)S(1)} %collective-permute-done) | data formatting | bytes 131072 | tf_op jit(solution)/shard_map/ppermute | solution.py:133
  50.3 1.5 collective-permute-start.3
  51.8 3.5 %pad_maximum_fusion.lanes_ref = f32[128,32,128]{2,1,0:T(8,128)} fusion(f32[128,32,4]{2,1,0:T(8,128)S(1)} %copy.69, f32[128,32,4]{2,1,0:T(8,128)} %copy.68, f32[128]{0:T(128)S(1)} %pad.29.clone), kind=kLoop, calls=%fused_computation.4 | loop fusion | flops 1048576 | bytes 2228736 | tf_op jit(solution)/shard_map/concatenate | solution.py:140
  55.3 1.8 collective-permute-done.6
  57.1 4.0 %collective-permute-done.4 = f32[128,4,4]{2,1,0:T(4,128)} collective-permute-done((f32[128,4,4]{2,1,0:T(4,128)}, f32[128,4,4]{2,1,0:T(4,128)}, u32[]{:S(2)}, u32[]{:S(2)}) %collective-permute-start.4) | collective-permute-done | bytes 8224 | tf_op jit(solution)/shard_map/ppermute | solution.py:136
  61.1 7.1 %collective-permute-done.3 = f32[128,4,4]{2,1,0:T(4,128)S(1)} collective-permute-done((f32[128,4,4]{2,1,0:T(4,128)}, f32[128,4,4]{2,1,0:T(4,128)S(1)}, u32[]{:S(2)}, u32[]{:S(2)}) %collective-permute-start.3) | collective-permute-done | bytes 8224 | tf_op jit(solution)/shard_map/ppermute | solution.py:135
  68.2 3.9 %maximum_maximum_fusion.rows_ref = f32[128,8,640]{2,1,0:T(8,128)} fusion(f32[128,4,4]{2,1,0:T(4,128)S(1)} %collective-permute-done.7, f32[128,4,120]{2,1,0:T(4,128)S(1)} %broadcast_in_dim.52, f32[128,4,4]{2,1,0:T(4,128)} %collective-permute-done.6, f32[128,4,512]{2,1,0:T(4,128)S(1)} %collective-permute-done.5, f32[128,4,4]{2,1,0:T(4,128)} %collective-permute-done.4, ...), kind=kLoop, calls=%fused_computation.3 | loop fusion | flops 4587520 | bytes 4997120 | tf_op jit(solution)/shard_map/concatenate | solution.py:142
  72.1 57.8 %shard_map.111 = (f32[128,32,512]{2,1,0:T(8,128)}, f32[4,32,512]{2,1,0:T(8,128)}) custom-call(f32[128]{0:T(128)} %kappa_ref.1, f32[4,128]{1,0:T(4,128)} %weight_ref.1, f32[128,32,512]{2,1,0:T(8,128)} %core_ref.1, f32[128,32,128]{2,1,0:T(8,128)} %pad_maximum_fusion.lanes_ref, f32[128,8,640]{2,1,0:T(8,128)} %maximum_maximum_fusion.rows_ref, ...), custom_call_target="tpu_custom_call" | custom-call | flops 131072000 | bytes 16777216 | tf_op jit(solution)/shard_map/pallas_call | solution.py:160
  129.9 1.0 convert_element_type.40
  131.1 0.6 gather_fusion.1
  132.1 0.7 gather_fusion
  132.8 3.3 %collective-permute-done.8 = bf16[32,4,128]{2,1,0:T(4,128)(2,1)S(1)} collective-permute-done((bf16[32,4,128]{2,1,0:T(4,128)(2,1)S(1)}, bf16[32,4,128]{2,1,0:T(4,128)(2,1)S(1)}, u32[]{:S(2)}, u32[]{:S(2)}) %collective-permute-start.8) | collective-permute-done | bytes 32800 | tf_op jit(solution)/shard_map/ppermute | solution.py:29
  136.2 0.7 gather_fusion.2
  137.0 3.0 %convolution_bitcast_fusion = f32[4,32,128]{2,0,1:T(4,128)S(1)} fusion(bf16[32,4,128,128]{3,2,1,0:T(8,128)(2,1)} %param.13, bf16[32,4,4,128]{3,2,1,0:T(4,128)(2,1)S(1)} %bitcast.37, bf16[32,4,4,128]{3,2,1,0:T(4,128)(2,1)S(1)} %bitcast.38, pred[32,4]{1,0:T(8,128)(4,1)S(1)} %and.117, pred[32,4]{1,0:T(8,128)(4,1)S(1)} %and.113), kind=kOutput, calls=%fused_computation.5 | convolution fusion | flops 16908288 | bytes 4522240 | tf_op jit(solution)/shard_map/bkij,bkcj->cbi/dot_general | solution.py:356
  140.1 0.6 constant_dynamic-update-slice_fusion.43
  140.7 3.5 %collective-permute-start.16 = (f32[1,16,256]{2,1,0:T(8,128)S(1)}, f32[1,16,256]{2,1,0:T(8,128)S(1)}, u32[]{:S(2)}, u32[]{:S(2)}) collective-permute-start(f32[1,16,256]{2,1,0:T(8,128)S(1)} %get-tuple-element.15), channel_id=1, source_target_pairs={{0,2},{1,3},{2,0},{3,1},{4,6},{5,7},{6,4},{7,5},{8,10},{9,11},{10,... | collective-permute-start | bytes 49160 | tf_op jit(solution)/shard_map/ppermute | solution.py:61
  144.3 1.7 collective-permute-done.9
  146.0 2.9 %collective-permute-start.10 = (f32[2,16,256]{2,1,0:T(8,128)S(1)}, f32[2,16,256]{2,1,0:T(8,128)S(1)}, u32[]{:S(2)}, u32[]{:S(2)}) collective-permute-start(f32[2,16,256]{2,1,0:T(8,128)S(1)} %pad_maximum_fusion.5), channel_id=1, source_target_pairs={{0,8},{1,9},{2,10},{3,11},{4,12},{5,13},{6,14},{7,15},{8,0},{9,1},... | collective-permute-start | bytes 98312 | tf_op jit(solution)/shard_map/ppermute | solution.py:61
  148.9 0.6 collective-permute-start.17
  149.5 0.6 constant_dynamic-update-slice_fusion.16
  150.1 0.6 constant_dynamic-update-slice_fusion.42
  150.7 0.7 collective-permute-done.10
  151.4 4.4 %collective-permute-start.11 = (f32[4,16,256]{2,1,0:T(8,128)S(1)}, f32[4,16,256]{2,1,0:T(8,128)S(1)}, u32[]{:S(2)}, u32[]{:S(2)}) collective-permute-start(f32[4,16,256]{2,1,0:T(8,128)S(1)} %pad_maximum_fusion.3), channel_id=1, source_target_pairs={{0,64},{16,80},{32,96},{48,112},{64,0},{80,16},{96,32},{112,48},{1... | collective-permute-start | bytes 196616 | tf_op jit(solution)/shard_map/ppermute | solution.py:61
  155.8 2.7 %collective-permute-start.18 = (f32[4,16,256]{2,1,0:T(8,128)S(1)}, f32[4,16,256]{2,1,0:T(8,128)S(1)}, u32[]{:S(2)}, u32[]{:S(2)}) collective-permute-start(f32[4,16,256]{2,1,0:T(8,128)S(1)} %pad_maximum_fusion.4), channel_id=1, source_target_pairs={{0,64},{16,80},{32,96},{48,112},{64,0},{80,16},{96,32},{112,48},{1... | collective-permute-start | bytes 196616 | tf_op jit(solution)/shard_map/ppermute | solution.py:61
  158.5 0.6 constant_dynamic-update-slice_fusion.15
  159.1 0.6 constant_dynamic-update-slice_fusion.41
  159.8 1.8 collective-permute-done.18
  161.9 0.6 constant_dynamic-update-slice_fusion.14
  162.6 2.2 %collective-permute-done.12 = f32[8,16,256]{2,1,0:T(8,128)S(1)} collective-permute-done((f32[8,16,256]{2,1,0:T(8,128)S(1)}, f32[8,16,256]{2,1,0:T(8,128)S(1)}, u32[]{:S(2)}, u32[]{:S(2)}) %collective-permute-start.12) | collective-permute-done | bytes 131104 | tf_op jit(solution)/shard_map/ppermute | solution.py:61
  164.8 0.7 constant_dynamic-update-slice_fusion.13
  166.0 0.6 constant_dynamic-update-slice_fusion.40
  166.7 0.7 constant_dynamic-update-slice_fusion.39
  167.4 1.4 collective-permute-start.20
  168.8 3.8 %collective-permute-done.13 = f32[16,16,256]{2,1,0:T(8,128)S(1)} collective-permute-done((f32[16,16,256]{2,1,0:T(8,128)S(1)}, f32[16,16,256]{2,1,0:T(8,128)S(1)}, u32[]{:S(2)}, u32[]{:S(2)}) %collective-permute-start.13) | collective-permute-done | bytes 262176 | tf_op jit(solution)/shard_map/ppermute | solution.py:61
  172.6 0.8 constant_dynamic-update-slice_fusion.12
  173.4 2.4 %collective-permute-start.14 = (f32[32,16,256]{2,1,0:T(8,128)S(1)}, f32[32,16,256]{2,1,0:T(8,128)S(1)}, u32[]{:S(2)}, u32[]{:S(2)}) collective-permute-start(f32[32,16,256]{2,1,0:T(8,128)S(1)} %get-tuple-element.41), channel_id=1, source_target_pairs={{0,32},{16,48},{32,0},{48,16},{64,96},{80,112},{96,64},{112,80},{1... | collective-permute-start | bytes 1572872 | tf_op jit(solution)/shard_map/ppermute | solution.py:61
  175.8 0.8 constant_dynamic-update-slice_fusion.38
  176.6 2.0 collective-permute-start.21
  178.6 8.5 %collective-permute-done.14 = f32[32,16,256]{2,1,0:T(8,128)S(1)} collective-permute-done((f32[32,16,256]{2,1,0:T(8,128)S(1)}, f32[32,16,256]{2,1,0:T(8,128)S(1)}, u32[]{:S(2)}, u32[]{:S(2)}) %collective-permute-start.14) | collective-permute-done | bytes 524320 | tf_op jit(solution)/shard_map/ppermute | solution.py:61
  187.1 0.9 constant_dynamic-update-slice_fusion.11
  188.0 4.7 %collective-permute-done.21 = f32[32,16,256]{2,1,0:T(8,128)S(1)} collective-permute-done((f32[32,16,256]{2,1,0:T(8,128)S(1)}, f32[32,16,256]{2,1,0:T(8,128)S(1)}, u32[]{:S(2)}, u32[]{:S(2)}) %collective-permute-start.21) | collective-permute-done | bytes 524320 | tf_op jit(solution)/shard_map/ppermute | solution.py:61
  192.7 0.9 constant_dynamic-update-slice_fusion.37
  194.3 0.6 reshape.238
  194.9 1.1 constant_dynamic-update-slice_fusion.18.rhs_stack
  196.0 0.7 collective-permute-done.22
  196.7 1.3 constant_dynamic-update-slice_fusion.44.coded_stack
  198.0 1.3 copy-done
  199.3 13.1 %shard_map.112 = (f32[16,256]{1,0:T(8,128)}, f32[16,256]{1,0:T(8,128)}) custom-call(s32[2]{0:T(128)} %pad_add_fusion.index_ref, f32[128,16,256]{2,1,0:T(8,128)} %constant_dynamic-update-slice_fusion.18.rhs_stack, f32[128,16,256]{2,1,0:T(8,128)} %copy-done), custom_call_target="tpu_custom_call" | custom-call | tf_op jit(solution)/shard_map/pallas_call | solution.py:290
  (74 shorter events, 5.0 us)
Async XLA Ops:
  8.2 30.3 %collective-permute-start.1 = (f32[128,32,4]{0,1,2:T(8,128)}, f32[128,32,4]{0,1,2:T(8,128)}, u32[]{:S(2)}, u32[]{:S(2)}) collective-permute-start(f32[128,32,4]{0,1,2:T(8,128)} %copy.86), channel_id=1, source_target_pairs={{0,16},{16,32},{32,48},{48,64},{64,80},{80,96},{96,112},{1,17},{17... | collective-permute-start | bytes 196616 | tf_op jit(solution)/shard_map/ppermute | solution.py:134
  12.5 30.0 %collective-permute-start = (f32[128,32,4]{0,1,2:T(8,128)}, f32[128,32,4]{0,1,2:T(8,128)S(1)}, u32[]{:S(2)}, u32[]{:S(2)}) collective-permute-start(f32[128,32,4]{0,1,2:T(8,128)} %copy.85), channel_id=1, source_target_pairs={{16,0},{32,16},{48,32},{64,48},{80,64},{96,80},{112,96},{17,1},{33... | collective-permute-start | bytes 196616 | tf_op jit(solution)/shard_map/ppermute | solution.py:133
  16.6 15.9 %copy-start.2 = (s32[4096,4]{0,1:T(4,128)S(1)}, s32[4096,4]{0,1:T(4,128)}, u32[]{:S(2)}) copy-start(s32[4096,4]{0,1:T(4,128)} %param.11) | copy-start | bytes 196612
  16.6 33.7 %collective-permute-start.7 = (f32[128,4,4]{2,1,0:T(4,128)}, f32[128,4,4]{2,1,0:T(4,128)S(1)}, u32[]{:S(2)}, u32[]{:S(2)}) collective-permute-start(f32[128,4,4]{2,1,0:T(4,128)} %get-tuple-element.29), channel_id=1, source_target_pairs={{0,17},{1,18},{2,19},{3,20},{4,21},{5,22},{6,23},{7,24},{8,25},{9,... | collective-permute-start | bytes 24584 | tf_op jit(solution)/shard_map/ppermute | solution.py:138
  26.1 42.1 %collective-permute-start.5 = (f32[128,4,512]{2,1,0:T(4,128)}, f32[128,4,512]{2,1,0:T(4,128)S(1)}, u32[]{:S(2)}, u32[]{:S(2)}) collective-permute-start(f32[128,4,512]{2,1,0:T(4,128)} %get-tuple-element.25), channel_id=1, source_target_pairs={{0,1},{1,2},{2,3},{3,4},{4,5},{5,6},{6,7},{7,8},{8,9},{9,10},{10,1... | collective-permute-start | bytes 3145736 | tf_op jit(solution)/shard_map/ppermute | solution.py:132
  29.5 38.7 %collective-permute-start.2 = (f32[128,4,512]{2,1,0:T(4,128)}, f32[128,4,512]{2,1,0:T(4,128)}, u32[]{:S(2)}, u32[]{:S(2)}) collective-permute-start(f32[128,4,512]{2,1,0:T(4,128)} %get-tuple-element.24), channel_id=1, source_target_pairs={{1,0},{2,1},{3,2},{4,3},{5,4},{6,5},{7,6},{8,7},{9,8},{10,9},{11,1... | collective-permute-start | bytes 3145736 | tf_op jit(solution)/shard_map/ppermute | solution.py:131
  32.5 2.5 %copy-start.3 = (s32[4096]{0:T(1024)S(1)}, s32[4096]{0:T(1024)}, u32[]{:S(2)}) copy-start(s32[4096]{0:T(1024)} %param.12) | copy-start | bytes 49156
  38.5 18.7 %collective-permute-start.6 = (f32[128,4,4]{2,1,0:T(4,128)}, f32[128,4,4]{2,1,0:T(4,128)}, u32[]{:S(2)}, u32[]{:S(2)}) collective-permute-start(f32[128,4,4]{2,1,0:T(4,128)} %get-tuple-element.28), channel_id=1, source_target_pairs={{16,1},{17,2},{18,3},{19,4},{20,5},{21,6},{22,7},{23,8},{24,9},{25... | collective-permute-start | bytes 24584 | tf_op jit(solution)/shard_map/ppermute | solution.py:137
  42.5 18.6 %collective-permute-start.4 = (f32[128,4,4]{2,1,0:T(4,128)}, f32[128,4,4]{2,1,0:T(4,128)}, u32[]{:S(2)}, u32[]{:S(2)}) collective-permute-start(f32[128,4,4]{2,1,0:T(4,128)} %get-tuple-element.27), channel_id=1, source_target_pairs={{1,16},{2,17},{3,18},{4,19},{5,20},{6,21},{7,22},{8,23},{9,24},{10... | collective-permute-start | bytes 24584 | tf_op jit(solution)/shard_map/ppermute | solution.py:136
  50.3 17.8 %collective-permute-start.3 = (f32[128,4,4]{2,1,0:T(4,128)}, f32[128,4,4]{2,1,0:T(4,128)S(1)}, u32[]{:S(2)}, u32[]{:S(2)}) collective-permute-start(f32[128,4,4]{2,1,0:T(4,128)} %get-tuple-element.26), channel_id=1, source_target_pairs={{17,0},{18,1},{19,2},{20,3},{21,4},{22,5},{23,6},{24,7},{25,8},{26... | collective-permute-start | bytes 24584 | tf_op jit(solution)/shard_map/ppermute | solution.py:135
  131.8 4.4 %collective-permute-start.8 = (bf16[32,4,128]{2,1,0:T(4,128)(2,1)S(1)}, bf16[32,4,128]{2,1,0:T(4,128)(2,1)S(1)}, u32[]{:S(2)}, u32[]{:S(2)}) collective-permute-start(bf16[32,4,128]{2,1,0:T(4,128)(2,1)S(1)} %broadcast_multiply_fusion), channel_id=1, source_target_pairs={{0,112},{16,0},{32,16},{48,32},{64,48},{80,64},{96,80},{112,96},{1... | collective-permute-start | bytes 98312 | tf_op jit(solution)/shard_map/ppermute | solution.py:29
  136.9 3.1 %copy-start.4 = (f32[16,256]{1,0:T(8,128)S(1)}, f32[16,256]{1,0:T(8,128)}, u32[]{:S(2)}) copy-start(f32[16,256]{1,0:T(8,128)} %param.15) | copy-start | bytes 49156
  136.9 3.1 %copy-start.5 = (s32[16,256]{1,0:T(8,128)S(1)}, s32[16,256]{1,0:T(8,128)}, u32[]{:S(2)}) copy-start(s32[16,256]{1,0:T(8,128)} %param.14) | copy-start | bytes 49156
  140.7 5.2 %collective-permute-start.9 = (f32[1,16,256]{2,1,0:T(8,128)S(1)}, f32[1,16,256]{2,1,0:T(8,128)S(1)}, u32[]{:S(2)}, u32[]{:S(2)}) collective-permute-start(f32[1,16,256]{2,1,0:T(8,128)S(1)} %get-tuple-element.80), channel_id=1, source_target_pairs={{0,2},{1,3},{2,0},{3,1},{4,6},{5,7},{6,4},{7,5},{8,10},{9,11},{10,... | collective-permute-start | bytes 49160 | tf_op jit(solution)/shard_map/ppermute | solution.py:61
  140.7 8.1 %collective-permute-start.16 = (f32[1,16,256]{2,1,0:T(8,128)S(1)}, f32[1,16,256]{2,1,0:T(8,128)S(1)}, u32[]{:S(2)}, u32[]{:S(2)}) collective-permute-start(f32[1,16,256]{2,1,0:T(8,128)S(1)} %get-tuple-element.15), channel_id=1, source_target_pairs={{0,2},{1,3},{2,0},{3,1},{4,6},{5,7},{6,4},{7,5},{8,10},{9,11},{10,... | collective-permute-start | bytes 49160 | tf_op jit(solution)/shard_map/ppermute | solution.py:61
  146.0 5.4 %collective-permute-start.10 = (f32[2,16,256]{2,1,0:T(8,128)S(1)}, f32[2,16,256]{2,1,0:T(8,128)S(1)}, u32[]{:S(2)}, u32[]{:S(2)}) collective-permute-start(f32[2,16,256]{2,1,0:T(8,128)S(1)} %pad_maximum_fusion.5), channel_id=1, source_target_pairs={{0,8},{1,9},{2,10},{3,11},{4,12},{5,13},{6,14},{7,15},{8,0},{9,1},... | collective-permute-start | bytes 98312 | tf_op jit(solution)/shard_map/ppermute | solution.py:61
  148.9 6.9 %collective-permute-start.17 = (f32[2,16,256]{2,1,0:T(8,128)S(1)}, f32[2,16,256]{2,1,0:T(8,128)S(1)}, u32[]{:S(2)}, u32[]{:S(2)}) collective-permute-start(f32[2,16,256]{2,1,0:T(8,128)S(1)} %pad_maximum_fusion.6), channel_id=1, source_target_pairs={{0,8},{1,9},{2,10},{3,11},{4,12},{5,13},{6,14},{7,15},{8,0},{9,1},... | collective-permute-start | bytes 98312 | tf_op jit(solution)/shard_map/ppermute | solution.py:61
  151.4 8.3 %collective-permute-start.11 = (f32[4,16,256]{2,1,0:T(8,128)S(1)}, f32[4,16,256]{2,1,0:T(8,128)S(1)}, u32[]{:S(2)}, u32[]{:S(2)}) collective-permute-start(f32[4,16,256]{2,1,0:T(8,128)S(1)} %pad_maximum_fusion.3), channel_id=1, source_target_pairs={{0,64},{16,80},{32,96},{48,112},{64,0},{80,16},{96,32},{112,48},{1... | collective-permute-start | bytes 196616 | tf_op jit(solution)/shard_map/ppermute | solution.py:61
  155.8 5.8 %collective-permute-start.18 = (f32[4,16,256]{2,1,0:T(8,128)S(1)}, f32[4,16,256]{2,1,0:T(8,128)S(1)}, u32[]{:S(2)}, u32[]{:S(2)}) collective-permute-start(f32[4,16,256]{2,1,0:T(8,128)S(1)} %pad_maximum_fusion.4), channel_id=1, source_target_pairs={{0,64},{16,80},{32,96},{48,112},{64,0},{80,16},{96,32},{112,48},{1... | collective-permute-start | bytes 196616 | tf_op jit(solution)/shard_map/ppermute | solution.py:61
  159.7 5.0 %collective-permute-start.12 = (f32[8,16,256]{2,1,0:T(8,128)S(1)}, f32[8,16,256]{2,1,0:T(8,128)S(1)}, u32[]{:S(2)}, u32[]{:S(2)}) collective-permute-start(f32[8,16,256]{2,1,0:T(8,128)S(1)} %pad_maximum_fusion.1), channel_id=1, source_target_pairs={{0,1},{1,0},{2,3},{3,2},{4,5},{5,4},{6,7},{7,6},{8,9},{9,8},{10,11... | collective-permute-start | bytes 393224 | tf_op jit(solution)/shard_map/ppermute | solution.py:61
  161.7 5.0 %collective-permute-start.19 = (f32[8,16,256]{2,1,0:T(8,128)S(1)}, f32[8,16,256]{2,1,0:T(8,128)S(1)}, u32[]{:S(2)}, u32[]{:S(2)}) collective-permute-start(f32[8,16,256]{2,1,0:T(8,128)S(1)} %pad_maximum_fusion.2), channel_id=1, source_target_pairs={{0,1},{1,0},{2,3},{3,2},{4,5},{5,4},{6,7},{7,6},{8,9},{9,8},{10,11... | collective-permute-start | bytes 393224 | tf_op jit(solution)/shard_map/ppermute | solution.py:61
  165.5 7.2 %collective-permute-start.13 = (f32[16,16,256]{2,1,0:T(8,128)S(1)}, f32[16,16,256]{2,1,0:T(8,128)S(1)}, u32[]{:S(2)}, u32[]{:S(2)}) collective-permute-start(f32[16,16,256]{2,1,0:T(8,128)S(1)} %get-tuple-element.49), channel_id=1, source_target_pairs={{0,4},{1,5},{2,6},{3,7},{4,0},{5,1},{6,2},{7,3},{8,12},{9,13},{10,... | collective-permute-start | bytes 786440 | tf_op jit(solution)/shard_map/ppermute | solution.py:61
  167.4 8.4 %collective-permute-start.20 = (f32[16,16,256]{2,1,0:T(8,128)S(1)}, f32[16,16,256]{2,1,0:T(8,128)S(1)}, u32[]{:S(2)}, u32[]{:S(2)}) collective-permute-start(f32[16,16,256]{2,1,0:T(8,128)S(1)} %get-tuple-element.45), channel_id=1, source_target_pairs={{0,4},{1,5},{2,6},{3,7},{4,0},{5,1},{6,2},{7,3},{8,12},{9,13},{10,... | collective-permute-start | bytes 786440 | tf_op jit(solution)/shard_map/ppermute | solution.py:61
  173.4 13.7 %collective-permute-start.14 = (f32[32,16,256]{2,1,0:T(8,128)S(1)}, f32[32,16,256]{2,1,0:T(8,128)S(1)}, u32[]{:S(2)}, u32[]{:S(2)}) collective-permute-start(f32[32,16,256]{2,1,0:T(8,128)S(1)} %get-tuple-element.41), channel_id=1, source_target_pairs={{0,32},{16,48},{32,0},{48,16},{64,96},{80,112},{96,64},{112,80},{1... | collective-permute-start | bytes 1572872 | tf_op jit(solution)/shard_map/ppermute | solution.py:61
  176.6 16.1 %collective-permute-start.21 = (f32[32,16,256]{2,1,0:T(8,128)S(1)}, f32[32,16,256]{2,1,0:T(8,128)S(1)}, u32[]{:S(2)}, u32[]{:S(2)}) collective-permute-start(f32[32,16,256]{2,1,0:T(8,128)S(1)} %get-tuple-element.38), channel_id=1, source_target_pairs={{0,32},{16,48},{32,0},{48,16},{64,96},{80,112},{96,64},{112,80},{1... | collective-permute-start | bytes 1572872 | tf_op jit(solution)/shard_map/ppermute | solution.py:61
  188.0 5.7 %copy-start.1 = (f32[128,16,256]{2,1,0:T(8,128)}, f32[128,16,256]{2,1,0:T(8,128)S(1)}, u32[]{:S(2)}) copy-start(f32[128,16,256]{2,1,0:T(8,128)S(1)} %get-tuple-element.35) | copy-start | bytes 6291460
  188.0 6.9 %collective-permute-start.15 = (f32[64,16,256]{2,1,0:T(8,128)}, f32[64,16,256]{2,1,0:T(8,128)S(1)}, u32[]{:S(2)}, u32[]{:S(2)}) collective-permute-start(f32[64,16,256]{2,1,0:T(8,128)} %get-tuple-element.34), channel_id=1, source_target_pairs={{0,16},{16,0},{32,48},{48,32},{64,80},{80,64},{96,112},{112,96},{1... | collective-permute-start | bytes 3145736 | tf_op jit(solution)/shard_map/ppermute | solution.py:61
  193.7 3.0 %collective-permute-start.22 = (f32[64,16,256]{2,1,0:T(8,128)}, f32[64,16,256]{2,1,0:T(8,128)}, u32[]{:S(2)}, u32[]{:S(2)}) collective-permute-start(f32[64,16,256]{2,1,0:T(8,128)} %get-tuple-element.32), channel_id=1, source_target_pairs={{0,16},{16,0},{32,48},{48,32},{64,80},{80,64},{96,112},{112,96},{1... | collective-permute-start | bytes 3145736 | tf_op jit(solution)/shard_map/ppermute | solution.py:61
  198.0 1.3 copy-start

commit v14 on v11

--- a/solution.py
+++ b/solution.py
@@ -251,8 +251,9 @@
         return acc + v * w
 
     norm_now = strip_sum(lax.fori_loop(0, strips, init, zeros, unroll=8))
+    dot = strip_sum(lax.fori_loop(0, strips, image, zeros, unroll=8))
     for step in range(ITERS):
-        alpha = norm_now / strip_sum(lax.fori_loop(0, strips, image, zeros, unroll=8))
+        alpha = norm_now / dot
 
         def update(k, acc):
             v = dir_ref[at(k), :]
@@ -271,8 +272,14 @@
             pad_ref[at(k, 8), :] = m * d
             return carry
 
+        def direct_then_image(k, acc):
+            direct(k, 0)
+            return image(k - 1, acc)
+
         if step < ITERS - 1:
-            lax.fori_loop(0, strips, direct, 0, unroll=8)
+            direct(0, 0)
+            acc = lax.fori_loop(1, strips, direct_then_image, zeros, unroll=8)
+            dot = strip_sum(image(strips - 1, acc))
         norm_now = norm_next
     r0 = pl.multiple_of(gy * tile_rows, tile_rows)
     c0 = pl.multiple_of(gx * tile_cols, tile_cols)

time: 214 us -> 216 us (level)
  no operation moved by 1% of the time
where the time goes in v14:
time: 216 us; the launch traced here: 213 us
  Pallas kernels  71.8 us (33%)
  starting transfers between devices  43.5 us (20%)
  local copies, waits for them, and re-layouts  40.5 us (19%)
  waiting for transfers between devices  40.3 us (19%)
  other arithmetic  13.1 us (6%)
  matrix products  3.04 us (1%)
    pallas_call x1, Pallas kernels, diffuse(): pl.pallas_call(diffusion_kernel, grid=(blocks,), in_specs=[smem, smem, pl...  57.1 us
    ppermute x14, waiting for transfers between devices, stack_gather(): other = lax.ppermute(x, axis, [(j, j ^ distance) for j in range(size)])  24.1 us
    ppermute x14, starting transfers between devices, stack_gather(): other = lax.ppermute(x, axis, [(j, j ^ distance) for j in range(size)])  20.9 us
    pallas_call x1, Pallas kernels, solve_grid(): pl.pallas_call(functools.partial(cg_kernel, rounds), in_specs=[pl.BlockSp...  14.7 us
    unnamed x27, local copies, waits for them, and re-layouts  13.8 us
    ppermute x1, waiting for transfers between devices, diffuse(): south_east = lax.ppermute(field[:, :HALO, :HALO], both, pairs(1, 1))  7.07 us
    ppermute x1, starting transfers between devices, diffuse(): lax.ppermute(field[:, rows - HALO:, cols - HALO:], both, pairs(-1, -1))  5.35 us
    ppermute x1, starting transfers between devices, diffuse(): south_west = lax.ppermute(field[:, :HALO, cols - HALO:], both, pairs(-1, 1))  4.98 us
  transfers between devices with their start and end apart: 23, of which 13 were waited for; matrix products, arithmetic and copies ran while one was open for 17% of the time, Pallas kernels for 0%

profile of v14, /device:TPU:6, one launch (start us, length us, event | category | flops | bytes accessed | tf_op | source)
XLA Modules:
  0.0 213.2 jit_solution(141472961468668914)
XLA Ops:
  0.6 4.3 %fusion.26 = (f32[128,32,4]{2,1,0:T(8,128)S(1)}, f32[128,32,4]{2,1,0:T(8,128)}) fusion(f32[128,32,512]{2,1,0:T(8,128)} %core_ref.1), kind=kLoop, calls=%fused_computation.126 | loop fusion | bytes 262144 | tf_op jit(solution)/shard_map/slice | solution.py:133
  4.9 3.3 %copy.86 = f32[128,32,4]{0,1,2:T(8,128)} copy(f32[128,32,4]{2,1,0:T(8,128)} %get-tuple-element.31) | data formatting | bytes 131072
  8.2 2.4 %collective-permute-start.1 = (f32[128,32,4]{0,1,2:T(8,128)}, f32[128,32,4]{0,1,2:T(8,128)}, u32[]{:S(2)}, u32[]{:S(2)}) collective-permute-start(f32[128,32,4]{0,1,2:T(8,128)} %copy.86), channel_id=1, source_target_pairs={{0,16},{16,32},{32,48},{48,64},{64,80},{80,96},{96,112},{1,17},{17... | collective-permute-start | bytes 196616 | tf_op jit(solution)/shard_map/ppermute | solution.py:134
  10.5 1.9 copy.85
  12.5 1.3 collective-permute-start
  13.8 2.9 %fusion.25 = (f32[128,4,4]{2,1,0:T(4,128)}, f32[128,4,4]{2,1,0:T(4,128)}, f32[128,4,4]{2,1,0:T(4,128)}, f32[128,4,4]{2,1,0:T(4,128)}) fusion(f32[128,32,512]{2,1,0:T(8,128)} %core_ref.1), kind=kLoop, calls=%fused_computation.125 | loop fusion | bytes 65536 | tf_op jit(solution)/shard_map/slice | solution.py:135
  16.6 5.3 %collective-permute-start.7 = (f32[128,4,4]{2,1,0:T(4,128)}, f32[128,4,4]{2,1,0:T(4,128)S(1)}, u32[]{:S(2)}, u32[]{:S(2)}) collective-permute-start(f32[128,4,4]{2,1,0:T(4,128)} %get-tuple-element.29), channel_id=1, source_target_pairs={{0,17},{1,18},{2,19},{3,20},{4,21},{5,22},{6,23},{7,24},{8,25},{9,... | collective-permute-start | bytes 24584 | tf_op jit(solution)/shard_map/ppermute | solution.py:138
  22.0 4.1 %fusion.24 = (f32[128,4,512]{2,1,0:T(4,128)}, f32[128,4,512]{2,1,0:T(4,128)}) fusion(f32[128,32,512]{2,1,0:T(8,128)} %core_ref.1), kind=kLoop, calls=%fused_computation.124 | loop fusion | bytes 4194304 | tf_op jit(solution)/shard_map/slice | solution.py:131
  26.1 3.4 %collective-permute-start.5 = (f32[128,4,512]{2,1,0:T(4,128)}, f32[128,4,512]{2,1,0:T(4,128)S(1)}, u32[]{:S(2)}, u32[]{:S(2)}) collective-permute-start(f32[128,4,512]{2,1,0:T(4,128)} %get-tuple-element.25), channel_id=1, source_target_pairs={{0,1},{1,2},{2,3},{3,4},{4,5},{5,6},{6,7},{7,8},{8,9},{9,10},{10,1... | collective-permute-start | bytes 3145736 | tf_op jit(solution)/shard_map/ppermute | solution.py:132
  29.5 2.4 %collective-permute-start.2 = (f32[128,4,512]{2,1,0:T(4,128)}, f32[128,4,512]{2,1,0:T(4,128)}, u32[]{:S(2)}, u32[]{:S(2)}) collective-permute-start(f32[128,4,512]{2,1,0:T(4,128)} %get-tuple-element.24), channel_id=1, source_target_pairs={{1,0},{2,1},{3,2},{4,3},{5,4},{6,5},{7,6},{8,7},{9,8},{10,9},{11,1... | collective-permute-start | bytes 3145736 | tf_op jit(solution)/shard_map/ppermute | solution.py:131
  32.5 0.6 copy.71
  33.2 1.6 reshape.236
  37.0 1.4 and_convert_fusion.mask_ref
  38.5 1.3 collective-permute-start.6
  39.7 2.7 %copy.69 = f32[128,32,4]{2,1,0:T(8,128)S(1)} copy(f32[128,32,4]{0,1,2:T(8,128)} %collective-permute-done.1) | data formatting | bytes 131072 | tf_op jit(solution)/shard_map/ppermute | solution.py:134
  42.5 5.0 %collective-permute-start.4 = (f32[128,4,4]{2,1,0:T(4,128)}, f32[128,4,4]{2,1,0:T(4,128)}, u32[]{:S(2)}, u32[]{:S(2)}) collective-permute-start(f32[128,4,4]{2,1,0:T(4,128)} %get-tuple-element.27), channel_id=1, source_target_pairs={{1,16},{2,17},{3,18},{4,19},{5,20},{6,21},{7,22},{8,23},{9,24},{10... | collective-permute-start | bytes 24584 | tf_op jit(solution)/shard_map/ppermute | solution.py:136
  47.5 2.9 %copy.68 = f32[128,32,4]{2,1,0:T(8,128)} copy(f32[128,32,4]{0,1,2:T(8,128)S(1)} %collective-permute-done) | data formatting | bytes 131072 | tf_op jit(solution)/shard_map/ppermute | solution.py:133
  50.3 1.5 collective-permute-start.3
  51.8 3.5 %pad_maximum_fusion.lanes_ref = f32[128,32,128]{2,1,0:T(8,128)} fusion(f32[128,32,4]{2,1,0:T(8,128)S(1)} %copy.69, f32[128,32,4]{2,1,0:T(8,128)} %copy.68, f32[128]{0:T(128)S(1)} %pad.29.clone), kind=kLoop, calls=%fused_computation.4 | loop fusion | flops 1048576 | bytes 2228736 | tf_op jit(solution)/shard_map/concatenate | solution.py:140
  55.3 1.8 collective-permute-done.6
  57.1 4.0 %collective-permute-done.4 = f32[128,4,4]{2,1,0:T(4,128)} collective-permute-done((f32[128,4,4]{2,1,0:T(4,128)}, f32[128,4,4]{2,1,0:T(4,128)}, u32[]{:S(2)}, u32[]{:S(2)}) %collective-permute-start.4) | collective-permute-done | bytes 8224 | tf_op jit(solution)/shard_map/ppermute | solution.py:136
  61.1 7.1 %collective-permute-done.3 = f32[128,4,4]{2,1,0:T(4,128)S(1)} collective-permute-done((f32[128,4,4]{2,1,0:T(4,128)}, f32[128,4,4]{2,1,0:T(4,128)S(1)}, u32[]{:S(2)}, u32[]{:S(2)}) %collective-permute-start.3) | collective-permute-done | bytes 8224 | tf_op jit(solution)/shard_map/ppermute | solution.py:135
  68.2 3.9 %maximum_maximum_fusion.rows_ref = f32[128,8,640]{2,1,0:T(8,128)} fusion(f32[128,4,4]{2,1,0:T(4,128)S(1)} %collective-permute-done.7, f32[128,4,120]{2,1,0:T(4,128)S(1)} %broadcast_in_dim.52, f32[128,4,4]{2,1,0:T(4,128)} %collective-permute-done.6, f32[128,4,512]{2,1,0:T(4,128)S(1)} %collective-permute-done.5, f32[128,4,4]{2,1,0:T(4,128)} %collective-permute-done.4, ...), kind=kLoop, calls=%fused_computation.3 | loop fusion | flops 4587520 | bytes 4997120 | tf_op jit(solution)/shard_map/concatenate | solution.py:142
  72.1 57.1 %shard_map.111 = (f32[128,32,512]{2,1,0:T(8,128)}, f32[4,32,512]{2,1,0:T(8,128)}) custom-call(f32[128]{0:T(128)} %kappa_ref.1, f32[4,128]{1,0:T(4,128)} %weight_ref.1, f32[128,32,512]{2,1,0:T(8,128)} %core_ref.1, f32[128,32,128]{2,1,0:T(8,128)} %pad_maximum_fusion.lanes_ref, f32[128,8,640]{2,1,0:T(8,128)} %maximum_maximum_fusion.rows_ref, ...), custom_call_target="tpu_custom_call" | custom-call | flops 131072000 | bytes 16777216 | tf_op jit(solution)/shard_map/pallas_call | solution.py:160
  129.2 1.0 convert_element_type.40
  130.4 0.6 gather_fusion.1
  131.4 0.7 gather_fusion
  132.1 3.3 %collective-permute-done.8 = bf16[32,4,128]{2,1,0:T(4,128)(2,1)S(1)} collective-permute-done((bf16[32,4,128]{2,1,0:T(4,128)(2,1)S(1)}, bf16[32,4,128]{2,1,0:T(4,128)(2,1)S(1)}, u32[]{:S(2)}, u32[]{:S(2)}) %collective-permute-start.8) | collective-permute-done | bytes 32800 | tf_op jit(solution)/shard_map/ppermute | solution.py:29
  135.5 0.7 gather_fusion.2
  136.2 3.0 %convolution_bitcast_fusion = f32[4,32,128]{2,0,1:T(4,128)S(1)} fusion(bf16[32,4,128,128]{3,2,1,0:T(8,128)(2,1)} %param.13, bf16[32,4,4,128]{3,2,1,0:T(4,128)(2,1)S(1)} %bitcast.37, bf16[32,4,4,128]{3,2,1,0:T(4,128)(2,1)S(1)} %bitcast.38, pred[32,4]{1,0:T(8,128)(4,1)S(1)} %and.117, pred[32,4]{1,0:T(8,128)(4,1)S(1)} %and.113), kind=kOutput, calls=%fused_computation.5 | convolution fusion | flops 16908288 | bytes 4522240 | tf_op jit(solution)/shard_map/bkij,bkcj->cbi/dot_general | solution.py:363
  139.4 0.6 constant_dynamic-update-slice_fusion.43
  140.0 3.5 %collective-permute-start.16 = (f32[1,16,256]{2,1,0:T(8,128)S(1)}, f32[1,16,256]{2,1,0:T(8,128)S(1)}, u32[]{:S(2)}, u32[]{:S(2)}) collective-permute-start(f32[1,16,256]{2,1,0:T(8,128)S(1)} %get-tuple-element.15), channel_id=1, source_target_pairs={{0,2},{1,3},{2,0},{3,1},{4,6},{5,7},{6,4},{7,5},{8,10},{9,11},{10,... | collective-permute-start | bytes 49160 | tf_op jit(solution)/shard_map/ppermute | solution.py:61
  143.5 1.7 collective-permute-done.9
  145.3 2.9 %collective-permute-start.10 = (f32[2,16,256]{2,1,0:T(8,128)S(1)}, f32[2,16,256]{2,1,0:T(8,128)S(1)}, u32[]{:S(2)}, u32[]{:S(2)}) collective-permute-start(f32[2,16,256]{2,1,0:T(8,128)S(1)} %pad_maximum_fusion.5), channel_id=1, source_target_pairs={{0,8},{1,9},{2,10},{3,11},{4,12},{5,13},{6,14},{7,15},{8,0},{9,1},... | collective-permute-start | bytes 98312 | tf_op jit(solution)/shard_map/ppermute | solution.py:61
  148.2 0.6 collective-permute-start.17
  148.8 0.6 constant_dynamic-update-slice_fusion.16
  149.4 0.6 constant_dynamic-update-slice_fusion.42
  150.0 0.7 collective-permute-done.10
  150.7 4.4 %collective-permute-start.11 = (f32[4,16,256]{2,1,0:T(8,128)S(1)}, f32[4,16,256]{2,1,0:T(8,128)S(1)}, u32[]{:S(2)}, u32[]{:S(2)}) collective-permute-start(f32[4,16,256]{2,1,0:T(8,128)S(1)} %pad_maximum_fusion.3), channel_id=1, source_target_pairs={{0,64},{16,80},{32,96},{48,112},{64,0},{80,16},{96,32},{112,48},{1... | collective-permute-start | bytes 196616 | tf_op jit(solution)/shard_map/ppermute | solution.py:61
  155.1 2.7 %collective-permute-start.18 = (f32[4,16,256]{2,1,0:T(8,128)S(1)}, f32[4,16,256]{2,1,0:T(8,128)S(1)}, u32[]{:S(2)}, u32[]{:S(2)}) collective-permute-start(f32[4,16,256]{2,1,0:T(8,128)S(1)} %pad_maximum_fusion.4), channel_id=1, source_target_pairs={{0,64},{16,80},{32,96},{48,112},{64,0},{80,16},{96,32},{112,48},{1... | collective-permute-start | bytes 196616 | tf_op jit(solution)/shard_map/ppermute | solution.py:61
  157.8 0.6 constant_dynamic-update-slice_fusion.15
  158.4 0.6 constant_dynamic-update-slice_fusion.41
  159.1 1.8 collective-permute-done.18
  161.2 0.6 constant_dynamic-update-slice_fusion.14
  161.8 2.2 %collective-permute-done.12 = f32[8,16,256]{2,1,0:T(8,128)S(1)} collective-permute-done((f32[8,16,256]{2,1,0:T(8,128)S(1)}, f32[8,16,256]{2,1,0:T(8,128)S(1)}, u32[]{:S(2)}, u32[]{:S(2)}) %collective-permute-start.12) | collective-permute-done | bytes 131104 | tf_op jit(solution)/shard_map/ppermute | solution.py:61
  164.1 0.7 constant_dynamic-update-slice_fusion.13
  165.3 0.6 constant_dynamic-update-slice_fusion.40
  166.0 0.7 constant_dynamic-update-slice_fusion.39
  166.7 1.4 collective-permute-start.20
  168.1 3.8 %collective-permute-done.13 = f32[16,16,256]{2,1,0:T(8,128)S(1)} collective-permute-done((f32[16,16,256]{2,1,0:T(8,128)S(1)}, f32[16,16,256]{2,1,0:T(8,128)S(1)}, u32[]{:S(2)}, u32[]{:S(2)}) %collective-permute-start.13) | collective-permute-done | bytes 262176 | tf_op jit(solution)/shard_map/ppermute | solution.py:61
  171.9 0.8 constant_dynamic-update-slice_fusion.12
  172.7 2.4 %collective-permute-start.14 = (f32[32,16,256]{2,1,0:T(8,128)S(1)}, f32[32,16,256]{2,1,0:T(8,128)S(1)}, u32[]{:S(2)}, u32[]{:S(2)}) collective-permute-start(f32[32,16,256]{2,1,0:T(8,128)S(1)} %get-tuple-element.41), channel_id=1, source_target_pairs={{0,32},{16,48},{32,0},{48,16},{64,96},{80,112},{96,64},{112,80},{1... | collective-permute-start | bytes 1572872 | tf_op jit(solution)/shard_map/ppermute | solution.py:61
  175.1 0.8 constant_dynamic-update-slice_fusion.38
  175.9 2.0 collective-permute-start.21
  177.9 8.5 %collective-permute-done.14 = f32[32,16,256]{2,1,0:T(8,128)S(1)} collective-permute-done((f32[32,16,256]{2,1,0:T(8,128)S(1)}, f32[32,16,256]{2,1,0:T(8,128)S(1)}, u32[]{:S(2)}, u32[]{:S(2)}) %collective-permute-start.14) | collective-permute-done | bytes 524320 | tf_op jit(solution)/shard_map/ppermute | solution.py:61
  186.4 0.9 constant_dynamic-update-slice_fusion.11
  187.3 4.7 %collective-permute-done.21 = f32[32,16,256]{2,1,0:T(8,128)S(1)} collective-permute-done((f32[32,16,256]{2,1,0:T(8,128)S(1)}, f32[32,16,256]{2,1,0:T(8,128)S(1)}, u32[]{:S(2)}, u32[]{:S(2)}) %collective-permute-start.21) | collective-permute-done | bytes 524320 | tf_op jit(solution)/shard_map/ppermute | solution.py:61
  192.0 0.9 constant_dynamic-update-slice_fusion.37
  193.5 0.6 reshape.238
  194.2 1.1 constant_dynamic-update-slice_fusion.18.rhs_stack
  195.3 0.7 collective-permute-done.22
  195.9 1.3 constant_dynamic-update-slice_fusion.44.coded_stack
  197.3 1.3 copy-done
  198.6 14.7 %shard_map.112 = (f32[16,256]{1,0:T(8,128)}, f32[16,256]{1,0:T(8,128)}) custom-call(s32[2]{0:T(128)} %pad_add_fusion.index_ref, f32[128,16,256]{2,1,0:T(8,128)} %constant_dynamic-update-slice_fusion.18.rhs_stack, f32[128,16,256]{2,1,0:T(8,128)} %copy-done), custom_call_target="tpu_custom_call" | custom-call | tf_op jit(solution)/shard_map/pallas_call | solution.py:297
  (74 shorter events, 5.0 us)
Async XLA Ops:
  8.2 30.3 %collective-permute-start.1 = (f32[128,32,4]{0,1,2:T(8,128)}, f32[128,32,4]{0,1,2:T(8,128)}, u32[]{:S(2)}, u32[]{:S(2)}) collective-permute-start(f32[128,32,4]{0,1,2:T(8,128)} %copy.86), channel_id=1, source_target_pairs={{0,16},{16,32},{32,48},{48,64},{64,80},{80,96},{96,112},{1,17},{17... | collective-permute-start | bytes 196616 | tf_op jit(solution)/shard_map/ppermute | solution.py:134
  12.5 30.0 %collective-permute-start = (f32[128,32,4]{0,1,2:T(8,128)}, f32[128,32,4]{0,1,2:T(8,128)S(1)}, u32[]{:S(2)}, u32[]{:S(2)}) collective-permute-start(f32[128,32,4]{0,1,2:T(8,128)} %copy.85), channel_id=1, source_target_pairs={{16,0},{32,16},{48,32},{64,48},{80,64},{96,80},{112,96},{17,1},{33... | collective-permute-start | bytes 196616 | tf_op jit(solution)/shard_map/ppermute | solution.py:133
  16.6 15.9 %copy-start.2 = (s32[4096,4]{0,1:T(4,128)S(1)}, s32[4096,4]{0,1:T(4,128)}, u32[]{:S(2)}) copy-start(s32[4096,4]{0,1:T(4,128)} %param.11) | copy-start | bytes 196612
  16.6 33.7 %collective-permute-start.7 = (f32[128,4,4]{2,1,0:T(4,128)}, f32[128,4,4]{2,1,0:T(4,128)S(1)}, u32[]{:S(2)}, u32[]{:S(2)}) collective-permute-start(f32[128,4,4]{2,1,0:T(4,128)} %get-tuple-element.29), channel_id=1, source_target_pairs={{0,17},{1,18},{2,19},{3,20},{4,21},{5,22},{6,23},{7,24},{8,25},{9,... | collective-permute-start | bytes 24584 | tf_op jit(solution)/shard_map/ppermute | solution.py:138
  26.1 42.1 %collective-permute-start.5 = (f32[128,4,512]{2,1,0:T(4,128)}, f32[128,4,512]{2,1,0:T(4,128)S(1)}, u32[]{:S(2)}, u32[]{:S(2)}) collective-permute-start(f32[128,4,512]{2,1,0:T(4,128)} %get-tuple-element.25), channel_id=1, source_target_pairs={{0,1},{1,2},{2,3},{3,4},{4,5},{5,6},{6,7},{7,8},{8,9},{9,10},{10,1... | collective-permute-start | bytes 3145736 | tf_op jit(solution)/shard_map/ppermute | solution.py:132
  29.5 38.7 %collective-permute-start.2 = (f32[128,4,512]{2,1,0:T(4,128)}, f32[128,4,512]{2,1,0:T(4,128)}, u32[]{:S(2)}, u32[]{:S(2)}) collective-permute-start(f32[128,4,512]{2,1,0:T(4,128)} %get-tuple-element.24), channel_id=1, source_target_pairs={{1,0},{2,1},{3,2},{4,3},{5,4},{6,5},{7,6},{8,7},{9,8},{10,9},{11,1... | collective-permute-start | bytes 3145736 | tf_op jit(solution)/shard_map/ppermute | solution.py:131
  32.5 2.5 %copy-start.3 = (s32[4096]{0:T(1024)S(1)}, s32[4096]{0:T(1024)}, u32[]{:S(2)}) copy-start(s32[4096]{0:T(1024)} %param.12) | copy-start | bytes 49156
  38.5 18.7 %collective-permute-start.6 = (f32[128,4,4]{2,1,0:T(4,128)}, f32[128,4,4]{2,1,0:T(4,128)}, u32[]{:S(2)}, u32[]{:S(2)}) collective-permute-start(f32[128,4,4]{2,1,0:T(4,128)} %get-tuple-element.28), channel_id=1, source_target_pairs={{16,1},{17,2},{18,3},{19,4},{20,5},{21,6},{22,7},{23,8},{24,9},{25... | collective-permute-start | bytes 24584 | tf_op jit(solution)/shard_map/ppermute | solution.py:137
  42.5 18.6 %collective-permute-start.4 = (f32[128,4,4]{2,1,0:T(4,128)}, f32[128,4,4]{2,1,0:T(4,128)}, u32[]{:S(2)}, u32[]{:S(2)}) collective-permute-start(f32[128,4,4]{2,1,0:T(4,128)} %get-tuple-element.27), channel_id=1, source_target_pairs={{1,16},{2,17},{3,18},{4,19},{5,20},{6,21},{7,22},{8,23},{9,24},{10... | collective-permute-start | bytes 24584 | tf_op jit(solution)/shard_map/ppermute | solution.py:136
  50.3 17.8 %collective-permute-start.3 = (f32[128,4,4]{2,1,0:T(4,128)}, f32[128,4,4]{2,1,0:T(4,128)S(1)}, u32[]{:S(2)}, u32[]{:S(2)}) collective-permute-start(f32[128,4,4]{2,1,0:T(4,128)} %get-tuple-element.26), channel_id=1, source_target_pairs={{17,0},{18,1},{19,2},{20,3},{21,4},{22,5},{23,6},{24,7},{25,8},{26... | collective-permute-start | bytes 24584 | tf_op jit(solution)/shard_map/ppermute | solution.py:135
  131.1 4.4 %collective-permute-start.8 = (bf16[32,4,128]{2,1,0:T(4,128)(2,1)S(1)}, bf16[32,4,128]{2,1,0:T(4,128)(2,1)S(1)}, u32[]{:S(2)}, u32[]{:S(2)}) collective-permute-start(bf16[32,4,128]{2,1,0:T(4,128)(2,1)S(1)} %broadcast_multiply_fusion), channel_id=1, source_target_pairs={{0,112},{16,0},{32,16},{48,32},{64,48},{80,64},{96,80},{112,96},{1... | collective-permute-start | bytes 98312 | tf_op jit(solution)/shard_map/ppermute | solution.py:29
  136.2 3.1 %copy-start.4 = (f32[16,256]{1,0:T(8,128)S(1)}, f32[16,256]{1,0:T(8,128)}, u32[]{:S(2)}) copy-start(f32[16,256]{1,0:T(8,128)} %param.15) | copy-start | bytes 49156
  136.2 3.1 %copy-start.5 = (s32[16,256]{1,0:T(8,128)S(1)}, s32[16,256]{1,0:T(8,128)}, u32[]{:S(2)}) copy-start(s32[16,256]{1,0:T(8,128)} %param.14) | copy-start | bytes 49156
  140.0 5.2 %collective-permute-start.9 = (f32[1,16,256]{2,1,0:T(8,128)S(1)}, f32[1,16,256]{2,1,0:T(8,128)S(1)}, u32[]{:S(2)}, u32[]{:S(2)}) collective-permute-start(f32[1,16,256]{2,1,0:T(8,128)S(1)} %get-tuple-element.80), channel_id=1, source_target_pairs={{0,2},{1,3},{2,0},{3,1},{4,6},{5,7},{6,4},{7,5},{8,10},{9,11},{10,... | collective-permute-start | bytes 49160 | tf_op jit(solution)/shard_map/ppermute | solution.py:61
  140.0 8.1 %collective-permute-start.16 = (f32[1,16,256]{2,1,0:T(8,128)S(1)}, f32[1,16,256]{2,1,0:T(8,128)S(1)}, u32[]{:S(2)}, u32[]{:S(2)}) collective-permute-start(f32[1,16,256]{2,1,0:T(8,128)S(1)} %get-tuple-element.15), channel_id=1, source_target_pairs={{0,2},{1,3},{2,0},{3,1},{4,6},{5,7},{6,4},{7,5},{8,10},{9,11},{10,... | collective-permute-start | bytes 49160 | tf_op jit(solution)/shard_map/ppermute | solution.py:61
  145.3 5.4 %collective-permute-start.10 = (f32[2,16,256]{2,1,0:T(8,128)S(1)}, f32[2,16,256]{2,1,0:T(8,128)S(1)}, u32[]{:S(2)}, u32[]{:S(2)}) collective-permute-start(f32[2,16,256]{2,1,0:T(8,128)S(1)} %pad_maximum_fusion.5), channel_id=1, source_target_pairs={{0,8},{1,9},{2,10},{3,11},{4,12},{5,13},{6,14},{7,15},{8,0},{9,1},... | collective-permute-start | bytes 98312 | tf_op jit(solution)/shard_map/ppermute | solution.py:61
  148.2 6.9 %collective-permute-start.17 = (f32[2,16,256]{2,1,0:T(8,128)S(1)}, f32[2,16,256]{2,1,0:T(8,128)S(1)}, u32[]{:S(2)}, u32[]{:S(2)}) collective-permute-start(f32[2,16,256]{2,1,0:T(8,128)S(1)} %pad_maximum_fusion.6), channel_id=1, source_target_pairs={{0,8},{1,9},{2,10},{3,11},{4,12},{5,13},{6,14},{7,15},{8,0},{9,1},... | collective-permute-start | bytes 98312 | tf_op jit(solution)/shard_map/ppermute | solution.py:61
  150.7 8.3 %collective-permute-start.11 = (f32[4,16,256]{2,1,0:T(8,128)S(1)}, f32[4,16,256]{2,1,0:T(8,128)S(1)}, u32[]{:S(2)}, u32[]{:S(2)}) collective-permute-start(f32[4,16,256]{2,1,0:T(8,128)S(1)} %pad_maximum_fusion.3), channel_id=1, source_target_pairs={{0,64},{16,80},{32,96},{48,112},{64,0},{80,16},{96,32},{112,48},{1... | collective-permute-start | bytes 196616 | tf_op jit(solution)/shard_map/ppermute | solution.py:61
  155.1 5.8 %collective-permute-start.18 = (f32[4,16,256]{2,1,0:T(8,128)S(1)}, f32[4,16,256]{2,1,0:T(8,128)S(1)}, u32[]{:S(2)}, u32[]{:S(2)}) collective-permute-start(f32[4,16,256]{2,1,0:T(8,128)S(1)} %pad_maximum_fusion.4), channel_id=1, source_target_pairs={{0,64},{16,80},{32,96},{48,112},{64,0},{80,16},{96,32},{112,48},{1... | collective-permute-start | bytes 196616 | tf_op jit(solution)/shard_map/ppermute | solution.py:61
  159.0 5.0 %collective-permute-start.12 = (f32[8,16,256]{2,1,0:T(8,128)S(1)}, f32[8,16,256]{2,1,0:T(8,128)S(1)}, u32[]{:S(2)}, u32[]{:S(2)}) collective-permute-start(f32[8,16,256]{2,1,0:T(8,128)S(1)} %pad_maximum_fusion.1), channel_id=1, source_target_pairs={{0,1},{1,0},{2,3},{3,2},{4,5},{5,4},{6,7},{7,6},{8,9},{9,8},{10,11... | collective-permute-start | bytes 393224 | tf_op jit(solution)/shard_map/ppermute | solution.py:61
  160.9 5.0 %collective-permute-start.19 = (f32[8,16,256]{2,1,0:T(8,128)S(1)}, f32[8,16,256]{2,1,0:T(8,128)S(1)}, u32[]{:S(2)}, u32[]{:S(2)}) collective-permute-start(f32[8,16,256]{2,1,0:T(8,128)S(1)} %pad_maximum_fusion.2), channel_id=1, source_target_pairs={{0,1},{1,0},{2,3},{3,2},{4,5},{5,4},{6,7},{7,6},{8,9},{9,8},{10,11... | collective-permute-start | bytes 393224 | tf_op jit(solution)/shard_map/ppermute | solution.py:61
  164.8 7.2 %collective-permute-start.13 = (f32[16,16,256]{2,1,0:T(8,128)S(1)}, f32[16,16,256]{2,1,0:T(8,128)S(1)}, u32[]{:S(2)}, u32[]{:S(2)}) collective-permute-start(f32[16,16,256]{2,1,0:T(8,128)S(1)} %get-tuple-element.49), channel_id=1, source_target_pairs={{0,4},{1,5},{2,6},{3,7},{4,0},{5,1},{6,2},{7,3},{8,12},{9,13},{10,... | collective-permute-start | bytes 786440 | tf_op jit(solution)/shard_map/ppermute | solution.py:61
  166.7 8.4 %collective-permute-start.20 = (f32[16,16,256]{2,1,0:T(8,128)S(1)}, f32[16,16,256]{2,1,0:T(8,128)S(1)}, u32[]{:S(2)}, u32[]{:S(2)}) collective-permute-start(f32[16,16,256]{2,1,0:T(8,128)S(1)} %get-tuple-element.45), channel_id=1, source_target_pairs={{0,4},{1,5},{2,6},{3,7},{4,0},{5,1},{6,2},{7,3},{8,12},{9,13},{10,... | collective-permute-start | bytes 786440 | tf_op jit(solution)/shard_map/ppermute | solution.py:61
  172.7 13.7 %collective-permute-start.14 = (f32[32,16,256]{2,1,0:T(8,128)S(1)}, f32[32,16,256]{2,1,0:T(8,128)S(1)}, u32[]{:S(2)}, u32[]{:S(2)}) collective-permute-start(f32[32,16,256]{2,1,0:T(8,128)S(1)} %get-tuple-element.41), channel_id=1, source_target_pairs={{0,32},{16,48},{32,0},{48,16},{64,96},{80,112},{96,64},{112,80},{1... | collective-permute-start | bytes 1572872 | tf_op jit(solution)/shard_map/ppermute | solution.py:61
  175.9 16.1 %collective-permute-start.21 = (f32[32,16,256]{2,1,0:T(8,128)S(1)}, f32[32,16,256]{2,1,0:T(8,128)S(1)}, u32[]{:S(2)}, u32[]{:S(2)}) collective-permute-start(f32[32,16,256]{2,1,0:T(8,128)S(1)} %get-tuple-element.38), channel_id=1, source_target_pairs={{0,32},{16,48},{32,0},{48,16},{64,96},{80,112},{96,64},{112,80},{1... | collective-permute-start | bytes 1572872 | tf_op jit(solution)/shard_map/ppermute | solution.py:61
  187.3 5.7 %copy-start.1 = (f32[128,16,256]{2,1,0:T(8,128)}, f32[128,16,256]{2,1,0:T(8,128)S(1)}, u32[]{:S(2)}) copy-start(f32[128,16,256]{2,1,0:T(8,128)S(1)} %get-tuple-element.35) | copy-start | bytes 6291460
  187.3 6.9 %collective-permute-start.15 = (f32[64,16,256]{2,1,0:T(8,128)}, f32[64,16,256]{2,1,0:T(8,128)S(1)}, u32[]{:S(2)}, u32[]{:S(2)}) collective-permute-start(f32[64,16,256]{2,1,0:T(8,128)} %get-tuple-element.34), channel_id=1, source_target_pairs={{0,16},{16,0},{32,48},{48,32},{64,80},{80,64},{96,112},{112,96},{1... | collective-permute-start | bytes 3145736 | tf_op jit(solution)/shard_map/ppermute | solution.py:61
  192.9 3.0 %collective-permute-start.22 = (f32[64,16,256]{2,1,0:T(8,128)}, f32[64,16,256]{2,1,0:T(8,128)}, u32[]{:S(2)}, u32[]{:S(2)}) collective-permute-start(f32[64,16,256]{2,1,0:T(8,128)} %get-tuple-element.32), channel_id=1, source_target_pairs={{0,16},{16,0},{32,48},{48,32},{64,80},{80,64},{96,112},{112,96},{1... | collective-permute-start | bytes 3145736 | tf_op jit(solution)/shard_map/ppermute | solution.py:61
  197.2 1.3 copy-start

commit v15 on v14

--- a/solution.py
+++ b/solution.py
@@ -214,7 +214,7 @@
         coded_ref[pl.ds(r0, tile_rows), pl.ds(c0, tile_cols)] = coded_stack[k]
         return carry
 
-    lax.fori_loop(0, rhs_stack.shape[0], place, 0, unroll=4)
+    lax.fori_loop(0, rhs_stack.shape[0], place, 0, unroll=8)
     strips = rows // 8
     zeros = jnp.zeros((8, cols), jnp.float32)
     pad_ref[0:8, :] = zeros
@@ -250,8 +250,14 @@
         img_ref[at(k), :] = w
         return acc + v * w
 
-    norm_now = strip_sum(lax.fori_loop(0, strips, init, zeros, unroll=8))
-    dot = strip_sum(lax.fori_loop(0, strips, image, zeros, unroll=8))
+    def init_then_image(k, accs):
+        squares, dots = accs
+        return init(k, squares), image(k - 1, dots)
+
+    first = init(0, zeros)
+    squares, dots = lax.fori_loop(1, strips, init_then_image, (first, zeros), unroll=8)
+    norm_now = strip_sum(squares)
+    dot = strip_sum(image(strips - 1, dots))
     for step in range(ITERS):
         alpha = norm_now / dot
 

time: 216 us -> 216 us (level)
  no operation moved by 1% of the time
where the time goes in v15:
time: 216 us; the launch traced here: 214 us
  Pallas kernels  72.4 us (34%)
  starting transfers between devices  43.5 us (20%)
  local copies, waits for them, and re-layouts  40.5 us (19%)
  waiting for transfers between devices  40.3 us (19%)
  other arithmetic  13.1 us (6%)
  matrix products  3.04 us (1%)
    pallas_call x1, Pallas kernels, diffuse(): pl.pallas_call(diffusion_kernel, grid=(blocks,), in_specs=[smem, smem, pl...  57.1 us
    ppermute x14, waiting for transfers between devices, stack_gather(): other = lax.ppermute(x, axis, [(j, j ^ distance) for j in range(size)])  24.2 us
    ppermute x14, starting transfers between devices, stack_gather(): other = lax.ppermute(x, axis, [(j, j ^ distance) for j in range(size)])  20.9 us
    pallas_call x1, Pallas kernels, solve_grid(): pl.pallas_call(functools.partial(cg_kernel, rounds), in_specs=[pl.BlockSp...  15.3 us
    unnamed x27, local copies, waits for them, and re-layouts  13.8 us
    ppermute x1, waiting for transfers between devices, diffuse(): south_east = lax.ppermute(field[:, :HALO, :HALO], both, pairs(1, 1))  7.07 us
    ppermute x1, starting transfers between devices, diffuse(): lax.ppermute(field[:, rows - HALO:, cols - HALO:], both, pairs(-1, -1))  5.35 us
    ppermute x1, starting transfers between devices, diffuse(): south_west = lax.ppermute(field[:, :HALO, cols - HALO:], both, pairs(-1, 1))  4.98 us
  transfers between devices with their start and end apart: 23, of which 13 were waited for; matrix products, arithmetic and copies ran while one was open for 17% of the time, Pallas kernels for 0%

profile of v15, /device:TPU:6, one launch (start us, length us, event | category | flops | bytes accessed | tf_op | source)
XLA Modules:
  0.0 213.9 jit_solution(16941501999754049448)
XLA Ops:
  0.6 4.3 %fusion.26 = (f32[128,32,4]{2,1,0:T(8,128)S(1)}, f32[128,32,4]{2,1,0:T(8,128)}) fusion(f32[128,32,512]{2,1,0:T(8,128)} %core_ref.1), kind=kLoop, calls=%fused_computation.126 | loop fusion | bytes 262144 | tf_op jit(solution)/shard_map/slice | solution.py:133
  4.9 3.3 %copy.86 = f32[128,32,4]{0,1,2:T(8,128)} copy(f32[128,32,4]{2,1,0:T(8,128)} %get-tuple-element.31) | data formatting | bytes 131072
  8.2 2.4 %collective-permute-start.1 = (f32[128,32,4]{0,1,2:T(8,128)}, f32[128,32,4]{0,1,2:T(8,128)}, u32[]{:S(2)}, u32[]{:S(2)}) collective-permute-start(f32[128,32,4]{0,1,2:T(8,128)} %copy.86), channel_id=1, source_target_pairs={{0,16},{16,32},{32,48},{48,64},{64,80},{80,96},{96,112},{1,17},{17... | collective-permute-start | bytes 196616 | tf_op jit(solution)/shard_map/ppermute | solution.py:134
  10.5 1.9 copy.85
  12.5 1.3 collective-permute-start
  13.8 2.9 %fusion.25 = (f32[128,4,4]{2,1,0:T(4,128)}, f32[128,4,4]{2,1,0:T(4,128)}, f32[128,4,4]{2,1,0:T(4,128)}, f32[128,4,4]{2,1,0:T(4,128)}) fusion(f32[128,32,512]{2,1,0:T(8,128)} %core_ref.1), kind=kLoop, calls=%fused_computation.125 | loop fusion | bytes 65536 | tf_op jit(solution)/shard_map/slice | solution.py:135
  16.6 5.3 %collective-permute-start.7 = (f32[128,4,4]{2,1,0:T(4,128)}, f32[128,4,4]{2,1,0:T(4,128)S(1)}, u32[]{:S(2)}, u32[]{:S(2)}) collective-permute-start(f32[128,4,4]{2,1,0:T(4,128)} %get-tuple-element.29), channel_id=1, source_target_pairs={{0,17},{1,18},{2,19},{3,20},{4,21},{5,22},{6,23},{7,24},{8,25},{9,... | collective-permute-start | bytes 24584 | tf_op jit(solution)/shard_map/ppermute | solution.py:138
  22.0 4.1 %fusion.24 = (f32[128,4,512]{2,1,0:T(4,128)}, f32[128,4,512]{2,1,0:T(4,128)}) fusion(f32[128,32,512]{2,1,0:T(8,128)} %core_ref.1), kind=kLoop, calls=%fused_computation.124 | loop fusion | bytes 4194304 | tf_op jit(solution)/shard_map/slice | solution.py:131
  26.1 3.4 %collective-permute-start.5 = (f32[128,4,512]{2,1,0:T(4,128)}, f32[128,4,512]{2,1,0:T(4,128)S(1)}, u32[]{:S(2)}, u32[]{:S(2)}) collective-permute-start(f32[128,4,512]{2,1,0:T(4,128)} %get-tuple-element.25), channel_id=1, source_target_pairs={{0,1},{1,2},{2,3},{3,4},{4,5},{5,6},{6,7},{7,8},{8,9},{9,10},{10,1... | collective-permute-start | bytes 3145736 | tf_op jit(solution)/shard_map/ppermute | solution.py:132
  29.5 2.4 %collective-permute-start.2 = (f32[128,4,512]{2,1,0:T(4,128)}, f32[128,4,512]{2,1,0:T(4,128)}, u32[]{:S(2)}, u32[]{:S(2)}) collective-permute-start(f32[128,4,512]{2,1,0:T(4,128)} %get-tuple-element.24), channel_id=1, source_target_pairs={{1,0},{2,1},{3,2},{4,3},{5,4},{6,5},{7,6},{8,7},{9,8},{10,9},{11,1... | collective-permute-start | bytes 3145736 | tf_op jit(solution)/shard_map/ppermute | solution.py:131
  32.5 0.6 copy.71
  33.2 1.6 reshape.236
  37.0 1.4 and_convert_fusion.mask_ref
  38.5 1.3 collective-permute-start.6
  39.7 2.7 %copy.69 = f32[128,32,4]{2,1,0:T(8,128)S(1)} copy(f32[128,32,4]{0,1,2:T(8,128)} %collective-permute-done.1) | data formatting | bytes 131072 | tf_op jit(solution)/shard_map/ppermute | solution.py:134
  42.5 5.0 %collective-permute-start.4 = (f32[128,4,4]{2,1,0:T(4,128)}, f32[128,4,4]{2,1,0:T(4,128)}, u32[]{:S(2)}, u32[]{:S(2)}) collective-permute-start(f32[128,4,4]{2,1,0:T(4,128)} %get-tuple-element.27), channel_id=1, source_target_pairs={{1,16},{2,17},{3,18},{4,19},{5,20},{6,21},{7,22},{8,23},{9,24},{10... | collective-permute-start | bytes 24584 | tf_op jit(solution)/shard_map/ppermute | solution.py:136
  47.5 2.9 %copy.68 = f32[128,32,4]{2,1,0:T(8,128)} copy(f32[128,32,4]{0,1,2:T(8,128)S(1)} %collective-permute-done) | data formatting | bytes 131072 | tf_op jit(solution)/shard_map/ppermute | solution.py:133
  50.3 1.5 collective-permute-start.3
  51.8 3.5 %pad_maximum_fusion.lanes_ref = f32[128,32,128]{2,1,0:T(8,128)} fusion(f32[128,32,4]{2,1,0:T(8,128)S(1)} %copy.69, f32[128,32,4]{2,1,0:T(8,128)} %copy.68, f32[128]{0:T(128)S(1)} %pad.29.clone), kind=kLoop, calls=%fused_computation.4 | loop fusion | flops 1048576 | bytes 2228736 | tf_op jit(solution)/shard_map/concatenate | solution.py:140
  55.3 1.8 collective-permute-done.6
  57.1 4.0 %collective-permute-done.4 = f32[128,4,4]{2,1,0:T(4,128)} collective-permute-done((f32[128,4,4]{2,1,0:T(4,128)}, f32[128,4,4]{2,1,0:T(4,128)}, u32[]{:S(2)}, u32[]{:S(2)}) %collective-permute-start.4) | collective-permute-done | bytes 8224 | tf_op jit(solution)/shard_map/ppermute | solution.py:136
  61.1 7.1 %collective-permute-done.3 = f32[128,4,4]{2,1,0:T(4,128)S(1)} collective-permute-done((f32[128,4,4]{2,1,0:T(4,128)}, f32[128,4,4]{2,1,0:T(4,128)S(1)}, u32[]{:S(2)}, u32[]{:S(2)}) %collective-permute-start.3) | collective-permute-done | bytes 8224 | tf_op jit(solution)/shard_map/ppermute | solution.py:135
  68.2 3.9 %maximum_maximum_fusion.rows_ref = f32[128,8,640]{2,1,0:T(8,128)} fusion(f32[128,4,4]{2,1,0:T(4,128)S(1)} %collective-permute-done.7, f32[128,4,120]{2,1,0:T(4,128)S(1)} %broadcast_in_dim.52, f32[128,4,4]{2,1,0:T(4,128)} %collective-permute-done.6, f32[128,4,512]{2,1,0:T(4,128)S(1)} %collective-permute-done.5, f32[128,4,4]{2,1,0:T(4,128)} %collective-permute-done.4, ...), kind=kLoop, calls=%fused_computation.3 | loop fusion | flops 4587520 | bytes 4997120 | tf_op jit(solution)/shard_map/concatenate | solution.py:142
  72.1 57.1 %shard_map.111 = (f32[128,32,512]{2,1,0:T(8,128)}, f32[4,32,512]{2,1,0:T(8,128)}) custom-call(f32[128]{0:T(128)} %kappa_ref.1, f32[4,128]{1,0:T(4,128)} %weight_ref.1, f32[128,32,512]{2,1,0:T(8,128)} %core_ref.1, f32[128,32,128]{2,1,0:T(8,128)} %pad_maximum_fusion.lanes_ref, f32[128,8,640]{2,1,0:T(8,128)} %maximum_maximum_fusion.rows_ref, ...), custom_call_target="tpu_custom_call" | custom-call | flops 131072000 | bytes 16777216 | tf_op jit(solution)/shard_map/pallas_call | solution.py:160
  129.2 1.0 convert_element_type.40
  130.4 0.6 gather_fusion.1
  131.4 0.7 gather_fusion
  132.1 3.3 %collective-permute-done.8 = bf16[32,4,128]{2,1,0:T(4,128)(2,1)S(1)} collective-permute-done((bf16[32,4,128]{2,1,0:T(4,128)(2,1)S(1)}, bf16[32,4,128]{2,1,0:T(4,128)(2,1)S(1)}, u32[]{:S(2)}, u32[]{:S(2)}) %collective-permute-start.8) | collective-permute-done | bytes 32800 | tf_op jit(solution)/shard_map/ppermute | solution.py:29
  135.5 0.7 gather_fusion.2
  136.2 3.0 %convolution_bitcast_fusion = f32[4,32,128]{2,0,1:T(4,128)S(1)} fusion(bf16[32,4,128,128]{3,2,1,0:T(8,128)(2,1)} %param.13, bf16[32,4,4,128]{3,2,1,0:T(4,128)(2,1)S(1)} %bitcast.37, bf16[32,4,4,128]{3,2,1,0:T(4,128)(2,1)S(1)} %bitcast.38, pred[32,4]{1,0:T(8,128)(4,1)S(1)} %and.117, pred[32,4]{1,0:T(8,128)(4,1)S(1)} %and.113), kind=kOutput, calls=%fused_computation.5 | convolution fusion | flops 16908288 | bytes 4522240 | tf_op jit(solution)/shard_map/bkij,bkcj->cbi/dot_general | solution.py:369
  139.4 0.6 constant_dynamic-update-slice_fusion.43
  140.0 3.5 %collective-permute-start.16 = (f32[1,16,256]{2,1,0:T(8,128)S(1)}, f32[1,16,256]{2,1,0:T(8,128)S(1)}, u32[]{:S(2)}, u32[]{:S(2)}) collective-permute-start(f32[1,16,256]{2,1,0:T(8,128)S(1)} %get-tuple-element.15), channel_id=1, source_target_pairs={{0,2},{1,3},{2,0},{3,1},{4,6},{5,7},{6,4},{7,5},{8,10},{9,11},{10,... | collective-permute-start | bytes 49160 | tf_op jit(solution)/shard_map/ppermute | solution.py:61
  143.5 1.7 collective-permute-done.9
  145.3 2.9 %collective-permute-start.10 = (f32[2,16,256]{2,1,0:T(8,128)S(1)}, f32[2,16,256]{2,1,0:T(8,128)S(1)}, u32[]{:S(2)}, u32[]{:S(2)}) collective-permute-start(f32[2,16,256]{2,1,0:T(8,128)S(1)} %pad_maximum_fusion.5), channel_id=1, source_target_pairs={{0,8},{1,9},{2,10},{3,11},{4,12},{5,13},{6,14},{7,15},{8,0},{9,1},... | collective-permute-start | bytes 98312 | tf_op jit(solution)/shard_map/ppermute | solution.py:61
  148.2 0.6 collective-permute-start.17
  148.8 0.6 constant_dynamic-update-slice_fusion.16
  149.4 0.6 constant_dynamic-update-slice_fusion.42
  150.0 0.7 collective-permute-done.10
  150.7 4.4 %collective-permute-start.11 = (f32[4,16,256]{2,1,0:T(8,128)S(1)}, f32[4,16,256]{2,1,0:T(8,128)S(1)}, u32[]{:S(2)}, u32[]{:S(2)}) collective-permute-start(f32[4,16,256]{2,1,0:T(8,128)S(1)} %pad_maximum_fusion.3), channel_id=1, source_target_pairs={{0,64},{16,80},{32,96},{48,112},{64,0},{80,16},{96,32},{112,48},{1... | collective-permute-start | bytes 196616 | tf_op jit(solution)/shard_map/ppermute | solution.py:61
  155.1 2.7 %collective-permute-start.18 = (f32[4,16,256]{2,1,0:T(8,128)S(1)}, f32[4,16,256]{2,1,0:T(8,128)S(1)}, u32[]{:S(2)}, u32[]{:S(2)}) collective-permute-start(f32[4,16,256]{2,1,0:T(8,128)S(1)} %pad_maximum_fusion.4), channel_id=1, source_target_pairs={{0,64},{16,80},{32,96},{48,112},{64,0},{80,16},{96,32},{112,48},{1... | collective-permute-start | bytes 196616 | tf_op jit(solution)/shard_map/ppermute | solution.py:61
  157.8 0.6 constant_dynamic-update-slice_fusion.15
  158.4 0.6 constant_dynamic-update-slice_fusion.41
  159.1 1.8 collective-permute-done.18
  161.2 0.6 constant_dynamic-update-slice_fusion.14
  161.8 2.2 %collective-permute-done.12 = f32[8,16,256]{2,1,0:T(8,128)S(1)} collective-permute-done((f32[8,16,256]{2,1,0:T(8,128)S(1)}, f32[8,16,256]{2,1,0:T(8,128)S(1)}, u32[]{:S(2)}, u32[]{:S(2)}) %collective-permute-start.12) | collective-permute-done | bytes 131104 | tf_op jit(solution)/shard_map/ppermute | solution.py:61
  164.1 0.7 constant_dynamic-update-slice_fusion.13
  165.3 0.6 constant_dynamic-update-slice_fusion.40
  166.0 0.7 constant_dynamic-update-slice_fusion.39
  166.7 1.4 collective-permute-start.20
  168.1 3.8 %collective-permute-done.13 = f32[16,16,256]{2,1,0:T(8,128)S(1)} collective-permute-done((f32[16,16,256]{2,1,0:T(8,128)S(1)}, f32[16,16,256]{2,1,0:T(8,128)S(1)}, u32[]{:S(2)}, u32[]{:S(2)}) %collective-permute-start.13) | collective-permute-done | bytes 262176 | tf_op jit(solution)/shard_map/ppermute | solution.py:61
  171.9 0.8 constant_dynamic-update-slice_fusion.12
  172.7 2.4 %collective-permute-start.14 = (f32[32,16,256]{2,1,0:T(8,128)S(1)}, f32[32,16,256]{2,1,0:T(8,128)S(1)}, u32[]{:S(2)}, u32[]{:S(2)}) collective-permute-start(f32[32,16,256]{2,1,0:T(8,128)S(1)} %get-tuple-element.41), channel_id=1, source_target_pairs={{0,32},{16,48},{32,0},{48,16},{64,96},{80,112},{96,64},{112,80},{1... | collective-permute-start | bytes 1572872 | tf_op jit(solution)/shard_map/ppermute | solution.py:61
  175.1 0.8 constant_dynamic-update-slice_fusion.38
  175.9 2.0 collective-permute-start.21
  177.9 8.5 %collective-permute-done.14 = f32[32,16,256]{2,1,0:T(8,128)S(1)} collective-permute-done((f32[32,16,256]{2,1,0:T(8,128)S(1)}, f32[32,16,256]{2,1,0:T(8,128)S(1)}, u32[]{:S(2)}, u32[]{:S(2)}) %collective-permute-start.14) | collective-permute-done | bytes 524320 | tf_op jit(solution)/shard_map/ppermute | solution.py:61
  186.4 0.9 constant_dynamic-update-slice_fusion.11
  187.3 4.7 %collective-permute-done.21 = f32[32,16,256]{2,1,0:T(8,128)S(1)} collective-permute-done((f32[32,16,256]{2,1,0:T(8,128)S(1)}, f32[32,16,256]{2,1,0:T(8,128)S(1)}, u32[]{:S(2)}, u32[]{:S(2)}) %collective-permute-start.21) | collective-permute-done | bytes 524320 | tf_op jit(solution)/shard_map/ppermute | solution.py:61
  192.0 0.9 constant_dynamic-update-slice_fusion.37
  193.5 0.6 reshape.238
  194.2 1.1 constant_dynamic-update-slice_fusion.18.rhs_stack
  195.3 0.7 collective-permute-done.22
  195.9 1.3 constant_dynamic-update-slice_fusion.44.coded_stack
  197.2 1.3 copy-done
  198.6 15.3 %shard_map.112 = (f32[16,256]{1,0:T(8,128)}, f32[16,256]{1,0:T(8,128)}) custom-call(s32[2]{0:T(128)} %pad_add_fusion.index_ref, f32[128,16,256]{2,1,0:T(8,128)} %constant_dynamic-update-slice_fusion.18.rhs_stack, f32[128,16,256]{2,1,0:T(8,128)} %copy-done), custom_call_target="tpu_custom_call" | custom-call | tf_op jit(solution)/shard_map/pallas_call | solution.py:303
  (74 shorter events, 5.0 us)
Async XLA Ops:
  8.2 30.3 %collective-permute-start.1 = (f32[128,32,4]{0,1,2:T(8,128)}, f32[128,32,4]{0,1,2:T(8,128)}, u32[]{:S(2)}, u32[]{:S(2)}) collective-permute-start(f32[128,32,4]{0,1,2:T(8,128)} %copy.86), channel_id=1, source_target_pairs={{0,16},{16,32},{32,48},{48,64},{64,80},{80,96},{96,112},{1,17},{17... | collective-permute-start | bytes 196616 | tf_op jit(solution)/shard_map/ppermute | solution.py:134
  12.5 30.0 %collective-permute-start = (f32[128,32,4]{0,1,2:T(8,128)}, f32[128,32,4]{0,1,2:T(8,128)S(1)}, u32[]{:S(2)}, u32[]{:S(2)}) collective-permute-start(f32[128,32,4]{0,1,2:T(8,128)} %copy.85), channel_id=1, source_target_pairs={{16,0},{32,16},{48,32},{64,48},{80,64},{96,80},{112,96},{17,1},{33... | collective-permute-start | bytes 196616 | tf_op jit(solution)/shard_map/ppermute | solution.py:133
  16.6 15.9 %copy-start.2 = (s32[4096,4]{0,1:T(4,128)S(1)}, s32[4096,4]{0,1:T(4,128)}, u32[]{:S(2)}) copy-start(s32[4096,4]{0,1:T(4,128)} %param.11) | copy-start | bytes 196612
  16.6 33.7 %collective-permute-start.7 = (f32[128,4,4]{2,1,0:T(4,128)}, f32[128,4,4]{2,1,0:T(4,128)S(1)}, u32[]{:S(2)}, u32[]{:S(2)}) collective-permute-start(f32[128,4,4]{2,1,0:T(4,128)} %get-tuple-element.29), channel_id=1, source_target_pairs={{0,17},{1,18},{2,19},{3,20},{4,21},{5,22},{6,23},{7,24},{8,25},{9,... | collective-permute-start | bytes 24584 | tf_op jit(solution)/shard_map/ppermute | solution.py:138
  26.1 42.1 %collective-permute-start.5 = (f32[128,4,512]{2,1,0:T(4,128)}, f32[128,4,512]{2,1,0:T(4,128)S(1)}, u32[]{:S(2)}, u32[]{:S(2)}) collective-permute-start(f32[128,4,512]{2,1,0:T(4,128)} %get-tuple-element.25), channel_id=1, source_target_pairs={{0,1},{1,2},{2,3},{3,4},{4,5},{5,6},{6,7},{7,8},{8,9},{9,10},{10,1... | collective-permute-start | bytes 3145736 | tf_op jit(solution)/shard_map/ppermute | solution.py:132
  29.5 38.7 %collective-permute-start.2 = (f32[128,4,512]{2,1,0:T(4,128)}, f32[128,4,512]{2,1,0:T(4,128)}, u32[]{:S(2)}, u32[]{:S(2)}) collective-permute-start(f32[128,4,512]{2,1,0:T(4,128)} %get-tuple-element.24), channel_id=1, source_target_pairs={{1,0},{2,1},{3,2},{4,3},{5,4},{6,5},{7,6},{8,7},{9,8},{10,9},{11,1... | collective-permute-start | bytes 3145736 | tf_op jit(solution)/shard_map/ppermute | solution.py:131
  32.5 2.5 %copy-start.3 = (s32[4096]{0:T(1024)S(1)}, s32[4096]{0:T(1024)}, u32[]{:S(2)}) copy-start(s32[4096]{0:T(1024)} %param.12) | copy-start | bytes 49156
  38.5 18.7 %collective-permute-start.6 = (f32[128,4,4]{2,1,0:T(4,128)}, f32[128,4,4]{2,1,0:T(4,128)}, u32[]{:S(2)}, u32[]{:S(2)}) collective-permute-start(f32[128,4,4]{2,1,0:T(4,128)} %get-tuple-element.28), channel_id=1, source_target_pairs={{16,1},{17,2},{18,3},{19,4},{20,5},{21,6},{22,7},{23,8},{24,9},{25... | collective-permute-start | bytes 24584 | tf_op jit(solution)/shard_map/ppermute | solution.py:137
  42.5 18.6 %collective-permute-start.4 = (f32[128,4,4]{2,1,0:T(4,128)}, f32[128,4,4]{2,1,0:T(4,128)}, u32[]{:S(2)}, u32[]{:S(2)}) collective-permute-start(f32[128,4,4]{2,1,0:T(4,128)} %get-tuple-element.27), channel_id=1, source_target_pairs={{1,16},{2,17},{3,18},{4,19},{5,20},{6,21},{7,22},{8,23},{9,24},{10... | collective-permute-start | bytes 24584 | tf_op jit(solution)/shard_map/ppermute | solution.py:136
  50.3 17.8 %collective-permute-start.3 = (f32[128,4,4]{2,1,0:T(4,128)}, f32[128,4,4]{2,1,0:T(4,128)S(1)}, u32[]{:S(2)}, u32[]{:S(2)}) collective-permute-start(f32[128,4,4]{2,1,0:T(4,128)} %get-tuple-element.26), channel_id=1, source_target_pairs={{17,0},{18,1},{19,2},{20,3},{21,4},{22,5},{23,6},{24,7},{25,8},{26... | collective-permute-start | bytes 24584 | tf_op jit(solution)/shard_map/ppermute | solution.py:135
  131.1 4.4 %collective-permute-start.8 = (bf16[32,4,128]{2,1,0:T(4,128)(2,1)S(1)}, bf16[32,4,128]{2,1,0:T(4,128)(2,1)S(1)}, u32[]{:S(2)}, u32[]{:S(2)}) collective-permute-start(bf16[32,4,128]{2,1,0:T(4,128)(2,1)S(1)} %broadcast_multiply_fusion), channel_id=1, source_target_pairs={{0,112},{16,0},{32,16},{48,32},{64,48},{80,64},{96,80},{112,96},{1... | collective-permute-start | bytes 98312 | tf_op jit(solution)/shard_map/ppermute | solution.py:29
  136.2 3.1 %copy-start.4 = (f32[16,256]{1,0:T(8,128)S(1)}, f32[16,256]{1,0:T(8,128)}, u32[]{:S(2)}) copy-start(f32[16,256]{1,0:T(8,128)} %param.15) | copy-start | bytes 49156
  136.2 3.1 %copy-start.5 = (s32[16,256]{1,0:T(8,128)S(1)}, s32[16,256]{1,0:T(8,128)}, u32[]{:S(2)}) copy-start(s32[16,256]{1,0:T(8,128)} %param.14) | copy-start | bytes 49156
  140.0 5.2 %collective-permute-start.9 = (f32[1,16,256]{2,1,0:T(8,128)S(1)}, f32[1,16,256]{2,1,0:T(8,128)S(1)}, u32[]{:S(2)}, u32[]{:S(2)}) collective-permute-start(f32[1,16,256]{2,1,0:T(8,128)S(1)} %get-tuple-element.80), channel_id=1, source_target_pairs={{0,2},{1,3},{2,0},{3,1},{4,6},{5,7},{6,4},{7,5},{8,10},{9,11},{10,... | collective-permute-start | bytes 49160 | tf_op jit(solution)/shard_map/ppermute | solution.py:61
  140.0 8.1 %collective-permute-start.16 = (f32[1,16,256]{2,1,0:T(8,128)S(1)}, f32[1,16,256]{2,1,0:T(8,128)S(1)}, u32[]{:S(2)}, u32[]{:S(2)}) collective-permute-start(f32[1,16,256]{2,1,0:T(8,128)S(1)} %get-tuple-element.15), channel_id=1, source_target_pairs={{0,2},{1,3},{2,0},{3,1},{4,6},{5,7},{6,4},{7,5},{8,10},{9,11},{10,... | collective-permute-start | bytes 49160 | tf_op jit(solution)/shard_map/ppermute | solution.py:61
  145.3 5.4 %collective-permute-start.10 = (f32[2,16,256]{2,1,0:T(8,128)S(1)}, f32[2,16,256]{2,1,0:T(8,128)S(1)}, u32[]{:S(2)}, u32[]{:S(2)}) collective-permute-start(f32[2,16,256]{2,1,0:T(8,128)S(1)} %pad_maximum_fusion.5), channel_id=1, source_target_pairs={{0,8},{1,9},{2,10},{3,11},{4,12},{5,13},{6,14},{7,15},{8,0},{9,1},... | collective-permute-start | bytes 98312 | tf_op jit(solution)/shard_map/ppermute | solution.py:61
  148.2 6.9 %collective-permute-start.17 = (f32[2,16,256]{2,1,0:T(8,128)S(1)}, f32[2,16,256]{2,1,0:T(8,128)S(1)}, u32[]{:S(2)}, u32[]{:S(2)}) collective-permute-start(f32[2,16,256]{2,1,0:T(8,128)S(1)} %pad_maximum_fusion.6), channel_id=1, source_target_pairs={{0,8},{1,9},{2,10},{3,11},{4,12},{5,13},{6,14},{7,15},{8,0},{9,1},... | collective-permute-start | bytes 98312 | tf_op jit(solution)/shard_map/ppermute | solution.py:61
  150.7 8.3 %collective-permute-start.11 = (f32[4,16,256]{2,1,0:T(8,128)S(1)}, f32[4,16,256]{2,1,0:T(8,128)S(1)}, u32[]{:S(2)}, u32[]{:S(2)}) collective-permute-start(f32[4,16,256]{2,1,0:T(8,128)S(1)} %pad_maximum_fusion.3), channel_id=1, source_target_pairs={{0,64},{16,80},{32,96},{48,112},{64,0},{80,16},{96,32},{112,48},{1... | collective-permute-start | bytes 196616 | tf_op jit(solution)/shard_map/ppermute | solution.py:61
  155.1 5.8 %collective-permute-start.18 = (f32[4,16,256]{2,1,0:T(8,128)S(1)}, f32[4,16,256]{2,1,0:T(8,128)S(1)}, u32[]{:S(2)}, u32[]{:S(2)}) collective-permute-start(f32[4,16,256]{2,1,0:T(8,128)S(1)} %pad_maximum_fusion.4), channel_id=1, source_target_pairs={{0,64},{16,80},{32,96},{48,112},{64,0},{80,16},{96,32},{112,48},{1... | collective-permute-start | bytes 196616 | tf_op jit(solution)/shard_map/ppermute | solution.py:61
  159.0 5.0 %collective-permute-start.12 = (f32[8,16,256]{2,1,0:T(8,128)S(1)}, f32[8,16,256]{2,1,0:T(8,128)S(1)}, u32[]{:S(2)}, u32[]{:S(2)}) collective-permute-start(f32[8,16,256]{2,1,0:T(8,128)S(1)} %pad_maximum_fusion.1), channel_id=1, source_target_pairs={{0,1},{1,0},{2,3},{3,2},{4,5},{5,4},{6,7},{7,6},{8,9},{9,8},{10,11... | collective-permute-start | bytes 393224 | tf_op jit(solution)/shard_map/ppermute | solution.py:61
  161.0 5.0 %collective-permute-start.19 = (f32[8,16,256]{2,1,0:T(8,128)S(1)}, f32[8,16,256]{2,1,0:T(8,128)S(1)}, u32[]{:S(2)}, u32[]{:S(2)}) collective-permute-start(f32[8,16,256]{2,1,0:T(8,128)S(1)} %pad_maximum_fusion.2), channel_id=1, source_target_pairs={{0,1},{1,0},{2,3},{3,2},{4,5},{5,4},{6,7},{7,6},{8,9},{9,8},{10,11... | collective-permute-start | bytes 393224 | tf_op jit(solution)/shard_map/ppermute | solution.py:61
  164.8 7.2 %collective-permute-start.13 = (f32[16,16,256]{2,1,0:T(8,128)S(1)}, f32[16,16,256]{2,1,0:T(8,128)S(1)}, u32[]{:S(2)}, u32[]{:S(2)}) collective-permute-start(f32[16,16,256]{2,1,0:T(8,128)S(1)} %get-tuple-element.49), channel_id=1, source_target_pairs={{0,4},{1,5},{2,6},{3,7},{4,0},{5,1},{6,2},{7,3},{8,12},{9,13},{10,... | collective-permute-start | bytes 786440 | tf_op jit(solution)/shard_map/ppermute | solution.py:61
  166.7 8.4 %collective-permute-start.20 = (f32[16,16,256]{2,1,0:T(8,128)S(1)}, f32[16,16,256]{2,1,0:T(8,128)S(1)}, u32[]{:S(2)}, u32[]{:S(2)}) collective-permute-start(f32[16,16,256]{2,1,0:T(8,128)S(1)} %get-tuple-element.45), channel_id=1, source_target_pairs={{0,4},{1,5},{2,6},{3,7},{4,0},{5,1},{6,2},{7,3},{8,12},{9,13},{10,... | collective-permute-start | bytes 786440 | tf_op jit(solution)/shard_map/ppermute | solution.py:61
  172.7 13.7 %collective-permute-start.14 = (f32[32,16,256]{2,1,0:T(8,128)S(1)}, f32[32,16,256]{2,1,0:T(8,128)S(1)}, u32[]{:S(2)}, u32[]{:S(2)}) collective-permute-start(f32[32,16,256]{2,1,0:T(8,128)S(1)} %get-tuple-element.41), channel_id=1, source_target_pairs={{0,32},{16,48},{32,0},{48,16},{64,96},{80,112},{96,64},{112,80},{1... | collective-permute-start | bytes 1572872 | tf_op jit(solution)/shard_map/ppermute | solution.py:61
  175.9 16.1 %collective-permute-start.21 = (f32[32,16,256]{2,1,0:T(8,128)S(1)}, f32[32,16,256]{2,1,0:T(8,128)S(1)}, u32[]{:S(2)}, u32[]{:S(2)}) collective-permute-start(f32[32,16,256]{2,1,0:T(8,128)S(1)} %get-tuple-element.38), channel_id=1, source_target_pairs={{0,32},{16,48},{32,0},{48,16},{64,96},{80,112},{96,64},{112,80},{1... | collective-permute-start | bytes 1572872 | tf_op jit(solution)/shard_map/ppermute | solution.py:61
  187.3 5.7 %copy-start.1 = (f32[128,16,256]{2,1,0:T(8,128)}, f32[128,16,256]{2,1,0:T(8,128)S(1)}, u32[]{:S(2)}) copy-start(f32[128,16,256]{2,1,0:T(8,128)S(1)} %get-tuple-element.35) | copy-start | bytes 6291460
  187.3 6.9 %collective-permute-start.15 = (f32[64,16,256]{2,1,0:T(8,128)}, f32[64,16,256]{2,1,0:T(8,128)S(1)}, u32[]{:S(2)}, u32[]{:S(2)}) collective-permute-start(f32[64,16,256]{2,1,0:T(8,128)} %get-tuple-element.34), channel_id=1, source_target_pairs={{0,16},{16,0},{32,48},{48,32},{64,80},{80,64},{96,112},{112,96},{1... | collective-permute-start | bytes 3145736 | tf_op jit(solution)/shard_map/ppermute | solution.py:61
  192.9 3.0 %collective-permute-start.22 = (f32[64,16,256]{2,1,0:T(8,128)}, f32[64,16,256]{2,1,0:T(8,128)}, u32[]{:S(2)}, u32[]{:S(2)}) collective-permute-start(f32[64,16,256]{2,1,0:T(8,128)} %get-tuple-element.32), channel_id=1, source_target_pairs={{0,16},{16,0},{32,48},{48,32},{64,80},{80,64},{96,112},{112,96},{1... | collective-permute-start | bytes 3145736 | tf_op jit(solution)/shard_map/ppermute | solution.py:61
  197.2 1.3 copy-start

commit v16 on v11

--- a/solution.py
+++ b/solution.py
@@ -73,7 +73,7 @@
 LEVEL_BLOCK = 16
 
 
-def diffusion_kernel(kappa_ref, weight_ref, core_ref, lanes_ref, rows_ref, mask_ref, out_ref, flux_ref):
+def diffusion_kernel(grid_rows, grid_cols, kappa_ref, weight_ref, core_ref, lanes_ref, rows_ref, index_ref, out_ref, flux_ref):
     block = pl.program_id(0)
     levels, rows, cols = core_ref.shape
 
@@ -81,7 +81,14 @@
     def _():
         flux_ref[...] = jnp.zeros_like(flux_ref)
 
-    mask = mask_ref[...]
+    height, width = rows + 2 * HALO, cols + 128
+    r = lax.broadcasted_iota(jnp.int32, (height, width), 0)
+    c = lax.broadcasted_iota(jnp.int32, (height, width), 1)
+    global_r = index_ref[0] * rows + jnp.where(r < rows + HALO, r, r - height)
+    global_c = index_ref[1] * cols + jnp.where(c < cols + HALO, c, c - width)
+    inside = (global_r >= 0) & (global_r < grid_rows) & (global_c >= 0) & (global_c < grid_cols)
+    inside = inside & ((c < cols + HALO) | (c >= width - HALO))
+    mask = inside.astype(jnp.float32)
     mask_side = mask[:rows, cols:]
     mask_low = mask[rows:, :]
 
@@ -148,17 +155,11 @@
     )
     height = rows + 2 * HALO
     width = cols + 128
-    r = jnp.arange(height, dtype=jnp.int32)
-    c = jnp.arange(width, dtype=jnp.int32)
-    global_r = gy_index * rows + jnp.where(r < rows + HALO, r, r - height)
-    global_c = gx_index * cols + jnp.where(c < cols + HALO, c, c - width)
-    inside_r = (global_r >= 0) & (global_r < count_gy * rows)
-    inside_c = (global_c >= 0) & (global_c < count_gx * cols) & ((c < cols + HALO) | (c >= width - HALO))
-    mask = (inside_r[:, None] & inside_c[None, :]).astype(jnp.float32)
+    index = jnp.stack([gy_index, gx_index]).astype(jnp.int32)
     blocks = levels // LEVEL_BLOCK
     smem = pl.BlockSpec(memory_space=pltpu.SMEM)
     out, flux = pl.pallas_call(
-        diffusion_kernel,
+        functools.partial(diffusion_kernel, count_gy * rows, count_gx * cols),
         grid=(blocks,),
         in_specs=[
             smem,
@@ -166,7 +167,7 @@
             pl.BlockSpec((LEVEL_BLOCK, rows, cols), lambda b: (b, 0, 0)),
             pl.BlockSpec((LEVEL_BLOCK, rows, 128), lambda b: (b, 0, 0)),
             pl.BlockSpec((LEVEL_BLOCK, 2 * HALO, width), lambda b: (b, 0, 0)),
-            pl.BlockSpec((height, width), lambda b: (0, 0)),
+            smem,
         ],
         out_specs=[
             pl.BlockSpec((LEVEL_BLOCK, rows, cols), lambda b: (b, 0, 0)),
@@ -182,7 +183,7 @@
             transcendentals=0,
             bytes_accessed=2 * field.size * 4,
         ),
-    )(atm_kappa, vert_weight, field, lanes, halo_rows, mask)
+    )(atm_kappa, vert_weight, field, lanes, halo_rows, index)
     return out, flux
 
 

time: 214 us -> 214 us (level)
  transfers between devices with their start and end apart: 23 -> 23, of which waited for: 13 -> 13; matrix products, arithmetic and copies ran while one was open for 17% -> 16% of each run, Pallas kernels for 0% -> 0%
where the time goes in v16:
time: 214 us; the launch traced here: 212 us
  Pallas kernels  70.3 us (33%)
  starting transfers between devices  43.5 us (20%)
  waiting for transfers between devices  42.2 us (20%)
  local copies, waits for them, and re-layouts  40.5 us (19%)
  other arithmetic  11.2 us (5%)
  matrix products  3.04 us (1%)
    pallas_call x1, Pallas kernels, diffuse(): pl.pallas_call(functools.partial(diffusion_kernel, count_gy * rows, count...  57.2 us
    ppermute x14, waiting for transfers between devices, stack_gather(): other = lax.ppermute(x, axis, [(j, j ^ distance) for j in range(size)])  24.7 us
    ppermute x14, starting transfers between devices, stack_gather(): other = lax.ppermute(x, axis, [(j, j ^ distance) for j in range(size)])  20.9 us
    unnamed x27, local copies, waits for them, and re-layouts  13.9 us
    pallas_call x1, Pallas kernels, solve_grid(): pl.pallas_call(functools.partial(cg_kernel, rounds), in_specs=[pl.BlockSp...  13.1 us
    ppermute x1, waiting for transfers between devices, diffuse(): south_east = lax.ppermute(field[:, :HALO, :HALO], both, pairs(1, 1))  7.07 us
    ppermute x1, starting transfers between devices, diffuse(): lax.ppermute(field[:, rows - HALO:, cols - HALO:], both, pairs(-1, -1))  5.35 us
    ppermute x1, starting transfers between devices, diffuse(): south_west = lax.ppermute(field[:, :HALO, cols - HALO:], both, pairs(-1, 1))  4.98 us
  transfers between devices with their start and end apart: 23, of which 13 were waited for; matrix products, arithmetic and copies ran while one was open for 16% of the time, Pallas kernels for 0%

profile of v16, /device:TPU:6, one launch (start us, length us, event | category | flops | bytes accessed | tf_op | source)
XLA Modules:
  0.0 211.7 jit_solution(4642203304732035556)
XLA Ops:
  0.6 4.3 %fusion.19 = (f32[128,32,4]{2,1,0:T(8,128)S(1)}, f32[128,32,4]{2,1,0:T(8,128)}) fusion(f32[128,32,512]{2,1,0:T(8,128)} %core_ref.1), kind=kLoop, calls=%fused_computation.112 | loop fusion | bytes 262144 | tf_op jit(solution)/shard_map/slice | solution.py:140
  4.9 3.3 %copy.86 = f32[128,32,4]{0,1,2:T(8,128)} copy(f32[128,32,4]{2,1,0:T(8,128)} %get-tuple-element.31) | data formatting | bytes 131072
  8.2 2.4 %collective-permute-start.1 = (f32[128,32,4]{0,1,2:T(8,128)}, f32[128,32,4]{0,1,2:T(8,128)}, u32[]{:S(2)}, u32[]{:S(2)}) collective-permute-start(f32[128,32,4]{0,1,2:T(8,128)} %copy.86), channel_id=1, source_target_pairs={{0,16},{16,32},{32,48},{48,64},{64,80},{80,96},{96,112},{1,17},{17... | collective-permute-start | bytes 196616 | tf_op jit(solution)/shard_map/ppermute | solution.py:141
  10.5 1.9 copy.85
  12.5 1.3 collective-permute-start
  13.8 2.9 %fusion.18 = (f32[128,4,4]{2,1,0:T(4,128)}, f32[128,4,4]{2,1,0:T(4,128)}, f32[128,4,4]{2,1,0:T(4,128)}, f32[128,4,4]{2,1,0:T(4,128)}) fusion(f32[128,32,512]{2,1,0:T(8,128)} %core_ref.1), kind=kLoop, calls=%fused_computation.111 | loop fusion | bytes 65536 | tf_op jit(solution)/shard_map/slice | solution.py:142
  16.6 5.4 %collective-permute-start.7 = (f32[128,4,4]{2,1,0:T(4,128)}, f32[128,4,4]{2,1,0:T(4,128)S(1)}, u32[]{:S(2)}, u32[]{:S(2)}) collective-permute-start(f32[128,4,4]{2,1,0:T(4,128)} %get-tuple-element.29), channel_id=1, source_target_pairs={{0,17},{1,18},{2,19},{3,20},{4,21},{5,22},{6,23},{7,24},{8,25},{9,... | collective-permute-start | bytes 24584 | tf_op jit(solution)/shard_map/ppermute | solution.py:145
  22.0 4.1 %fusion.17 = (f32[128,4,512]{2,1,0:T(4,128)}, f32[128,4,512]{2,1,0:T(4,128)}) fusion(f32[128,32,512]{2,1,0:T(8,128)} %core_ref.1), kind=kLoop, calls=%fused_computation.110 | loop fusion | bytes 4194304 | tf_op jit(solution)/shard_map/slice | solution.py:138
  26.1 3.4 %collective-permute-start.5 = (f32[128,4,512]{2,1,0:T(4,128)}, f32[128,4,512]{2,1,0:T(4,128)S(1)}, u32[]{:S(2)}, u32[]{:S(2)}) collective-permute-start(f32[128,4,512]{2,1,0:T(4,128)} %get-tuple-element.25), channel_id=1, source_target_pairs={{0,1},{1,2},{2,3},{3,4},{4,5},{5,6},{6,7},{7,8},{8,9},{9,10},{10,1... | collective-permute-start | bytes 3145736 | tf_op jit(solution)/shard_map/ppermute | solution.py:139
  29.5 2.4 %collective-permute-start.2 = (f32[128,4,512]{2,1,0:T(4,128)}, f32[128,4,512]{2,1,0:T(4,128)}, u32[]{:S(2)}, u32[]{:S(2)}) collective-permute-start(f32[128,4,512]{2,1,0:T(4,128)} %get-tuple-element.24), channel_id=1, source_target_pairs={{1,0},{2,1},{3,2},{4,3},{5,4},{6,5},{7,6},{8,7},{9,8},{10,9},{11,1... | collective-permute-start | bytes 3145736 | tf_op jit(solution)/shard_map/ppermute | solution.py:138
  32.0 0.6 copy.71
  32.6 1.6 reshape.208
  36.4 0.7 pad_add_fusion.index_ref
  37.1 1.3 collective-permute-start.6
  38.4 2.7 %copy.69 = f32[128,32,4]{2,1,0:T(8,128)S(1)} copy(f32[128,32,4]{0,1,2:T(8,128)} %collective-permute-done.1) | data formatting | bytes 131072 | tf_op jit(solution)/shard_map/ppermute | solution.py:141
  41.2 5.0 %collective-permute-start.4 = (f32[128,4,4]{2,1,0:T(4,128)}, f32[128,4,4]{2,1,0:T(4,128)}, u32[]{:S(2)}, u32[]{:S(2)}) collective-permute-start(f32[128,4,4]{2,1,0:T(4,128)} %get-tuple-element.27), channel_id=1, source_target_pairs={{1,16},{2,17},{3,18},{4,19},{5,20},{6,21},{7,22},{8,23},{9,24},{10... | collective-permute-start | bytes 24584 | tf_op jit(solution)/shard_map/ppermute | solution.py:143
  46.2 2.9 %copy.68 = f32[128,32,4]{2,1,0:T(8,128)} copy(f32[128,32,4]{0,1,2:T(8,128)S(1)} %collective-permute-done) | data formatting | bytes 131072 | tf_op jit(solution)/shard_map/ppermute | solution.py:140
  49.0 1.5 collective-permute-start.3
  50.5 3.5 %pad_maximum_fusion.lanes_ref = f32[128,32,128]{2,1,0:T(8,128)} fusion(f32[128,32,4]{2,1,0:T(8,128)S(1)} %copy.69, f32[128,32,4]{2,1,0:T(8,128)} %copy.68, f32[128]{0:T(128)S(1)} %pad.29.clone), kind=kLoop, calls=%fused_computation.4 | loop fusion | flops 1048576 | bytes 2228736 | tf_op jit(solution)/shard_map/concatenate | solution.py:147
  54.0 3.1 %collective-permute-done.6 = f32[128,4,4]{2,1,0:T(4,128)} collective-permute-done((f32[128,4,4]{2,1,0:T(4,128)}, f32[128,4,4]{2,1,0:T(4,128)}, u32[]{:S(2)}, u32[]{:S(2)}) %collective-permute-start.6) | collective-permute-done | bytes 8224 | tf_op jit(solution)/shard_map/ppermute | solution.py:144
  57.1 4.0 %collective-permute-done.4 = f32[128,4,4]{2,1,0:T(4,128)} collective-permute-done((f32[128,4,4]{2,1,0:T(4,128)}, f32[128,4,4]{2,1,0:T(4,128)}, u32[]{:S(2)}, u32[]{:S(2)}) %collective-permute-start.4) | collective-permute-done | bytes 8224 | tf_op jit(solution)/shard_map/ppermute | solution.py:143
  61.1 7.1 %collective-permute-done.3 = f32[128,4,4]{2,1,0:T(4,128)S(1)} collective-permute-done((f32[128,4,4]{2,1,0:T(4,128)}, f32[128,4,4]{2,1,0:T(4,128)S(1)}, u32[]{:S(2)}, u32[]{:S(2)}) %collective-permute-start.3) | collective-permute-done | bytes 8224 | tf_op jit(solution)/shard_map/ppermute | solution.py:142
  68.2 3.9 %maximum_maximum_fusion.rows_ref = f32[128,8,640]{2,1,0:T(8,128)} fusion(f32[128,4,4]{2,1,0:T(4,128)S(1)} %collective-permute-done.7, f32[128,4,120]{2,1,0:T(4,128)S(1)} %broadcast_in_dim.50, f32[128,4,4]{2,1,0:T(4,128)} %collective-permute-done.6, f32[128,4,512]{2,1,0:T(4,128)S(1)} %collective-permute-done.5, f32[128,4,4]{2,1,0:T(4,128)} %collective-permute-done.4, ...), kind=kLoop, calls=%fused_computation.3 | loop fusion | flops 4587520 | bytes 4997120 | tf_op jit(solution)/shard_map/concatenate | solution.py:149
  72.1 57.2 %shard_map.111 = (f32[128,32,512]{2,1,0:T(8,128)}, f32[4,32,512]{2,1,0:T(8,128)}) custom-call(f32[128]{0:T(128)} %kappa_ref.1, f32[4,128]{1,0:T(4,128)} %weight_ref.1, f32[128,32,512]{2,1,0:T(8,128)} %core_ref.1, f32[128,32,128]{2,1,0:T(8,128)} %pad_maximum_fusion.lanes_ref, f32[128,8,640]{2,1,0:T(8,128)} %maximum_maximum_fusion.rows_ref, ...), custom_call_target="tpu_custom_call" | custom-call | flops 131072000 | bytes 16777216 | tf_op jit(solution)/shard_map/pallas_call | solution.py:161
  129.2 1.0 convert_element_type.36
  130.4 0.6 gather_fusion.1
  131.4 0.7 gather_fusion
  132.2 3.3 %collective-permute-done.8 = bf16[32,4,128]{2,1,0:T(4,128)(2,1)S(1)} collective-permute-done((bf16[32,4,128]{2,1,0:T(4,128)(2,1)S(1)}, bf16[32,4,128]{2,1,0:T(4,128)(2,1)S(1)}, u32[]{:S(2)}, u32[]{:S(2)}) %collective-permute-start.8) | collective-permute-done | bytes 32800 | tf_op jit(solution)/shard_map/ppermute | solution.py:29
  135.5 0.7 gather_fusion.2
  136.3 3.0 %convolution_bitcast_fusion = f32[4,32,128]{2,0,1:T(4,128)S(1)} fusion(bf16[32,4,128,128]{3,2,1,0:T(8,128)(2,1)} %param.13, bf16[32,4,4,128]{3,2,1,0:T(4,128)(2,1)S(1)} %bitcast.37, bf16[32,4,4,128]{3,2,1,0:T(4,128)(2,1)S(1)} %bitcast.38, pred[32,4]{1,0:T(8,128)(4,1)S(1)} %and.77, pred[32,4]{1,0:T(8,128)(4,1)S(1)} %and.73), kind=kOutput, calls=%fused_computation.5 | convolution fusion | flops 16908288 | bytes 4522240 | tf_op jit(solution)/shard_map/bkij,bkcj->cbi/dot_general | solution.py:357
  139.4 0.6 constant_dynamic-update-slice_fusion.43
  140.0 3.5 %collective-permute-start.16 = (f32[1,16,256]{2,1,0:T(8,128)S(1)}, f32[1,16,256]{2,1,0:T(8,128)S(1)}, u32[]{:S(2)}, u32[]{:S(2)}) collective-permute-start(f32[1,16,256]{2,1,0:T(8,128)S(1)} %get-tuple-element.15), channel_id=1, source_target_pairs={{0,2},{1,3},{2,0},{3,1},{4,6},{5,7},{6,4},{7,5},{8,10},{9,11},{10,... | collective-permute-start | bytes 49160 | tf_op jit(solution)/shard_map/ppermute | solution.py:61
  143.6 1.7 collective-permute-done.9
  145.3 2.9 %collective-permute-start.10 = (f32[2,16,256]{2,1,0:T(8,128)S(1)}, f32[2,16,256]{2,1,0:T(8,128)S(1)}, u32[]{:S(2)}, u32[]{:S(2)}) collective-permute-start(f32[2,16,256]{2,1,0:T(8,128)S(1)} %pad_maximum_fusion.5), channel_id=1, source_target_pairs={{0,8},{1,9},{2,10},{3,11},{4,12},{5,13},{6,14},{7,15},{8,0},{9,1},... | collective-permute-start | bytes 98312 | tf_op jit(solution)/shard_map/ppermute | solution.py:61
  148.2 0.6 collective-permute-start.17
  148.8 0.6 constant_dynamic-update-slice_fusion.16
  149.4 0.6 constant_dynamic-update-slice_fusion.42
  150.0 0.7 collective-permute-done.10
  150.7 4.4 %collective-permute-start.11 = (f32[4,16,256]{2,1,0:T(8,128)S(1)}, f32[4,16,256]{2,1,0:T(8,128)S(1)}, u32[]{:S(2)}, u32[]{:S(2)}) collective-permute-start(f32[4,16,256]{2,1,0:T(8,128)S(1)} %pad_maximum_fusion.3), channel_id=1, source_target_pairs={{0,64},{16,80},{32,96},{48,112},{64,0},{80,16},{96,32},{112,48},{1... | collective-permute-start | bytes 196616 | tf_op jit(solution)/shard_map/ppermute | solution.py:61
  155.1 2.7 %collective-permute-start.18 = (f32[4,16,256]{2,1,0:T(8,128)S(1)}, f32[4,16,256]{2,1,0:T(8,128)S(1)}, u32[]{:S(2)}, u32[]{:S(2)}) collective-permute-start(f32[4,16,256]{2,1,0:T(8,128)S(1)} %pad_maximum_fusion.4), channel_id=1, source_target_pairs={{0,64},{16,80},{32,96},{48,112},{64,0},{80,16},{96,32},{112,48},{1... | collective-permute-start | bytes 196616 | tf_op jit(solution)/shard_map/ppermute | solution.py:61
  157.8 0.6 constant_dynamic-update-slice_fusion.15
  158.4 0.6 constant_dynamic-update-slice_fusion.41
  159.1 1.8 collective-permute-done.18
  161.2 0.6 constant_dynamic-update-slice_fusion.14
  161.9 2.2 %collective-permute-done.12 = f32[8,16,256]{2,1,0:T(8,128)S(1)} collective-permute-done((f32[8,16,256]{2,1,0:T(8,128)S(1)}, f32[8,16,256]{2,1,0:T(8,128)S(1)}, u32[]{:S(2)}, u32[]{:S(2)}) %collective-permute-start.12) | collective-permute-done | bytes 131104 | tf_op jit(solution)/shard_map/ppermute | solution.py:61
  164.1 0.7 constant_dynamic-update-slice_fusion.13
  165.3 0.6 constant_dynamic-update-slice_fusion.40
  166.0 0.7 constant_dynamic-update-slice_fusion.39
  166.7 1.4 collective-permute-start.20
  168.1 3.8 %collective-permute-done.13 = f32[16,16,256]{2,1,0:T(8,128)S(1)} collective-permute-done((f32[16,16,256]{2,1,0:T(8,128)S(1)}, f32[16,16,256]{2,1,0:T(8,128)S(1)}, u32[]{:S(2)}, u32[]{:S(2)}) %collective-permute-start.13) | collective-permute-done | bytes 262176 | tf_op jit(solution)/shard_map/ppermute | solution.py:61
  171.9 0.8 constant_dynamic-update-slice_fusion.12
  172.7 2.4 %collective-permute-start.14 = (f32[32,16,256]{2,1,0:T(8,128)S(1)}, f32[32,16,256]{2,1,0:T(8,128)S(1)}, u32[]{:S(2)}, u32[]{:S(2)}) collective-permute-start(f32[32,16,256]{2,1,0:T(8,128)S(1)} %get-tuple-element.41), channel_id=1, source_target_pairs={{0,32},{16,48},{32,0},{48,16},{64,96},{80,112},{96,64},{112,80},{1... | collective-permute-start | bytes 1572872 | tf_op jit(solution)/shard_map/ppermute | solution.py:61
  175.1 0.8 constant_dynamic-update-slice_fusion.38
  175.9 2.0 collective-permute-start.21
  177.9 8.5 %collective-permute-done.14 = f32[32,16,256]{2,1,0:T(8,128)S(1)} collective-permute-done((f32[32,16,256]{2,1,0:T(8,128)S(1)}, f32[32,16,256]{2,1,0:T(8,128)S(1)}, u32[]{:S(2)}, u32[]{:S(2)}) %collective-permute-start.14) | collective-permute-done | bytes 524320 | tf_op jit(solution)/shard_map/ppermute | solution.py:61
  186.4 0.9 constant_dynamic-update-slice_fusion.11
  187.3 4.7 %collective-permute-done.21 = f32[32,16,256]{2,1,0:T(8,128)S(1)} collective-permute-done((f32[32,16,256]{2,1,0:T(8,128)S(1)}, f32[32,16,256]{2,1,0:T(8,128)S(1)}, u32[]{:S(2)}, u32[]{:S(2)}) %collective-permute-start.21) | collective-permute-done | bytes 524320 | tf_op jit(solution)/shard_map/ppermute | solution.py:61
  192.0 0.9 constant_dynamic-update-slice_fusion.37
  193.0 0.6 reshape.210
  193.6 1.1 constant_dynamic-update-slice_fusion.18.rhs_stack
  194.7 1.3 collective-permute-done.22
  196.0 1.3 constant_dynamic-update-slice_fusion.44.coded_stack
  197.3 1.3 copy-done
  198.6 13.1 %shard_map.112 = (f32[16,256]{1,0:T(8,128)}, f32[16,256]{1,0:T(8,128)}) custom-call(s32[2]{0:T(128)} %pad_add_fusion.index_ref, f32[128,16,256]{2,1,0:T(8,128)} %constant_dynamic-update-slice_fusion.18.rhs_stack, f32[128,16,256]{2,1,0:T(8,128)} %copy-done), custom_call_target="tpu_custom_call" | custom-call | tf_op jit(solution)/shard_map/pallas_call | solution.py:291
  (71 shorter events, 3.8 us)
Async XLA Ops:
  8.2 29.0 %collective-permute-start.1 = (f32[128,32,4]{0,1,2:T(8,128)}, f32[128,32,4]{0,1,2:T(8,128)}, u32[]{:S(2)}, u32[]{:S(2)}) collective-permute-start(f32[128,32,4]{0,1,2:T(8,128)} %copy.86), channel_id=1, source_target_pairs={{0,16},{16,32},{32,48},{48,64},{64,80},{80,96},{96,112},{1,17},{17... | collective-permute-start | bytes 196616 | tf_op jit(solution)/shard_map/ppermute | solution.py:141
  12.5 28.7 %collective-permute-start = (f32[128,32,4]{0,1,2:T(8,128)}, f32[128,32,4]{0,1,2:T(8,128)S(1)}, u32[]{:S(2)}, u32[]{:S(2)}) collective-permute-start(f32[128,32,4]{0,1,2:T(8,128)} %copy.85), channel_id=1, source_target_pairs={{16,0},{32,16},{48,32},{64,48},{80,64},{96,80},{112,96},{17,1},{33... | collective-permute-start | bytes 196616 | tf_op jit(solution)/shard_map/ppermute | solution.py:140
  16.6 15.3 %copy-start.2 = (s32[4096,4]{0,1:T(4,128)S(1)}, s32[4096,4]{0,1:T(4,128)}, u32[]{:S(2)}) copy-start(s32[4096,4]{0,1:T(4,128)} %param.11) | copy-start | bytes 196612
  16.6 32.4 %collective-permute-start.7 = (f32[128,4,4]{2,1,0:T(4,128)}, f32[128,4,4]{2,1,0:T(4,128)S(1)}, u32[]{:S(2)}, u32[]{:S(2)}) collective-permute-start(f32[128,4,4]{2,1,0:T(4,128)} %get-tuple-element.29), channel_id=1, source_target_pairs={{0,17},{1,18},{2,19},{3,20},{4,21},{5,22},{6,23},{7,24},{8,25},{9,... | collective-permute-start | bytes 24584 | tf_op jit(solution)/shard_map/ppermute | solution.py:145
  26.1 42.1 %collective-permute-start.5 = (f32[128,4,512]{2,1,0:T(4,128)}, f32[128,4,512]{2,1,0:T(4,128)S(1)}, u32[]{:S(2)}, u32[]{:S(2)}) collective-permute-start(f32[128,4,512]{2,1,0:T(4,128)} %get-tuple-element.25), channel_id=1, source_target_pairs={{0,1},{1,2},{2,3},{3,4},{4,5},{5,6},{6,7},{7,8},{8,9},{9,10},{10,1... | collective-permute-start | bytes 3145736 | tf_op jit(solution)/shard_map/ppermute | solution.py:139
  29.5 38.7 %collective-permute-start.2 = (f32[128,4,512]{2,1,0:T(4,128)}, f32[128,4,512]{2,1,0:T(4,128)}, u32[]{:S(2)}, u32[]{:S(2)}) collective-permute-start(f32[128,4,512]{2,1,0:T(4,128)} %get-tuple-element.24), channel_id=1, source_target_pairs={{1,0},{2,1},{3,2},{4,3},{5,4},{6,5},{7,6},{8,7},{9,8},{10,9},{11,1... | collective-permute-start | bytes 3145736 | tf_op jit(solution)/shard_map/ppermute | solution.py:138
  32.0 2.5 %copy-start.3 = (s32[4096]{0:T(1024)S(1)}, s32[4096]{0:T(1024)}, u32[]{:S(2)}) copy-start(s32[4096]{0:T(1024)} %param.12) | copy-start | bytes 49156
  37.1 20.0 %collective-permute-start.6 = (f32[128,4,4]{2,1,0:T(4,128)}, f32[128,4,4]{2,1,0:T(4,128)}, u32[]{:S(2)}, u32[]{:S(2)}) collective-permute-start(f32[128,4,4]{2,1,0:T(4,128)} %get-tuple-element.28), channel_id=1, source_target_pairs={{16,1},{17,2},{18,3},{19,4},{20,5},{21,6},{22,7},{23,8},{24,9},{25... | collective-permute-start | bytes 24584 | tf_op jit(solution)/shard_map/ppermute | solution.py:144
  41.2 19.9 %collective-permute-start.4 = (f32[128,4,4]{2,1,0:T(4,128)}, f32[128,4,4]{2,1,0:T(4,128)}, u32[]{:S(2)}, u32[]{:S(2)}) collective-permute-start(f32[128,4,4]{2,1,0:T(4,128)} %get-tuple-element.27), channel_id=1, source_target_pairs={{1,16},{2,17},{3,18},{4,19},{5,20},{6,21},{7,22},{8,23},{9,24},{10... | collective-permute-start | bytes 24584 | tf_op jit(solution)/shard_map/ppermute | solution.py:143
  49.0 19.1 %collective-permute-start.3 = (f32[128,4,4]{2,1,0:T(4,128)}, f32[128,4,4]{2,1,0:T(4,128)S(1)}, u32[]{:S(2)}, u32[]{:S(2)}) collective-permute-start(f32[128,4,4]{2,1,0:T(4,128)} %get-tuple-element.26), channel_id=1, source_target_pairs={{17,0},{18,1},{19,2},{20,3},{21,4},{22,5},{23,6},{24,7},{25,8},{26... | collective-permute-start | bytes 24584 | tf_op jit(solution)/shard_map/ppermute | solution.py:142
  131.1 4.4 %collective-permute-start.8 = (bf16[32,4,128]{2,1,0:T(4,128)(2,1)S(1)}, bf16[32,4,128]{2,1,0:T(4,128)(2,1)S(1)}, u32[]{:S(2)}, u32[]{:S(2)}) collective-permute-start(bf16[32,4,128]{2,1,0:T(4,128)(2,1)S(1)} %broadcast_multiply_fusion), channel_id=1, source_target_pairs={{0,112},{16,0},{32,16},{48,32},{64,48},{80,64},{96,80},{112,96},{1... | collective-permute-start | bytes 98312 | tf_op jit(solution)/shard_map/ppermute | solution.py:29
  136.2 3.1 %copy-start.4 = (f32[16,256]{1,0:T(8,128)S(1)}, f32[16,256]{1,0:T(8,128)}, u32[]{:S(2)}) copy-start(f32[16,256]{1,0:T(8,128)} %param.15) | copy-start | bytes 49156
  136.3 3.1 %copy-start.5 = (s32[16,256]{1,0:T(8,128)S(1)}, s32[16,256]{1,0:T(8,128)}, u32[]{:S(2)}) copy-start(s32[16,256]{1,0:T(8,128)} %param.14) | copy-start | bytes 49156
  140.0 5.2 %collective-permute-start.9 = (f32[1,16,256]{2,1,0:T(8,128)S(1)}, f32[1,16,256]{2,1,0:T(8,128)S(1)}, u32[]{:S(2)}, u32[]{:S(2)}) collective-permute-start(f32[1,16,256]{2,1,0:T(8,128)S(1)} %get-tuple-element.80), channel_id=1, source_target_pairs={{0,2},{1,3},{2,0},{3,1},{4,6},{5,7},{6,4},{7,5},{8,10},{9,11},{10,... | collective-permute-start | bytes 49160 | tf_op jit(solution)/shard_map/ppermute | solution.py:61
  140.0 8.1 %collective-permute-start.16 = (f32[1,16,256]{2,1,0:T(8,128)S(1)}, f32[1,16,256]{2,1,0:T(8,128)S(1)}, u32[]{:S(2)}, u32[]{:S(2)}) collective-permute-start(f32[1,16,256]{2,1,0:T(8,128)S(1)} %get-tuple-element.15), channel_id=1, source_target_pairs={{0,2},{1,3},{2,0},{3,1},{4,6},{5,7},{6,4},{7,5},{8,10},{9,11},{10,... | collective-permute-start | bytes 49160 | tf_op jit(solution)/shard_map/ppermute | solution.py:61
  145.3 5.4 %collective-permute-start.10 = (f32[2,16,256]{2,1,0:T(8,128)S(1)}, f32[2,16,256]{2,1,0:T(8,128)S(1)}, u32[]{:S(2)}, u32[]{:S(2)}) collective-permute-start(f32[2,16,256]{2,1,0:T(8,128)S(1)} %pad_maximum_fusion.5), channel_id=1, source_target_pairs={{0,8},{1,9},{2,10},{3,11},{4,12},{5,13},{6,14},{7,15},{8,0},{9,1},... | collective-permute-start | bytes 98312 | tf_op jit(solution)/shard_map/ppermute | solution.py:61
  148.2 6.9 %collective-permute-start.17 = (f32[2,16,256]{2,1,0:T(8,128)S(1)}, f32[2,16,256]{2,1,0:T(8,128)S(1)}, u32[]{:S(2)}, u32[]{:S(2)}) collective-permute-start(f32[2,16,256]{2,1,0:T(8,128)S(1)} %pad_maximum_fusion.6), channel_id=1, source_target_pairs={{0,8},{1,9},{2,10},{3,11},{4,12},{5,13},{6,14},{7,15},{8,0},{9,1},... | collective-permute-start | bytes 98312 | tf_op jit(solution)/shard_map/ppermute | solution.py:61
  150.7 8.3 %collective-permute-start.11 = (f32[4,16,256]{2,1,0:T(8,128)S(1)}, f32[4,16,256]{2,1,0:T(8,128)S(1)}, u32[]{:S(2)}, u32[]{:S(2)}) collective-permute-start(f32[4,16,256]{2,1,0:T(8,128)S(1)} %pad_maximum_fusion.3), channel_id=1, source_target_pairs={{0,64},{16,80},{32,96},{48,112},{64,0},{80,16},{96,32},{112,48},{1... | collective-permute-start | bytes 196616 | tf_op jit(solution)/shard_map/ppermute | solution.py:61
  155.1 5.8 %collective-permute-start.18 = (f32[4,16,256]{2,1,0:T(8,128)S(1)}, f32[4,16,256]{2,1,0:T(8,128)S(1)}, u32[]{:S(2)}, u32[]{:S(2)}) collective-permute-start(f32[4,16,256]{2,1,0:T(8,128)S(1)} %pad_maximum_fusion.4), channel_id=1, source_target_pairs={{0,64},{16,80},{32,96},{48,112},{64,0},{80,16},{96,32},{112,48},{1... | collective-permute-start | bytes 196616 | tf_op jit(solution)/shard_map/ppermute | solution.py:61
  159.0 5.0 %collective-permute-start.12 = (f32[8,16,256]{2,1,0:T(8,128)S(1)}, f32[8,16,256]{2,1,0:T(8,128)S(1)}, u32[]{:S(2)}, u32[]{:S(2)}) collective-permute-start(f32[8,16,256]{2,1,0:T(8,128)S(1)} %pad_maximum_fusion.1), channel_id=1, source_target_pairs={{0,1},{1,0},{2,3},{3,2},{4,5},{5,4},{6,7},{7,6},{8,9},{9,8},{10,11... | collective-permute-start | bytes 393224 | tf_op jit(solution)/shard_map/ppermute | solution.py:61
  161.0 5.0 %collective-permute-start.19 = (f32[8,16,256]{2,1,0:T(8,128)S(1)}, f32[8,16,256]{2,1,0:T(8,128)S(1)}, u32[]{:S(2)}, u32[]{:S(2)}) collective-permute-start(f32[8,16,256]{2,1,0:T(8,128)S(1)} %pad_maximum_fusion.2), channel_id=1, source_target_pairs={{0,1},{1,0},{2,3},{3,2},{4,5},{5,4},{6,7},{7,6},{8,9},{9,8},{10,11... | collective-permute-start | bytes 393224 | tf_op jit(solution)/shard_map/ppermute | solution.py:61
  164.8 7.2 %collective-permute-start.13 = (f32[16,16,256]{2,1,0:T(8,128)S(1)}, f32[16,16,256]{2,1,0:T(8,128)S(1)}, u32[]{:S(2)}, u32[]{:S(2)}) collective-permute-start(f32[16,16,256]{2,1,0:T(8,128)S(1)} %get-tuple-element.49), channel_id=1, source_target_pairs={{0,4},{1,5},{2,6},{3,7},{4,0},{5,1},{6,2},{7,3},{8,12},{9,13},{10,... | collective-permute-start | bytes 786440 | tf_op jit(solution)/shard_map/ppermute | solution.py:61
  166.7 8.4 %collective-permute-start.20 = (f32[16,16,256]{2,1,0:T(8,128)S(1)}, f32[16,16,256]{2,1,0:T(8,128)S(1)}, u32[]{:S(2)}, u32[]{:S(2)}) collective-permute-start(f32[16,16,256]{2,1,0:T(8,128)S(1)} %get-tuple-element.45), channel_id=1, source_target_pairs={{0,4},{1,5},{2,6},{3,7},{4,0},{5,1},{6,2},{7,3},{8,12},{9,13},{10,... | collective-permute-start | bytes 786440 | tf_op jit(solution)/shard_map/ppermute | solution.py:61
  172.7 13.7 %collective-permute-start.14 = (f32[32,16,256]{2,1,0:T(8,128)S(1)}, f32[32,16,256]{2,1,0:T(8,128)S(1)}, u32[]{:S(2)}, u32[]{:S(2)}) collective-permute-start(f32[32,16,256]{2,1,0:T(8,128)S(1)} %get-tuple-element.41), channel_id=1, source_target_pairs={{0,32},{16,48},{32,0},{48,16},{64,96},{80,112},{96,64},{112,80},{1... | collective-permute-start | bytes 1572872 | tf_op jit(solution)/shard_map/ppermute | solution.py:61
  175.9 16.1 %collective-permute-start.21 = (f32[32,16,256]{2,1,0:T(8,128)S(1)}, f32[32,16,256]{2,1,0:T(8,128)S(1)}, u32[]{:S(2)}, u32[]{:S(2)}) collective-permute-start(f32[32,16,256]{2,1,0:T(8,128)S(1)} %get-tuple-element.38), channel_id=1, source_target_pairs={{0,32},{16,48},{32,0},{48,16},{64,96},{80,112},{96,64},{112,80},{1... | collective-permute-start | bytes 1572872 | tf_op jit(solution)/shard_map/ppermute | solution.py:61
  187.3 5.7 %copy-start.1 = (f32[128,16,256]{2,1,0:T(8,128)}, f32[128,16,256]{2,1,0:T(8,128)S(1)}, u32[]{:S(2)}) copy-start(f32[128,16,256]{2,1,0:T(8,128)S(1)} %get-tuple-element.35) | copy-start | bytes 6291460
  187.3 6.3 %collective-permute-start.15 = (f32[64,16,256]{2,1,0:T(8,128)}, f32[64,16,256]{2,1,0:T(8,128)S(1)}, u32[]{:S(2)}, u32[]{:S(2)}) collective-permute-start(f32[64,16,256]{2,1,0:T(8,128)} %get-tuple-element.34), channel_id=1, source_target_pairs={{0,16},{16,0},{32,48},{48,32},{64,80},{80,64},{96,112},{112,96},{1... | collective-permute-start | bytes 3145736 | tf_op jit(solution)/shard_map/ppermute | solution.py:61
  192.9 3.0 %collective-permute-start.22 = (f32[64,16,256]{2,1,0:T(8,128)}, f32[64,16,256]{2,1,0:T(8,128)}, u32[]{:S(2)}, u32[]{:S(2)}) collective-permute-start(f32[64,16,256]{2,1,0:T(8,128)} %get-tuple-element.32), channel_id=1, source_target_pairs={{0,16},{16,0},{32,48},{48,32},{64,80},{80,64},{96,112},{112,96},{1... | collective-permute-start | bytes 3145736 | tf_op jit(solution)/shard_map/ppermute | solution.py:61
  197.2 1.3 copy-start

commit v17 on v16

--- a/solution.py
+++ b/solution.py
@@ -114,7 +114,7 @@
             flux_ref[c] += weight_ref[c, lev] * core
         return carry
 
-    lax.fori_loop(0, levels, level, 0, unroll=8)
+    lax.fori_loop(0, levels, level, 0, unroll=16)
 
 
 def diffuse(field, atm_kappa, vert_weight):

time: 214 us -> 214 us (level)
  no operation moved by 1% of the time
where the time goes in v17:
time: 214 us; the launch traced here: 211 us
  Pallas kernels  69.9 us (33%)
  starting transfers between devices  43.5 us (20%)
  waiting for transfers between devices  42.2 us (20%)
  local copies, waits for them, and re-layouts  40.5 us (19%)
  other arithmetic  11.2 us (5%)
  matrix products  3.04 us (1%)
    pallas_call x1, Pallas kernels, diffuse(): pl.pallas_call(functools.partial(diffusion_kernel, count_gy * rows, count...  56.8 us
    ppermute x14, waiting for transfers between devices, stack_gather(): other = lax.ppermute(x, axis, [(j, j ^ distance) for j in range(size)])  24.7 us
    ppermute x14, starting transfers between devices, stack_gather(): other = lax.ppermute(x, axis, [(j, j ^ distance) for j in range(size)])  20.9 us
    unnamed x27, local copies, waits for them, and re-layouts  13.9 us
    pallas_call x1, Pallas kernels, solve_grid(): pl.pallas_call(functools.partial(cg_kernel, rounds), in_specs=[pl.BlockSp...  13.1 us
    ppermute x1, waiting for transfers between devices, diffuse(): south_east = lax.ppermute(field[:, :HALO, :HALO], both, pairs(1, 1))  7.07 us
    ppermute x1, starting transfers between devices, diffuse(): lax.ppermute(field[:, rows - HALO:, cols - HALO:], both, pairs(-1, -1))  5.35 us
    ppermute x1, starting transfers between devices, diffuse(): south_west = lax.ppermute(field[:, :HALO, cols - HALO:], both, pairs(-1, 1))  4.98 us
  transfers between devices with their start and end apart: 23, of which 13 were waited for; matrix products, arithmetic and copies ran while one was open for 16% of the time, Pallas kernels for 0%

profile of v17, /device:TPU:6, one launch (start us, length us, event | category | flops | bytes accessed | tf_op | source)
XLA Modules:
  0.0 211.3 jit_solution(15184967603149209206)
XLA Ops:
  0.6 4.3 %fusion.19 = (f32[128,32,4]{2,1,0:T(8,128)S(1)}, f32[128,32,4]{2,1,0:T(8,128)}) fusion(f32[128,32,512]{2,1,0:T(8,128)} %core_ref.1), kind=kLoop, calls=%fused_computation.112 | loop fusion | bytes 262144 | tf_op jit(solution)/shard_map/slice | solution.py:140
  4.9 3.3 %copy.86 = f32[128,32,4]{0,1,2:T(8,128)} copy(f32[128,32,4]{2,1,0:T(8,128)} %get-tuple-element.31) | data formatting | bytes 131072
  8.2 2.4 %collective-permute-start.1 = (f32[128,32,4]{0,1,2:T(8,128)}, f32[128,32,4]{0,1,2:T(8,128)}, u32[]{:S(2)}, u32[]{:S(2)}) collective-permute-start(f32[128,32,4]{0,1,2:T(8,128)} %copy.86), channel_id=1, source_target_pairs={{0,16},{16,32},{32,48},{48,64},{64,80},{80,96},{96,112},{1,17},{17... | collective-permute-start | bytes 196616 | tf_op jit(solution)/shard_map/ppermute | solution.py:141
  10.5 1.9 copy.85
  12.5 1.3 collective-permute-start
  13.8 2.9 %fusion.18 = (f32[128,4,4]{2,1,0:T(4,128)}, f32[128,4,4]{2,1,0:T(4,128)}, f32[128,4,4]{2,1,0:T(4,128)}, f32[128,4,4]{2,1,0:T(4,128)}) fusion(f32[128,32,512]{2,1,0:T(8,128)} %core_ref.1), kind=kLoop, calls=%fused_computation.111 | loop fusion | bytes 65536 | tf_op jit(solution)/shard_map/slice | solution.py:142
  16.6 5.4 %collective-permute-start.7 = (f32[128,4,4]{2,1,0:T(4,128)}, f32[128,4,4]{2,1,0:T(4,128)S(1)}, u32[]{:S(2)}, u32[]{:S(2)}) collective-permute-start(f32[128,4,4]{2,1,0:T(4,128)} %get-tuple-element.29), channel_id=1, source_target_pairs={{0,17},{1,18},{2,19},{3,20},{4,21},{5,22},{6,23},{7,24},{8,25},{9,... | collective-permute-start | bytes 24584 | tf_op jit(solution)/shard_map/ppermute | solution.py:145
  22.0 4.1 %fusion.17 = (f32[128,4,512]{2,1,0:T(4,128)}, f32[128,4,512]{2,1,0:T(4,128)}) fusion(f32[128,32,512]{2,1,0:T(8,128)} %core_ref.1), kind=kLoop, calls=%fused_computation.110 | loop fusion | bytes 4194304 | tf_op jit(solution)/shard_map/slice | solution.py:138
  26.1 3.4 %collective-permute-start.5 = (f32[128,4,512]{2,1,0:T(4,128)}, f32[128,4,512]{2,1,0:T(4,128)S(1)}, u32[]{:S(2)}, u32[]{:S(2)}) collective-permute-start(f32[128,4,512]{2,1,0:T(4,128)} %get-tuple-element.25), channel_id=1, source_target_pairs={{0,1},{1,2},{2,3},{3,4},{4,5},{5,6},{6,7},{7,8},{8,9},{9,10},{10,1... | collective-permute-start | bytes 3145736 | tf_op jit(solution)/shard_map/ppermute | solution.py:139
  29.5 2.4 %collective-permute-start.2 = (f32[128,4,512]{2,1,0:T(4,128)}, f32[128,4,512]{2,1,0:T(4,128)}, u32[]{:S(2)}, u32[]{:S(2)}) collective-permute-start(f32[128,4,512]{2,1,0:T(4,128)} %get-tuple-element.24), channel_id=1, source_target_pairs={{1,0},{2,1},{3,2},{4,3},{5,4},{6,5},{7,6},{8,7},{9,8},{10,9},{11,1... | collective-permute-start | bytes 3145736 | tf_op jit(solution)/shard_map/ppermute | solution.py:138
  32.0 0.6 copy.71
  32.6 1.6 reshape.208
  36.4 0.7 pad_add_fusion.index_ref
  37.1 1.3 collective-permute-start.6
  38.4 2.7 %copy.69 = f32[128,32,4]{2,1,0:T(8,128)S(1)} copy(f32[128,32,4]{0,1,2:T(8,128)} %collective-permute-done.1) | data formatting | bytes 131072 | tf_op jit(solution)/shard_map/ppermute | solution.py:141
  41.2 5.0 %collective-permute-start.4 = (f32[128,4,4]{2,1,0:T(4,128)}, f32[128,4,4]{2,1,0:T(4,128)}, u32[]{:S(2)}, u32[]{:S(2)}) collective-permute-start(f32[128,4,4]{2,1,0:T(4,128)} %get-tuple-element.27), channel_id=1, source_target_pairs={{1,16},{2,17},{3,18},{4,19},{5,20},{6,21},{7,22},{8,23},{9,24},{10... | collective-permute-start | bytes 24584 | tf_op jit(solution)/shard_map/ppermute | solution.py:143
  46.2 2.9 %copy.68 = f32[128,32,4]{2,1,0:T(8,128)} copy(f32[128,32,4]{0,1,2:T(8,128)S(1)} %collective-permute-done) | data formatting | bytes 131072 | tf_op jit(solution)/shard_map/ppermute | solution.py:140
  49.0 1.5 collective-permute-start.3
  50.5 3.5 %pad_maximum_fusion.lanes_ref = f32[128,32,128]{2,1,0:T(8,128)} fusion(f32[128,32,4]{2,1,0:T(8,128)S(1)} %copy.69, f32[128,32,4]{2,1,0:T(8,128)} %copy.68, f32[128]{0:T(128)S(1)} %pad.29.clone), kind=kLoop, calls=%fused_computation.4 | loop fusion | flops 1048576 | bytes 2228736 | tf_op jit(solution)/shard_map/concatenate | solution.py:147
  54.0 3.1 %collective-permute-done.6 = f32[128,4,4]{2,1,0:T(4,128)} collective-permute-done((f32[128,4,4]{2,1,0:T(4,128)}, f32[128,4,4]{2,1,0:T(4,128)}, u32[]{:S(2)}, u32[]{:S(2)}) %collective-permute-start.6) | collective-permute-done | bytes 8224 | tf_op jit(solution)/shard_map/ppermute | solution.py:144
  57.1 4.0 %collective-permute-done.4 = f32[128,4,4]{2,1,0:T(4,128)} collective-permute-done((f32[128,4,4]{2,1,0:T(4,128)}, f32[128,4,4]{2,1,0:T(4,128)}, u32[]{:S(2)}, u32[]{:S(2)}) %collective-permute-start.4) | collective-permute-done | bytes 8224 | tf_op jit(solution)/shard_map/ppermute | solution.py:143
  61.1 7.1 %collective-permute-done.3 = f32[128,4,4]{2,1,0:T(4,128)S(1)} collective-permute-done((f32[128,4,4]{2,1,0:T(4,128)}, f32[128,4,4]{2,1,0:T(4,128)S(1)}, u32[]{:S(2)}, u32[]{:S(2)}) %collective-permute-start.3) | collective-permute-done | bytes 8224 | tf_op jit(solution)/shard_map/ppermute | solution.py:142
  68.2 3.9 %maximum_maximum_fusion.rows_ref = f32[128,8,640]{2,1,0:T(8,128)} fusion(f32[128,4,4]{2,1,0:T(4,128)S(1)} %collective-permute-done.7, f32[128,4,120]{2,1,0:T(4,128)S(1)} %broadcast_in_dim.50, f32[128,4,4]{2,1,0:T(4,128)} %collective-permute-done.6, f32[128,4,512]{2,1,0:T(4,128)S(1)} %collective-permute-done.5, f32[128,4,4]{2,1,0:T(4,128)} %collective-permute-done.4, ...), kind=kLoop, calls=%fused_computation.3 | loop fusion | flops 4587520 | bytes 4997120 | tf_op jit(solution)/shard_map/concatenate | solution.py:149
  72.1 56.8 %shard_map.111 = (f32[128,32,512]{2,1,0:T(8,128)}, f32[4,32,512]{2,1,0:T(8,128)}) custom-call(f32[128]{0:T(128)} %kappa_ref.1, f32[4,128]{1,0:T(4,128)} %weight_ref.1, f32[128,32,512]{2,1,0:T(8,128)} %core_ref.1, f32[128,32,128]{2,1,0:T(8,128)} %pad_maximum_fusion.lanes_ref, f32[128,8,640]{2,1,0:T(8,128)} %maximum_maximum_fusion.rows_ref, ...), custom_call_target="tpu_custom_call" | custom-call | flops 131072000 | bytes 16777216 | tf_op jit(solution)/shard_map/pallas_call | solution.py:161
  128.9 1.0 convert_element_type.36
  130.0 0.6 gather_fusion.1
  131.0 0.8 gather_fusion
  131.8 3.3 %collective-permute-done.8 = bf16[32,4,128]{2,1,0:T(4,128)(2,1)S(1)} collective-permute-done((bf16[32,4,128]{2,1,0:T(4,128)(2,1)S(1)}, bf16[32,4,128]{2,1,0:T(4,128)(2,1)S(1)}, u32[]{:S(2)}, u32[]{:S(2)}) %collective-permute-start.8) | collective-permute-done | bytes 32800 | tf_op jit(solution)/shard_map/ppermute | solution.py:29
  135.1 0.7 gather_fusion.2
  135.9 3.0 %convolution_bitcast_fusion = f32[4,32,128]{2,0,1:T(4,128)S(1)} fusion(bf16[32,4,128,128]{3,2,1,0:T(8,128)(2,1)} %param.13, bf16[32,4,4,128]{3,2,1,0:T(4,128)(2,1)S(1)} %bitcast.37, bf16[32,4,4,128]{3,2,1,0:T(4,128)(2,1)S(1)} %bitcast.38, pred[32,4]{1,0:T(8,128)(4,1)S(1)} %and.77, pred[32,4]{1,0:T(8,128)(4,1)S(1)} %and.73), kind=kOutput, calls=%fused_computation.5 | convolution fusion | flops 16908288 | bytes 4522240 | tf_op jit(solution)/shard_map/bkij,bkcj->cbi/dot_general | solution.py:357
  139.0 0.6 constant_dynamic-update-slice_fusion.43
  139.7 3.5 %collective-permute-start.16 = (f32[1,16,256]{2,1,0:T(8,128)S(1)}, f32[1,16,256]{2,1,0:T(8,128)S(1)}, u32[]{:S(2)}, u32[]{:S(2)}) collective-permute-start(f32[1,16,256]{2,1,0:T(8,128)S(1)} %get-tuple-element.15), channel_id=1, source_target_pairs={{0,2},{1,3},{2,0},{3,1},{4,6},{5,7},{6,4},{7,5},{8,10},{9,11},{10,... | collective-permute-start | bytes 49160 | tf_op jit(solution)/shard_map/ppermute | solution.py:61
  143.2 1.7 collective-permute-done.9
  144.9 2.9 %collective-permute-start.10 = (f32[2,16,256]{2,1,0:T(8,128)S(1)}, f32[2,16,256]{2,1,0:T(8,128)S(1)}, u32[]{:S(2)}, u32[]{:S(2)}) collective-permute-start(f32[2,16,256]{2,1,0:T(8,128)S(1)} %pad_maximum_fusion.5), channel_id=1, source_target_pairs={{0,8},{1,9},{2,10},{3,11},{4,12},{5,13},{6,14},{7,15},{8,0},{9,1},... | collective-permute-start | bytes 98312 | tf_op jit(solution)/shard_map/ppermute | solution.py:61
  147.8 0.6 collective-permute-start.17
  148.4 0.6 constant_dynamic-update-slice_fusion.16
  149.1 0.6 constant_dynamic-update-slice_fusion.42
  149.7 0.7 collective-permute-done.10
  150.3 4.4 %collective-permute-start.11 = (f32[4,16,256]{2,1,0:T(8,128)S(1)}, f32[4,16,256]{2,1,0:T(8,128)S(1)}, u32[]{:S(2)}, u32[]{:S(2)}) collective-permute-start(f32[4,16,256]{2,1,0:T(8,128)S(1)} %pad_maximum_fusion.3), channel_id=1, source_target_pairs={{0,64},{16,80},{32,96},{48,112},{64,0},{80,16},{96,32},{112,48},{1... | collective-permute-start | bytes 196616 | tf_op jit(solution)/shard_map/ppermute | solution.py:61
  154.7 2.7 %collective-permute-start.18 = (f32[4,16,256]{2,1,0:T(8,128)S(1)}, f32[4,16,256]{2,1,0:T(8,128)S(1)}, u32[]{:S(2)}, u32[]{:S(2)}) collective-permute-start(f32[4,16,256]{2,1,0:T(8,128)S(1)} %pad_maximum_fusion.4), channel_id=1, source_target_pairs={{0,64},{16,80},{32,96},{48,112},{64,0},{80,16},{96,32},{112,48},{1... | collective-permute-start | bytes 196616 | tf_op jit(solution)/shard_map/ppermute | solution.py:61
  157.4 0.6 constant_dynamic-update-slice_fusion.15
  158.0 0.6 constant_dynamic-update-slice_fusion.41
  158.8 1.8 collective-permute-done.18
  160.9 0.6 constant_dynamic-update-slice_fusion.14
  161.5 2.2 %collective-permute-done.12 = f32[8,16,256]{2,1,0:T(8,128)S(1)} collective-permute-done((f32[8,16,256]{2,1,0:T(8,128)S(1)}, f32[8,16,256]{2,1,0:T(8,128)S(1)}, u32[]{:S(2)}, u32[]{:S(2)}) %collective-permute-start.12) | collective-permute-done | bytes 131104 | tf_op jit(solution)/shard_map/ppermute | solution.py:61
  163.7 0.7 constant_dynamic-update-slice_fusion.13
  165.0 0.6 constant_dynamic-update-slice_fusion.40
  165.7 0.7 constant_dynamic-update-slice_fusion.39
  166.3 1.4 collective-permute-start.20
  167.8 3.8 %collective-permute-done.13 = f32[16,16,256]{2,1,0:T(8,128)S(1)} collective-permute-done((f32[16,16,256]{2,1,0:T(8,128)S(1)}, f32[16,16,256]{2,1,0:T(8,128)S(1)}, u32[]{:S(2)}, u32[]{:S(2)}) %collective-permute-start.13) | collective-permute-done | bytes 262176 | tf_op jit(solution)/shard_map/ppermute | solution.py:61
  171.6 0.8 constant_dynamic-update-slice_fusion.12
  172.3 2.4 %collective-permute-start.14 = (f32[32,16,256]{2,1,0:T(8,128)S(1)}, f32[32,16,256]{2,1,0:T(8,128)S(1)}, u32[]{:S(2)}, u32[]{:S(2)}) collective-permute-start(f32[32,16,256]{2,1,0:T(8,128)S(1)} %get-tuple-element.41), channel_id=1, source_target_pairs={{0,32},{16,48},{32,0},{48,16},{64,96},{80,112},{96,64},{112,80},{1... | collective-permute-start | bytes 1572872 | tf_op jit(solution)/shard_map/ppermute | solution.py:61
  174.8 0.8 constant_dynamic-update-slice_fusion.38
  175.5 2.0 collective-permute-start.21
  177.6 8.5 %collective-permute-done.14 = f32[32,16,256]{2,1,0:T(8,128)S(1)} collective-permute-done((f32[32,16,256]{2,1,0:T(8,128)S(1)}, f32[32,16,256]{2,1,0:T(8,128)S(1)}, u32[]{:S(2)}, u32[]{:S(2)}) %collective-permute-start.14) | collective-permute-done | bytes 524320 | tf_op jit(solution)/shard_map/ppermute | solution.py:61
  186.0 0.9 constant_dynamic-update-slice_fusion.11
  186.9 4.7 %collective-permute-done.21 = f32[32,16,256]{2,1,0:T(8,128)S(1)} collective-permute-done((f32[32,16,256]{2,1,0:T(8,128)S(1)}, f32[32,16,256]{2,1,0:T(8,128)S(1)}, u32[]{:S(2)}, u32[]{:S(2)}) %collective-permute-start.21) | collective-permute-done | bytes 524320 | tf_op jit(solution)/shard_map/ppermute | solution.py:61
  191.7 0.9 constant_dynamic-update-slice_fusion.37
  192.6 0.6 reshape.210
  193.3 1.1 constant_dynamic-update-slice_fusion.18.rhs_stack
  194.3 1.3 collective-permute-done.22
  195.6 1.3 constant_dynamic-update-slice_fusion.44.coded_stack
  196.9 1.3 copy-done
  198.2 13.1 %shard_map.112 = (f32[16,256]{1,0:T(8,128)}, f32[16,256]{1,0:T(8,128)}) custom-call(s32[2]{0:T(128)} %pad_add_fusion.index_ref, f32[128,16,256]{2,1,0:T(8,128)} %constant_dynamic-update-slice_fusion.18.rhs_stack, f32[128,16,256]{2,1,0:T(8,128)} %copy-done), custom_call_target="tpu_custom_call" | custom-call | tf_op jit(solution)/shard_map/pallas_call | solution.py:291
  (71 shorter events, 3.8 us)
Async XLA Ops:
  8.2 29.0 %collective-permute-start.1 = (f32[128,32,4]{0,1,2:T(8,128)}, f32[128,32,4]{0,1,2:T(8,128)}, u32[]{:S(2)}, u32[]{:S(2)}) collective-permute-start(f32[128,32,4]{0,1,2:T(8,128)} %copy.86), channel_id=1, source_target_pairs={{0,16},{16,32},{32,48},{48,64},{64,80},{80,96},{96,112},{1,17},{17... | collective-permute-start | bytes 196616 | tf_op jit(solution)/shard_map/ppermute | solution.py:141
  12.5 28.7 %collective-permute-start = (f32[128,32,4]{0,1,2:T(8,128)}, f32[128,32,4]{0,1,2:T(8,128)S(1)}, u32[]{:S(2)}, u32[]{:S(2)}) collective-permute-start(f32[128,32,4]{0,1,2:T(8,128)} %copy.85), channel_id=1, source_target_pairs={{16,0},{32,16},{48,32},{64,48},{80,64},{96,80},{112,96},{17,1},{33... | collective-permute-start | bytes 196616 | tf_op jit(solution)/shard_map/ppermute | solution.py:140
  16.6 15.3 %copy-start.2 = (s32[4096,4]{0,1:T(4,128)S(1)}, s32[4096,4]{0,1:T(4,128)}, u32[]{:S(2)}) copy-start(s32[4096,4]{0,1:T(4,128)} %param.11) | copy-start | bytes 196612
  16.6 32.4 %collective-permute-start.7 = (f32[128,4,4]{2,1,0:T(4,128)}, f32[128,4,4]{2,1,0:T(4,128)S(1)}, u32[]{:S(2)}, u32[]{:S(2)}) collective-permute-start(f32[128,4,4]{2,1,0:T(4,128)} %get-tuple-element.29), channel_id=1, source_target_pairs={{0,17},{1,18},{2,19},{3,20},{4,21},{5,22},{6,23},{7,24},{8,25},{9,... | collective-permute-start | bytes 24584 | tf_op jit(solution)/shard_map/ppermute | solution.py:145
  26.1 42.1 %collective-permute-start.5 = (f32[128,4,512]{2,1,0:T(4,128)}, f32[128,4,512]{2,1,0:T(4,128)S(1)}, u32[]{:S(2)}, u32[]{:S(2)}) collective-permute-start(f32[128,4,512]{2,1,0:T(4,128)} %get-tuple-element.25), channel_id=1, source_target_pairs={{0,1},{1,2},{2,3},{3,4},{4,5},{5,6},{6,7},{7,8},{8,9},{9,10},{10,1... | collective-permute-start | bytes 3145736 | tf_op jit(solution)/shard_map/ppermute | solution.py:139
  29.5 38.7 %collective-permute-start.2 = (f32[128,4,512]{2,1,0:T(4,128)}, f32[128,4,512]{2,1,0:T(4,128)}, u32[]{:S(2)}, u32[]{:S(2)}) collective-permute-start(f32[128,4,512]{2,1,0:T(4,128)} %get-tuple-element.24), channel_id=1, source_target_pairs={{1,0},{2,1},{3,2},{4,3},{5,4},{6,5},{7,6},{8,7},{9,8},{10,9},{11,1... | collective-permute-start | bytes 3145736 | tf_op jit(solution)/shard_map/ppermute | solution.py:138
  32.0 2.5 %copy-start.3 = (s32[4096]{0:T(1024)S(1)}, s32[4096]{0:T(1024)}, u32[]{:S(2)}) copy-start(s32[4096]{0:T(1024)} %param.12) | copy-start | bytes 49156
  37.1 20.0 %collective-permute-start.6 = (f32[128,4,4]{2,1,0:T(4,128)}, f32[128,4,4]{2,1,0:T(4,128)}, u32[]{:S(2)}, u32[]{:S(2)}) collective-permute-start(f32[128,4,4]{2,1,0:T(4,128)} %get-tuple-element.28), channel_id=1, source_target_pairs={{16,1},{17,2},{18,3},{19,4},{20,5},{21,6},{22,7},{23,8},{24,9},{25... | collective-permute-start | bytes 24584 | tf_op jit(solution)/shard_map/ppermute | solution.py:144
  41.2 19.9 %collective-permute-start.4 = (f32[128,4,4]{2,1,0:T(4,128)}, f32[128,4,4]{2,1,0:T(4,128)}, u32[]{:S(2)}, u32[]{:S(2)}) collective-permute-start(f32[128,4,4]{2,1,0:T(4,128)} %get-tuple-element.27), channel_id=1, source_target_pairs={{1,16},{2,17},{3,18},{4,19},{5,20},{6,21},{7,22},{8,23},{9,24},{10... | collective-permute-start | bytes 24584 | tf_op jit(solution)/shard_map/ppermute | solution.py:143
  49.0 19.1 %collective-permute-start.3 = (f32[128,4,4]{2,1,0:T(4,128)}, f32[128,4,4]{2,1,0:T(4,128)S(1)}, u32[]{:S(2)}, u32[]{:S(2)}) collective-permute-start(f32[128,4,4]{2,1,0:T(4,128)} %get-tuple-element.26), channel_id=1, source_target_pairs={{17,0},{18,1},{19,2},{20,3},{21,4},{22,5},{23,6},{24,7},{25,8},{26... | collective-permute-start | bytes 24584 | tf_op jit(solution)/shard_map/ppermute | solution.py:142
  130.8 4.4 %collective-permute-start.8 = (bf16[32,4,128]{2,1,0:T(4,128)(2,1)S(1)}, bf16[32,4,128]{2,1,0:T(4,128)(2,1)S(1)}, u32[]{:S(2)}, u32[]{:S(2)}) collective-permute-start(bf16[32,4,128]{2,1,0:T(4,128)(2,1)S(1)} %broadcast_multiply_fusion), channel_id=1, source_target_pairs={{0,112},{16,0},{32,16},{48,32},{64,48},{80,64},{96,80},{112,96},{1... | collective-permute-start | bytes 98312 | tf_op jit(solution)/shard_map/ppermute | solution.py:29
  135.9 3.1 %copy-start.4 = (f32[16,256]{1,0:T(8,128)S(1)}, f32[16,256]{1,0:T(8,128)}, u32[]{:S(2)}) copy-start(f32[16,256]{1,0:T(8,128)} %param.15) | copy-start | bytes 49156
  135.9 3.1 %copy-start.5 = (s32[16,256]{1,0:T(8,128)S(1)}, s32[16,256]{1,0:T(8,128)}, u32[]{:S(2)}) copy-start(s32[16,256]{1,0:T(8,128)} %param.14) | copy-start | bytes 49156
  139.7 5.2 %collective-permute-start.9 = (f32[1,16,256]{2,1,0:T(8,128)S(1)}, f32[1,16,256]{2,1,0:T(8,128)S(1)}, u32[]{:S(2)}, u32[]{:S(2)}) collective-permute-start(f32[1,16,256]{2,1,0:T(8,128)S(1)} %get-tuple-element.80), channel_id=1, source_target_pairs={{0,2},{1,3},{2,0},{3,1},{4,6},{5,7},{6,4},{7,5},{8,10},{9,11},{10,... | collective-permute-start | bytes 49160 | tf_op jit(solution)/shard_map/ppermute | solution.py:61
  139.7 8.1 %collective-permute-start.16 = (f32[1,16,256]{2,1,0:T(8,128)S(1)}, f32[1,16,256]{2,1,0:T(8,128)S(1)}, u32[]{:S(2)}, u32[]{:S(2)}) collective-permute-start(f32[1,16,256]{2,1,0:T(8,128)S(1)} %get-tuple-element.15), channel_id=1, source_target_pairs={{0,2},{1,3},{2,0},{3,1},{4,6},{5,7},{6,4},{7,5},{8,10},{9,11},{10,... | collective-permute-start | bytes 49160 | tf_op jit(solution)/shard_map/ppermute | solution.py:61
  144.9 5.4 %collective-permute-start.10 = (f32[2,16,256]{2,1,0:T(8,128)S(1)}, f32[2,16,256]{2,1,0:T(8,128)S(1)}, u32[]{:S(2)}, u32[]{:S(2)}) collective-permute-start(f32[2,16,256]{2,1,0:T(8,128)S(1)} %pad_maximum_fusion.5), channel_id=1, source_target_pairs={{0,8},{1,9},{2,10},{3,11},{4,12},{5,13},{6,14},{7,15},{8,0},{9,1},... | collective-permute-start | bytes 98312 | tf_op jit(solution)/shard_map/ppermute | solution.py:61
  147.8 6.9 %collective-permute-start.17 = (f32[2,16,256]{2,1,0:T(8,128)S(1)}, f32[2,16,256]{2,1,0:T(8,128)S(1)}, u32[]{:S(2)}, u32[]{:S(2)}) collective-permute-start(f32[2,16,256]{2,1,0:T(8,128)S(1)} %pad_maximum_fusion.6), channel_id=1, source_target_pairs={{0,8},{1,9},{2,10},{3,11},{4,12},{5,13},{6,14},{7,15},{8,0},{9,1},... | collective-permute-start | bytes 98312 | tf_op jit(solution)/shard_map/ppermute | solution.py:61
  150.3 8.3 %collective-permute-start.11 = (f32[4,16,256]{2,1,0:T(8,128)S(1)}, f32[4,16,256]{2,1,0:T(8,128)S(1)}, u32[]{:S(2)}, u32[]{:S(2)}) collective-permute-start(f32[4,16,256]{2,1,0:T(8,128)S(1)} %pad_maximum_fusion.3), channel_id=1, source_target_pairs={{0,64},{16,80},{32,96},{48,112},{64,0},{80,16},{96,32},{112,48},{1... | collective-permute-start | bytes 196616 | tf_op jit(solution)/shard_map/ppermute | solution.py:61
  154.7 5.8 %collective-permute-start.18 = (f32[4,16,256]{2,1,0:T(8,128)S(1)}, f32[4,16,256]{2,1,0:T(8,128)S(1)}, u32[]{:S(2)}, u32[]{:S(2)}) collective-permute-start(f32[4,16,256]{2,1,0:T(8,128)S(1)} %pad_maximum_fusion.4), channel_id=1, source_target_pairs={{0,64},{16,80},{32,96},{48,112},{64,0},{80,16},{96,32},{112,48},{1... | collective-permute-start | bytes 196616 | tf_op jit(solution)/shard_map/ppermute | solution.py:61
  158.7 5.0 %collective-permute-start.12 = (f32[8,16,256]{2,1,0:T(8,128)S(1)}, f32[8,16,256]{2,1,0:T(8,128)S(1)}, u32[]{:S(2)}, u32[]{:S(2)}) collective-permute-start(f32[8,16,256]{2,1,0:T(8,128)S(1)} %pad_maximum_fusion.1), channel_id=1, source_target_pairs={{0,1},{1,0},{2,3},{3,2},{4,5},{5,4},{6,7},{7,6},{8,9},{9,8},{10,11... | collective-permute-start | bytes 393224 | tf_op jit(solution)/shard_map/ppermute | solution.py:61
  160.6 5.0 %collective-permute-start.19 = (f32[8,16,256]{2,1,0:T(8,128)S(1)}, f32[8,16,256]{2,1,0:T(8,128)S(1)}, u32[]{:S(2)}, u32[]{:S(2)}) collective-permute-start(f32[8,16,256]{2,1,0:T(8,128)S(1)} %pad_maximum_fusion.2), channel_id=1, source_target_pairs={{0,1},{1,0},{2,3},{3,2},{4,5},{5,4},{6,7},{7,6},{8,9},{9,8},{10,11... | collective-permute-start | bytes 393224 | tf_op jit(solution)/shard_map/ppermute | solution.py:61
  164.4 7.2 %collective-permute-start.13 = (f32[16,16,256]{2,1,0:T(8,128)S(1)}, f32[16,16,256]{2,1,0:T(8,128)S(1)}, u32[]{:S(2)}, u32[]{:S(2)}) collective-permute-start(f32[16,16,256]{2,1,0:T(8,128)S(1)} %get-tuple-element.49), channel_id=1, source_target_pairs={{0,4},{1,5},{2,6},{3,7},{4,0},{5,1},{6,2},{7,3},{8,12},{9,13},{10,... | collective-permute-start | bytes 786440 | tf_op jit(solution)/shard_map/ppermute | solution.py:61
  166.3 8.4 %collective-permute-start.20 = (f32[16,16,256]{2,1,0:T(8,128)S(1)}, f32[16,16,256]{2,1,0:T(8,128)S(1)}, u32[]{:S(2)}, u32[]{:S(2)}) collective-permute-start(f32[16,16,256]{2,1,0:T(8,128)S(1)} %get-tuple-element.45), channel_id=1, source_target_pairs={{0,4},{1,5},{2,6},{3,7},{4,0},{5,1},{6,2},{7,3},{8,12},{9,13},{10,... | collective-permute-start | bytes 786440 | tf_op jit(solution)/shard_map/ppermute | solution.py:61
  172.3 13.7 %collective-permute-start.14 = (f32[32,16,256]{2,1,0:T(8,128)S(1)}, f32[32,16,256]{2,1,0:T(8,128)S(1)}, u32[]{:S(2)}, u32[]{:S(2)}) collective-permute-start(f32[32,16,256]{2,1,0:T(8,128)S(1)} %get-tuple-element.41), channel_id=1, source_target_pairs={{0,32},{16,48},{32,0},{48,16},{64,96},{80,112},{96,64},{112,80},{1... | collective-permute-start | bytes 1572872 | tf_op jit(solution)/shard_map/ppermute | solution.py:61
  175.5 16.1 %collective-permute-start.21 = (f32[32,16,256]{2,1,0:T(8,128)S(1)}, f32[32,16,256]{2,1,0:T(8,128)S(1)}, u32[]{:S(2)}, u32[]{:S(2)}) collective-permute-start(f32[32,16,256]{2,1,0:T(8,128)S(1)} %get-tuple-element.38), channel_id=1, source_target_pairs={{0,32},{16,48},{32,0},{48,16},{64,96},{80,112},{96,64},{112,80},{1... | collective-permute-start | bytes 1572872 | tf_op jit(solution)/shard_map/ppermute | solution.py:61
  186.9 5.7 %copy-start.1 = (f32[128,16,256]{2,1,0:T(8,128)}, f32[128,16,256]{2,1,0:T(8,128)S(1)}, u32[]{:S(2)}) copy-start(f32[128,16,256]{2,1,0:T(8,128)S(1)} %get-tuple-element.35) | copy-start | bytes 6291460
  186.9 6.3 %collective-permute-start.15 = (f32[64,16,256]{2,1,0:T(8,128)}, f32[64,16,256]{2,1,0:T(8,128)S(1)}, u32[]{:S(2)}, u32[]{:S(2)}) collective-permute-start(f32[64,16,256]{2,1,0:T(8,128)} %get-tuple-element.34), channel_id=1, source_target_pairs={{0,16},{16,0},{32,48},{48,32},{64,80},{80,64},{96,112},{112,96},{1... | collective-permute-start | bytes 3145736 | tf_op jit(solution)/shard_map/ppermute | solution.py:61
  192.6 3.0 %collective-permute-start.22 = (f32[64,16,256]{2,1,0:T(8,128)}, f32[64,16,256]{2,1,0:T(8,128)}, u32[]{:S(2)}, u32[]{:S(2)}) collective-permute-start(f32[64,16,256]{2,1,0:T(8,128)} %get-tuple-element.32), channel_id=1, source_target_pairs={{0,16},{16,0},{32,48},{48,32},{64,80},{80,64},{96,112},{112,96},{1... | collective-permute-start | bytes 3145736 | tf_op jit(solution)/shard_map/ppermute | solution.py:61
  196.9 1.3 copy-start
